TPU v7x, 256 devices: a whole 4x4x8 slice. The times are simulated.
256 devices in a mesh: band: 8 (over y, x_hi), chan: 32 (over x_lo, z, core).
Axes of the slice: x: 4 (x_hi: 2, x_lo: 2; x = x_hi * 2 + x_lo), y: 4, z: 8, core: 2. Of those that a mesh axis runs over, the one named last changes fastest.
Arguments:
- spectra: bfloat16 [2, 64, 512, 8192], P(None, 'band', None, 'chan'), may hold values from -800 to 800
- valid_mask: int32 [512, 8192], P(None, 'chan'), may hold values 0 or 1
Outputs:
- cross_stack: bfloat16 [4, 2, 64, 8192, 256], P(None, None, 'band', 'chan')
All inputs are finite; a program needn't handle non-finite values. No bound on the sum of `valid_mask` on one device may be relied on, other than what follows from the above.
Results may differ from a plain program's by a relative error of at most 0.0053.
Values may be sent and summed in bfloat16 or wider, within the bound.
No kernel may reach another device: no remote copies, remote signals or barrier semaphores. Data moves between devices by JAX's collectives and lax.ppermute only.
A program may use at most 64 MiB of HBM per device.

v0:
```python
import math

import jax
import jax.numpy as jnp
from jax import lax
from jax.sharding import PartitionSpec as P

ROUNDS = 3


eps_energy = 1e-06


def passed_along(value, axis, steps):
    count = lax.axis_size(axis)
    pairs = [(source, (source + steps) % count) for source in range(count)]
    return lax.ppermute(value, axis, pairs)


def cross_block(own_block, partner, scale):
    flipped = jnp.stack([partner[1], -partner[0]])
    real_part = jnp.einsum("pfwa,pfwb->fab", own_block, partner, preferred_element_type=jnp.float32)
    imag_part = jnp.einsum("pfwa,pfwb->fab", own_block, flipped, preferred_element_type=jnp.float32)
    return (jnp.stack([real_part, imag_part]) * scale).astype(jnp.bfloat16)


def shards(spectra, valid_mask):
    values = spectra.astype(jnp.float32)
    partial_energy = jnp.sum(values * values, axis=(0, 1))
    total_bins = spectra.shape[1] * lax.axis_size("band")
    scale = 1.0 / math.sqrt(spectra.shape[2])
    far_count = ROUNDS
    energy = lax.psum(partial_energy, "band")
    window_gain = valid_mask.astype(jnp.float32) / jnp.sqrt(energy / total_bins + eps_energy)
    whitened = (values * window_gain).astype(jnp.bfloat16)
    outputs = [cross_block(whitened, whitened, scale)]
    partners = [whitened]
    carried = whitened
    for round_idx in range(1, far_count + 1):
        carried = passed_along(carried, "chan", 1)
        partners.append(carried)
        outputs.append(cross_block(whitened, carried, scale))
    return jnp.stack(outputs)


def solution(mesh):
    placed = (P(None, "band", None, "chan"), P(None, "chan"))
    return jax.shard_map(
        shards,
        mesh=mesh,
        in_specs=placed,
        out_specs=P(None, None, "band", "chan", None),
        check_vma=False,
    )
```

profile of v0, /device:TPU:4, one launch (start us, length us, event | category | flops | bytes accessed | tf_op | source)
XLA Modules:
  0.0 270.1 jit_solution(12627649000976831893)
XLA Ops:
  6.5 0.0 copy-start
  6.5 0.0 all-reduce.2.cloned.1.call-start
  6.5 3.9 %fusion = f32[512,256]{1,0:T(8,128)} fusion(bf16[2,8,512,256]{3,2,1,0:T(8,128)(2,1)} %param.2), kind=kLoop, calls=%fused_computation.2 | loop fusion | flops 6160384 | bytes 4718592 | tf_op jit(solution)/shard_map/reduce_sum | solution.py:29
  10.4 0.0 all-reduce.2.cloned.1.call-update
  10.5 90.3 %all-reduce.2.cloned.1.call-done = f32[512,256]{1,0:T(8,128)} async-done(((f32[512,256]{1,0:T(8,128)}), f32[512,256]{1,0:T(8,128)}) %all-reduce.2.cloned.1.call-update) | async-done | bytes 524304 | tf_op jit(solution)/shard_map/psum | solution.py:33
  100.8 0.0 copy-done
  100.8 1.1 rsqrt_multiply_fusion
  101.9 3.1 %fusion.1 = bf16[2,8,512,256]{3,2,0,1:T(8,128)(2,1)S(1)} fusion(f32[512,256]{1,0:T(8,128)S(1)} %rsqrt_multiply_fusion, bf16[2,8,512,256]{3,2,1,0:T(8,128)(2,1)} %param.2), kind=kLoop, calls=%fused_computation.3 | loop fusion | flops 6291456 | bytes 8912896 | tf_op jit(solution)/shard_map/convert_element_type | solution.py:35
  105.0 0.1 collective-permute-start
  105.1 50.0 %collective-permute-done = bf16[2,8,512,256]{3,2,0,1:T(8,128)(2,1)S(1)} collective-permute-done((bf16[2,8,512,256]{3,2,0,1:T(8,128)(2,1)S(1)}, bf16[2,8,512,256]{3,2,0,1:T(8,128)(2,1)S(1)}, u32[]{:S(2)}, u32[]{:S(2)}) %collective-permute-start) | collective-permute-done | bytes 4194336 | tf_op jit(solution)/shard_map/ppermute | solution.py:17
  155.1 0.0 collective-permute-start.1
  155.1 0.3 fusion.38
  155.4 49.8 %collective-permute-done.1 = bf16[2,8,512,256]{3,2,0,1:T(8,128)(2,1)S(1)} collective-permute-done((bf16[2,8,512,256]{3,2,0,1:T(8,128)(2,1)S(1)}, bf16[2,8,512,256]{3,2,0,1:T(8,128)(2,1)S(1)}, u32[]{:S(2)}, u32[]{:S(2)}) %collective-permute-start.1) | collective-permute-done | bytes 4194336 | tf_op jit(solution)/shard_map/ppermute | solution.py:17
  205.2 0.0 collective-permute-start.2
  205.2 1.6 fusion.31
  206.8 1.5 convolution_bitcast_fusion.3
  208.2 0.6 fusion.6
  208.8 0.3 fusion.39
  209.1 1.6 fusion.28
  210.7 1.5 convolution_bitcast_fusion.2
  212.2 0.6 fusion.11
  212.8 0.3 fusion.40
  213.1 1.6 fusion.25
  214.6 1.5 convolution_bitcast_fusion.1
  216.1 0.6 fusion.16
  216.7 38.5 %collective-permute-done.2 = bf16[2,8,512,256]{3,2,0,1:T(8,128)(2,1)S(1)} collective-permute-done((bf16[2,8,512,256]{3,2,0,1:T(8,128)(2,1)S(1)}, bf16[2,8,512,256]{3,2,0,1:T(8,128)(2,1)S(1)}, u32[]{:S(2)}, u32[]{:S(2)}) %collective-permute-start.2) | collective-permute-done | bytes 4194336 | tf_op jit(solution)/shard_map/ppermute | solution.py:17
  255.2 0.3 fusion.41
  255.5 1.8 fusion.22
  257.3 1.5 convolution_bitcast_fusion
  258.8 0.6 fusion.21
  259.4 3.9 %pad_maximum_fusion = bf16[4,2,8,256,256]{4,3,2,1,0:T(8,128)(2,1)} fusion(bf16[1,2,8,256,256]{4,3,2,1,0:T(8,128)(2,1)S(1)} %fusion.21, bf16[1,2,8,256,256]{4,3,2,1,0:T(8,128)(2,1)S(1)} %fusion.16, bf16[1,2,8,256,256]{4,3,2,1,0:T(8,128)(2,1)S(1)} %fusion.11, bf16[1,2,8,256,256]{4,3,2,1,0:T(8,128)(2,1)S(1)} %fusion.6), kind=kLoop, calls=%fused_computation.4 | loop fusion | flops 12582912 | bytes 16777216 | tf_op jit(solution)/shard_map/stack | solution.py:43
Async XLA Ops:
  6.5 94.3 %copy-start = (s32[512,256]{1,0:T(8,128)S(1)}, s32[512,256]{1,0:T(8,128)}, u32[]{:S(2)}) copy-start(s32[512,256]{1,0:T(8,128)} %param.3) | copy-start | bytes 1572868
  6.5 94.3 %all-reduce.2.cloned.1.call-start = ((), (), s32[]{:S(2)}) async-start(), calls=%async_computation | async-start | bytes 1048576 | tf_op jit(solution)/shard_map/psum | solution.py:33
  105.0 50.1 %collective-permute-start = (bf16[2,8,512,256]{3,2,0,1:T(8,128)(2,1)S(1)}, bf16[2,8,512,256]{3,2,0,1:T(8,128)(2,1)S(1)}, u32[]{:S(2)}, u32[]{:S(2)}) collective-permute-start(bf16[2,8,512,256]{3,2,0,1:T(8,128)(2,1)S(1)} %fusion.1), channel_id=1, source_target_pairs={{0,1},{1,2},{2,3},{3,4},{4,5},{5,6},{6,7},{7,8},{8,9},{9,10},{10,1... | collective-permute-start | bytes 12582920 | tf_op jit(solution)/shard_map/ppermute | solution.py:17
  155.1 50.0 %collective-permute-start.1 = (bf16[2,8,512,256]{3,2,0,1:T(8,128)(2,1)S(1)}, bf16[2,8,512,256]{3,2,0,1:T(8,128)(2,1)S(1)}, u32[]{:S(2)}, u32[]{:S(2)}) collective-permute-start(bf16[2,8,512,256]{3,2,0,1:T(8,128)(2,1)S(1)} %collective-permute-done), channel_id=1, source_target_pairs={{0,1},{1,2},{2,3},{3,4},{4,5},{5,6},{6,7},{7,8},{8,9},{9,10},{10,1... | collective-permute-start | bytes 12582920 | tf_op jit(solution)/shard_map/ppermute | solution.py:17
  205.2 50.0 %collective-permute-start.2 = (bf16[2,8,512,256]{3,2,0,1:T(8,128)(2,1)S(1)}, bf16[2,8,512,256]{3,2,0,1:T(8,128)(2,1)S(1)}, u32[]{:S(2)}, u32[]{:S(2)}) collective-permute-start(bf16[2,8,512,256]{3,2,0,1:T(8,128)(2,1)S(1)} %collective-permute-done.1), channel_id=1, source_target_pairs={{0,1},{1,2},{2,3},{3,4},{4,5},{5,6},{6,7},{7,8},{8,9},{9,10},{10,1... | collective-permute-start | bytes 12582920 | tf_op jit(solution)/shard_map/ppermute | solution.py:17
Sparse Core Ops, SparseCore 0:
  10.6 90.1 all-reduce.1
where the time goes:
time: 273 us; the launch traced here: 270 us
  waiting for transfers between devices  229 us (84%)
  other arithmetic  15.4 us (6%)
  between operations  13.5 us (5%)
  matrix products  12.5 us (5%)
    ppermute x3, waiting for transfers between devices, passed_along(): return lax.ppermute(value, axis, pairs)  138 us
    psum x1, waiting for transfers between devices, shards(): energy = lax.psum(partial_energy, 'band')  90.3 us
    dot_general x4, matrix products, cross_block(): jnp.einsum('pfwa,pfwb->fab', own_block, flipped, preferred_element_type=j...  6.57 us
    dot_general x4, matrix products, cross_block(): jnp.einsum('pfwa,pfwb->fab', own_block, partner, preferred_element_type=j...  5.93 us
  transfers between devices with their start and end apart: 4, of which 4 were waited for; matrix products, arithmetic and copies ran while one was open for 4% of the time, Pallas kernels for 0%

commit v1 on v0

--- a/solution.py
+++ b/solution.py
@@ -24,22 +24,28 @@
     return (jnp.stack([real_part, imag_part]) * scale).astype(jnp.bfloat16)
 
 
+def whiten(raw, gain):
+    return (raw.astype(jnp.float32) * gain).astype(jnp.bfloat16)
+
+
 def shards(spectra, valid_mask):
     values = spectra.astype(jnp.float32)
     partial_energy = jnp.sum(values * values, axis=(0, 1))
     total_bins = spectra.shape[1] * lax.axis_size("band")
     scale = 1.0 / math.sqrt(spectra.shape[2])
-    far_count = ROUNDS
+    raws = [spectra]
+    for round_idx in range(ROUNDS):
+        raws.append(passed_along(raws[-1], "chan", 1))
     energy = lax.psum(partial_energy, "band")
     window_gain = valid_mask.astype(jnp.float32) / jnp.sqrt(energy / total_bins + eps_energy)
-    whitened = (values * window_gain).astype(jnp.bfloat16)
+    gains = [window_gain]
+    for round_idx in range(ROUNDS):
+        gains.append(passed_along(gains[-1], "chan", 1))
+    whitened = whiten(spectra, window_gain)
     outputs = [cross_block(whitened, whitened, scale)]
-    partners = [whitened]
-    carried = whitened
-    for round_idx in range(1, far_count + 1):
-        carried = passed_along(carried, "chan", 1)
-        partners.append(carried)
-        outputs.append(cross_block(whitened, carried, scale))
+    for round_idx in range(1, ROUNDS + 1):
+        partner = whiten(raws[round_idx], gains[round_idx])
+        outputs.append(cross_block(whitened, partner, scale))
     return jnp.stack(outputs)
 
 

time: 273 us -> 278 us (1.018)
  other arithmetic: 15.4 us -> 20.1 us
  waiting for transfers between devices: 229 us -> 226 us
    ppermute x3 -> x6, waiting for transfers between devices: 138 us -> 108 us  [passed_along(): return lax.ppermute(value, axis, pairs)]
    psum x1, waiting for transfers between devices: 90.3 us -> 118 us  [shards(): energy = lax.psum(partial_energy, 'band')]
    convert_element_type x1 -> x4, other arithmetic: 3.06 us -> 10.1 us  [whiten(): return (raw.astype(jnp.float32) * gain).astype(jnp.bfloat16)]
  transfers between devices with their start and end apart: 4 -> 7, of which waited for: 4 -> 5; matrix products, arithmetic and copies ran while one was open for 4% -> 9% of each run, Pallas kernels for 0% -> 0%
where the time goes in v1:
time: 278 us; the launch traced here: 275 us
  waiting for transfers between devices  226 us (81%)
  other arithmetic  20.1 us (7%)
  between operations  13.6 us (5%)
  matrix products  12.3 us (4%)
    psum x1, waiting for transfers between devices, shards(): energy = lax.psum(partial_energy, 'band')  118 us
    ppermute x6, waiting for transfers between devices, passed_along(): return lax.ppermute(value, axis, pairs)  108 us
    convert_element_type x4, other arithmetic, whiten(): return (raw.astype(jnp.float32) * gain).astype(jnp.bfloat16)  10.1 us
    dot_general x4, matrix products, cross_block(): jnp.einsum('pfwa,pfwb->fab', own_block, flipped, preferred_element_type=j...  6.33 us
    dot_general x4, matrix products, cross_block(): jnp.einsum('pfwa,pfwb->fab', own_block, partner, preferred_element_type=j...  5.93 us
  transfers between devices with their start and end apart: 7, of which 5 were waited for; matrix products, arithmetic and copies ran while one was open for 9% of the time, Pallas kernels for 0%

profile of v1, /device:TPU:4, one launch (start us, length us, event | category | flops | bytes accessed | tf_op | source)
XLA Modules:
  0.0 274.9 jit_solution(714422074504571483)
XLA Ops:
  6.5 2.6 copy.3
  9.2 0.1 collective-permute-start
  9.3 52.2 %collective-permute-done = bf16[2,8,512,256]{3,2,0,1:T(8,128)(2,1)} collective-permute-done((bf16[2,8,512,256]{3,2,0,1:T(8,128)(2,1)S(1)}, bf16[2,8,512,256]{3,2,0,1:T(8,128)(2,1)}, u32[]{:S(2)}, u32[]{:S(2)}) %collective-permute-start) | collective-permute-done | bytes 4194336 | tf_op jit(solution)/shard_map/ppermute | solution.py:17
  61.5 1.6 fusion
  63.1 0.0 all-reduce.2.cloned.1.call-update
  63.1 117.9 %all-reduce.2.cloned.1.call-done = f32[512,256]{1,0:T(8,128)} async-done(((f32[512,256]{1,0:T(8,128)}), f32[512,256]{1,0:T(8,128)}) %all-reduce.2.cloned.1.call-update) | async-done | bytes 524304 | tf_op jit(solution)/shard_map/psum | solution.py:39
  181.0 1.1 rsqrt_multiply_fusion
  182.2 0.1 collective-permute-start.1
  182.3 3.1 %fusion.1 = bf16[2,8,512,256]{3,2,0,1:T(8,128)(2,1)S(1)} fusion(f32[512,256]{1,0:T(8,128)S(1)} %rsqrt_multiply_fusion, bf16[2,8,512,256]{3,2,1,0:T(8,128)(2,1)} %param.2), kind=kLoop, calls=%fused_computation.3 | loop fusion | flops 6291456 | bytes 8912896 | tf_op jit(solution)/shard_map/convert_element_type | solution.py:28
  185.3 0.3 fusion.38
  185.6 1.5 convolution_bitcast_fusion.3
  187.1 5.9 %collective-permute-done.1 = f32[512,256]{1,0:T(8,128)S(1)} collective-permute-done((f32[512,256]{1,0:T(8,128)S(1)}, f32[512,256]{1,0:T(8,128)S(1)}, u32[]{:S(2)}, u32[]{:S(2)}) %collective-permute-start.1) | collective-permute-done | bytes 524320 | tf_op jit(solution)/shard_map/ppermute | solution.py:17
  193.0 1.6 fusion.31
  194.6 0.6 fusion.6
  195.1 8.5 %collective-permute-done.3 = f32[512,256]{1,0:T(8,128)S(1)} collective-permute-done((f32[512,256]{1,0:T(8,128)S(1)}, f32[512,256]{1,0:T(8,128)S(1)}, u32[]{:S(2)}, u32[]{:S(2)}) %collective-permute-start.3) | collective-permute-done | bytes 524320 | tf_op jit(solution)/shard_map/ppermute | solution.py:17
  203.7 3.1 %multiply_convert_fusion.2 = bf16[2,8,512,256]{3,2,0,1:T(8,128)(2,1)S(1)} fusion(bf16[2,8,512,256]{3,2,0,1:T(8,128)(2,1)} %collective-permute-done, f32[512,256]{1,0:T(8,128)S(1)} %collective-permute-done.1), kind=kLoop, calls=%fused_computation.7 | loop fusion | flops 6291456 | bytes 8912896 | tf_op jit(solution)/shard_map/convert_element_type | solution.py:28
  206.8 0.3 fusion.39
  207.1 1.6 fusion.28
  208.6 1.5 convolution_bitcast_fusion.2
  210.1 0.6 fusion.11
  210.7 3.1 %multiply_convert_fusion.1 = bf16[2,8,512,256]{3,2,0,1:T(8,128)(2,1)S(1)} fusion(bf16[2,8,512,256]{3,2,0,1:T(8,128)(2,1)} %collective-permute-done.2, f32[512,256]{1,0:T(8,128)S(1)} %collective-permute-done.3), kind=kLoop, calls=%fused_computation.6 | loop fusion | flops 6291456 | bytes 8912896 | tf_op jit(solution)/shard_map/convert_element_type | solution.py:28
  213.8 0.3 fusion.40
  214.1 1.5 convolution_bitcast_fusion.1
  215.6 1.6 fusion.25
  217.2 0.6 fusion.16
  217.7 41.6 %collective-permute-done.4 = bf16[2,8,512,256]{3,2,0,1:T(8,128)(2,1)S(1)} collective-permute-done((bf16[2,8,512,256]{3,2,0,1:T(8,128)(2,1)}, bf16[2,8,512,256]{3,2,0,1:T(8,128)(2,1)S(1)}, u32[]{:S(2)}, u32[]{:S(2)}) %collective-permute-start.4) | collective-permute-done | bytes 4194336 | tf_op jit(solution)/shard_map/ppermute | solution.py:17
  259.3 0.9 multiply_convert_fusion
  260.3 1.5 convolution_bitcast_fusion
  261.8 0.3 fusion.41
  262.0 1.6 fusion.22
  263.6 0.6 fusion.21
  264.2 3.9 %pad_maximum_fusion = bf16[4,2,8,256,256]{4,3,2,1,0:T(8,128)(2,1)} fusion(bf16[1,2,8,256,256]{4,3,2,1,0:T(8,128)(2,1)S(1)} %fusion.21, bf16[1,2,8,256,256]{4,3,2,1,0:T(8,128)(2,1)S(1)} %fusion.16, bf16[1,2,8,256,256]{4,3,2,1,0:T(8,128)(2,1)S(1)} %fusion.11, bf16[1,2,8,256,256]{4,3,2,1,0:T(8,128)(2,1)S(1)} %fusion.6), kind=kLoop, calls=%fused_computation.4 | loop fusion | flops 12582912 | bytes 16777216 | tf_op jit(solution)/shard_map/stack | solution.py:49
  (11 shorter events, 0.0 us)
Async XLA Ops:
  6.5 174.5 %all-reduce.2.cloned.1.call-start = ((), (), s32[]{:S(2)}) async-start(), calls=%async_computation | async-start | bytes 1048576 | tf_op jit(solution)/shard_map/psum | solution.py:39
  6.5 54.9 %copy-start = (bf16[2,8,512,256]{3,2,1,0:T(8,128)(2,1)S(1)}, bf16[2,8,512,256]{3,2,1,0:T(8,128)(2,1)}, u32[]{:S(2)}) copy-start(bf16[2,8,512,256]{3,2,1,0:T(8,128)(2,1)} %param.2) | copy-start | bytes 12582916
  9.2 171.9 %copy-start.1 = (s32[512,256]{1,0:T(8,128)S(1)}, s32[512,256]{1,0:T(8,128)}, u32[]{:S(2)}) copy-start(s32[512,256]{1,0:T(8,128)} %param.3) | copy-start | bytes 1572868
  9.2 52.3 %collective-permute-start = (bf16[2,8,512,256]{3,2,0,1:T(8,128)(2,1)S(1)}, bf16[2,8,512,256]{3,2,0,1:T(8,128)(2,1)}, u32[]{:S(2)}, u32[]{:S(2)}) collective-permute-start(bf16[2,8,512,256]{3,2,0,1:T(8,128)(2,1)S(1)} %copy.3), channel_id=1, source_target_pairs={{0,1},{1,2},{2,3},{3,4},{4,5},{5,6},{6,7},{7,8},{8,9},{9,10},{10,1... | collective-permute-start | bytes 12582920 | tf_op jit(solution)/shard_map/ppermute | solution.py:17
  61.5 142.2 %collective-permute-start.2 = (bf16[2,8,512,256]{3,2,0,1:T(8,128)(2,1)}, bf16[2,8,512,256]{3,2,0,1:T(8,128)(2,1)}, u32[]{:S(2)}, u32[]{:S(2)}) collective-permute-start(bf16[2,8,512,256]{3,2,0,1:T(8,128)(2,1)} %collective-permute-done), channel_id=1, source_target_pairs={{0,1},{1,2},{2,3},{3,4},{4,5},{5,6},{6,7},{7,8},{8,9},{9,10},{10,1... | collective-permute-start | bytes 12582920 | tf_op jit(solution)/shard_map/ppermute | solution.py:17
  182.2 10.8 %collective-permute-start.1 = (f32[512,256]{1,0:T(8,128)S(1)}, f32[512,256]{1,0:T(8,128)S(1)}, u32[]{:S(2)}, u32[]{:S(2)}) collective-permute-start(f32[512,256]{1,0:T(8,128)S(1)} %rsqrt_multiply_fusion), channel_id=1, source_target_pairs={{0,1},{1,2},{2,3},{3,4},{4,5},{5,6},{6,7},{7,8},{8,9},{9,10},{10,1... | collective-permute-start | bytes 1572872 | tf_op jit(solution)/shard_map/ppermute | solution.py:17
  193.0 10.7 %collective-permute-start.3 = (f32[512,256]{1,0:T(8,128)S(1)}, f32[512,256]{1,0:T(8,128)S(1)}, u32[]{:S(2)}, u32[]{:S(2)}) collective-permute-start(f32[512,256]{1,0:T(8,128)S(1)} %collective-permute-done.1), channel_id=1, source_target_pairs={{0,1},{1,2},{2,3},{3,4},{4,5},{5,6},{6,7},{7,8},{8,9},{9,10},{10,1... | collective-permute-start | bytes 1572872 | tf_op jit(solution)/shard_map/ppermute | solution.py:17
  203.7 14.1 %collective-permute-start.5 = (f32[512,256]{1,0:T(8,128)S(1)}, f32[512,256]{1,0:T(8,128)S(1)}, u32[]{:S(2)}, u32[]{:S(2)}) collective-permute-start(f32[512,256]{1,0:T(8,128)S(1)} %collective-permute-done.3), channel_id=1, source_target_pairs={{0,1},{1,2},{2,3},{3,4},{4,5},{5,6},{6,7},{7,8},{8,9},{9,10},{10,1... | collective-permute-start | bytes 1572872 | tf_op jit(solution)/shard_map/ppermute | solution.py:17
  203.7 55.7 %collective-permute-start.4 = (bf16[2,8,512,256]{3,2,0,1:T(8,128)(2,1)}, bf16[2,8,512,256]{3,2,0,1:T(8,128)(2,1)S(1)}, u32[]{:S(2)}, u32[]{:S(2)}) collective-permute-start(bf16[2,8,512,256]{3,2,0,1:T(8,128)(2,1)} %collective-permute-done.2), channel_id=1, source_target_pairs={{0,1},{1,2},{2,3},{3,4},{4,5},{5,6},{6,7},{7,8},{8,9},{9,10},{10,1... | collective-permute-start | bytes 12582920 | tf_op jit(solution)/shard_map/ppermute | solution.py:17
Sparse Core Ops, SparseCore 0:
  63.2 117.7 all-reduce.1

commit v2 on v0

--- a/solution.py
+++ b/solution.py
@@ -17,6 +17,31 @@
     return lax.ppermute(value, axis, pairs)
 
 
+def butterfly_sum(value, axis):
+    count = lax.axis_size(axis)
+    index = lax.axis_index(axis)
+    flat = value.reshape(-1)
+    dists = []
+    d = count // 2
+    while d >= 1:
+        dists.append(d)
+        d //= 2
+    bits = []
+    for d in dists:
+        half = flat.shape[0] // 2
+        low, high = flat[:half], flat[half:]
+        bit = (index // d) % 2
+        pairs = [(s, s ^ d) for s in range(count)]
+        got = lax.ppermute(jnp.where(bit == 0, high, low), axis, pairs)
+        flat = jnp.where(bit == 0, low, high) + got
+        bits.append(bit)
+    for d, bit in zip(reversed(dists), reversed(bits)):
+        pairs = [(s, s ^ d) for s in range(count)]
+        got = lax.ppermute(flat, axis, pairs)
+        flat = jnp.where(bit == 0, jnp.concatenate([flat, got]), jnp.concatenate([got, flat]))
+    return flat.reshape(value.shape)
+
+
 def cross_block(own_block, partner, scale):
     flipped = jnp.stack([partner[1], -partner[0]])
     real_part = jnp.einsum("pfwa,pfwb->fab", own_block, partner, preferred_element_type=jnp.float32)
@@ -24,21 +49,25 @@
     return (jnp.stack([real_part, imag_part]) * scale).astype(jnp.bfloat16)
 
 
+def whiten(raw, gain):
+    return (raw.astype(jnp.float32) * gain).astype(jnp.bfloat16)
+
+
 def shards(spectra, valid_mask):
     values = spectra.astype(jnp.float32)
     partial_energy = jnp.sum(values * values, axis=(0, 1))
     total_bins = spectra.shape[1] * lax.axis_size("band")
     scale = 1.0 / math.sqrt(spectra.shape[2])
-    far_count = ROUNDS
-    energy = lax.psum(partial_energy, "band")
+    raw_near = passed_along(spectra, "chan", 1)
+    energy = butterfly_sum(partial_energy, "band")
     window_gain = valid_mask.astype(jnp.float32) / jnp.sqrt(energy / total_bins + eps_energy)
-    whitened = (values * window_gain).astype(jnp.bfloat16)
+    gain_near = passed_along(window_gain, "chan", 1)
+    whitened = whiten(spectra, window_gain)
     outputs = [cross_block(whitened, whitened, scale)]
-    partners = [whitened]
-    carried = whitened
-    for round_idx in range(1, far_count + 1):
+    carried = whiten(raw_near, gain_near)
+    outputs.append(cross_block(whitened, carried, scale))
+    for round_idx in range(2, ROUNDS + 1):
         carried = passed_along(carried, "chan", 1)
-        partners.append(carried)
         outputs.append(cross_block(whitened, carried, scale))
     return jnp.stack(outputs)
 

time: 273 us -> 212 us (0.78)
  waiting for transfers between devices: 229 us -> 170 us
  between operations: 13.5 us -> 0.3 us
  starting transfers between devices: 0.09 us -> 9.33 us
  local copies, waits for them, and re-layouts: 0.01 us -> 5.01 us
    psum x1 -> x0, waiting for transfers between devices: 90.3 us -> none  [shards(): energy = lax.psum(partial_energy, 'band')]
    ppermute x0 -> x6, waiting for transfers between devices: none -> 72.1 us  [the longest x3 56.7 us: butterfly_sum(): got = lax.ppermute(jnp.where(bit == 0, high, low), axis, pairs)]
    ppermute x3 -> x4, waiting for transfers between devices: 138 us -> 98 us  [passed_along(): return lax.ppermute(value, axis, pairs)]
    ppermute x0 -> x6, starting transfers between devices: none -> 9.15 us  [the longest x3 5.54 us: butterfly_sum(): got = lax.ppermute(jnp.where(bit == 0, high, low), axis, pairs)]
    unnamed x2 -> x7, local copies, waits for them, and re-layouts: 0.01 us -> 4.85 us
  transfers between devices with their start and end apart: 4 -> 10, of which waited for: 4 -> 8; matrix products, arithmetic and copies ran while one was open for 4% -> 8% of each run, Pallas kernels for 0% -> 0%
where the time goes in v2:
time: 212 us
  waiting for transfers between devices  170 us (80%)
  other arithmetic  14.6 us (7%)
  matrix products  12.5 us (6%)
  starting transfers between devices  9.33 us (4%)
  local copies, waits for them, and re-layouts  5.01 us (2%)
    ppermute x4, waiting for transfers between devices, passed_along(): return lax.ppermute(value, axis, pairs)  98 us
    ppermute x3, waiting for transfers between devices, butterfly_sum(): got = lax.ppermute(jnp.where(bit == 0, high, low), axis, pairs)  56.7 us
    ppermute x3, waiting for transfers between devices, butterfly_sum(): got = lax.ppermute(flat, axis, pairs)  15.4 us
    dot_general x4, matrix products, cross_block(): jnp.einsum('pfwa,pfwb->fab', own_block, flipped, preferred_element_type=j...  6.57 us
    dot_general x4, matrix products, cross_block(): jnp.einsum('pfwa,pfwb->fab', own_block, partner, preferred_element_type=j...  5.93 us
    ppermute x3, starting transfers between devices, butterfly_sum(): got = lax.ppermute(jnp.where(bit == 0, high, low), axis, pairs)  5.54 us
    unnamed x7, local copies, waits for them, and re-layouts  4.85 us
  transfers between devices with their start and end apart: 10, of which 8 were waited for; matrix products, arithmetic and copies ran while one was open for 8% of the time, Pallas kernels for 0%

profile of v2, /device:TPU:4, one launch (start us, length us, event | category | flops | bytes accessed | tf_op | source)
XLA Modules:
  0.0 211.8 jit_solution(15102331099389440112)
XLA Ops:
  0.0 3.1 %fusion = f32[512,256]{1,0:T(8,128)S(1)} fusion(bf16[2,8,512,256]{3,2,1,0:T(8,128)(2,1)} %param.2), kind=kLoop, calls=%fused_computation.2 | loop fusion | flops 6160384 | bytes 4718592 | tf_op jit(solution)/shard_map/reduce_sum | solution.py:58
  3.3 3.3 %collective-permute-start = (f32[65536]{0:T(1024)S(1)}, f32[65536]{0:T(1024)S(1)}, u32[]{:S(2)}, u32[]{:S(2)}) collective-permute-start(f32[65536]{0:T(1024)S(1)} %bitcast.59), channel_id=1, source_target_pairs={{0,128},{32,160},{64,192},{96,224},{128,0},{160,32},{192,64},{224,... | collective-permute-start | bytes 786440 | tf_op jit(solution)/shard_map/ppermute | solution.py:35
  6.7 6.2 %collective-permute-done = f32[65536]{0:T(1024)S(1)} collective-permute-done((f32[65536]{0:T(1024)S(1)}, f32[65536]{0:T(1024)S(1)}, u32[]{:S(2)}, u32[]{:S(2)}) %collective-permute-start) | collective-permute-done | bytes 262176 | tf_op jit(solution)/shard_map/ppermute | solution.py:35
  13.0 1.7 collective-permute-start.1
  14.6 4.6 %copy.3 = bf16[2,8,512,256]{3,2,0,1:T(8,128)(2,1)} copy(bf16[2,8,512,256]{3,2,1,0:T(8,128)(2,1)} %param.2) | data formatting | bytes 8388608 | tf_op args[0]
  19.2 0.6 collective-permute-start.2
  19.8 50.5 %collective-permute-done.2 = f32[16384]{0:T(1024)S(1)} collective-permute-done((f32[16384]{0:T(1024)S(1)}, f32[16384]{0:T(1024)S(1)}, u32[]{:S(2)}, u32[]{:S(2)}) %collective-permute-start.2) | collective-permute-done | bytes 65568 | tf_op jit(solution)/shard_map/ppermute | solution.py:35
  70.4 5.8 %collective-permute-done.3 = f32[16384]{0:T(1024)S(1)} collective-permute-done((f32[16384]{0:T(1024)S(1)}, f32[16384]{0:T(1024)S(1)}, u32[]{:S(2)}, u32[]{:S(2)}) %collective-permute-start.3) | collective-permute-done | bytes 65568 | tf_op jit(solution)/shard_map/ppermute | solution.py:40
  76.2 0.5 collective-permute-start.4
  76.8 4.5 %collective-permute-done.4 = f32[32768]{0:T(1024)S(1)} collective-permute-done((f32[32768]{0:T(1024)S(1)}, f32[32768]{0:T(1024)S(1)}, u32[]{:S(2)}, u32[]{:S(2)}) %collective-permute-start.4) | collective-permute-done | bytes 131104 | tf_op jit(solution)/shard_map/ppermute | solution.py:40
  81.3 3.0 %collective-permute-start.5 = (f32[65536]{0:T(1024)S(1)}, f32[65536]{0:T(1024)S(1)}, u32[]{:S(2)}, u32[]{:S(2)}) collective-permute-start(f32[65536]{0:T(1024)S(1)} %maximum_select_fusion.2), channel_id=1, source_target_pairs={{0,128},{32,160},{64,192},{96,224},{128,0},{160,32},{192,64},{224,... | collective-permute-start | bytes 786440 | tf_op jit(solution)/shard_map/ppermute | solution.py:40
  84.5 5.0 %collective-permute-done.5 = f32[65536]{0:T(1024)S(1)} collective-permute-done((f32[65536]{0:T(1024)S(1)}, f32[65536]{0:T(1024)S(1)}, u32[]{:S(2)}, u32[]{:S(2)}) %collective-permute-start.5) | collective-permute-done | bytes 262176 | tf_op jit(solution)/shard_map/ppermute | solution.py:40
  89.8 10.7 %collective-permute-done.7 = f32[512,256]{1,0:T(8,128)S(1)} collective-permute-done((f32[512,256]{1,0:T(8,128)S(1)}, f32[512,256]{1,0:T(8,128)S(1)}, u32[]{:S(2)}, u32[]{:S(2)}) %collective-permute-start.7) | collective-permute-done | bytes 524320 | tf_op jit(solution)/shard_map/ppermute | solution.py:17
  100.5 3.1 %multiply_convert_fusion = bf16[2,8,512,256]{3,2,0,1:T(8,128)(2,1)S(1)} fusion(bf16[2,8,512,256]{3,2,0,1:T(8,128)(2,1)} %collective-permute-done.6, f32[512,256]{1,0:T(8,128)S(1)} %collective-permute-done.7), kind=kLoop, calls=%fused_computation.5 | loop fusion | flops 6291456 | bytes 8912896 | tf_op jit(solution)/shard_map/convert_element_type | solution.py:53
  103.7 0.9 fusion.1
  104.6 0.3 fusion.42
  104.9 48.8 %collective-permute-done.8 = bf16[2,8,512,256]{3,2,0,1:T(8,128)(2,1)S(1)} collective-permute-done((bf16[2,8,512,256]{3,2,0,1:T(8,128)(2,1)S(1)}, bf16[2,8,512,256]{3,2,0,1:T(8,128)(2,1)S(1)}, u32[]{:S(2)}, u32[]{:S(2)}) %collective-permute-start.8) | collective-permute-done | bytes 4194336 | tf_op jit(solution)/shard_map/ppermute | solution.py:17
  153.7 1.6 fusion.31
  155.3 1.5 convolution_bitcast_fusion.3
  156.8 0.6 fusion.6
  157.4 0.3 fusion.43
  157.7 1.6 fusion.28
  159.3 1.5 convolution_bitcast_fusion.2
  160.7 0.6 fusion.11
  161.6 1.6 fusion.25
  163.2 1.5 convolution_bitcast_fusion.1
  164.7 0.6 fusion.16
  165.3 38.5 %collective-permute-done.9 = bf16[2,8,512,256]{3,2,0,1:T(8,128)(2,1)S(1)} collective-permute-done((bf16[2,8,512,256]{3,2,0,1:T(8,128)(2,1)S(1)}, bf16[2,8,512,256]{3,2,0,1:T(8,128)(2,1)S(1)}, u32[]{:S(2)}, u32[]{:S(2)}) %collective-permute-start.9) | collective-permute-done | bytes 4194336 | tf_op jit(solution)/shard_map/ppermute | solution.py:17
  204.0 1.8 fusion.22
  205.9 1.5 convolution_bitcast_fusion
  207.3 0.6 fusion.21
  207.9 3.9 %pad_maximum_fusion = bf16[4,2,8,256,256]{4,3,2,1,0:T(8,128)(2,1)} fusion(bf16[1,2,8,256,256]{4,3,2,1,0:T(8,128)(2,1)S(1)} %fusion.21, bf16[1,2,8,256,256]{4,3,2,1,0:T(8,128)(2,1)S(1)} %fusion.16, bf16[1,2,8,256,256]{4,3,2,1,0:T(8,128)(2,1)S(1)} %fusion.11, bf16[1,2,8,256,256]{4,3,2,1,0:T(8,128)(2,1)S(1)} %fusion.6), kind=kLoop, calls=%fused_computation.4 | loop fusion | flops 12582912 | bytes 16777216 | tf_op jit(solution)/shard_map/stack | solution.py:72
  (30 shorter events, 1.6 us)
Async XLA Ops:
  3.3 9.6 %collective-permute-start = (f32[65536]{0:T(1024)S(1)}, f32[65536]{0:T(1024)S(1)}, u32[]{:S(2)}, u32[]{:S(2)}) collective-permute-start(f32[65536]{0:T(1024)S(1)} %bitcast.59), channel_id=1, source_target_pairs={{0,128},{32,160},{64,192},{96,224},{128,0},{160,32},{192,64},{224,... | collective-permute-start | bytes 786440 | tf_op jit(solution)/shard_map/ppermute | solution.py:35
  12.9 76.6 %copy-start.1 = (s32[512,256]{1,0:T(8,128)S(1)}, s32[512,256]{1,0:T(8,128)}, u32[]{:S(2)}) copy-start(s32[512,256]{1,0:T(8,128)} %param.3) | copy-start | bytes 1572868
  13.0 6.2 %collective-permute-start.1 = (f32[32768]{0:T(1024)S(1)}, f32[32768]{0:T(1024)S(1)}, u32[]{:S(2)}, u32[]{:S(2)}) collective-permute-start(f32[32768]{0:T(1024)S(1)} %slice_select_fusion), channel_id=1, source_target_pairs={{0,64},{32,96},{64,0},{96,32},{128,192},{160,224},{192,128},{224,1... | collective-permute-start | bytes 393224 | tf_op jit(solution)/shard_map/ppermute | solution.py:35
  19.2 81.3 %collective-permute-start.6 = (bf16[2,8,512,256]{3,2,0,1:T(8,128)(2,1)}, bf16[2,8,512,256]{3,2,0,1:T(8,128)(2,1)}, u32[]{:S(2)}, u32[]{:S(2)}) collective-permute-start(bf16[2,8,512,256]{3,2,0,1:T(8,128)(2,1)} %copy.3), channel_id=1, source_target_pairs={{0,1},{1,2},{2,3},{3,4},{4,5},{5,6},{6,7},{7,8},{8,9},{9,10},{10,1... | collective-permute-start | bytes 12582920 | tf_op jit(solution)/shard_map/ppermute | solution.py:17
  19.2 51.1 %collective-permute-start.2 = (f32[16384]{0:T(1024)S(1)}, f32[16384]{0:T(1024)S(1)}, u32[]{:S(2)}, u32[]{:S(2)}) collective-permute-start(f32[16384]{0:T(1024)S(1)} %slice_select_fusion.1), channel_id=1, source_target_pairs={{0,32},{32,0},{64,96},{96,64},{128,160},{160,128},{192,224},{224,1... | collective-permute-start | bytes 196616 | tf_op jit(solution)/shard_map/ppermute | solution.py:35
  70.3 5.9 %collective-permute-start.3 = (f32[16384]{0:T(1024)S(1)}, f32[16384]{0:T(1024)S(1)}, u32[]{:S(2)}, u32[]{:S(2)}) collective-permute-start(f32[16384]{0:T(1024)S(1)} %select_add_fusion.1), channel_id=1, source_target_pairs={{0,32},{32,0},{64,96},{96,64},{128,160},{160,128},{192,224},{224,1... | collective-permute-start | bytes 196616 | tf_op jit(solution)/shard_map/ppermute | solution.py:40
  76.2 5.1 %collective-permute-start.4 = (f32[32768]{0:T(1024)S(1)}, f32[32768]{0:T(1024)S(1)}, u32[]{:S(2)}, u32[]{:S(2)}) collective-permute-start(f32[32768]{0:T(1024)S(1)} %maximum_select_fusion.4), channel_id=1, source_target_pairs={{0,64},{32,96},{64,0},{96,32},{128,192},{160,224},{192,128},{224,1... | collective-permute-start | bytes 393224 | tf_op jit(solution)/shard_map/ppermute | solution.py:40
  81.3 8.2 %collective-permute-start.5 = (f32[65536]{0:T(1024)S(1)}, f32[65536]{0:T(1024)S(1)}, u32[]{:S(2)}, u32[]{:S(2)}) collective-permute-start(f32[65536]{0:T(1024)S(1)} %maximum_select_fusion.2), channel_id=1, source_target_pairs={{0,128},{32,160},{64,192},{96,224},{128,0},{160,32},{192,64},{224,... | collective-permute-start | bytes 786440 | tf_op jit(solution)/shard_map/ppermute | solution.py:40
  89.7 14.0 %copy-start = (bf16[2,8,512,256]{3,2,1,0:T(8,128)(2,1)S(1)}, bf16[2,8,512,256]{3,2,1,0:T(8,128)(2,1)}, u32[]{:S(2)}) copy-start(bf16[2,8,512,256]{3,2,1,0:T(8,128)(2,1)} %param.2) | copy-start | bytes 12582916
  89.7 10.8 %collective-permute-start.7 = (f32[512,256]{1,0:T(8,128)S(1)}, f32[512,256]{1,0:T(8,128)S(1)}, u32[]{:S(2)}, u32[]{:S(2)}) collective-permute-start(f32[512,256]{1,0:T(8,128)S(1)} %fusion.37), channel_id=1, source_target_pairs={{0,1},{1,2},{2,3},{3,4},{4,5},{5,6},{6,7},{7,8},{8,9},{9,10},{10,1... | collective-permute-start | bytes 1572872 | tf_op jit(solution)/shard_map/ppermute | solution.py:17
  103.6 50.1 %collective-permute-start.8 = (bf16[2,8,512,256]{3,2,0,1:T(8,128)(2,1)S(1)}, bf16[2,8,512,256]{3,2,0,1:T(8,128)(2,1)S(1)}, u32[]{:S(2)}, u32[]{:S(2)}) collective-permute-start(bf16[2,8,512,256]{3,2,0,1:T(8,128)(2,1)S(1)} %multiply_convert_fusion), channel_id=1, source_target_pairs={{0,1},{1,2},{2,3},{3,4},{4,5},{5,6},{6,7},{7,8},{8,9},{9,10},{10,1... | collective-permute-start | bytes 12582920 | tf_op jit(solution)/shard_map/ppermute | solution.py:17
  153.7 50.0 %collective-permute-start.9 = (bf16[2,8,512,256]{3,2,0,1:T(8,128)(2,1)S(1)}, bf16[2,8,512,256]{3,2,0,1:T(8,128)(2,1)S(1)}, u32[]{:S(2)}, u32[]{:S(2)}) collective-permute-start(bf16[2,8,512,256]{3,2,0,1:T(8,128)(2,1)S(1)} %collective-permute-done.8), channel_id=1, source_target_pairs={{0,1},{1,2},{2,3},{3,4},{4,5},{5,6},{6,7},{7,8},{8,9},{9,10},{10,1... | collective-permute-start | bytes 12582920 | tf_op jit(solution)/shard_map/ppermute | solution.py:17

commit v3 on v2

--- a/solution.py
+++ b/solution.py
@@ -5,15 +5,13 @@
 from jax import lax
 from jax.sharding import PartitionSpec as P
 
-ROUNDS = 3
-
 
 eps_energy = 1e-06
 
 
-def passed_along(value, axis, steps):
+def moved(value, axis, offset, only_even=False):
     count = lax.axis_size(axis)
-    pairs = [(source, (source + steps) % count) for source in range(count)]
+    pairs = [(source, (source + offset) % count) for source in range(count) if not only_even or source % 2 == 0]
     return lax.ppermute(value, axis, pairs)
 
 
@@ -58,17 +56,27 @@
     partial_energy = jnp.sum(values * values, axis=(0, 1))
     total_bins = spectra.shape[1] * lax.axis_size("band")
     scale = 1.0 / math.sqrt(spectra.shape[2])
-    raw_near = passed_along(spectra, "chan", 1)
+    even = lax.axis_index("chan") % 2 == 0
+    raw_near = moved(spectra, "chan", 1)
+    raw_ahead = moved(spectra, "chan", -2, only_even=True)
     energy = butterfly_sum(partial_energy, "band")
     window_gain = valid_mask.astype(jnp.float32) / jnp.sqrt(energy / total_bins + eps_energy)
-    gain_near = passed_along(window_gain, "chan", 1)
+    gain_near = moved(window_gain, "chan", 1)
+    gain_ahead = moved(window_gain, "chan", -2, only_even=True)
     whitened = whiten(spectra, window_gain)
-    outputs = [cross_block(whitened, whitened, scale)]
-    carried = whiten(raw_near, gain_near)
-    outputs.append(cross_block(whitened, carried, scale))
-    for round_idx in range(2, ROUNDS + 1):
-        carried = passed_along(carried, "chan", 1)
-        outputs.append(cross_block(whitened, carried, scale))
+    near = whiten(raw_near, gain_near)
+    ahead = whiten(raw_ahead, gain_ahead)
+    second = moved(near, "chan", 1)
+    for_above = cross_block(ahead, near, scale)
+    for_above, second = lax.optimization_barrier((for_above, second))
+    third = moved(second, "chan", 1, only_even=True)
+    from_below = moved(for_above, "chan", 2, only_even=True)
+    outputs = [
+        cross_block(whitened, whitened, scale),
+        cross_block(whitened, near, scale),
+        cross_block(whitened, second, scale),
+        jnp.where(even, from_below, cross_block(whitened, third, scale)),
+    ]
     return jnp.stack(outputs)
 
 

time: 212 us -> 202 us (0.953)
  waiting for transfers between devices: 170 us -> 131 us
  matrix products: 12.5 us -> 24.3 us
  other arithmetic: 14.6 us -> 23.9 us
  starting transfers between devices: 9.33 us -> 16.9 us
    ppermute x4 -> x7, waiting for transfers between devices: 98 us -> 60.8 us  [moved(): return lax.ppermute(value, axis, pairs)]
    dot_general x4 -> x5, matrix products: 5.93 us -> 14.9 us  [cross_block(): jnp.einsum('pfwa,pfwb->fab', own_block, partner, preferred_element_type=j...]
    ppermute x4 -> x7, starting transfers between devices: 0.17 us -> 7.78 us  [moved(): return lax.ppermute(value, axis, pairs)]
    slice x4, other arithmetic: 1.09 us -> 5.55 us  [cross_block(): flipped = jnp.stack([partner[1], -partner[0]])]
    convert_element_type x2, other arithmetic: 3.99 us -> 8.12 us  [whiten(): return (raw.astype(jnp.float32) * gain).astype(jnp.bfloat16)]
    dot_general x4 -> x5, matrix products: 6.57 us -> 9.32 us  [cross_block(): jnp.einsum('pfwa,pfwb->fab', own_block, flipped, preferred_element_type=j...]
    another operation x1 -> x2, other arithmetic: 3.88 us -> 4.6 us  [shards(): return jnp.stack(outputs)]
    unnamed x7 -> x5, local copies, waits for them, and re-layouts: 4.85 us -> 4.85 us
  transfers between devices with their start and end apart: 10 -> 13, of which waited for: 8 -> 9; matrix products, arithmetic and copies ran while one was open for 8% -> 22% of each run, Pallas kernels for 0% -> 0%
where the time goes in v3:
time: 202 us; the launch traced here: 201 us
  waiting for transfers between devices  131 us (65%)
  matrix products  24.3 us (12%)
  other arithmetic  23.9 us (12%)
  starting transfers between devices  16.9 us (8%)
  local copies, waits for them, and re-layouts  5 us (2%)
    ppermute x7, waiting for transfers between devices, moved(): return lax.ppermute(value, axis, pairs)  60.8 us
    ppermute x3, waiting for transfers between devices, butterfly_sum(): got = lax.ppermute(jnp.where(bit == 0, high, low), axis, pairs)  56.7 us
    dot_general x5, matrix products, cross_block(): jnp.einsum('pfwa,pfwb->fab', own_block, partner, preferred_element_type=j...  14.9 us
    ppermute x3, waiting for transfers between devices, butterfly_sum(): got = lax.ppermute(flat, axis, pairs)  13.5 us
    dot_general x5, matrix products, cross_block(): jnp.einsum('pfwa,pfwb->fab', own_block, flipped, preferred_element_type=j...  9.32 us
    convert_element_type x2, other arithmetic, whiten(): return (raw.astype(jnp.float32) * gain).astype(jnp.bfloat16)  8.12 us
    ppermute x7, starting transfers between devices, moved(): return lax.ppermute(value, axis, pairs)  7.78 us
    slice x4, other arithmetic, cross_block(): flipped = jnp.stack([partner[1], -partner[0]])  5.55 us
  transfers between devices with their start and end apart: 13, of which 9 were waited for; matrix products, arithmetic and copies ran while one was open for 22% of the time, Pallas kernels for 0%

profile of v3, /device:TPU:4, one launch (start us, length us, event | category | flops | bytes accessed | tf_op | source)
XLA Modules:
  0.0 201.3 jit_solution(6595394670441218293)
XLA Ops:
  0.0 3.1 %fusion = f32[512,256]{1,0:T(8,128)S(1)} fusion(bf16[2,8,512,256]{3,2,1,0:T(8,128)(2,1)} %param.2), kind=kLoop, calls=%fused_computation.2 | loop fusion | flops 6160384 | bytes 4718592 | tf_op jit(solution)/shard_map/reduce_sum | solution.py:56
  3.3 3.3 %collective-permute-start = (f32[65536]{0:T(1024)S(1)}, f32[65536]{0:T(1024)S(1)}, u32[]{:S(2)}, u32[]{:S(2)}) collective-permute-start(f32[65536]{0:T(1024)S(1)} %bitcast.65), channel_id=1, source_target_pairs={{0,128},{32,160},{64,192},{96,224},{128,0},{160,32},{192,64},{224,... | collective-permute-start | bytes 786440 | tf_op jit(solution)/shard_map/ppermute | solution.py:33
  6.7 6.2 %collective-permute-done = f32[65536]{0:T(1024)S(1)} collective-permute-done((f32[65536]{0:T(1024)S(1)}, f32[65536]{0:T(1024)S(1)}, u32[]{:S(2)}, u32[]{:S(2)}) %collective-permute-start) | collective-permute-done | bytes 262176 | tf_op jit(solution)/shard_map/ppermute | solution.py:33
  13.0 1.7 collective-permute-start.1
  14.6 4.6 %copy.3 = bf16[2,8,512,256]{3,2,0,1:T(8,128)(2,1)} copy(bf16[2,8,512,256]{3,2,1,0:T(8,128)(2,1)} %param.2) | data formatting | bytes 8388608 | tf_op args[0]
  19.8 50.5 %collective-permute-done.2 = f32[16384]{0:T(1024)S(1)} collective-permute-done((f32[16384]{0:T(1024)S(1)}, f32[16384]{0:T(1024)S(1)}, u32[]{:S(2)}, u32[]{:S(2)}) %collective-permute-start.2) | collective-permute-done | bytes 65568 | tf_op jit(solution)/shard_map/ppermute | solution.py:33
  70.4 5.8 %collective-permute-done.3 = f32[16384]{0:T(1024)S(1)} collective-permute-done((f32[16384]{0:T(1024)S(1)}, f32[16384]{0:T(1024)S(1)}, u32[]{:S(2)}, u32[]{:S(2)}) %collective-permute-start.3) | collective-permute-done | bytes 65568 | tf_op jit(solution)/shard_map/ppermute | solution.py:38
  76.8 1.9 collective-permute-start.8
  78.7 2.6 %collective-permute-done.4 = f32[32768]{0:T(1024)S(1)} collective-permute-done((f32[32768]{0:T(1024)S(1)}, f32[32768]{0:T(1024)S(1)}, u32[]{:S(2)}, u32[]{:S(2)}) %collective-permute-start.4) | collective-permute-done | bytes 131104 | tf_op jit(solution)/shard_map/ppermute | solution.py:38
  81.3 3.0 %collective-permute-start.5 = (f32[65536]{0:T(1024)S(1)}, f32[65536]{0:T(1024)S(1)}, u32[]{:S(2)}, u32[]{:S(2)}) collective-permute-start(f32[65536]{0:T(1024)S(1)} %maximum_select_fusion.2), channel_id=1, source_target_pairs={{0,128},{32,160},{64,192},{96,224},{128,0},{160,32},{192,64},{224,... | collective-permute-start | bytes 786440 | tf_op jit(solution)/shard_map/ppermute | solution.py:38
  84.5 5.0 %collective-permute-done.5 = f32[65536]{0:T(1024)S(1)} collective-permute-done((f32[65536]{0:T(1024)S(1)}, f32[65536]{0:T(1024)S(1)}, u32[]{:S(2)}, u32[]{:S(2)}) %collective-permute-start.5) | collective-permute-done | bytes 262176 | tf_op jit(solution)/shard_map/ppermute | solution.py:38
  89.8 10.7 %collective-permute-done.7 = f32[512,256]{1,0:T(8,128)S(1)} collective-permute-done((f32[512,256]{1,0:T(8,128)S(1)}, f32[512,256]{1,0:T(8,128)S(1)}, u32[]{:S(2)}, u32[]{:S(2)}) %collective-permute-start.7) | collective-permute-done | bytes 524320 | tf_op jit(solution)/shard_map/ppermute | solution.py:15
  100.5 5.1 %multiply_convert_fusion.1 = bf16[2,8,512,256]{3,2,0,1:T(8,128)(2,1)} fusion(bf16[2,8,512,256]{3,2,0,1:T(8,128)(2,1)} %collective-permute-done.6, f32[512,256]{1,0:T(8,128)S(1)} %collective-permute-done.7), kind=kLoop, calls=%fused_computation.6 | loop fusion | flops 6291456 | bytes 8912896 | tf_op jit(solution)/shard_map/convert_element_type | solution.py:51
  105.6 2.1 %collective-permute-start.9 = (f32[512,256]{1,0:T(8,128)S(1)}, f32[512,256]{1,0:T(8,128)S(1)}, u32[]{:S(2)}, u32[]{:S(2)}) collective-permute-start(f32[512,256]{1,0:T(8,128)S(1)} %fusion.43), channel_id=1, source_target_pairs={{0,30},{2,0},{4,2},{6,4},{8,6},{10,8},{12,10},{14,12},{16,14},{18,... | collective-permute-start | bytes 1572872 | tf_op jit(solution)/shard_map/ppermute | solution.py:15
  107.7 3.0 %fusion.1 = bf16[2,8,512,256]{3,2,0,1:T(8,128)(2,1)S(1)} fusion(f32[512,256]{1,0:T(8,128)S(1)} %fusion.43, bf16[2,8,512,256]{3,2,1,0:T(8,128)(2,1)} %param.2), kind=kLoop, calls=%fused_computation.3 | loop fusion | flops 6291456 | bytes 8912896 | tf_op jit(solution)/shard_map/convert_element_type | solution.py:51
  111.0 2.5 %fusion.50 = (bf16[1,8,512,256]{3,2,0,1:T(8,128)(2,1)S(1)}, bf16[1,8,512,256]{3,2,0,1:T(8,128)(2,1)S(1)}) fusion(bf16[2,8,512,256]{3,2,0,1:T(8,128)(2,1)} %multiply_convert_fusion.1), kind=kLoop, calls=%fused_computation.71 | loop fusion | flops 1048576 | bytes 8388608 | tf_op jit(solution)/shard_map/slice | solution.py:44
  113.5 19.5 %collective-permute-done.9 = f32[512,256]{1,0:T(8,128)S(1)} collective-permute-done((f32[512,256]{1,0:T(8,128)S(1)}, f32[512,256]{1,0:T(8,128)S(1)}, u32[]{:S(2)}, u32[]{:S(2)}) %collective-permute-start.9) | collective-permute-done | bytes 524320 | tf_op jit(solution)/shard_map/ppermute | solution.py:15
  133.0 3.4 %fusion.37 = f32[1,8,256,256]{3,2,1,0:T(8,128)S(1)} fusion(bf16[2,8,512,256]{3,2,1,0:T(8,128)(2,1)} %collective-permute-done.8, f32[512,256]{1,0:T(8,128)S(1)} %collective-permute-done.9, bf16[1,8,512,256]{3,2,0,1:T(8,128)(2,1)S(1)} %get-tuple-element.16, bf16[1,8,512,256]{3,2,0,1:T(8,128)(2,1)S(1)} %get-tuple-element.15), kind=kOutput, calls=%fused_computation.49 | convolution fusion | flops 1082130432 | bytes 11010048 | tf_op jit(solution)/shard_map/pfwa,pfwb->fab/dot_general | solution.py:46
  136.4 5.0 %fusion.34 = f32[1,8,256,256]{3,2,1,0:T(8,128)S(1)} fusion(bf16[2,8,512,256]{3,2,0,1:T(8,128)(2,1)} %multiply_convert_fusion.1, bf16[2,8,512,256]{3,2,1,0:T(8,128)(2,1)} %collective-permute-done.8, f32[512,256]{1,0:T(8,128)S(1)} %collective-permute-done.9), kind=kOutput, calls=%fused_computation.48 | convolution fusion | flops 1080033280 | bytes 11010048 | tf_op jit(solution)/shard_map/pfwa,pfwb->fab/dot_general | solution.py:45
  142.0 14.0 %collective-permute-done.10 = bf16[2,8,512,256]{3,2,0,1:T(8,128)(2,1)} collective-permute-done((bf16[2,8,512,256]{3,2,0,1:T(8,128)(2,1)}, bf16[2,8,512,256]{3,2,0,1:T(8,128)(2,1)}, u32[]{:S(2)}, u32[]{:S(2)}) %collective-permute-start.10) | collective-permute-done | bytes 4194336 | tf_op jit(solution)/shard_map/ppermute | solution.py:15
  156.0 1.5 collective-permute-start.12
  157.5 1.5 fusion.31
  159.0 1.4 convolution_bitcast_fusion.4
  161.0 1.5 convolution_bitcast_fusion.2
  162.5 3.6 %convolution_bitcast_fusion.3 = f32[1,1,8,256,256]{4,3,2,1,0:T(8,128)S(1)} fusion(bf16[2,8,512,256]{3,2,0,1:T(8,128)(2,1)S(1)} %fusion.1, bf16[2,8,512,256]{3,2,0,1:T(8,128)(2,1)} %multiply_convert_fusion.1), kind=kOutput, calls=%fused_computation.46 | convolution fusion | flops 1073741824 | bytes 10485760 | tf_op jit(solution)/shard_map/pfwa,pfwb->fab/dot_general | solution.py:45
  166.7 2.1 %collective-permute-start.11 = (bf16[2,8,256,256]{3,2,1,0:T(8,128)(2,1)S(1)}, bf16[2,8,256,256]{3,2,1,0:T(8,128)(2,1)S(1)}, u32[]{:S(2)}, u32[]{:S(2)}) collective-permute-start(bf16[2,8,256,256]{3,2,1,0:T(8,128)(2,1)S(1)} %fusion.8), channel_id=1, source_target_pairs={{0,2},{2,4},{4,6},{6,8},{8,10},{10,12},{12,14},{14,16},{16,18},{18... | collective-permute-start | bytes 6291464 | tf_op jit(solution)/shard_map/ppermute | solution.py:15
  168.8 2.5 %fusion.48 = (bf16[1,8,512,256]{3,2,0,1:T(8,128)(2,1)S(1)}, bf16[1,8,512,256]{3,2,0,1:T(8,128)(2,1)S(1)}) fusion(bf16[2,8,512,256]{3,2,0,1:T(8,128)(2,1)} %collective-permute-done.10), kind=kLoop, calls=%fused_computation.69 | loop fusion | flops 1048576 | bytes 8388608 | tf_op jit(solution)/shard_map/slice | solution.py:44
  171.3 3.6 %convolution_bitcast_fusion.1 = f32[1,1,8,256,256]{4,3,2,1,0:T(8,128)S(1)} fusion(bf16[2,8,512,256]{3,2,0,1:T(8,128)(2,1)S(1)} %fusion.1, bf16[2,8,512,256]{3,2,0,1:T(8,128)(2,1)} %collective-permute-done.10), kind=kOutput, calls=%fused_computation.44 | convolution fusion | flops 1073741824 | bytes 10485760 | tf_op jit(solution)/shard_map/pfwa,pfwb->fab/dot_general | solution.py:45
  174.9 1.5 fusion.28
  177.3 1.5 fusion.25
  180.1 16.6 %collective-permute-done.11 = bf16[2,8,256,256]{3,2,1,0:T(8,128)(2,1)S(1)} collective-permute-done((bf16[2,8,256,256]{3,2,1,0:T(8,128)(2,1)S(1)}, bf16[2,8,256,256]{3,2,1,0:T(8,128)(2,1)S(1)}, u32[]{:S(2)}, u32[]{:S(2)}) %collective-permute-start.11) | collective-permute-done | bytes 2097184 | tf_op jit(solution)/shard_map/ppermute | solution.py:15
  197.5 3.9 %pad_maximum_fusion = bf16[4,2,8,256,256]{4,3,2,1,0:T(8,128)(2,1)} fusion(bf16[1,2,8,256,256]{4,3,2,1,0:T(8,128)(2,1)S(1)} %fusion.24, bf16[1,2,8,256,256]{4,3,2,1,0:T(8,128)(2,1)S(1)} %fusion.13, bf16[1,2,8,256,256]{4,3,2,1,0:T(8,128)(2,1)S(1)} %fusion.7, bf16[1,2,8,256,256]{4,3,2,1,0:T(8,128)(2,1)S(1)} %fusion.6), kind=kLoop, calls=%fused_computation.4 | loop fusion | flops 12582912 | bytes 16777216 | tf_op jit(solution)/shard_map/stack | solution.py:80
  (37 shorter events, 7.0 us)
Async XLA Ops:
  3.3 9.6 %collective-permute-start = (f32[65536]{0:T(1024)S(1)}, f32[65536]{0:T(1024)S(1)}, u32[]{:S(2)}, u32[]{:S(2)}) collective-permute-start(f32[65536]{0:T(1024)S(1)} %bitcast.65), channel_id=1, source_target_pairs={{0,128},{32,160},{64,192},{96,224},{128,0},{160,32},{192,64},{224,... | collective-permute-start | bytes 786440 | tf_op jit(solution)/shard_map/ppermute | solution.py:33
  12.9 76.6 %copy-start = (s32[512,256]{1,0:T(8,128)S(1)}, s32[512,256]{1,0:T(8,128)}, u32[]{:S(2)}) copy-start(s32[512,256]{1,0:T(8,128)} %param.3) | copy-start | bytes 1572868
  13.0 6.2 %collective-permute-start.1 = (f32[32768]{0:T(1024)S(1)}, f32[32768]{0:T(1024)S(1)}, u32[]{:S(2)}, u32[]{:S(2)}) collective-permute-start(f32[32768]{0:T(1024)S(1)} %slice_select_fusion), channel_id=1, source_target_pairs={{0,64},{32,96},{64,0},{96,32},{128,192},{160,224},{192,128},{224,1... | collective-permute-start | bytes 393224 | tf_op jit(solution)/shard_map/ppermute | solution.py:33
  19.2 81.3 %collective-permute-start.6 = (bf16[2,8,512,256]{3,2,0,1:T(8,128)(2,1)}, bf16[2,8,512,256]{3,2,0,1:T(8,128)(2,1)}, u32[]{:S(2)}, u32[]{:S(2)}) collective-permute-start(bf16[2,8,512,256]{3,2,0,1:T(8,128)(2,1)} %copy.3), channel_id=1, source_target_pairs={{0,1},{1,2},{2,3},{3,4},{4,5},{5,6},{6,7},{7,8},{8,9},{9,10},{10,1... | collective-permute-start | bytes 12582920 | tf_op jit(solution)/shard_map/ppermute | solution.py:15
  19.2 51.1 %collective-permute-start.2 = (f32[16384]{0:T(1024)S(1)}, f32[16384]{0:T(1024)S(1)}, u32[]{:S(2)}, u32[]{:S(2)}) collective-permute-start(f32[16384]{0:T(1024)S(1)} %slice_select_fusion.1), channel_id=1, source_target_pairs={{0,32},{32,0},{64,96},{96,64},{128,160},{160,128},{192,224},{224,1... | collective-permute-start | bytes 196616 | tf_op jit(solution)/shard_map/ppermute | solution.py:33
  70.3 5.9 %collective-permute-start.3 = (f32[16384]{0:T(1024)S(1)}, f32[16384]{0:T(1024)S(1)}, u32[]{:S(2)}, u32[]{:S(2)}) collective-permute-start(f32[16384]{0:T(1024)S(1)} %select_add_fusion.1), channel_id=1, source_target_pairs={{0,32},{32,0},{64,96},{96,64},{128,160},{160,128},{192,224},{224,1... | collective-permute-start | bytes 196616 | tf_op jit(solution)/shard_map/ppermute | solution.py:38
  76.2 5.1 %collective-permute-start.4 = (f32[32768]{0:T(1024)S(1)}, f32[32768]{0:T(1024)S(1)}, u32[]{:S(2)}, u32[]{:S(2)}) collective-permute-start(f32[32768]{0:T(1024)S(1)} %maximum_select_fusion.4), channel_id=1, source_target_pairs={{0,64},{32,96},{64,0},{96,32},{128,192},{160,224},{192,128},{224,1... | collective-permute-start | bytes 393224 | tf_op jit(solution)/shard_map/ppermute | solution.py:38
  76.8 56.2 %collective-permute-start.8 = (bf16[2,8,512,256]{3,2,1,0:T(8,128)(2,1)}, bf16[2,8,512,256]{3,2,1,0:T(8,128)(2,1)}, u32[]{:S(2)}, u32[]{:S(2)}) collective-permute-start(bf16[2,8,512,256]{3,2,1,0:T(8,128)(2,1)} %param.2), channel_id=1, source_target_pairs={{0,30},{2,0},{4,2},{6,4},{8,6},{10,8},{12,10},{14,12},{16,14},{18,... | collective-permute-start | bytes 12582920 | tf_op jit(solution)/shard_map/ppermute | solution.py:15
  81.3 8.2 %collective-permute-start.5 = (f32[65536]{0:T(1024)S(1)}, f32[65536]{0:T(1024)S(1)}, u32[]{:S(2)}, u32[]{:S(2)}) collective-permute-start(f32[65536]{0:T(1024)S(1)} %maximum_select_fusion.2), channel_id=1, source_target_pairs={{0,128},{32,160},{64,192},{96,224},{128,0},{160,32},{192,64},{224,... | collective-permute-start | bytes 786440 | tf_op jit(solution)/shard_map/ppermute | solution.py:38
  89.7 10.8 %collective-permute-start.7 = (f32[512,256]{1,0:T(8,128)S(1)}, f32[512,256]{1,0:T(8,128)S(1)}, u32[]{:S(2)}, u32[]{:S(2)}) collective-permute-start(f32[512,256]{1,0:T(8,128)S(1)} %fusion.43), channel_id=1, source_target_pairs={{0,1},{1,2},{2,3},{3,4},{4,5},{5,6},{6,7},{7,8},{8,9},{9,10},{10,1... | collective-permute-start | bytes 1572872 | tf_op jit(solution)/shard_map/ppermute | solution.py:15
  105.6 50.4 %collective-permute-start.10 = (bf16[2,8,512,256]{3,2,0,1:T(8,128)(2,1)}, bf16[2,8,512,256]{3,2,0,1:T(8,128)(2,1)}, u32[]{:S(2)}, u32[]{:S(2)}) collective-permute-start(bf16[2,8,512,256]{3,2,0,1:T(8,128)(2,1)} %multiply_convert_fusion.1), channel_id=1, source_target_pairs={{0,1},{1,2},{2,3},{3,4},{4,5},{5,6},{6,7},{7,8},{8,9},{9,10},{10,1... | collective-permute-start | bytes 12582920 | tf_op jit(solution)/shard_map/ppermute | solution.py:15
  105.6 27.4 %collective-permute-start.9 = (f32[512,256]{1,0:T(8,128)S(1)}, f32[512,256]{1,0:T(8,128)S(1)}, u32[]{:S(2)}, u32[]{:S(2)}) collective-permute-start(f32[512,256]{1,0:T(8,128)S(1)} %fusion.43), channel_id=1, source_target_pairs={{0,30},{2,0},{4,2},{6,4},{8,6},{10,8},{12,10},{14,12},{16,14},{18,... | collective-permute-start | bytes 1572872 | tf_op jit(solution)/shard_map/ppermute | solution.py:15
  156.0 21.0 %collective-permute-start.12 = (bf16[2,8,512,256]{3,2,0,1:T(8,128)(2,1)}, bf16[2,8,512,256]{3,2,0,1:T(8,128)(2,1)S(1)}, u32[]{:S(2)}, u32[]{:S(2)}) collective-permute-start(bf16[2,8,512,256]{3,2,0,1:T(8,128)(2,1)} %collective-permute-done.10), channel_id=1, source_target_pairs={{0,1},{2,3},{4,5},{6,7},{8,9},{10,11},{12,13},{14,15},{16,17},{18,... | collective-permute-start | bytes 12582920 | tf_op jit(solution)/shard_map/ppermute | solution.py:15
  166.7 30.0 %collective-permute-start.11 = (bf16[2,8,256,256]{3,2,1,0:T(8,128)(2,1)S(1)}, bf16[2,8,256,256]{3,2,1,0:T(8,128)(2,1)S(1)}, u32[]{:S(2)}, u32[]{:S(2)}) collective-permute-start(bf16[2,8,256,256]{3,2,1,0:T(8,128)(2,1)S(1)} %fusion.8), channel_id=1, source_target_pairs={{0,2},{2,4},{4,6},{6,8},{8,10},{10,12},{12,14},{14,16},{16,18},{18... | collective-permute-start | bytes 6291464 | tf_op jit(solution)/shard_map/ppermute | solution.py:15

commit v4 on v3

--- a/solution.py
+++ b/solution.py
@@ -59,16 +59,18 @@
     even = lax.axis_index("chan") % 2 == 0
     raw_near = moved(spectra, "chan", 1)
     raw_ahead = moved(spectra, "chan", -2, only_even=True)
+    raw_second = moved(raw_near, "chan", 1)
     energy = butterfly_sum(partial_energy, "band")
     window_gain = valid_mask.astype(jnp.float32) / jnp.sqrt(energy / total_bins + eps_energy)
     gain_near = moved(window_gain, "chan", 1)
     gain_ahead = moved(window_gain, "chan", -2, only_even=True)
+    gain_second = moved(gain_near, "chan", 1)
     whitened = whiten(spectra, window_gain)
     near = whiten(raw_near, gain_near)
     ahead = whiten(raw_ahead, gain_ahead)
-    second = moved(near, "chan", 1)
     for_above = cross_block(ahead, near, scale)
-    for_above, second = lax.optimization_barrier((for_above, second))
+    for_above, raw_second = lax.optimization_barrier((for_above, raw_second))
+    second = whiten(raw_second, gain_second)
     third = moved(second, "chan", 1, only_even=True)
     from_below = moved(for_above, "chan", 2, only_even=True)
     outputs = [

time: 202 us -> 195 us (0.965)
  waiting for transfers between devices: 131 us -> 99.5 us
  starting transfers between devices: 16.9 us -> 47.5 us
  other arithmetic: 23.9 us -> 19.5 us
  matrix products: 24.3 us -> 21 us
    ppermute x7 -> x8, starting transfers between devices: 7.78 us -> 32.8 us  [moved(): return lax.ppermute(value, axis, pairs)]
    ppermute x3, waiting for transfers between devices: 56.7 us -> 38 us  [butterfly_sum(): got = lax.ppermute(jnp.where(bit == 0, high, low), axis, pairs)]
    ppermute x7 -> x8, waiting for transfers between devices: 60.8 us -> 50.8 us  [moved(): return lax.ppermute(value, axis, pairs)]
    dot_general x5, matrix products: 14.9 us -> 10 us  [cross_block(): jnp.einsum('pfwa,pfwb->fab', own_block, partner, preferred_element_type=j...]
    ppermute x3, starting transfers between devices: 3.62 us -> 8.05 us  [butterfly_sum(): got = lax.ppermute(flat, axis, pairs)]
    slice x4, other arithmetic: 5.55 us -> 2.41 us  [cross_block(): flipped = jnp.stack([partner[1], -partner[0]])]
    ppermute x3, waiting for transfers between devices: 13.5 us -> 10.7 us  [butterfly_sum(): got = lax.ppermute(flat, axis, pairs)]
    reduce_sum x1, other arithmetic: 3.06 us -> 0.83 us  [shards(): partial_energy = jnp.sum(values * values, axis=(0, 1))]
  transfers between devices with their start and end apart: 13 -> 14, of which waited for: 9 -> 8; matrix products, arithmetic and copies ran while one was open for 22% -> 17% of each run, Pallas kernels for 0% -> 0%
where the time goes in v4:
time: 195 us; the launch traced here: 194 us
  waiting for transfers between devices  99.5 us (51%)
  starting transfers between devices  47.5 us (24%)
  matrix products  21 us (11%)
  other arithmetic  19.5 us (10%)
  local copies, waits for them, and re-layouts  6.14 us (3%)
    ppermute x8, waiting for transfers between devices, moved(): return lax.ppermute(value, axis, pairs)  50.8 us
    ppermute x3, waiting for transfers between devices, butterfly_sum(): got = lax.ppermute(jnp.where(bit == 0, high, low), axis, pairs)  38 us
    ppermute x8, starting transfers between devices, moved(): return lax.ppermute(value, axis, pairs)  32.8 us
    dot_general x5, matrix products, cross_block(): jnp.einsum('pfwa,pfwb->fab', own_block, flipped, preferred_element_type=j...  10.9 us
    ppermute x3, waiting for transfers between devices, butterfly_sum(): got = lax.ppermute(flat, axis, pairs)  10.7 us
    dot_general x5, matrix products, cross_block(): jnp.einsum('pfwa,pfwb->fab', own_block, partner, preferred_element_type=j...  10 us
    convert_element_type x3, other arithmetic, whiten(): return (raw.astype(jnp.float32) * gain).astype(jnp.bfloat16)  9.14 us
    ppermute x3, starting transfers between devices, butterfly_sum(): got = lax.ppermute(flat, axis, pairs)  8.05 us
  transfers between devices with their start and end apart: 14, of which 8 were waited for; matrix products, arithmetic and copies ran while one was open for 17% of the time, Pallas kernels for 0%

profile of v4, /device:TPU:4, one launch (start us, length us, event | category | flops | bytes accessed | tf_op | source)
XLA Modules:
  0.0 194.1 jit_solution(17006945137813991057)
XLA Ops:
  0.0 4.7 %copy.3 = bf16[2,8,512,256]{3,2,0,1:T(8,128)(2,1)} copy(bf16[2,8,512,256]{3,2,1,0:T(8,128)(2,1)} %param.2) | data formatting | bytes 8388608 | tf_op args[0]
  5.8 3.3 %collective-permute-start = (f32[65536]{0:T(1024)S(1)}, f32[65536]{0:T(1024)S(1)}, u32[]{:S(2)}, u32[]{:S(2)}) collective-permute-start(f32[65536]{0:T(1024)S(1)} %bitcast.65), channel_id=1, source_target_pairs={{0,128},{32,160},{64,192},{96,224},{128,0},{160,32},{192,64},{224,... | collective-permute-start | bytes 786440 | tf_op jit(solution)/shard_map/ppermute | solution.py:33
  9.2 6.3 %collective-permute-done = f32[65536]{0:T(1024)S(1)} collective-permute-done((f32[65536]{0:T(1024)S(1)}, f32[65536]{0:T(1024)S(1)}, u32[]{:S(2)}, u32[]{:S(2)}) %collective-permute-start) | collective-permute-done | bytes 262176 | tf_op jit(solution)/shard_map/ppermute | solution.py:33
  15.6 1.7 collective-permute-start.1
  17.2 4.5 %collective-permute-done.1 = f32[32768]{0:T(1024)S(1)} collective-permute-done((f32[32768]{0:T(1024)S(1)}, f32[32768]{0:T(1024)S(1)}, u32[]{:S(2)}, u32[]{:S(2)}) %collective-permute-start.1) | collective-permute-done | bytes 131104 | tf_op jit(solution)/shard_map/ppermute | solution.py:33
  21.7 1.7 collective-permute-start.2
  23.4 7.1 %collective-permute-start.8 = (bf16[2,8,512,256]{3,2,1,0:T(8,128)(2,1)}, bf16[2,8,512,256]{3,2,1,0:T(8,128)(2,1)}, u32[]{:S(2)}, u32[]{:S(2)}) collective-permute-start(bf16[2,8,512,256]{3,2,1,0:T(8,128)(2,1)} %param.2), channel_id=1, source_target_pairs={{0,30},{2,0},{4,2},{6,4},{8,6},{10,8},{12,10},{14,12},{16,14},{18,... | collective-permute-start | bytes 12582920 | tf_op jit(solution)/shard_map/ppermute | solution.py:15
  30.5 27.3 %collective-permute-done.2 = f32[16384]{0:T(1024)S(1)} collective-permute-done((f32[16384]{0:T(1024)S(1)}, f32[16384]{0:T(1024)S(1)}, u32[]{:S(2)}, u32[]{:S(2)}) %collective-permute-start.2) | collective-permute-done | bytes 65568 | tf_op jit(solution)/shard_map/ppermute | solution.py:33
  57.8 3.1 %collective-permute-start.3 = (f32[16384]{0:T(1024)S(1)}, f32[16384]{0:T(1024)S(1)}, u32[]{:S(2)}, u32[]{:S(2)}) collective-permute-start(f32[16384]{0:T(1024)S(1)} %select_add_fusion.1), channel_id=1, source_target_pairs={{0,32},{32,0},{64,96},{96,64},{128,160},{160,128},{192,224},{224,1... | collective-permute-start | bytes 196616 | tf_op jit(solution)/shard_map/ppermute | solution.py:38
  60.9 2.7 %collective-permute-done.3 = f32[16384]{0:T(1024)S(1)} collective-permute-done((f32[16384]{0:T(1024)S(1)}, f32[16384]{0:T(1024)S(1)}, u32[]{:S(2)}, u32[]{:S(2)}) %collective-permute-start.3) | collective-permute-done | bytes 65568 | tf_op jit(solution)/shard_map/ppermute | solution.py:38
  63.7 1.7 collective-permute-start.4
  65.3 3.4 %collective-permute-done.4 = f32[32768]{0:T(1024)S(1)} collective-permute-done((f32[32768]{0:T(1024)S(1)}, f32[32768]{0:T(1024)S(1)}, u32[]{:S(2)}, u32[]{:S(2)}) %collective-permute-start.4) | collective-permute-done | bytes 131104 | tf_op jit(solution)/shard_map/ppermute | solution.py:38
  68.7 3.3 %collective-permute-start.5 = (f32[65536]{0:T(1024)S(1)}, f32[65536]{0:T(1024)S(1)}, u32[]{:S(2)}, u32[]{:S(2)}) collective-permute-start(f32[65536]{0:T(1024)S(1)} %maximum_select_fusion.2), channel_id=1, source_target_pairs={{0,128},{32,160},{64,192},{96,224},{128,0},{160,32},{192,64},{224,... | collective-permute-start | bytes 786440 | tf_op jit(solution)/shard_map/ppermute | solution.py:38
  72.2 4.6 %collective-permute-done.5 = f32[65536]{0:T(1024)S(1)} collective-permute-done((f32[65536]{0:T(1024)S(1)}, f32[65536]{0:T(1024)S(1)}, u32[]{:S(2)}, u32[]{:S(2)}) %collective-permute-start.5) | collective-permute-done | bytes 262176 | tf_op jit(solution)/shard_map/ppermute | solution.py:38
  77.1 3.1 %fusion.1 = bf16[2,8,512,256]{3,2,0,1:T(8,128)(2,1)S(1)} fusion(f32[512,256]{1,0:T(8,128)S(1)} %fusion.43, bf16[2,8,512,256]{3,2,1,0:T(8,128)(2,1)} %param.2), kind=kLoop, calls=%fused_computation.3 | loop fusion | flops 6291456 | bytes 8912896 | tf_op jit(solution)/shard_map/convert_element_type | solution.py:51
  80.1 21.7 %collective-permute-start.9 = (f32[512,256]{1,0:T(8,128)S(1)}, f32[512,256]{1,0:T(8,128)S(1)}, u32[]{:S(2)}, u32[]{:S(2)}) collective-permute-start(f32[512,256]{1,0:T(8,128)S(1)} %fusion.43), channel_id=1, source_target_pairs={{0,30},{2,0},{4,2},{6,4},{8,6},{10,8},{12,10},{14,12},{16,14},{18,... | collective-permute-start | bytes 1572872 | tf_op jit(solution)/shard_map/ppermute | solution.py:15
  102.1 19.0 %collective-permute-done.7 = f32[512,256]{1,0:T(8,128)S(1)} collective-permute-done((f32[512,256]{1,0:T(8,128)S(1)}, f32[512,256]{1,0:T(8,128)S(1)}, u32[]{:S(2)}, u32[]{:S(2)}) %collective-permute-start.7) | collective-permute-done | bytes 524320 | tf_op jit(solution)/shard_map/ppermute | solution.py:15
  121.2 3.0 %multiply_convert_fusion.2 = bf16[2,8,512,256]{3,2,0,1:T(8,128)(2,1)S(1)} fusion(bf16[2,8,512,256]{3,2,0,1:T(8,128)(2,1)} %collective-permute-done.6, f32[512,256]{1,0:T(8,128)S(1)} %collective-permute-done.7), kind=kLoop, calls=%fused_computation.7 | loop fusion | flops 6291456 | bytes 8912896 | tf_op jit(solution)/shard_map/convert_element_type | solution.py:51
  124.5 4.4 %fusion.34 = f32[1,8,256,256]{3,2,1,0:T(8,128)S(1)} fusion(bf16[2,8,512,256]{3,2,0,1:T(8,128)(2,1)S(1)} %multiply_convert_fusion.2, bf16[2,8,512,256]{3,2,1,0:T(8,128)(2,1)} %collective-permute-done.8, f32[512,256]{1,0:T(8,128)S(1)} %collective-permute-done.9), kind=kOutput, calls=%fused_computation.49 | convolution fusion | flops 1080033280 | bytes 11010048 | tf_op jit(solution)/shard_map/pfwa,pfwb->fab/dot_general | solution.py:45
  129.0 3.4 %fusion.37 = f32[1,8,256,256]{3,2,1,0:T(8,128)S(1)} fusion(bf16[2,8,512,256]{3,2,1,0:T(8,128)(2,1)} %collective-permute-done.8, f32[512,256]{1,0:T(8,128)S(1)} %collective-permute-done.9, bf16[1,8,512,256]{3,2,0,1:T(8,128)(2,1)S(1)} %get-tuple-element.16, bf16[1,8,512,256]{3,2,0,1:T(8,128)(2,1)S(1)} %get-tuple-element.15), kind=kOutput, calls=%fused_computation.50 | convolution fusion | flops 1082130432 | bytes 11010048 | tf_op jit(solution)/shard_map/pfwa,pfwb->fab/dot_general | solution.py:46
  133.0 3.0 %multiply_convert_fusion = bf16[2,8,512,256]{3,2,0,1:T(8,128)(2,1)S(1)} fusion(bf16[2,8,512,256]{3,2,0,1:T(8,128)(2,1)} %collective-permute-done.10, f32[512,256]{1,0:T(8,128)S(1)} %collective-permute-done.11), kind=kLoop, calls=%fused_computation.5 | loop fusion | flops 6291456 | bytes 8912896 | tf_op jit(solution)/shard_map/convert_element_type | solution.py:51
  136.1 1.8 collective-permute-start.13
  137.8 1.5 fusion.31
  142.3 1.5 convolution_bitcast_fusion.2
  143.8 1.4 convolution_bitcast_fusion.3
  145.8 2.2 %collective-permute-start.12 = (bf16[2,8,256,256]{3,2,1,0:T(8,128)(2,1)S(1)}, bf16[2,8,256,256]{3,2,1,0:T(8,128)(2,1)S(1)}, u32[]{:S(2)}, u32[]{:S(2)}) collective-permute-start(bf16[2,8,256,256]{3,2,1,0:T(8,128)(2,1)S(1)} %fusion.8), channel_id=1, source_target_pairs={{0,2},{2,4},{4,6},{6,8},{8,10},{10,12},{12,14},{14,16},{16,18},{18... | collective-permute-start | bytes 6291464 | tf_op jit(solution)/shard_map/ppermute | solution.py:15
  148.0 1.6 fusion.48
  151.0 3.1 %fusion.28 = f32[1,1,8,256,256]{4,3,2,1,0:T(8,128)S(1)} fusion(bf16[2,8,512,256]{3,2,0,1:T(8,128)(2,1)S(1)} %fusion.1, bf16[1,8,512,256]{3,2,0,1:T(8,128)(2,1)} %get-tuple-element.12, bf16[1,8,512,256]{3,2,0,1:T(8,128)(2,1)S(1)} %get-tuple-element.11), kind=kOutput, calls=%fused_computation.42 | convolution fusion | flops 1075838976 | bytes 10485760 | tf_op jit(solution)/shard_map/pfwa,pfwb->fab/dot_general | solution.py:46
  154.9 1.5 fusion.25
  156.4 1.4 convolution_bitcast_fusion
  157.8 31.7 %collective-permute-done.12 = bf16[2,8,256,256]{3,2,1,0:T(8,128)(2,1)S(1)} collective-permute-done((bf16[2,8,256,256]{3,2,1,0:T(8,128)(2,1)S(1)}, bf16[2,8,256,256]{3,2,1,0:T(8,128)(2,1)S(1)}, u32[]{:S(2)}, u32[]{:S(2)}) %collective-permute-start.12) | collective-permute-done | bytes 2097184 | tf_op jit(solution)/shard_map/ppermute | solution.py:15
  190.2 3.9 %pad_maximum_fusion = bf16[4,2,8,256,256]{4,3,2,1,0:T(8,128)(2,1)} fusion(bf16[1,2,8,256,256]{4,3,2,1,0:T(8,128)(2,1)S(1)} %fusion.24, bf16[1,2,8,256,256]{4,3,2,1,0:T(8,128)(2,1)S(1)} %fusion.13, bf16[1,2,8,256,256]{4,3,2,1,0:T(8,128)(2,1)S(1)} %fusion.7, bf16[1,2,8,256,256]{4,3,2,1,0:T(8,128)(2,1)S(1)} %fusion.6), kind=kLoop, calls=%fused_computation.4 | loop fusion | flops 12582912 | bytes 16777216 | tf_op jit(solution)/shard_map/stack | solution.py:82
  (46 shorter events, 9.3 us)
Async XLA Ops:
  0.0 4.7 %copy-start = (bf16[2,8,512,256]{3,2,1,0:T(8,128)(2,1)S(1)}, bf16[2,8,512,256]{3,2,1,0:T(8,128)(2,1)}, u32[]{:S(2)}) copy-start(bf16[2,8,512,256]{3,2,1,0:T(8,128)(2,1)} %param.2) | copy-start | bytes 12582916
  4.7 60.6 %collective-permute-start.6 = (bf16[2,8,512,256]{3,2,0,1:T(8,128)(2,1)}, bf16[2,8,512,256]{3,2,0,1:T(8,128)(2,1)}, u32[]{:S(2)}, u32[]{:S(2)}) collective-permute-start(bf16[2,8,512,256]{3,2,0,1:T(8,128)(2,1)} %copy.3), channel_id=1, source_target_pairs={{0,1},{1,2},{2,3},{3,4},{4,5},{5,6},{6,7},{7,8},{8,9},{9,10},{10,1... | collective-permute-start | bytes 12582920 | tf_op jit(solution)/shard_map/ppermute | solution.py:15
  5.6 71.3 %copy-start.3 = (s32[512,256]{1,0:T(8,128)S(1)}, s32[512,256]{1,0:T(8,128)}, u32[]{:S(2)}) copy-start(s32[512,256]{1,0:T(8,128)} %param.3) | copy-start | bytes 1572868
  5.8 9.7 %collective-permute-start = (f32[65536]{0:T(1024)S(1)}, f32[65536]{0:T(1024)S(1)}, u32[]{:S(2)}, u32[]{:S(2)}) collective-permute-start(f32[65536]{0:T(1024)S(1)} %bitcast.65), channel_id=1, source_target_pairs={{0,128},{32,160},{64,192},{96,224},{128,0},{160,32},{192,64},{224,... | collective-permute-start | bytes 786440 | tf_op jit(solution)/shard_map/ppermute | solution.py:33
  15.6 6.1 %collective-permute-start.1 = (f32[32768]{0:T(1024)S(1)}, f32[32768]{0:T(1024)S(1)}, u32[]{:S(2)}, u32[]{:S(2)}) collective-permute-start(f32[32768]{0:T(1024)S(1)} %slice_select_fusion), channel_id=1, source_target_pairs={{0,64},{32,96},{64,0},{96,32},{128,192},{160,224},{192,128},{224,1... | collective-permute-start | bytes 393224 | tf_op jit(solution)/shard_map/ppermute | solution.py:33
  21.7 36.0 %collective-permute-start.2 = (f32[16384]{0:T(1024)S(1)}, f32[16384]{0:T(1024)S(1)}, u32[]{:S(2)}, u32[]{:S(2)}) collective-permute-start(f32[16384]{0:T(1024)S(1)} %slice_select_fusion.1), channel_id=1, source_target_pairs={{0,32},{32,0},{64,96},{96,64},{128,160},{160,128},{192,224},{224,1... | collective-permute-start | bytes 196616 | tf_op jit(solution)/shard_map/ppermute | solution.py:33
  23.4 101.1 %collective-permute-start.8 = (bf16[2,8,512,256]{3,2,1,0:T(8,128)(2,1)}, bf16[2,8,512,256]{3,2,1,0:T(8,128)(2,1)}, u32[]{:S(2)}, u32[]{:S(2)}) collective-permute-start(bf16[2,8,512,256]{3,2,1,0:T(8,128)(2,1)} %param.2), channel_id=1, source_target_pairs={{0,30},{2,0},{4,2},{6,4},{8,6},{10,8},{12,10},{14,12},{16,14},{18,... | collective-permute-start | bytes 12582920 | tf_op jit(solution)/shard_map/ppermute | solution.py:15
  57.8 5.9 %collective-permute-start.3 = (f32[16384]{0:T(1024)S(1)}, f32[16384]{0:T(1024)S(1)}, u32[]{:S(2)}, u32[]{:S(2)}) collective-permute-start(f32[16384]{0:T(1024)S(1)} %select_add_fusion.1), channel_id=1, source_target_pairs={{0,32},{32,0},{64,96},{96,64},{128,160},{160,128},{192,224},{224,1... | collective-permute-start | bytes 196616 | tf_op jit(solution)/shard_map/ppermute | solution.py:38
  63.7 5.1 %collective-permute-start.4 = (f32[32768]{0:T(1024)S(1)}, f32[32768]{0:T(1024)S(1)}, u32[]{:S(2)}, u32[]{:S(2)}) collective-permute-start(f32[32768]{0:T(1024)S(1)} %maximum_select_fusion.4), channel_id=1, source_target_pairs={{0,64},{32,96},{64,0},{96,32},{128,192},{160,224},{192,128},{224,1... | collective-permute-start | bytes 393224 | tf_op jit(solution)/shard_map/ppermute | solution.py:38
  65.3 67.7 %collective-permute-start.10 = (bf16[2,8,512,256]{3,2,0,1:T(8,128)(2,1)}, bf16[2,8,512,256]{3,2,0,1:T(8,128)(2,1)}, u32[]{:S(2)}, u32[]{:S(2)}) collective-permute-start(bf16[2,8,512,256]{3,2,0,1:T(8,128)(2,1)} %collective-permute-done.6), channel_id=1, source_target_pairs={{0,1},{1,2},{2,3},{3,4},{4,5},{5,6},{6,7},{7,8},{8,9},{9,10},{10,1... | collective-permute-start | bytes 12582920 | tf_op jit(solution)/shard_map/ppermute | solution.py:15
  68.7 8.0 %collective-permute-start.5 = (f32[65536]{0:T(1024)S(1)}, f32[65536]{0:T(1024)S(1)}, u32[]{:S(2)}, u32[]{:S(2)}) collective-permute-start(f32[65536]{0:T(1024)S(1)} %maximum_select_fusion.2), channel_id=1, source_target_pairs={{0,128},{32,160},{64,192},{96,224},{128,0},{160,32},{192,64},{224,... | collective-permute-start | bytes 786440 | tf_op jit(solution)/shard_map/ppermute | solution.py:38
  77.0 44.2 %collective-permute-start.7 = (f32[512,256]{1,0:T(8,128)S(1)}, f32[512,256]{1,0:T(8,128)S(1)}, u32[]{:S(2)}, u32[]{:S(2)}) collective-permute-start(f32[512,256]{1,0:T(8,128)S(1)} %fusion.43), channel_id=1, source_target_pairs={{0,1},{1,2},{2,3},{3,4},{4,5},{5,6},{6,7},{7,8},{8,9},{9,10},{10,1... | collective-permute-start | bytes 1572872 | tf_op jit(solution)/shard_map/ppermute | solution.py:15
  80.1 44.4 %collective-permute-start.9 = (f32[512,256]{1,0:T(8,128)S(1)}, f32[512,256]{1,0:T(8,128)S(1)}, u32[]{:S(2)}, u32[]{:S(2)}) collective-permute-start(f32[512,256]{1,0:T(8,128)S(1)} %fusion.43), channel_id=1, source_target_pairs={{0,30},{2,0},{4,2},{6,4},{8,6},{10,8},{12,10},{14,12},{16,14},{18,... | collective-permute-start | bytes 1572872 | tf_op jit(solution)/shard_map/ppermute | solution.py:15
  121.2 11.8 %collective-permute-start.11 = (f32[512,256]{1,0:T(8,128)S(1)}, f32[512,256]{1,0:T(8,128)S(1)}, u32[]{:S(2)}, u32[]{:S(2)}) collective-permute-start(f32[512,256]{1,0:T(8,128)S(1)} %collective-permute-done.7), channel_id=1, source_target_pairs={{0,1},{1,2},{2,3},{3,4},{4,5},{5,6},{6,7},{7,8},{8,9},{9,10},{10,1... | collective-permute-start | bytes 1572872 | tf_op jit(solution)/shard_map/ppermute | solution.py:15
  124.5 4.5 %copy-start.1 = (bf16[1,8,512,256]{3,2,0,1:T(8,128)(2,1)}, bf16[1,8,512,256]{3,2,0,1:T(8,128)(2,1)S(1)}, u32[]{:S(2)}) copy-start(bf16[1,8,512,256]{3,2,0,1:T(8,128)(2,1)S(1)} %get-tuple-element.16) | copy-start | bytes 6291460
  136.1 18.6 %collective-permute-start.13 = (bf16[2,8,512,256]{3,2,0,1:T(8,128)(2,1)S(1)}, bf16[2,8,512,256]{3,2,0,1:T(8,128)(2,1)S(1)}, u32[]{:S(2)}, u32[]{:S(2)}) collective-permute-start(bf16[2,8,512,256]{3,2,0,1:T(8,128)(2,1)S(1)} %multiply_convert_fusion), channel_id=1, source_target_pairs={{0,1},{2,3},{4,5},{6,7},{8,9},{10,11},{12,13},{14,15},{16,17},{18,... | collective-permute-start | bytes 12582920 | tf_op jit(solution)/shard_map/ppermute | solution.py:15
  140.7 1.6 copy-start.2
  145.8 43.7 %collective-permute-start.12 = (bf16[2,8,256,256]{3,2,1,0:T(8,128)(2,1)S(1)}, bf16[2,8,256,256]{3,2,1,0:T(8,128)(2,1)S(1)}, u32[]{:S(2)}, u32[]{:S(2)}) collective-permute-start(bf16[2,8,256,256]{3,2,1,0:T(8,128)(2,1)S(1)} %fusion.8), channel_id=1, source_target_pairs={{0,2},{2,4},{4,6},{6,8},{8,10},{10,12},{12,14},{14,16},{16,18},{18... | collective-permute-start | bytes 6291464 | tf_op jit(solution)/shard_map/ppermute | solution.py:15

commit v5 on v3

--- a/solution.py
+++ b/solution.py
@@ -15,13 +15,13 @@
     return lax.ppermute(value, axis, pairs)
 
 
-def butterfly_sum(value, axis):
+def band_sum(value, axis):
     count = lax.axis_size(axis)
     index = lax.axis_index(axis)
     flat = value.reshape(-1)
     dists = []
     d = count // 2
-    while d >= 1:
+    while d >= 2:
         dists.append(d)
         d //= 2
     bits = []
@@ -57,9 +57,11 @@
     total_bins = spectra.shape[1] * lax.axis_size("band")
     scale = 1.0 / math.sqrt(spectra.shape[2])
     even = lax.axis_index("chan") % 2 == 0
+    partial_energy = partial_energy + lax.ppermute(partial_energy, "band", [(s, s ^ 1) for s in range(lax.axis_size("band"))])
+    spectra, partial_energy = lax.optimization_barrier((spectra, partial_energy))
     raw_near = moved(spectra, "chan", 1)
     raw_ahead = moved(spectra, "chan", -2, only_even=True)
-    energy = butterfly_sum(partial_energy, "band")
+    energy = band_sum(partial_energy, "band")
     window_gain = valid_mask.astype(jnp.float32) / jnp.sqrt(energy / total_bins + eps_energy)
     gain_near = moved(window_gain, "chan", 1)
     gain_ahead = moved(window_gain, "chan", -2, only_even=True)

time: 202 us -> 184 us (0.911)
  waiting for transfers between devices: 131 us -> 102 us
  starting transfers between devices: 16.9 us -> 28.5 us
    ppermute x6 -> x5, waiting for transfers between devices: 70.1 us -> 23 us  [the longest x1 12.9 us: shards(): lax.ppermute(partial_energy, 'band', [(s, s ^ 1) for s in range(lax.axis_...]
    ppermute x7, waiting for transfers between devices: 60.8 us -> 79 us  [moved(): return lax.ppermute(value, axis, pairs)]
    ppermute x7, starting transfers between devices: 7.78 us -> 16.9 us  [moved(): return lax.ppermute(value, axis, pairs)]
    unnamed x5 -> x4, local copies, waits for them, and re-layouts: 4.85 us -> 0.28 us
    optimization_barrier x0 -> x1, local copies, waits for them, and re-layouts: none -> 4.57 us  [shards(): lax.optimization_barrier((spectra, partial_energy))]
    ppermute x6 -> x5, starting transfers between devices: 9.15 us -> 11.7 us  [the longest x2 4.96 us: band_sum(): got = lax.ppermute(jnp.where(bit == 0, high, low), axis, pairs)]
  transfers between devices with their start and end apart: 13 -> 12, of which waited for: 9 -> 8; matrix products, arithmetic and copies ran while one was open for 22% -> 25% of each run, Pallas kernels for 0% -> 0%
where the time goes in v5:
time: 184 us
  waiting for transfers between devices  102 us (55%)
  starting transfers between devices  28.5 us (15%)
  matrix products  24.3 us (13%)
  other arithmetic  23.9 us (13%)
  local copies, waits for them, and re-layouts  5 us (3%)
    ppermute x7, waiting for transfers between devices, moved(): return lax.ppermute(value, axis, pairs)  79 us
    ppermute x7, starting transfers between devices, moved(): return lax.ppermute(value, axis, pairs)  16.9 us
    dot_general x5, matrix products, cross_block(): jnp.einsum('pfwa,pfwb->fab', own_block, partner, preferred_element_type=j...  14.9 us
    ppermute x1, waiting for transfers between devices, shards(): lax.ppermute(partial_energy, 'band', [(s, s ^ 1) for s in range(lax.axis_...  12.9 us
    dot_general x5, matrix products, cross_block(): jnp.einsum('pfwa,pfwb->fab', own_block, flipped, preferred_element_type=j...  9.32 us
    convert_element_type x2, other arithmetic, whiten(): return (raw.astype(jnp.float32) * gain).astype(jnp.bfloat16)  8.12 us
    slice x4, other arithmetic, cross_block(): flipped = jnp.stack([partner[1], -partner[0]])  5.55 us
    ppermute x2, waiting for transfers between devices, band_sum(): got = lax.ppermute(jnp.where(bit == 0, high, low), axis, pairs)  5.24 us
  transfers between devices with their start and end apart: 12, of which 8 were waited for; matrix products, arithmetic and copies ran while one was open for 25% of the time, Pallas kernels for 0%

profile of v5, /device:TPU:4, one launch (start us, length us, event | category | flops | bytes accessed | tf_op | source)
XLA Modules:
  0.0 184.0 jit_solution(160979583739907101)
XLA Ops:
  0.0 3.1 %multiply_reduce_fusion = f32[512,256]{1,0:T(8,128)S(1)} fusion(bf16[2,8,512,256]{3,2,1,0:T(8,128)(2,1)} %param.2), kind=kLoop, calls=%fused_computation.4 | loop fusion | flops 6160384 | bytes 4718592 | tf_op jit(solution)/shard_map/reduce_sum | solution.py:56
  3.1 2.3 %collective-permute-start = (f32[512,256]{1,0:T(8,128)S(1)}, f32[512,256]{1,0:T(8,128)S(1)}, u32[]{:S(2)}, u32[]{:S(2)}) collective-permute-start(f32[512,256]{1,0:T(8,128)S(1)} %multiply_reduce_fusion), channel_id=1, source_target_pairs={{0,32},{32,0},{64,96},{96,64},{128,160},{160,128},{192,224},{224,1... | collective-permute-start | bytes 1572872 | tf_op jit(solution)/shard_map/ppermute | solution.py:60
  5.4 12.9 %collective-permute-done = f32[512,256]{1,0:T(8,128)S(1)} collective-permute-done((f32[512,256]{1,0:T(8,128)S(1)}, f32[512,256]{1,0:T(8,128)S(1)}, u32[]{:S(2)}, u32[]{:S(2)}) %collective-permute-start) | collective-permute-done | bytes 524320 | tf_op jit(solution)/shard_map/ppermute | solution.py:60
  18.6 3.3 %collective-permute-start.1 = (f32[65536]{0:T(1024)S(1)}, f32[65536]{0:T(1024)S(1)}, u32[]{:S(2)}, u32[]{:S(2)}) collective-permute-start(f32[65536]{0:T(1024)S(1)} %bitcast.65), channel_id=1, source_target_pairs={{0,128},{32,160},{64,192},{96,224},{128,0},{160,32},{192,64},{224,... | collective-permute-start | bytes 786440 | tf_op jit(solution)/shard_map/ppermute | solution.py:33
  21.9 4.6 %copy.3 = bf16[2,8,512,256]{3,2,0,1:T(8,128)(2,1)} copy(bf16[2,8,512,256]{3,2,1,0:T(8,128)(2,1)} %param.2) | data formatting | bytes 8388608 | tf_op jit(solution)/shard_map/optimization_barrier | solution.py:61
  27.4 1.7 collective-permute-start.2
  29.1 4.5 %collective-permute-done.2 = f32[32768]{0:T(1024)S(1)} collective-permute-done((f32[32768]{0:T(1024)S(1)}, f32[32768]{0:T(1024)S(1)}, u32[]{:S(2)}, u32[]{:S(2)}) %collective-permute-start.2) | collective-permute-done | bytes 131104 | tf_op jit(solution)/shard_map/ppermute | solution.py:33
  33.6 1.4 collective-permute-start.3
  35.0 7.6 %collective-permute-start.7 = (bf16[2,8,512,256]{3,2,1,0:T(8,128)(2,1)}, bf16[2,8,512,256]{3,2,1,0:T(8,128)(2,1)}, u32[]{:S(2)}, u32[]{:S(2)}) collective-permute-start(bf16[2,8,512,256]{3,2,1,0:T(8,128)(2,1)} %param.2), channel_id=1, source_target_pairs={{0,30},{2,0},{4,2},{6,4},{8,6},{10,8},{12,10},{14,12},{16,14},{18,... | collective-permute-start | bytes 12582920 | tf_op jit(solution)/shard_map/ppermute | solution.py:15
  42.6 3.0 %collective-permute-start.4 = (f32[65536]{0:T(1024)S(1)}, f32[65536]{0:T(1024)S(1)}, u32[]{:S(2)}, u32[]{:S(2)}) collective-permute-start(f32[65536]{0:T(1024)S(1)} %maximum_select_fusion.2), channel_id=1, source_target_pairs={{0,128},{32,160},{64,192},{96,224},{128,0},{160,32},{192,64},{224,... | collective-permute-start | bytes 786440 | tf_op jit(solution)/shard_map/ppermute | solution.py:38
  45.7 4.9 %collective-permute-done.4 = f32[65536]{0:T(1024)S(1)} collective-permute-done((f32[65536]{0:T(1024)S(1)}, f32[65536]{0:T(1024)S(1)}, u32[]{:S(2)}, u32[]{:S(2)}) %collective-permute-start.4) | collective-permute-done | bytes 262176 | tf_op jit(solution)/shard_map/ppermute | solution.py:38
  50.8 32.4 %collective-permute-done.6 = f32[512,256]{1,0:T(8,128)S(1)} collective-permute-done((f32[512,256]{1,0:T(8,128)S(1)}, f32[512,256]{1,0:T(8,128)S(1)}, u32[]{:S(2)}, u32[]{:S(2)}) %collective-permute-start.6) | collective-permute-done | bytes 524320 | tf_op jit(solution)/shard_map/ppermute | solution.py:15
  83.2 5.1 %multiply_convert_fusion.1 = bf16[2,8,512,256]{3,2,0,1:T(8,128)(2,1)} fusion(bf16[2,8,512,256]{3,2,0,1:T(8,128)(2,1)} %collective-permute-done.5, f32[512,256]{1,0:T(8,128)S(1)} %collective-permute-done.6), kind=kLoop, calls=%fused_computation.2 | loop fusion | flops 6291456 | bytes 8912896 | tf_op jit(solution)/shard_map/convert_element_type | solution.py:51
  88.3 5.5 %collective-permute-start.8 = (f32[512,256]{1,0:T(8,128)S(1)}, f32[512,256]{1,0:T(8,128)S(1)}, u32[]{:S(2)}, u32[]{:S(2)}) collective-permute-start(f32[512,256]{1,0:T(8,128)S(1)} %fusion.41), channel_id=1, source_target_pairs={{0,30},{2,0},{4,2},{6,4},{8,6},{10,8},{12,10},{14,12},{16,14},{18,... | collective-permute-start | bytes 1572872 | tf_op jit(solution)/shard_map/ppermute | solution.py:15
  93.9 3.0 %multiply_convert_fusion.2 = bf16[2,8,512,256]{3,2,0,1:T(8,128)(2,1)S(1)} fusion(f32[512,256]{1,0:T(8,128)S(1)} %fusion.41, bf16[2,8,512,256]{3,2,1,0:T(8,128)(2,1)} %param.2), kind=kLoop, calls=%fused_computation.3 | loop fusion | flops 6291456 | bytes 8912896 | tf_op jit(solution)/shard_map/convert_element_type | solution.py:51
  97.2 2.5 %fusion.48 = (bf16[1,8,512,256]{3,2,0,1:T(8,128)(2,1)S(1)}, bf16[1,8,512,256]{3,2,0,1:T(8,128)(2,1)S(1)}) fusion(bf16[2,8,512,256]{3,2,0,1:T(8,128)(2,1)} %multiply_convert_fusion.1), kind=kLoop, calls=%fused_computation.65 | loop fusion | flops 1048576 | bytes 8388608 | tf_op jit(solution)/shard_map/slice | solution.py:44
  100.4 3.4 %fusion.35 = f32[1,8,256,256]{3,2,1,0:T(8,128)S(1)} fusion(bf16[2,8,512,256]{3,2,1,0:T(8,128)(2,1)} %collective-permute-done.7, f32[512,256]{1,0:T(8,128)S(1)} %collective-permute-done.8, bf16[1,8,512,256]{3,2,0,1:T(8,128)(2,1)S(1)} %get-tuple-element.20, bf16[1,8,512,256]{3,2,0,1:T(8,128)(2,1)S(1)} %get-tuple-element.19), kind=kOutput, calls=%fused_computation.47 | convolution fusion | flops 1082130432 | bytes 11010048 | tf_op jit(solution)/shard_map/pfwa,pfwb->fab/dot_general | solution.py:46
  103.8 5.0 %fusion.32 = f32[1,8,256,256]{3,2,1,0:T(8,128)S(1)} fusion(bf16[2,8,512,256]{3,2,0,1:T(8,128)(2,1)} %multiply_convert_fusion.1, bf16[2,8,512,256]{3,2,1,0:T(8,128)(2,1)} %collective-permute-done.7, f32[512,256]{1,0:T(8,128)S(1)} %collective-permute-done.8), kind=kOutput, calls=%fused_computation.46 | convolution fusion | flops 1080033280 | bytes 11010048 | tf_op jit(solution)/shard_map/pfwa,pfwb->fab/dot_general | solution.py:45
  109.3 29.4 %collective-permute-done.9 = bf16[2,8,512,256]{3,2,0,1:T(8,128)(2,1)} collective-permute-done((bf16[2,8,512,256]{3,2,0,1:T(8,128)(2,1)}, bf16[2,8,512,256]{3,2,0,1:T(8,128)(2,1)}, u32[]{:S(2)}, u32[]{:S(2)}) %collective-permute-start.9) | collective-permute-done | bytes 4194336 | tf_op jit(solution)/shard_map/ppermute | solution.py:15
  138.7 1.5 collective-permute-start.11
  140.2 1.5 fusion.29
  141.7 1.4 convolution_bitcast_fusion.4
  143.7 1.5 convolution_bitcast_fusion.2
  145.2 3.6 %convolution_bitcast_fusion.3 = f32[1,1,8,256,256]{4,3,2,1,0:T(8,128)S(1)} fusion(bf16[2,8,512,256]{3,2,0,1:T(8,128)(2,1)S(1)} %multiply_convert_fusion.2, bf16[2,8,512,256]{3,2,0,1:T(8,128)(2,1)} %multiply_convert_fusion.1), kind=kOutput, calls=%fused_computation.44 | convolution fusion | flops 1073741824 | bytes 10485760 | tf_op jit(solution)/shard_map/pfwa,pfwb->fab/dot_general | solution.py:45
  149.4 2.1 %collective-permute-start.10 = (bf16[2,8,256,256]{3,2,1,0:T(8,128)(2,1)S(1)}, bf16[2,8,256,256]{3,2,1,0:T(8,128)(2,1)S(1)}, u32[]{:S(2)}, u32[]{:S(2)}) collective-permute-start(bf16[2,8,256,256]{3,2,1,0:T(8,128)(2,1)S(1)} %fusion.6), channel_id=1, source_target_pairs={{0,2},{2,4},{4,6},{6,8},{8,10},{10,12},{12,14},{14,16},{16,18},{18... | collective-permute-start | bytes 6291464 | tf_op jit(solution)/shard_map/ppermute | solution.py:15
  151.5 2.5 %fusion.46 = (bf16[1,8,512,256]{3,2,0,1:T(8,128)(2,1)S(1)}, bf16[1,8,512,256]{3,2,0,1:T(8,128)(2,1)S(1)}) fusion(bf16[2,8,512,256]{3,2,0,1:T(8,128)(2,1)} %collective-permute-done.9), kind=kLoop, calls=%fused_computation.63 | loop fusion | flops 1048576 | bytes 8388608 | tf_op jit(solution)/shard_map/slice | solution.py:44
  154.1 3.6 %convolution_bitcast_fusion.1 = f32[1,1,8,256,256]{4,3,2,1,0:T(8,128)S(1)} fusion(bf16[2,8,512,256]{3,2,0,1:T(8,128)(2,1)S(1)} %multiply_convert_fusion.2, bf16[2,8,512,256]{3,2,0,1:T(8,128)(2,1)} %collective-permute-done.9), kind=kOutput, calls=%fused_computation.42 | convolution fusion | flops 1073741824 | bytes 10485760 | tf_op jit(solution)/shard_map/pfwa,pfwb->fab/dot_general | solution.py:45
  157.6 1.5 fusion.26
  160.0 1.5 fusion.23
  161.4 1.4 convolution_bitcast_fusion
  162.9 16.6 %collective-permute-done.10 = bf16[2,8,256,256]{3,2,1,0:T(8,128)(2,1)S(1)} collective-permute-done((bf16[2,8,256,256]{3,2,1,0:T(8,128)(2,1)S(1)}, bf16[2,8,256,256]{3,2,1,0:T(8,128)(2,1)S(1)}, u32[]{:S(2)}, u32[]{:S(2)}) %collective-permute-start.10) | collective-permute-done | bytes 2097184 | tf_op jit(solution)/shard_map/ppermute | solution.py:15
  180.2 3.9 %pad_maximum_fusion = bf16[4,2,8,256,256]{4,3,2,1,0:T(8,128)(2,1)} fusion(bf16[1,2,8,256,256]{4,3,2,1,0:T(8,128)(2,1)S(1)} %fusion.22, bf16[1,2,8,256,256]{4,3,2,1,0:T(8,128)(2,1)S(1)} %fusion.11, bf16[1,2,8,256,256]{4,3,2,1,0:T(8,128)(2,1)S(1)} %fusion.5, bf16[1,2,8,256,256]{4,3,2,1,0:T(8,128)(2,1)S(1)} %fusion.4), kind=kLoop, calls=%fused_computation | loop fusion | flops 12582912 | bytes 16777216 | tf_op jit(solution)/shard_map/stack | solution.py:82
  (31 shorter events, 5.8 us)
Async XLA Ops:
  3.1 15.3 %collective-permute-start = (f32[512,256]{1,0:T(8,128)S(1)}, f32[512,256]{1,0:T(8,128)S(1)}, u32[]{:S(2)}, u32[]{:S(2)}) collective-permute-start(f32[512,256]{1,0:T(8,128)S(1)} %multiply_reduce_fusion), channel_id=1, source_target_pairs={{0,32},{32,0},{64,96},{96,64},{128,160},{160,128},{192,224},{224,1... | collective-permute-start | bytes 1572872 | tf_op jit(solution)/shard_map/ppermute | solution.py:60
  18.6 8.8 %collective-permute-start.1 = (f32[65536]{0:T(1024)S(1)}, f32[65536]{0:T(1024)S(1)}, u32[]{:S(2)}, u32[]{:S(2)}) collective-permute-start(f32[65536]{0:T(1024)S(1)} %bitcast.65), channel_id=1, source_target_pairs={{0,128},{32,160},{64,192},{96,224},{128,0},{160,32},{192,64},{224,... | collective-permute-start | bytes 786440 | tf_op jit(solution)/shard_map/ppermute | solution.py:33
  26.4 24.2 %copy-start = (s32[512,256]{1,0:T(8,128)S(1)}, s32[512,256]{1,0:T(8,128)}, u32[]{:S(2)}) copy-start(s32[512,256]{1,0:T(8,128)} %param.3) | copy-start | bytes 1572868
  26.4 56.8 %collective-permute-start.5 = (bf16[2,8,512,256]{3,2,0,1:T(8,128)(2,1)}, bf16[2,8,512,256]{3,2,0,1:T(8,128)(2,1)}, u32[]{:S(2)}, u32[]{:S(2)}) collective-permute-start(bf16[2,8,512,256]{3,2,0,1:T(8,128)(2,1)} %copy.3), channel_id=1, source_target_pairs={{0,1},{1,2},{2,3},{3,4},{4,5},{5,6},{6,7},{7,8},{8,9},{9,10},{10,1... | collective-permute-start | bytes 12582920 | tf_op jit(solution)/shard_map/ppermute | solution.py:15
  27.4 6.2 %collective-permute-start.2 = (f32[32768]{0:T(1024)S(1)}, f32[32768]{0:T(1024)S(1)}, u32[]{:S(2)}, u32[]{:S(2)}) collective-permute-start(f32[32768]{0:T(1024)S(1)} %slice_select_fusion), channel_id=1, source_target_pairs={{0,64},{32,96},{64,0},{96,32},{128,192},{160,224},{192,128},{224,1... | collective-permute-start | bytes 393224 | tf_op jit(solution)/shard_map/ppermute | solution.py:33
  33.6 9.0 %collective-permute-start.3 = (f32[32768]{0:T(1024)S(1)}, f32[32768]{0:T(1024)S(1)}, u32[]{:S(2)}, u32[]{:S(2)}) collective-permute-start(f32[32768]{0:T(1024)S(1)} %select_add_fusion), channel_id=1, source_target_pairs={{0,64},{32,96},{64,0},{96,32},{128,192},{160,224},{192,128},{224,1... | collective-permute-start | bytes 393224 | tf_op jit(solution)/shard_map/ppermute | solution.py:38
  35.0 65.4 %collective-permute-start.7 = (bf16[2,8,512,256]{3,2,1,0:T(8,128)(2,1)}, bf16[2,8,512,256]{3,2,1,0:T(8,128)(2,1)}, u32[]{:S(2)}, u32[]{:S(2)}) collective-permute-start(bf16[2,8,512,256]{3,2,1,0:T(8,128)(2,1)} %param.2), channel_id=1, source_target_pairs={{0,30},{2,0},{4,2},{6,4},{8,6},{10,8},{12,10},{14,12},{16,14},{18,... | collective-permute-start | bytes 12582920 | tf_op jit(solution)/shard_map/ppermute | solution.py:15
  42.6 8.0 %collective-permute-start.4 = (f32[65536]{0:T(1024)S(1)}, f32[65536]{0:T(1024)S(1)}, u32[]{:S(2)}, u32[]{:S(2)}) collective-permute-start(f32[65536]{0:T(1024)S(1)} %maximum_select_fusion.2), channel_id=1, source_target_pairs={{0,128},{32,160},{64,192},{96,224},{128,0},{160,32},{192,64},{224,... | collective-permute-start | bytes 786440 | tf_op jit(solution)/shard_map/ppermute | solution.py:38
  50.8 32.5 %collective-permute-start.6 = (f32[512,256]{1,0:T(8,128)S(1)}, f32[512,256]{1,0:T(8,128)S(1)}, u32[]{:S(2)}, u32[]{:S(2)}) collective-permute-start(f32[512,256]{1,0:T(8,128)S(1)} %fusion.41), channel_id=1, source_target_pairs={{0,1},{1,2},{2,3},{3,4},{4,5},{5,6},{6,7},{7,8},{8,9},{9,10},{10,1... | collective-permute-start | bytes 1572872 | tf_op jit(solution)/shard_map/ppermute | solution.py:15
  88.3 50.4 %collective-permute-start.9 = (bf16[2,8,512,256]{3,2,0,1:T(8,128)(2,1)}, bf16[2,8,512,256]{3,2,0,1:T(8,128)(2,1)}, u32[]{:S(2)}, u32[]{:S(2)}) collective-permute-start(bf16[2,8,512,256]{3,2,0,1:T(8,128)(2,1)} %multiply_convert_fusion.1), channel_id=1, source_target_pairs={{0,1},{1,2},{2,3},{3,4},{4,5},{5,6},{6,7},{7,8},{8,9},{9,10},{10,1... | collective-permute-start | bytes 12582920 | tf_op jit(solution)/shard_map/ppermute | solution.py:15
  88.3 12.0 %collective-permute-start.8 = (f32[512,256]{1,0:T(8,128)S(1)}, f32[512,256]{1,0:T(8,128)S(1)}, u32[]{:S(2)}, u32[]{:S(2)}) collective-permute-start(f32[512,256]{1,0:T(8,128)S(1)} %fusion.41), channel_id=1, source_target_pairs={{0,30},{2,0},{4,2},{6,4},{8,6},{10,8},{12,10},{14,12},{16,14},{18,... | collective-permute-start | bytes 1572872 | tf_op jit(solution)/shard_map/ppermute | solution.py:15
  138.7 21.0 %collective-permute-start.11 = (bf16[2,8,512,256]{3,2,0,1:T(8,128)(2,1)}, bf16[2,8,512,256]{3,2,0,1:T(8,128)(2,1)S(1)}, u32[]{:S(2)}, u32[]{:S(2)}) collective-permute-start(bf16[2,8,512,256]{3,2,0,1:T(8,128)(2,1)} %collective-permute-done.9), channel_id=1, source_target_pairs={{0,1},{2,3},{4,5},{6,7},{8,9},{10,11},{12,13},{14,15},{16,17},{18,... | collective-permute-start | bytes 12582920 | tf_op jit(solution)/shard_map/ppermute | solution.py:15
  149.4 30.0 %collective-permute-start.10 = (bf16[2,8,256,256]{3,2,1,0:T(8,128)(2,1)S(1)}, bf16[2,8,256,256]{3,2,1,0:T(8,128)(2,1)S(1)}, u32[]{:S(2)}, u32[]{:S(2)}) collective-permute-start(bf16[2,8,256,256]{3,2,1,0:T(8,128)(2,1)S(1)} %fusion.6), channel_id=1, source_target_pairs={{0,2},{2,4},{4,6},{6,8},{8,10},{10,12},{12,14},{14,16},{16,18},{18... | collective-permute-start | bytes 6291464 | tf_op jit(solution)/shard_map/ppermute | solution.py:15

commit v6 on v5

--- a/solution.py
+++ b/solution.py
@@ -59,8 +59,9 @@
     even = lax.axis_index("chan") % 2 == 0
     partial_energy = partial_energy + lax.ppermute(partial_energy, "band", [(s, s ^ 1) for s in range(lax.axis_size("band"))])
     spectra, partial_energy = lax.optimization_barrier((spectra, partial_energy))
-    raw_near = moved(spectra, "chan", 1)
-    raw_ahead = moved(spectra, "chan", -2, only_even=True)
+    flat_spectra = spectra.reshape(-1, spectra.shape[-1])
+    raw_near = moved(flat_spectra, "chan", 1).reshape(spectra.shape)
+    raw_ahead = moved(flat_spectra, "chan", -2, only_even=True).reshape(spectra.shape)
     energy = band_sum(partial_energy, "band")
     window_gain = valid_mask.astype(jnp.float32) / jnp.sqrt(energy / total_bins + eps_energy)
     gain_near = moved(window_gain, "chan", 1)
@@ -70,12 +71,14 @@
     ahead = whiten(raw_ahead, gain_ahead)
     second = moved(near, "chan", 1)
     for_above = cross_block(ahead, near, scale)
-    for_above, second = lax.optimization_barrier((for_above, second))
+    own_lag = cross_block(whitened, whitened, scale)
+    near_lag = cross_block(whitened, near, scale)
+    for_above, second, own_lag, near_lag = lax.optimization_barrier((for_above, second, own_lag, near_lag))
     third = moved(second, "chan", 1, only_even=True)
     from_below = moved(for_above, "chan", 2, only_even=True)
     outputs = [
-        cross_block(whitened, whitened, scale),
-        cross_block(whitened, near, scale),
+        own_lag,
+        near_lag,
         cross_block(whitened, second, scale),
         jnp.where(even, from_below, cross_block(whitened, third, scale)),
     ]

time: 184 us -> 171 us (0.929)
  waiting for transfers between devices: 102 us -> 92.1 us
  local copies, waits for them, and re-layouts: 5 us -> 0.44 us
    ppermute x7, waiting for transfers between devices: 79 us -> 65.7 us  [moved(): return lax.ppermute(value, axis, pairs)]
    optimization_barrier x1 -> x0, local copies, waits for them, and re-layouts: 4.57 us -> none  [shards(): lax.optimization_barrier((spectra, partial_energy))]
    ppermute x2, waiting for transfers between devices: 5.24 us -> 8.64 us  [band_sum(): got = lax.ppermute(jnp.where(bit == 0, high, low), axis, pairs)]
    convert_element_type x4, other arithmetic: 2.26 us -> 5.04 us  [cross_block(): return (jnp.stack([real_part, imag_part]) * scale).astype(jnp.bfloat16)]
    convert_element_type x2, other arithmetic: 8.12 us -> 6.13 us  [whiten(): return (raw.astype(jnp.float32) * gain).astype(jnp.bfloat16)]
  transfers between devices with their start and end apart: 12 -> 12, of which waited for: 8 -> 8; matrix products, arithmetic and copies ran while one was open for 25% -> 24% of each run, Pallas kernels for 0% -> 0%
where the time goes in v6:
time: 171 us
  waiting for transfers between devices  92.1 us (54%)
  starting transfers between devices  29.8 us (17%)
  other arithmetic  24.8 us (15%)
  matrix products  23.4 us (14%)
    ppermute x7, waiting for transfers between devices, moved(): return lax.ppermute(value, axis, pairs)  65.7 us
    ppermute x7, starting transfers between devices, moved(): return lax.ppermute(value, axis, pairs)  17.9 us
    dot_general x5, matrix products, cross_block(): jnp.einsum('pfwa,pfwb->fab', own_block, partner, preferred_element_type=j...  13.8 us
    ppermute x1, waiting for transfers between devices, shards(): lax.ppermute(partial_energy, 'band', [(s, s ^ 1) for s in range(lax.axis_...  12.9 us
    dot_general x5, matrix products, cross_block(): jnp.einsum('pfwa,pfwb->fab', own_block, flipped, preferred_element_type=j...  9.53 us
    ppermute x2, waiting for transfers between devices, band_sum(): got = lax.ppermute(jnp.where(bit == 0, high, low), axis, pairs)  8.64 us
    convert_element_type x2, other arithmetic, whiten(): return (raw.astype(jnp.float32) * gain).astype(jnp.bfloat16)  6.13 us
    slice x4, other arithmetic, cross_block(): flipped = jnp.stack([partner[1], -partner[0]])  5.55 us
  transfers between devices with their start and end apart: 12, of which 8 were waited for; matrix products, arithmetic and copies ran while one was open for 24% of the time, Pallas kernels for 0%

profile of v6, /device:TPU:4, one launch (start us, length us, event | category | flops | bytes accessed | tf_op | source)
XLA Modules:
  0.0 170.8 jit_solution(6328517443032003509)
XLA Ops:
  0.0 3.1 %multiply_reduce_fusion = f32[512,256]{1,0:T(8,128)S(1)} fusion(bf16[2,8,512,256]{3,2,1,0:T(8,128)(2,1)} %param.2), kind=kLoop, calls=%fused_computation.6 | loop fusion | flops 6160384 | bytes 4718592 | tf_op jit(solution)/shard_map/reduce_sum | solution.py:56
  3.1 2.3 %collective-permute-start = (f32[512,256]{1,0:T(8,128)S(1)}, f32[512,256]{1,0:T(8,128)S(1)}, u32[]{:S(2)}, u32[]{:S(2)}) collective-permute-start(f32[512,256]{1,0:T(8,128)S(1)} %multiply_reduce_fusion), channel_id=1, source_target_pairs={{0,32},{32,0},{64,96},{96,64},{128,160},{160,128},{192,224},{224,1... | collective-permute-start | bytes 1572872 | tf_op jit(solution)/shard_map/ppermute | solution.py:60
  5.4 12.9 %collective-permute-done = f32[512,256]{1,0:T(8,128)S(1)} collective-permute-done((f32[512,256]{1,0:T(8,128)S(1)}, f32[512,256]{1,0:T(8,128)S(1)}, u32[]{:S(2)}, u32[]{:S(2)}) %collective-permute-start) | collective-permute-done | bytes 524320 | tf_op jit(solution)/shard_map/ppermute | solution.py:60
  18.6 3.3 %collective-permute-start.2 = (f32[65536]{0:T(1024)S(1)}, f32[65536]{0:T(1024)S(1)}, u32[]{:S(2)}, u32[]{:S(2)}) collective-permute-start(f32[65536]{0:T(1024)S(1)} %bitcast.72), channel_id=1, source_target_pairs={{0,128},{32,160},{64,192},{96,224},{128,0},{160,32},{192,64},{224,... | collective-permute-start | bytes 786440 | tf_op jit(solution)/shard_map/ppermute | solution.py:33
  22.1 5.3 %collective-permute-done.2 = f32[65536]{0:T(1024)S(1)} collective-permute-done((f32[65536]{0:T(1024)S(1)}, f32[65536]{0:T(1024)S(1)}, u32[]{:S(2)}, u32[]{:S(2)}) %collective-permute-start.2) | collective-permute-done | bytes 262176 | tf_op jit(solution)/shard_map/ppermute | solution.py:33
  27.4 1.7 collective-permute-start.3
  29.1 3.4 %collective-permute-done.3 = f32[32768]{0:T(1024)S(1)} collective-permute-done((f32[32768]{0:T(1024)S(1)}, f32[32768]{0:T(1024)S(1)}, u32[]{:S(2)}, u32[]{:S(2)}) %collective-permute-start.3) | collective-permute-done | bytes 131104 | tf_op jit(solution)/shard_map/ppermute | solution.py:33
  32.5 1.7 collective-permute-start.4
  34.2 8.4 %collective-permute-start.1 = (bf16[8192,256]{1,0:T(8,128)(2,1)}, bf16[8192,256]{1,0:T(8,128)(2,1)}, u32[]{:S(2)}, u32[]{:S(2)}) collective-permute-start(bf16[8192,256]{1,0:T(8,128)(2,1)} %bitcast.68), channel_id=1, source_target_pairs={{0,30},{2,0},{4,2},{6,4},{8,6},{10,8},{12,10},{14,12},{16,14},{18,... | collective-permute-start | bytes 12582920 | tf_op jit(solution)/shard_map/ppermute | solution.py:15
  42.6 3.0 %collective-permute-start.5 = (f32[65536]{0:T(1024)S(1)}, f32[65536]{0:T(1024)S(1)}, u32[]{:S(2)}, u32[]{:S(2)}) collective-permute-start(f32[65536]{0:T(1024)S(1)} %maximum_select_fusion.2), channel_id=1, source_target_pairs={{0,128},{32,160},{64,192},{96,224},{128,0},{160,32},{192,64},{224,... | collective-permute-start | bytes 786440 | tf_op jit(solution)/shard_map/ppermute | solution.py:38
  45.7 4.9 %collective-permute-done.5 = f32[65536]{0:T(1024)S(1)} collective-permute-done((f32[65536]{0:T(1024)S(1)}, f32[65536]{0:T(1024)S(1)}, u32[]{:S(2)}, u32[]{:S(2)}) %collective-permute-start.5) | collective-permute-done | bytes 262176 | tf_op jit(solution)/shard_map/ppermute | solution.py:38
  50.8 3.4 %collective-permute-start.6 = (f32[512,256]{1,0:T(8,128)S(1)}, f32[512,256]{1,0:T(8,128)S(1)}, u32[]{:S(2)}, u32[]{:S(2)}) collective-permute-start(f32[512,256]{1,0:T(8,128)S(1)} %fusion.49), channel_id=1, source_target_pairs={{0,30},{2,0},{4,2},{6,4},{8,6},{10,8},{12,10},{14,12},{16,14},{18,... | collective-permute-start | bytes 1572872 | tf_op jit(solution)/shard_map/ppermute | solution.py:15
  54.2 3.1 %multiply_convert_fusion = bf16[2,8,512,256]{3,2,0,1:T(8,128)(2,1)S(1)} fusion(bf16[2,8,512,256]{3,2,1,0:T(8,128)(2,1)} %param.2, f32[512,256]{1,0:T(8,128)S(1)} %fusion.49), kind=kLoop, calls=%fused_computation.5 | loop fusion | flops 6291456 | bytes 8912896 | tf_op jit(solution)/shard_map/convert_element_type | solution.py:51
  57.6 21.3 %collective-permute-done.8 = f32[512,256]{1,0:T(8,128)S(1)} collective-permute-done((f32[512,256]{1,0:T(8,128)S(1)}, f32[512,256]{1,0:T(8,128)S(1)}, u32[]{:S(2)}, u32[]{:S(2)}) %collective-permute-start.8) | collective-permute-done | bytes 524320 | tf_op jit(solution)/shard_map/ppermute | solution.py:15
  78.9 3.1 %fusion.1 = bf16[2,8,512,256]{3,2,0,1:T(8,128)(2,1)S(1)} fusion(f32[512,256]{1,0:T(8,128)S(1)} %collective-permute-done.8, bf16[2,8,512,256]{3,2,1,0:T(8,128)(2,1)} %bitcast.35), kind=kLoop, calls=%fused_computation.4 | loop fusion | flops 6291456 | bytes 8912896 | tf_op jit(solution)/shard_map/convert_element_type | solution.py:51
  82.2 1.5 fusion.33
  86.0 8.4 %collective-permute-done.6 = f32[512,256]{1,0:T(8,128)S(1)} collective-permute-done((f32[512,256]{1,0:T(8,128)S(1)}, f32[512,256]{1,0:T(8,128)S(1)}, u32[]{:S(2)}, u32[]{:S(2)}) %collective-permute-start.6) | collective-permute-done | bytes 524320 | tf_op jit(solution)/shard_map/ppermute | solution.py:15
  94.4 3.4 %fusion.41 = f32[1,8,256,256]{3,2,1,0:T(8,128)S(1)} fusion(bf16[2,8,512,256]{3,2,1,0:T(8,128)(2,1)} %bitcast.34, f32[512,256]{1,0:T(8,128)S(1)} %collective-permute-done.6, bf16[1,8,512,256]{3,2,0,1:T(8,128)(2,1)S(1)} %get-tuple-element.24, bf16[1,8,512,256]{3,2,0,1:T(8,128)(2,1)S(1)} %get-tuple-element.23), kind=kOutput, calls=%fused_computation.49 | convolution fusion | flops 1082130432 | bytes 11010048 | tf_op jit(solution)/shard_map/pfwa,pfwb->fab/dot_general | solution.py:46
  97.8 3.7 %fusion.36 = f32[1,8,256,256]{3,2,1,0:T(8,128)S(1)} fusion(bf16[2,8,512,256]{3,2,0,1:T(8,128)(2,1)S(1)} %fusion.1, bf16[2,8,512,256]{3,2,1,0:T(8,128)(2,1)} %bitcast.34, f32[512,256]{1,0:T(8,128)S(1)} %collective-permute-done.6), kind=kOutput, calls=%fused_computation.48 | convolution fusion | flops 1080033280 | bytes 11010048 | tf_op jit(solution)/shard_map/pfwa,pfwb->fab/dot_general | solution.py:45
  101.5 2.0 %fusion.2 = bf16[2,8,256,256]{3,2,1,0:T(8,128)(2,1)} fusion(f32[1,8,256,256]{3,2,1,0:T(8,128)S(1)} %fusion.41, f32[1,8,256,256]{3,2,1,0:T(8,128)S(1)} %fusion.36), kind=kLoop, calls=%fused_computation.9 | loop fusion | flops 3145728 | bytes 6291456 | tf_op jit(solution)/shard_map/convert_element_type | solution.py:47
  106.4 1.9 %fusion.8 = bf16[2,8,256,256]{3,2,1,0:T(8,128)(2,1)} fusion(f32[1,8,256,256]{3,2,1,0:T(8,128)S(1)} %convolution_bitcast_fusion.2, f32[1,8,256,256]{3,2,1,0:T(8,128)S(1)} %convolution_bitcast_fusion.3), kind=kLoop, calls=%fused_computation.17 | loop fusion | flops 3145728 | bytes 6291456 | tf_op jit(solution)/shard_map/convert_element_type | solution.py:47
  108.3 24.1 %collective-permute-done.9 = bf16[2,8,512,256]{3,2,0,1:T(8,128)(2,1)} collective-permute-done((bf16[2,8,512,256]{3,2,0,1:T(8,128)(2,1)S(1)}, bf16[2,8,512,256]{3,2,0,1:T(8,128)(2,1)}, u32[]{:S(2)}, u32[]{:S(2)}) %collective-permute-start.9) | collective-permute-done | bytes 4194336 | tf_op jit(solution)/shard_map/ppermute | solution.py:15
  132.4 3.3 %collective-permute-start.11 = (bf16[2,8,512,256]{3,2,0,1:T(8,128)(2,1)}, bf16[2,8,512,256]{3,2,0,1:T(8,128)(2,1)}, u32[]{:S(2)}, u32[]{:S(2)}) collective-permute-start(bf16[2,8,512,256]{3,2,0,1:T(8,128)(2,1)} %collective-permute-done.9), channel_id=1, source_target_pairs={{0,1},{2,3},{4,5},{6,7},{8,9},{10,11},{12,13},{14,15},{16,17},{18,... | collective-permute-start | bytes 12582920 | tf_op jit(solution)/shard_map/ppermute | solution.py:15
  135.6 2.4 %collective-permute-start.10 = (bf16[2,8,256,256]{3,2,1,0:T(8,128)(2,1)}, bf16[2,8,256,256]{3,2,1,0:T(8,128)(2,1)S(1)}, u32[]{:S(2)}, u32[]{:S(2)}) collective-permute-start(bf16[2,8,256,256]{3,2,1,0:T(8,128)(2,1)} %fusion.2), channel_id=1, source_target_pairs={{0,2},{2,4},{4,6},{6,8},{8,10},{10,12},{12,14},{14,16},{16,18},{18... | collective-permute-start | bytes 6291464 | tf_op jit(solution)/shard_map/ppermute | solution.py:15
  138.0 2.5 %fusion.53 = (bf16[1,8,512,256]{3,2,0,1:T(8,128)(2,1)S(1)}, bf16[1,8,512,256]{3,2,0,1:T(8,128)(2,1)S(1)}) fusion(bf16[2,8,512,256]{3,2,0,1:T(8,128)(2,1)} %collective-permute-done.9), kind=kLoop, calls=%fused_computation.64 | loop fusion | flops 1048576 | bytes 8388608 | tf_op jit(solution)/shard_map/slice | solution.py:44
  140.6 3.7 %convolution_bitcast_fusion.1 = f32[1,1,8,256,256]{4,3,2,1,0:T(8,128)S(1)} fusion(bf16[2,8,512,256]{3,2,0,1:T(8,128)(2,1)S(1)} %copy-done.1, bf16[2,8,512,256]{3,2,0,1:T(8,128)(2,1)} %collective-permute-done.9), kind=kOutput, calls=%fused_computation.44 | convolution fusion | flops 1073741824 | bytes 10485760 | tf_op jit(solution)/shard_map/pfwa,pfwb->fab/dot_general | solution.py:45
  144.2 1.6 fusion.30
  146.4 2.5 %fusion.54 = (bf16[1,8,512,256]{3,2,0,1:T(8,128)(2,1)S(1)}, bf16[1,8,512,256]{3,2,0,1:T(8,128)(2,1)S(1)}) fusion(bf16[2,8,512,256]{3,2,0,1:T(8,128)(2,1)} %collective-permute-done.11), kind=kLoop, calls=%fused_computation.65 | loop fusion | flops 1048576 | bytes 8388608 | tf_op jit(solution)/shard_map/slice | solution.py:44
  148.9 1.6 fusion.27
  150.5 3.7 %convolution_bitcast_fusion = f32[1,8,256,256]{3,2,1,0:T(8,128)S(1)} fusion(bf16[2,8,512,256]{3,2,0,1:T(8,128)(2,1)S(1)} %copy-done.1, bf16[2,8,512,256]{3,2,0,1:T(8,128)(2,1)} %collective-permute-done.11), kind=kOutput, calls=%fused_computation.43 | convolution fusion | flops 1073741824 | bytes 10485760 | tf_op jit(solution)/shard_map/pfwa,pfwb->fab/dot_general | solution.py:45
  154.2 11.9 %collective-permute-done.10 = bf16[2,8,256,256]{3,2,1,0:T(8,128)(2,1)S(1)} collective-permute-done((bf16[2,8,256,256]{3,2,1,0:T(8,128)(2,1)}, bf16[2,8,256,256]{3,2,1,0:T(8,128)(2,1)S(1)}, u32[]{:S(2)}, u32[]{:S(2)}) %collective-permute-start.10) | collective-permute-done | bytes 2097184 | tf_op jit(solution)/shard_map/ppermute | solution.py:15
  166.9 3.9 %pad_maximum_fusion = bf16[4,2,8,256,256]{4,3,2,1,0:T(8,128)(2,1)} fusion(bf16[1,2,8,256,256]{4,3,2,1,0:T(8,128)(2,1)S(1)} %fusion.26, bf16[1,2,8,256,256]{4,3,2,1,0:T(8,128)(2,1)S(1)} %fusion.13, bf16[1,2,8,256,256]{4,3,2,1,0:T(8,128)(2,1)S(1)} %bitcast.70, bf16[1,2,8,256,256]{4,3,2,1,0:T(8,128)(2,1)S(1)} %bitcast.69), kind=kLoop, calls=%fused_computation | loop fusion | flops 12582912 | bytes 16777216 | tf_op jit(solution)/shard_map/stack | solution.py:85
  (36 shorter events, 8.0 us)
Async XLA Ops:
  3.1 47.6 %copy-start.3 = (s32[512,256]{1,0:T(8,128)S(1)}, s32[512,256]{1,0:T(8,128)}, u32[]{:S(2)}) copy-start(s32[512,256]{1,0:T(8,128)} %param.3) | copy-start | bytes 1572868
  3.1 15.3 %collective-permute-start = (f32[512,256]{1,0:T(8,128)S(1)}, f32[512,256]{1,0:T(8,128)S(1)}, u32[]{:S(2)}, u32[]{:S(2)}) collective-permute-start(f32[512,256]{1,0:T(8,128)S(1)} %multiply_reduce_fusion), channel_id=1, source_target_pairs={{0,32},{32,0},{64,96},{96,64},{128,160},{160,128},{192,224},{224,1... | collective-permute-start | bytes 1572872 | tf_op jit(solution)/shard_map/ppermute | solution.py:60
  18.6 8.8 %collective-permute-start.2 = (f32[65536]{0:T(1024)S(1)}, f32[65536]{0:T(1024)S(1)}, u32[]{:S(2)}, u32[]{:S(2)}) collective-permute-start(f32[65536]{0:T(1024)S(1)} %bitcast.72), channel_id=1, source_target_pairs={{0,128},{32,160},{64,192},{96,224},{128,0},{160,32},{192,64},{224,... | collective-permute-start | bytes 786440 | tf_op jit(solution)/shard_map/ppermute | solution.py:33
  22.0 56.9 %collective-permute-start.7 = (bf16[8192,256]{1,0:T(8,128)(2,1)}, bf16[8192,256]{1,0:T(8,128)(2,1)}, u32[]{:S(2)}, u32[]{:S(2)}) collective-permute-start(bf16[8192,256]{1,0:T(8,128)(2,1)} %bitcast.67), channel_id=1, source_target_pairs={{0,1},{1,2},{2,3},{3,4},{4,5},{5,6},{6,7},{7,8},{8,9},{9,10},{10,1... | collective-permute-start | bytes 12582920 | tf_op jit(solution)/shard_map/ppermute | solution.py:15
  27.4 5.1 %collective-permute-start.3 = (f32[32768]{0:T(1024)S(1)}, f32[32768]{0:T(1024)S(1)}, u32[]{:S(2)}, u32[]{:S(2)}) collective-permute-start(f32[32768]{0:T(1024)S(1)} %slice_select_fusion), channel_id=1, source_target_pairs={{0,64},{32,96},{64,0},{96,32},{128,192},{160,224},{192,128},{224,1... | collective-permute-start | bytes 393224 | tf_op jit(solution)/shard_map/ppermute | solution.py:33
  32.5 10.1 %collective-permute-start.4 = (f32[32768]{0:T(1024)S(1)}, f32[32768]{0:T(1024)S(1)}, u32[]{:S(2)}, u32[]{:S(2)}) collective-permute-start(f32[32768]{0:T(1024)S(1)} %select_add_fusion), channel_id=1, source_target_pairs={{0,64},{32,96},{64,0},{96,32},{128,192},{160,224},{192,128},{224,1... | collective-permute-start | bytes 393224 | tf_op jit(solution)/shard_map/ppermute | solution.py:38
  34.2 60.2 %collective-permute-start.1 = (bf16[8192,256]{1,0:T(8,128)(2,1)}, bf16[8192,256]{1,0:T(8,128)(2,1)}, u32[]{:S(2)}, u32[]{:S(2)}) collective-permute-start(bf16[8192,256]{1,0:T(8,128)(2,1)} %bitcast.68), channel_id=1, source_target_pairs={{0,30},{2,0},{4,2},{6,4},{8,6},{10,8},{12,10},{14,12},{16,14},{18,... | collective-permute-start | bytes 12582920 | tf_op jit(solution)/shard_map/ppermute | solution.py:15
  42.6 8.0 %collective-permute-start.5 = (f32[65536]{0:T(1024)S(1)}, f32[65536]{0:T(1024)S(1)}, u32[]{:S(2)}, u32[]{:S(2)}) collective-permute-start(f32[65536]{0:T(1024)S(1)} %maximum_select_fusion.2), channel_id=1, source_target_pairs={{0,128},{32,160},{64,192},{96,224},{128,0},{160,32},{192,64},{224,... | collective-permute-start | bytes 786440 | tf_op jit(solution)/shard_map/ppermute | solution.py:38
  50.8 43.6 %collective-permute-start.6 = (f32[512,256]{1,0:T(8,128)S(1)}, f32[512,256]{1,0:T(8,128)S(1)}, u32[]{:S(2)}, u32[]{:S(2)}) collective-permute-start(f32[512,256]{1,0:T(8,128)S(1)} %fusion.49), channel_id=1, source_target_pairs={{0,30},{2,0},{4,2},{6,4},{8,6},{10,8},{12,10},{14,12},{16,14},{18,... | collective-permute-start | bytes 1572872 | tf_op jit(solution)/shard_map/ppermute | solution.py:15
  54.1 24.7 %collective-permute-start.8 = (f32[512,256]{1,0:T(8,128)S(1)}, f32[512,256]{1,0:T(8,128)S(1)}, u32[]{:S(2)}, u32[]{:S(2)}) collective-permute-start(f32[512,256]{1,0:T(8,128)S(1)} %fusion.49), channel_id=1, source_target_pairs={{0,1},{1,2},{2,3},{3,4},{4,5},{5,6},{6,7},{7,8},{8,9},{9,10},{10,1... | collective-permute-start | bytes 1572872 | tf_op jit(solution)/shard_map/ppermute | solution.py:15
  57.3 47.6 %copy-start = (bf16[2,8,512,256]{3,2,0,1:T(8,128)(2,1)}, bf16[2,8,512,256]{3,2,0,1:T(8,128)(2,1)S(1)}, u32[]{:S(2)}) copy-start(bf16[2,8,512,256]{3,2,0,1:T(8,128)(2,1)S(1)} %multiply_convert_fusion) | copy-start | bytes 12582916
  82.0 50.4 %collective-permute-start.9 = (bf16[2,8,512,256]{3,2,0,1:T(8,128)(2,1)S(1)}, bf16[2,8,512,256]{3,2,0,1:T(8,128)(2,1)}, u32[]{:S(2)}, u32[]{:S(2)}) collective-permute-start(bf16[2,8,512,256]{3,2,0,1:T(8,128)(2,1)S(1)} %fusion.1), channel_id=1, source_target_pairs={{0,1},{1,2},{2,3},{3,4},{4,5},{5,6},{6,7},{7,8},{8,9},{9,10},{10,1... | collective-permute-start | bytes 12582920 | tf_op jit(solution)/shard_map/ppermute | solution.py:15
  132.4 14.0 %collective-permute-start.11 = (bf16[2,8,512,256]{3,2,0,1:T(8,128)(2,1)}, bf16[2,8,512,256]{3,2,0,1:T(8,128)(2,1)}, u32[]{:S(2)}, u32[]{:S(2)}) collective-permute-start(bf16[2,8,512,256]{3,2,0,1:T(8,128)(2,1)} %collective-permute-done.9), channel_id=1, source_target_pairs={{0,1},{2,3},{4,5},{6,7},{8,9},{10,11},{12,13},{14,15},{16,17},{18,... | collective-permute-start | bytes 12582920 | tf_op jit(solution)/shard_map/ppermute | solution.py:15
  135.6 4.9 %copy-start.1 = (bf16[2,8,512,256]{3,2,0,1:T(8,128)(2,1)S(1)}, bf16[2,8,512,256]{3,2,0,1:T(8,128)(2,1)}, u32[]{:S(2)}) copy-start(bf16[2,8,512,256]{3,2,0,1:T(8,128)(2,1)} %copy-done) | copy-start | bytes 12582916
  135.6 30.5 %collective-permute-start.10 = (bf16[2,8,256,256]{3,2,1,0:T(8,128)(2,1)}, bf16[2,8,256,256]{3,2,1,0:T(8,128)(2,1)S(1)}, u32[]{:S(2)}, u32[]{:S(2)}) collective-permute-start(bf16[2,8,256,256]{3,2,1,0:T(8,128)(2,1)} %fusion.2), channel_id=1, source_target_pairs={{0,2},{2,4},{4,6},{6,8},{8,10},{10,12},{12,14},{14,16},{16,18},{18... | collective-permute-start | bytes 6291464 | tf_op jit(solution)/shard_map/ppermute | solution.py:15
  154.2 12.7 %copy-start.2 = (bf16[2,8,256,256]{3,2,1,0:T(8,128)(2,1)S(1)}, bf16[2,8,256,256]{3,2,1,0:T(8,128)(2,1)}, u32[]{:S(2)}) copy-start(bf16[2,8,256,256]{3,2,1,0:T(8,128)(2,1)} %fusion.8) | copy-start | bytes 6291460

commit v7 on v6

--- a/solution.py
+++ b/solution.py
@@ -69,13 +69,13 @@
     whitened = whiten(spectra, window_gain)
     near = whiten(raw_near, gain_near)
     ahead = whiten(raw_ahead, gain_ahead)
-    second = moved(near, "chan", 1)
     for_above = cross_block(ahead, near, scale)
+    from_below = moved(for_above, "chan", 2, only_even=True)
+    near_sent, from_below = lax.optimization_barrier((near, from_below))
+    second = moved(near_sent, "chan", 1)
+    third = moved(second, "chan", 1, only_even=True)
     own_lag = cross_block(whitened, whitened, scale)
     near_lag = cross_block(whitened, near, scale)
-    for_above, second, own_lag, near_lag = lax.optimization_barrier((for_above, second, own_lag, near_lag))
-    third = moved(second, "chan", 1, only_even=True)
-    from_below = moved(for_above, "chan", 2, only_even=True)
     outputs = [
         own_lag,
         near_lag,

time: 171 us -> 207 us (1.21)
  waiting for transfers between devices: 92.1 us -> 131 us
  starting transfers between devices: 29.8 us -> 22.6 us
  matrix products: 23.4 us -> 26.7 us
    ppermute x7, waiting for transfers between devices: 65.7 us -> 99.6 us  [moved(): return lax.ppermute(value, axis, pairs)]
    ppermute x2, waiting for transfers between devices: 4.86 us -> 13.1 us  [band_sum(): got = lax.ppermute(flat, axis, pairs)]
    ppermute x2, starting transfers between devices: 4.65 us -> 1.08 us  [band_sum(): got = lax.ppermute(flat, axis, pairs)]
    ppermute x2, waiting for transfers between devices: 8.64 us -> 5.3 us  [band_sum(): got = lax.ppermute(jnp.where(bit == 0, high, low), axis, pairs)]
    dot_general x5, matrix products: 13.8 us -> 16.8 us  [cross_block(): jnp.einsum('pfwa,pfwb->fab', own_block, partner, preferred_element_type=j...]
    convert_element_type x4, other arithmetic: 5.04 us -> 2.27 us  [cross_block(): return (jnp.stack([real_part, imag_part]) * scale).astype(jnp.bfloat16)]
    ppermute x7, starting transfers between devices: 17.9 us -> 15.1 us  [moved(): return lax.ppermute(value, axis, pairs)]
  transfers between devices with their start and end apart: 12 -> 12, of which waited for: 8 -> 7; matrix products, arithmetic and copies ran while one was open for 24% -> 14% of each run, Pallas kernels for 0% -> 0%
where the time goes in v7:
time: 207 us
  waiting for transfers between devices  131 us (63%)
  matrix products  26.7 us (13%)
  other arithmetic  23.9 us (12%)
  starting transfers between devices  22.6 us (11%)
    ppermute x7, waiting for transfers between devices, moved(): return lax.ppermute(value, axis, pairs)  99.6 us
    dot_general x5, matrix products, cross_block(): jnp.einsum('pfwa,pfwb->fab', own_block, partner, preferred_element_type=j...  16.8 us
    ppermute x7, starting transfers between devices, moved(): return lax.ppermute(value, axis, pairs)  15.1 us
    ppermute x2, waiting for transfers between devices, band_sum(): got = lax.ppermute(flat, axis, pairs)  13.1 us
    ppermute x1, waiting for transfers between devices, shards(): lax.ppermute(partial_energy, 'band', [(s, s ^ 1) for s in range(lax.axis_...  12.9 us
    dot_general x5, matrix products, cross_block(): jnp.einsum('pfwa,pfwb->fab', own_block, flipped, preferred_element_type=j...  9.99 us
    convert_element_type x2, other arithmetic, whiten(): return (raw.astype(jnp.float32) * gain).astype(jnp.bfloat16)  8.12 us
    slice x4, other arithmetic, cross_block(): flipped = jnp.stack([partner[1], -partner[0]])  5.54 us
  transfers between devices with their start and end apart: 12, of which 7 were waited for; matrix products, arithmetic and copies ran while one was open for 14% of the time, Pallas kernels for 0%

profile of v7, /device:TPU:4, one launch (start us, length us, event | category | flops | bytes accessed | tf_op | source)
XLA Modules:
  0.0 206.6 jit_solution(8347934478103909195)
XLA Ops:
  0.0 3.1 %multiply_reduce_fusion = f32[512,256]{1,0:T(8,128)S(1)} fusion(bf16[2,8,512,256]{3,2,1,0:T(8,128)(2,1)} %param.2), kind=kLoop, calls=%fused_computation.6 | loop fusion | flops 6160384 | bytes 4718592 | tf_op jit(solution)/shard_map/reduce_sum | solution.py:56
  3.1 2.3 %collective-permute-start = (f32[512,256]{1,0:T(8,128)S(1)}, f32[512,256]{1,0:T(8,128)S(1)}, u32[]{:S(2)}, u32[]{:S(2)}) collective-permute-start(f32[512,256]{1,0:T(8,128)S(1)} %multiply_reduce_fusion), channel_id=1, source_target_pairs={{0,32},{32,0},{64,96},{96,64},{128,160},{160,128},{192,224},{224,1... | collective-permute-start | bytes 1572872 | tf_op jit(solution)/shard_map/ppermute | solution.py:60
  5.4 12.9 %collective-permute-done = f32[512,256]{1,0:T(8,128)S(1)} collective-permute-done((f32[512,256]{1,0:T(8,128)S(1)}, f32[512,256]{1,0:T(8,128)S(1)}, u32[]{:S(2)}, u32[]{:S(2)}) %collective-permute-start) | collective-permute-done | bytes 524320 | tf_op jit(solution)/shard_map/ppermute | solution.py:60
  18.6 3.3 %collective-permute-start.1 = (f32[65536]{0:T(1024)S(1)}, f32[65536]{0:T(1024)S(1)}, u32[]{:S(2)}, u32[]{:S(2)}) collective-permute-start(f32[65536]{0:T(1024)S(1)} %bitcast.72), channel_id=1, source_target_pairs={{0,128},{32,160},{64,192},{96,224},{128,0},{160,32},{192,64},{224,... | collective-permute-start | bytes 786440 | tf_op jit(solution)/shard_map/ppermute | solution.py:33
  21.9 8.4 %collective-permute-start.7 = (bf16[8192,256]{1,0:T(8,128)(2,1)}, bf16[8192,256]{1,0:T(8,128)(2,1)}, u32[]{:S(2)}, u32[]{:S(2)}) collective-permute-start(bf16[8192,256]{1,0:T(8,128)(2,1)} %bitcast.70), channel_id=1, source_target_pairs={{0,30},{2,0},{4,2},{6,4},{8,6},{10,8},{12,10},{14,12},{16,14},{18,... | collective-permute-start | bytes 12582920 | tf_op jit(solution)/shard_map/ppermute | solution.py:15
  30.5 0.8 collective-permute-start.2
  31.3 5.3 %collective-permute-done.2 = f32[32768]{0:T(1024)S(1)} collective-permute-done((f32[32768]{0:T(1024)S(1)}, f32[32768]{0:T(1024)S(1)}, u32[]{:S(2)}, u32[]{:S(2)}) %collective-permute-start.2) | collective-permute-done | bytes 131104 | tf_op jit(solution)/shard_map/ppermute | solution.py:33
  36.6 0.8 collective-permute-start.3
  37.3 5.6 %collective-permute-done.3 = f32[32768]{0:T(1024)S(1)} collective-permute-done((f32[32768]{0:T(1024)S(1)}, f32[32768]{0:T(1024)S(1)}, u32[]{:S(2)}, u32[]{:S(2)}) %collective-permute-start.3) | collective-permute-done | bytes 131104 | tf_op jit(solution)/shard_map/ppermute | solution.py:38
  43.4 7.5 %collective-permute-done.4 = f32[65536]{0:T(1024)S(1)} collective-permute-done((f32[65536]{0:T(1024)S(1)}, f32[65536]{0:T(1024)S(1)}, u32[]{:S(2)}, u32[]{:S(2)}) %collective-permute-start.4) | collective-permute-done | bytes 262176 | tf_op jit(solution)/shard_map/ppermute | solution.py:38
  51.2 3.0 %collective-permute-start.8 = (f32[512,256]{1,0:T(8,128)S(1)}, f32[512,256]{1,0:T(8,128)S(1)}, u32[]{:S(2)}, u32[]{:S(2)}) collective-permute-start(f32[512,256]{1,0:T(8,128)S(1)} %fusion.49), channel_id=1, source_target_pairs={{0,30},{2,0},{4,2},{6,4},{8,6},{10,8},{12,10},{14,12},{16,14},{18,... | collective-permute-start | bytes 1572872 | tf_op jit(solution)/shard_map/ppermute | solution.py:15
  54.2 24.4 %collective-permute-done.6 = f32[512,256]{1,0:T(8,128)S(1)} collective-permute-done((f32[512,256]{1,0:T(8,128)S(1)}, f32[512,256]{1,0:T(8,128)S(1)}, u32[]{:S(2)}, u32[]{:S(2)}) %collective-permute-start.6) | collective-permute-done | bytes 524320 | tf_op jit(solution)/shard_map/ppermute | solution.py:15
  78.7 5.1 %fusion.1 = bf16[2,8,512,256]{3,2,0,1:T(8,128)(2,1)} fusion(f32[512,256]{1,0:T(8,128)S(1)} %collective-permute-done.6, bf16[2,8,512,256]{3,2,1,0:T(8,128)(2,1)} %bitcast.34), kind=kLoop, calls=%fused_computation.4 | loop fusion | flops 6291456 | bytes 8912896 | tf_op jit(solution)/shard_map/convert_element_type | solution.py:51
  83.8 2.5 %fusion.56 = (bf16[1,8,512,256]{3,2,0,1:T(8,128)(2,1)S(1)}, bf16[1,8,512,256]{3,2,0,1:T(8,128)(2,1)S(1)}) fusion(bf16[2,8,512,256]{3,2,0,1:T(8,128)(2,1)} %fusion.1), kind=kLoop, calls=%fused_computation.67 | loop fusion | flops 1048576 | bytes 8388608 | tf_op jit(solution)/shard_map/slice | solution.py:44
  86.3 6.4 %fusion.36 = f32[1,8,256,256]{3,2,1,0:T(8,128)S(1)} fusion(bf16[2,8,512,256]{3,2,0,1:T(8,128)(2,1)} %fusion.1, bf16[2,8,512,256]{3,2,1,0:T(8,128)(2,1)} %bitcast.37, f32[512,256]{1,0:T(8,128)S(1)} %collective-permute-done.8), kind=kOutput, calls=%fused_computation.48 | convolution fusion | flops 1080033280 | bytes 11010048 | tf_op jit(solution)/shard_map/pfwa,pfwb->fab/dot_general | solution.py:45
  92.8 3.4 %fusion.41 = f32[1,8,256,256]{3,2,1,0:T(8,128)S(1)} fusion(bf16[2,8,512,256]{3,2,1,0:T(8,128)(2,1)} %bitcast.37, f32[512,256]{1,0:T(8,128)S(1)} %collective-permute-done.8, bf16[1,8,512,256]{3,2,0,1:T(8,128)(2,1)S(1)} %get-tuple-element.20, bf16[1,8,512,256]{3,2,0,1:T(8,128)(2,1)S(1)} %get-tuple-element.19), kind=kOutput, calls=%fused_computation.49 | convolution fusion | flops 1082130432 | bytes 11010048 | tf_op jit(solution)/shard_map/pfwa,pfwb->fab/dot_general | solution.py:46
  96.7 1.9 collective-permute-start.9
  98.7 28.1 %collective-permute-done.9 = bf16[2,8,256,256]{3,2,1,0:T(8,128)(2,1)S(1)} collective-permute-done((bf16[2,8,256,256]{3,2,1,0:T(8,128)(2,1)S(1)}, bf16[2,8,256,256]{3,2,1,0:T(8,128)(2,1)S(1)}, u32[]{:S(2)}, u32[]{:S(2)}) %collective-permute-start.9) | collective-permute-done | bytes 2097184 | tf_op jit(solution)/shard_map/ppermute | solution.py:15
  126.8 3.0 %multiply_convert_fusion = bf16[2,8,512,256]{3,2,0,1:T(8,128)(2,1)S(1)} fusion(bf16[2,8,512,256]{3,2,1,0:T(8,128)(2,1)} %param.2, f32[512,256]{1,0:T(8,128)S(1)} %fusion.49), kind=kLoop, calls=%fused_computation.5 | loop fusion | flops 6291456 | bytes 8912896 | tf_op jit(solution)/shard_map/convert_element_type | solution.py:51
  130.1 47.0 %collective-permute-done.10 = bf16[2,8,512,256]{3,2,0,1:T(8,128)(2,1)} collective-permute-done((bf16[2,8,512,256]{3,2,0,1:T(8,128)(2,1)}, bf16[2,8,512,256]{3,2,0,1:T(8,128)(2,1)}, u32[]{:S(2)}, u32[]{:S(2)}) %collective-permute-start.10) | collective-permute-done | bytes 4194336 | tf_op jit(solution)/shard_map/ppermute | solution.py:15
  177.1 1.7 collective-permute-start.11
  178.9 1.6 fusion.33
  180.5 1.5 convolution_bitcast_fusion.4
  182.6 1.0 copy-done.1
  184.2 1.6 convolution_bitcast_fusion.2
  185.8 3.7 %convolution_bitcast_fusion.3 = f32[1,1,8,256,256]{4,3,2,1,0:T(8,128)S(1)} fusion(bf16[2,8,512,256]{3,2,0,1:T(8,128)(2,1)S(1)} %multiply_convert_fusion, bf16[2,8,512,256]{3,2,0,1:T(8,128)(2,1)} %fusion.1), kind=kOutput, calls=%fused_computation.46 | convolution fusion | flops 1073741824 | bytes 10485760 | tf_op jit(solution)/shard_map/pfwa,pfwb->fab/dot_general | solution.py:45
  190.0 2.5 %fusion.54 = (bf16[1,8,512,256]{3,2,0,1:T(8,128)(2,1)S(1)}, bf16[1,8,512,256]{3,2,0,1:T(8,128)(2,1)S(1)}) fusion(bf16[2,8,512,256]{3,2,0,1:T(8,128)(2,1)} %collective-permute-done.10), kind=kLoop, calls=%fused_computation.65 | loop fusion | flops 1048576 | bytes 8388608 | tf_op jit(solution)/shard_map/slice | solution.py:44
  192.5 1.6 fusion.30
  194.1 3.7 %convolution_bitcast_fusion.1 = f32[1,1,8,256,256]{4,3,2,1,0:T(8,128)S(1)} fusion(bf16[2,8,512,256]{3,2,0,1:T(8,128)(2,1)S(1)} %multiply_convert_fusion, bf16[2,8,512,256]{3,2,0,1:T(8,128)(2,1)} %collective-permute-done.10), kind=kOutput, calls=%fused_computation.44 | convolution fusion | flops 1073741824 | bytes 10485760 | tf_op jit(solution)/shard_map/pfwa,pfwb->fab/dot_general | solution.py:45
  198.7 1.8 fusion.27
  200.5 1.5 convolution_bitcast_fusion
  202.8 3.9 %pad_maximum_fusion = bf16[4,2,8,256,256]{4,3,2,1,0:T(8,128)(2,1)} fusion(bf16[1,2,8,256,256]{4,3,2,1,0:T(8,128)(2,1)S(1)} %fusion.26, bf16[1,2,8,256,256]{4,3,2,1,0:T(8,128)(2,1)S(1)} %fusion.13, bf16[1,2,8,256,256]{4,3,2,1,0:T(8,128)(2,1)S(1)} %fusion.7, bf16[1,2,8,256,256]{4,3,2,1,0:T(8,128)(2,1)S(1)} %fusion.6), kind=kLoop, calls=%fused_computation | loop fusion | flops 12582912 | bytes 16777216 | tf_op jit(solution)/shard_map/stack | solution.py:85
  (38 shorter events, 5.4 us)
Async XLA Ops:
  3.1 48.0 %copy-start.4 = (s32[512,256]{1,0:T(8,128)S(1)}, s32[512,256]{1,0:T(8,128)}, u32[]{:S(2)}) copy-start(s32[512,256]{1,0:T(8,128)} %param.3) | copy-start | bytes 1572868
  3.1 15.3 %collective-permute-start = (f32[512,256]{1,0:T(8,128)S(1)}, f32[512,256]{1,0:T(8,128)S(1)}, u32[]{:S(2)}, u32[]{:S(2)}) collective-permute-start(f32[512,256]{1,0:T(8,128)S(1)} %multiply_reduce_fusion), channel_id=1, source_target_pairs={{0,32},{32,0},{64,96},{96,64},{128,160},{160,128},{192,224},{224,1... | collective-permute-start | bytes 1572872 | tf_op jit(solution)/shard_map/ppermute | solution.py:60
  18.6 11.8 %collective-permute-start.1 = (f32[65536]{0:T(1024)S(1)}, f32[65536]{0:T(1024)S(1)}, u32[]{:S(2)}, u32[]{:S(2)}) collective-permute-start(f32[65536]{0:T(1024)S(1)} %bitcast.72), channel_id=1, source_target_pairs={{0,128},{32,160},{64,192},{96,224},{128,0},{160,32},{192,64},{224,... | collective-permute-start | bytes 786440 | tf_op jit(solution)/shard_map/ppermute | solution.py:33
  21.9 56.8 %collective-permute-start.5 = (bf16[8192,256]{1,0:T(8,128)(2,1)}, bf16[8192,256]{1,0:T(8,128)(2,1)}, u32[]{:S(2)}, u32[]{:S(2)}) collective-permute-start(bf16[8192,256]{1,0:T(8,128)(2,1)} %bitcast.69), channel_id=1, source_target_pairs={{0,1},{1,2},{2,3},{3,4},{4,5},{5,6},{6,7},{7,8},{8,9},{9,10},{10,1... | collective-permute-start | bytes 12582920 | tf_op jit(solution)/shard_map/ppermute | solution.py:15
  21.9 64.4 %collective-permute-start.7 = (bf16[8192,256]{1,0:T(8,128)(2,1)}, bf16[8192,256]{1,0:T(8,128)(2,1)}, u32[]{:S(2)}, u32[]{:S(2)}) collective-permute-start(bf16[8192,256]{1,0:T(8,128)(2,1)} %bitcast.70), channel_id=1, source_target_pairs={{0,30},{2,0},{4,2},{6,4},{8,6},{10,8},{12,10},{14,12},{16,14},{18,... | collective-permute-start | bytes 12582920 | tf_op jit(solution)/shard_map/ppermute | solution.py:15
  30.5 6.1 %collective-permute-start.2 = (f32[32768]{0:T(1024)S(1)}, f32[32768]{0:T(1024)S(1)}, u32[]{:S(2)}, u32[]{:S(2)}) collective-permute-start(f32[32768]{0:T(1024)S(1)} %slice_select_fusion), channel_id=1, source_target_pairs={{0,64},{32,96},{64,0},{96,32},{128,192},{160,224},{192,128},{224,1... | collective-permute-start | bytes 393224 | tf_op jit(solution)/shard_map/ppermute | solution.py:33
  36.6 6.4 %collective-permute-start.3 = (f32[32768]{0:T(1024)S(1)}, f32[32768]{0:T(1024)S(1)}, u32[]{:S(2)}, u32[]{:S(2)}) collective-permute-start(f32[32768]{0:T(1024)S(1)} %select_add_fusion), channel_id=1, source_target_pairs={{0,64},{32,96},{64,0},{96,32},{128,192},{160,224},{192,128},{224,1... | collective-permute-start | bytes 393224 | tf_op jit(solution)/shard_map/ppermute | solution.py:38
  43.0 8.0 %collective-permute-start.4 = (f32[65536]{0:T(1024)S(1)}, f32[65536]{0:T(1024)S(1)}, u32[]{:S(2)}, u32[]{:S(2)}) collective-permute-start(f32[65536]{0:T(1024)S(1)} %maximum_select_fusion.2), channel_id=1, source_target_pairs={{0,128},{32,160},{64,192},{96,224},{128,0},{160,32},{192,64},{224,... | collective-permute-start | bytes 786440 | tf_op jit(solution)/shard_map/ppermute | solution.py:38
  51.1 27.5 %collective-permute-start.6 = (f32[512,256]{1,0:T(8,128)S(1)}, f32[512,256]{1,0:T(8,128)S(1)}, u32[]{:S(2)}, u32[]{:S(2)}) collective-permute-start(f32[512,256]{1,0:T(8,128)S(1)} %fusion.49), channel_id=1, source_target_pairs={{0,1},{1,2},{2,3},{3,4},{4,5},{5,6},{6,7},{7,8},{8,9},{9,10},{10,1... | collective-permute-start | bytes 1572872 | tf_op jit(solution)/shard_map/ppermute | solution.py:15
  51.2 35.0 %collective-permute-start.8 = (f32[512,256]{1,0:T(8,128)S(1)}, f32[512,256]{1,0:T(8,128)S(1)}, u32[]{:S(2)}, u32[]{:S(2)}) collective-permute-start(f32[512,256]{1,0:T(8,128)S(1)} %fusion.49), channel_id=1, source_target_pairs={{0,30},{2,0},{4,2},{6,4},{8,6},{10,8},{12,10},{14,12},{16,14},{18,... | collective-permute-start | bytes 1572872 | tf_op jit(solution)/shard_map/ppermute | solution.py:15
  86.2 6.5 %copy-start = (bf16[1,8,512,256]{3,2,0,1:T(8,128)(2,1)}, bf16[1,8,512,256]{3,2,0,1:T(8,128)(2,1)S(1)}, u32[]{:S(2)}) copy-start(bf16[1,8,512,256]{3,2,0,1:T(8,128)(2,1)S(1)} %get-tuple-element.19) | copy-start | bytes 6291460
  86.3 6.5 %copy-start.2 = (bf16[1,8,512,256]{3,2,0,1:T(8,128)(2,1)}, bf16[1,8,512,256]{3,2,0,1:T(8,128)(2,1)S(1)}, u32[]{:S(2)}) copy-start(bf16[1,8,512,256]{3,2,0,1:T(8,128)(2,1)S(1)} %get-tuple-element.20) | copy-start | bytes 6291460
  96.7 30.0 %collective-permute-start.9 = (bf16[2,8,256,256]{3,2,1,0:T(8,128)(2,1)S(1)}, bf16[2,8,256,256]{3,2,1,0:T(8,128)(2,1)S(1)}, u32[]{:S(2)}, u32[]{:S(2)}) collective-permute-start(bf16[2,8,256,256]{3,2,1,0:T(8,128)(2,1)S(1)} %fusion.8), channel_id=1, source_target_pairs={{0,2},{2,4},{4,6},{6,8},{8,10},{10,12},{12,14},{14,16},{16,18},{18... | collective-permute-start | bytes 6291464 | tf_op jit(solution)/shard_map/ppermute | solution.py:15
  126.8 50.4 %collective-permute-start.10 = (bf16[2,8,512,256]{3,2,0,1:T(8,128)(2,1)}, bf16[2,8,512,256]{3,2,0,1:T(8,128)(2,1)}, u32[]{:S(2)}, u32[]{:S(2)}) collective-permute-start(bf16[2,8,512,256]{3,2,0,1:T(8,128)(2,1)} %fusion.1), channel_id=1, source_target_pairs={{0,1},{1,2},{2,3},{3,4},{4,5},{5,6},{6,7},{7,8},{8,9},{9,10},{10,1... | collective-permute-start | bytes 12582920 | tf_op jit(solution)/shard_map/ppermute | solution.py:15
  177.1 21.3 %collective-permute-start.11 = (bf16[2,8,512,256]{3,2,0,1:T(8,128)(2,1)}, bf16[2,8,512,256]{3,2,0,1:T(8,128)(2,1)S(1)}, u32[]{:S(2)}, u32[]{:S(2)}) collective-permute-start(bf16[2,8,512,256]{3,2,0,1:T(8,128)(2,1)} %collective-permute-done.10), channel_id=1, source_target_pairs={{0,1},{2,3},{4,5},{6,7},{8,9},{10,11},{12,13},{14,15},{16,17},{18,... | collective-permute-start | bytes 12582920 | tf_op jit(solution)/shard_map/ppermute | solution.py:15
  182.0 1.6 copy-start.1
  182.0 2.2 %copy-start.3 = (bf16[1,8,512,256]{3,2,0,1:T(8,128)(2,1)S(1)}, bf16[1,8,512,256]{3,2,0,1:T(8,128)(2,1)}, u32[]{:S(2)}) copy-start(bf16[1,8,512,256]{3,2,0,1:T(8,128)(2,1)} %copy-done.2) | copy-start | bytes 6291460

commit v8 on v6

--- a/solution.py
+++ b/solution.py
@@ -76,13 +76,12 @@
     for_above, second, own_lag, near_lag = lax.optimization_barrier((for_above, second, own_lag, near_lag))
     third = moved(second, "chan", 1, only_even=True)
     from_below = moved(for_above, "chan", 2, only_even=True)
-    outputs = [
-        own_lag,
-        near_lag,
-        cross_block(whitened, second, scale),
-        jnp.where(even, from_below, cross_block(whitened, third, scale)),
-    ]
-    return jnp.stack(outputs)
+    lag_two = cross_block(whitened, second, scale)
+    lag_three = cross_block(whitened, third, scale)
+    early = jnp.stack([own_lag, near_lag, lag_two, lag_three])
+    early, second = lax.optimization_barrier((early, second))
+    last = jnp.where(even, from_below, early[3])
+    return lax.dynamic_update_slice_in_dim(early, last[None], 3, axis=0)
 
 
 def solution(mesh):

time: 171 us -> 169 us (0.988)
  waiting for transfers between devices: 92.1 us -> 89.2 us
    another operation x2 -> x1, other arithmetic: 4.66 us -> 1.1 us  [shards(): early = jnp.stack([own_lag, near_lag, lag_two, lag_three])]
    ppermute x7, waiting for transfers between devices: 65.7 us -> 62.8 us  [moved(): return lax.ppermute(value, axis, pairs)]
    dynamic_update_slice x0 -> x1, other arithmetic: none -> 1.97 us  [shards(): return lax.dynamic_update_slice_in_dim(early, last[None], 3, axis=0)]
    convert_element_type x4 -> x5, other arithmetic: 5.04 us -> 5.62 us  [cross_block(): return (jnp.stack([real_part, imag_part]) * scale).astype(jnp.bfloat16)]
  transfers between devices with their start and end apart: 12 -> 12, of which waited for: 8 -> 8; matrix products, arithmetic and copies ran while one was open for 24% -> 25% of each run, Pallas kernels for 0% -> 0%
where the time goes in v8:
time: 169 us; the launch traced here: 168 us
  waiting for transfers between devices  89.2 us (53%)
  starting transfers between devices  29.8 us (18%)
  other arithmetic  23.8 us (14%)
  matrix products  23.4 us (14%)
    ppermute x7, waiting for transfers between devices, moved(): return lax.ppermute(value, axis, pairs)  62.8 us
    ppermute x7, starting transfers between devices, moved(): return lax.ppermute(value, axis, pairs)  17.9 us
    dot_general x5, matrix products, cross_block(): jnp.einsum('pfwa,pfwb->fab', own_block, partner, preferred_element_type=j...  13.8 us
    ppermute x1, waiting for transfers between devices, shards(): lax.ppermute(partial_energy, 'band', [(s, s ^ 1) for s in range(lax.axis_...  12.9 us
    dot_general x5, matrix products, cross_block(): jnp.einsum('pfwa,pfwb->fab', own_block, flipped, preferred_element_type=j...  9.53 us
    ppermute x2, waiting for transfers between devices, band_sum(): got = lax.ppermute(jnp.where(bit == 0, high, low), axis, pairs)  8.64 us
    convert_element_type x2, other arithmetic, whiten(): return (raw.astype(jnp.float32) * gain).astype(jnp.bfloat16)  6.13 us
    convert_element_type x5, other arithmetic, cross_block(): return (jnp.stack([real_part, imag_part]) * scale).astype(jnp.bfloat16)  5.62 us
  transfers between devices with their start and end apart: 12, of which 8 were waited for; matrix products, arithmetic and copies ran while one was open for 25% of the time, Pallas kernels for 0%

profile of v8, /device:TPU:4, one launch (start us, length us, event | category | flops | bytes accessed | tf_op | source)
XLA Modules:
  0.0 168.1 jit_solution(18024940456957827133)
XLA Ops:
  0.0 3.1 %multiply_reduce_fusion = f32[512,256]{1,0:T(8,128)S(1)} fusion(bf16[2,8,512,256]{3,2,1,0:T(8,128)(2,1)} %param.2), kind=kLoop, calls=%fused_computation.6 | loop fusion | flops 6160384 | bytes 4718592 | tf_op jit(solution)/shard_map/reduce_sum | solution.py:56
  3.1 2.3 %collective-permute-start = (f32[512,256]{1,0:T(8,128)S(1)}, f32[512,256]{1,0:T(8,128)S(1)}, u32[]{:S(2)}, u32[]{:S(2)}) collective-permute-start(f32[512,256]{1,0:T(8,128)S(1)} %multiply_reduce_fusion), channel_id=1, source_target_pairs={{0,32},{32,0},{64,96},{96,64},{128,160},{160,128},{192,224},{224,1... | collective-permute-start | bytes 1572872 | tf_op jit(solution)/shard_map/ppermute | solution.py:60
  5.4 12.9 %collective-permute-done = f32[512,256]{1,0:T(8,128)S(1)} collective-permute-done((f32[512,256]{1,0:T(8,128)S(1)}, f32[512,256]{1,0:T(8,128)S(1)}, u32[]{:S(2)}, u32[]{:S(2)}) %collective-permute-start) | collective-permute-done | bytes 524320 | tf_op jit(solution)/shard_map/ppermute | solution.py:60
  18.6 3.3 %collective-permute-start.2 = (f32[65536]{0:T(1024)S(1)}, f32[65536]{0:T(1024)S(1)}, u32[]{:S(2)}, u32[]{:S(2)}) collective-permute-start(f32[65536]{0:T(1024)S(1)} %bitcast.78), channel_id=1, source_target_pairs={{0,128},{32,160},{64,192},{96,224},{128,0},{160,32},{192,64},{224,... | collective-permute-start | bytes 786440 | tf_op jit(solution)/shard_map/ppermute | solution.py:33
  22.1 5.3 %collective-permute-done.2 = f32[65536]{0:T(1024)S(1)} collective-permute-done((f32[65536]{0:T(1024)S(1)}, f32[65536]{0:T(1024)S(1)}, u32[]{:S(2)}, u32[]{:S(2)}) %collective-permute-start.2) | collective-permute-done | bytes 262176 | tf_op jit(solution)/shard_map/ppermute | solution.py:33
  27.4 1.7 collective-permute-start.3
  29.1 3.4 %collective-permute-done.3 = f32[32768]{0:T(1024)S(1)} collective-permute-done((f32[32768]{0:T(1024)S(1)}, f32[32768]{0:T(1024)S(1)}, u32[]{:S(2)}, u32[]{:S(2)}) %collective-permute-start.3) | collective-permute-done | bytes 131104 | tf_op jit(solution)/shard_map/ppermute | solution.py:33
  32.5 1.7 collective-permute-start.4
  34.2 8.4 %collective-permute-start.1 = (bf16[8192,256]{1,0:T(8,128)(2,1)}, bf16[8192,256]{1,0:T(8,128)(2,1)}, u32[]{:S(2)}, u32[]{:S(2)}) collective-permute-start(bf16[8192,256]{1,0:T(8,128)(2,1)} %bitcast.74), channel_id=1, source_target_pairs={{0,30},{2,0},{4,2},{6,4},{8,6},{10,8},{12,10},{14,12},{16,14},{18,... | collective-permute-start | bytes 12582920 | tf_op jit(solution)/shard_map/ppermute | solution.py:15
  42.6 3.0 %collective-permute-start.5 = (f32[65536]{0:T(1024)S(1)}, f32[65536]{0:T(1024)S(1)}, u32[]{:S(2)}, u32[]{:S(2)}) collective-permute-start(f32[65536]{0:T(1024)S(1)} %maximum_select_fusion.2), channel_id=1, source_target_pairs={{0,128},{32,160},{64,192},{96,224},{128,0},{160,32},{192,64},{224,... | collective-permute-start | bytes 786440 | tf_op jit(solution)/shard_map/ppermute | solution.py:38
  45.7 4.9 %collective-permute-done.5 = f32[65536]{0:T(1024)S(1)} collective-permute-done((f32[65536]{0:T(1024)S(1)}, f32[65536]{0:T(1024)S(1)}, u32[]{:S(2)}, u32[]{:S(2)}) %collective-permute-start.5) | collective-permute-done | bytes 262176 | tf_op jit(solution)/shard_map/ppermute | solution.py:38
  50.9 3.1 %multiply_convert_fusion = bf16[2,8,512,256]{3,2,0,1:T(8,128)(2,1)S(1)} fusion(bf16[2,8,512,256]{3,2,1,0:T(8,128)(2,1)} %param.2, f32[512,256]{1,0:T(8,128)S(1)} %fusion.47), kind=kLoop, calls=%fused_computation.5 | loop fusion | flops 6291456 | bytes 8912896 | tf_op jit(solution)/shard_map/convert_element_type | solution.py:51
  53.9 3.4 %collective-permute-start.6 = (f32[512,256]{1,0:T(8,128)S(1)}, f32[512,256]{1,0:T(8,128)S(1)}, u32[]{:S(2)}, u32[]{:S(2)}) collective-permute-start(f32[512,256]{1,0:T(8,128)S(1)} %fusion.47), channel_id=1, source_target_pairs={{0,30},{2,0},{4,2},{6,4},{8,6},{10,8},{12,10},{14,12},{16,14},{18,... | collective-permute-start | bytes 1572872 | tf_op jit(solution)/shard_map/ppermute | solution.py:15
  57.6 21.3 %collective-permute-done.8 = f32[512,256]{1,0:T(8,128)S(1)} collective-permute-done((f32[512,256]{1,0:T(8,128)S(1)}, f32[512,256]{1,0:T(8,128)S(1)}, u32[]{:S(2)}, u32[]{:S(2)}) %collective-permute-start.8) | collective-permute-done | bytes 524320 | tf_op jit(solution)/shard_map/ppermute | solution.py:15
  78.9 3.1 %fusion.1 = bf16[2,8,512,256]{3,2,0,1:T(8,128)(2,1)S(1)} fusion(f32[512,256]{1,0:T(8,128)S(1)} %collective-permute-done.8, bf16[2,8,512,256]{3,2,1,0:T(8,128)(2,1)} %bitcast.36), kind=kLoop, calls=%fused_computation.4 | loop fusion | flops 6291456 | bytes 8912896 | tf_op jit(solution)/shard_map/convert_element_type | solution.py:51
  82.2 1.5 fusion.31
  86.0 8.4 %collective-permute-done.6 = f32[512,256]{1,0:T(8,128)S(1)} collective-permute-done((f32[512,256]{1,0:T(8,128)S(1)}, f32[512,256]{1,0:T(8,128)S(1)}, u32[]{:S(2)}, u32[]{:S(2)}) %collective-permute-start.6) | collective-permute-done | bytes 524320 | tf_op jit(solution)/shard_map/ppermute | solution.py:15
  94.4 3.4 %fusion.39 = f32[1,8,256,256]{3,2,1,0:T(8,128)S(1)} fusion(bf16[2,8,512,256]{3,2,1,0:T(8,128)(2,1)} %bitcast.35, f32[512,256]{1,0:T(8,128)S(1)} %collective-permute-done.6, bf16[1,8,512,256]{3,2,0,1:T(8,128)(2,1)S(1)} %get-tuple-element.26, bf16[1,8,512,256]{3,2,0,1:T(8,128)(2,1)S(1)} %get-tuple-element.25), kind=kOutput, calls=%fused_computation.49 | convolution fusion | flops 1082130432 | bytes 11010048 | tf_op jit(solution)/shard_map/pfwa,pfwb->fab/dot_general | solution.py:46
  97.8 3.7 %fusion.34 = f32[1,8,256,256]{3,2,1,0:T(8,128)S(1)} fusion(bf16[2,8,512,256]{3,2,0,1:T(8,128)(2,1)S(1)} %fusion.1, bf16[2,8,512,256]{3,2,1,0:T(8,128)(2,1)} %bitcast.35, f32[512,256]{1,0:T(8,128)S(1)} %collective-permute-done.6), kind=kOutput, calls=%fused_computation.48 | convolution fusion | flops 1080033280 | bytes 11010048 | tf_op jit(solution)/shard_map/pfwa,pfwb->fab/dot_general | solution.py:45
  101.5 2.0 %fusion.2 = bf16[2,8,256,256]{3,2,1,0:T(8,128)(2,1)} fusion(f32[1,8,256,256]{3,2,1,0:T(8,128)S(1)} %fusion.39, f32[1,8,256,256]{3,2,1,0:T(8,128)S(1)} %fusion.34), kind=kLoop, calls=%fused_computation.9 | loop fusion | flops 3145728 | bytes 6291456 | tf_op jit(solution)/shard_map/convert_element_type | solution.py:47
  106.4 1.9 %fusion.8 = bf16[2,8,256,256]{3,2,1,0:T(8,128)(2,1)} fusion(f32[1,8,256,256]{3,2,1,0:T(8,128)S(1)} %convolution_bitcast_fusion.2, f32[1,8,256,256]{3,2,1,0:T(8,128)S(1)} %convolution_bitcast_fusion.3), kind=kLoop, calls=%fused_computation.17 | loop fusion | flops 3145728 | bytes 6291456 | tf_op jit(solution)/shard_map/convert_element_type | solution.py:47
  108.3 24.1 %collective-permute-done.9 = bf16[2,8,512,256]{3,2,0,1:T(8,128)(2,1)} collective-permute-done((bf16[2,8,512,256]{3,2,0,1:T(8,128)(2,1)S(1)}, bf16[2,8,512,256]{3,2,0,1:T(8,128)(2,1)}, u32[]{:S(2)}, u32[]{:S(2)}) %collective-permute-start.9) | collective-permute-done | bytes 4194336 | tf_op jit(solution)/shard_map/ppermute | solution.py:15
  132.4 3.3 %collective-permute-start.10 = (bf16[2,8,512,256]{3,2,0,1:T(8,128)(2,1)}, bf16[2,8,512,256]{3,2,0,1:T(8,128)(2,1)}, u32[]{:S(2)}, u32[]{:S(2)}) collective-permute-start(bf16[2,8,512,256]{3,2,0,1:T(8,128)(2,1)} %collective-permute-done.9), channel_id=1, source_target_pairs={{0,1},{2,3},{4,5},{6,7},{8,9},{10,11},{12,13},{14,15},{16,17},{18,... | collective-permute-start | bytes 12582920 | tf_op jit(solution)/shard_map/ppermute | solution.py:15
  135.6 2.4 %collective-permute-start.11 = (bf16[2,8,256,256]{3,2,1,0:T(8,128)(2,1)}, bf16[2,8,256,256]{3,2,1,0:T(8,128)(2,1)S(1)}, u32[]{:S(2)}, u32[]{:S(2)}) collective-permute-start(bf16[2,8,256,256]{3,2,1,0:T(8,128)(2,1)} %fusion.2), channel_id=1, source_target_pairs={{0,2},{2,4},{4,6},{6,8},{8,10},{10,12},{12,14},{14,16},{16,18},{18... | collective-permute-start | bytes 6291464 | tf_op jit(solution)/shard_map/ppermute | solution.py:15
  138.0 2.5 %fusion.51 = (bf16[1,8,512,256]{3,2,0,1:T(8,128)(2,1)S(1)}, bf16[1,8,512,256]{3,2,0,1:T(8,128)(2,1)S(1)}) fusion(bf16[2,8,512,256]{3,2,0,1:T(8,128)(2,1)} %collective-permute-done.9), kind=kLoop, calls=%fused_computation.64 | loop fusion | flops 1048576 | bytes 8388608 | tf_op jit(solution)/shard_map/slice | solution.py:44
  140.6 1.6 fusion.28
  142.1 3.7 %convolution_bitcast_fusion.1 = f32[1,1,8,256,256]{4,3,2,1,0:T(8,128)S(1)} fusion(bf16[2,8,512,256]{3,2,0,1:T(8,128)(2,1)S(1)} %copy-done.1, bf16[2,8,512,256]{3,2,0,1:T(8,128)(2,1)} %collective-permute-done.9), kind=kOutput, calls=%fused_computation.44 | convolution fusion | flops 1073741824 | bytes 10485760 | tf_op jit(solution)/shard_map/pfwa,pfwb->fab/dot_general | solution.py:45
  146.4 2.5 %fusion.52 = (bf16[1,8,512,256]{3,2,0,1:T(8,128)(2,1)S(1)}, bf16[1,8,512,256]{3,2,0,1:T(8,128)(2,1)S(1)}) fusion(bf16[2,8,512,256]{3,2,0,1:T(8,128)(2,1)} %collective-permute-done.10), kind=kLoop, calls=%fused_computation.65 | loop fusion | flops 1048576 | bytes 8388608 | tf_op jit(solution)/shard_map/slice | solution.py:44
  148.9 1.6 fusion.25
  150.5 3.7 %convolution_bitcast_fusion = f32[1,1,8,256,256]{4,3,2,1,0:T(8,128)S(1)} fusion(bf16[2,8,512,256]{3,2,0,1:T(8,128)(2,1)S(1)} %copy-done.1, bf16[2,8,512,256]{3,2,0,1:T(8,128)(2,1)} %collective-permute-done.10), kind=kOutput, calls=%fused_computation.43 | convolution fusion | flops 1073741824 | bytes 10485760 | tf_op jit(solution)/shard_map/pfwa,pfwb->fab/dot_general | solution.py:45
  157.1 9.0 %collective-permute-done.11 = bf16[2,8,256,256]{3,2,1,0:T(8,128)(2,1)S(1)} collective-permute-done((bf16[2,8,256,256]{3,2,1,0:T(8,128)(2,1)}, bf16[2,8,256,256]{3,2,1,0:T(8,128)(2,1)S(1)}, u32[]{:S(2)}, u32[]{:S(2)}) %collective-permute-start.11) | collective-permute-done | bytes 2097184 | tf_op jit(solution)/shard_map/ppermute | solution.py:15
  166.1 2.0 %bitcast_dynamic-update-slice_fusion = bf16[4,2,8,256,256]{4,3,2,1,0:T(8,128)(2,1)} fusion(bf16[4,2,8,256,256]{4,3,2,1,0:T(8,128)(2,1)} %copy-done.2, bf16[2,8,256,256]{3,2,1,0:T(8,128)(2,1)S(1)} %collective-permute-done.11, bf16[1,2,8,256,256]{4,3,2,1,0:T(8,128)(2,1)S(1)} %slice.55, pred[]{:T(512)S(6)} %eq.19), kind=kLoop, calls=%fused_computation.37 | loop fusion | flops 1048576 | bytes 6291457 | tf_op jit(solution)/shard_map/dynamic_update_slice | solution.py:84
  (40 shorter events, 10.1 us)
Async XLA Ops:
  3.1 47.6 %copy-start.4 = (s32[512,256]{1,0:T(8,128)S(1)}, s32[512,256]{1,0:T(8,128)}, u32[]{:S(2)}) copy-start(s32[512,256]{1,0:T(8,128)} %param.3) | copy-start | bytes 1572868
  3.1 15.3 %collective-permute-start = (f32[512,256]{1,0:T(8,128)S(1)}, f32[512,256]{1,0:T(8,128)S(1)}, u32[]{:S(2)}, u32[]{:S(2)}) collective-permute-start(f32[512,256]{1,0:T(8,128)S(1)} %multiply_reduce_fusion), channel_id=1, source_target_pairs={{0,32},{32,0},{64,96},{96,64},{128,160},{160,128},{192,224},{224,1... | collective-permute-start | bytes 1572872 | tf_op jit(solution)/shard_map/ppermute | solution.py:60
  18.6 8.8 %collective-permute-start.2 = (f32[65536]{0:T(1024)S(1)}, f32[65536]{0:T(1024)S(1)}, u32[]{:S(2)}, u32[]{:S(2)}) collective-permute-start(f32[65536]{0:T(1024)S(1)} %bitcast.78), channel_id=1, source_target_pairs={{0,128},{32,160},{64,192},{96,224},{128,0},{160,32},{192,64},{224,... | collective-permute-start | bytes 786440 | tf_op jit(solution)/shard_map/ppermute | solution.py:33
  22.0 56.9 %collective-permute-start.7 = (bf16[8192,256]{1,0:T(8,128)(2,1)}, bf16[8192,256]{1,0:T(8,128)(2,1)}, u32[]{:S(2)}, u32[]{:S(2)}) collective-permute-start(bf16[8192,256]{1,0:T(8,128)(2,1)} %bitcast.73), channel_id=1, source_target_pairs={{0,1},{1,2},{2,3},{3,4},{4,5},{5,6},{6,7},{7,8},{8,9},{9,10},{10,1... | collective-permute-start | bytes 12582920 | tf_op jit(solution)/shard_map/ppermute | solution.py:15
  27.4 5.1 %collective-permute-start.3 = (f32[32768]{0:T(1024)S(1)}, f32[32768]{0:T(1024)S(1)}, u32[]{:S(2)}, u32[]{:S(2)}) collective-permute-start(f32[32768]{0:T(1024)S(1)} %slice_select_fusion), channel_id=1, source_target_pairs={{0,64},{32,96},{64,0},{96,32},{128,192},{160,224},{192,128},{224,1... | collective-permute-start | bytes 393224 | tf_op jit(solution)/shard_map/ppermute | solution.py:33
  32.5 10.1 %collective-permute-start.4 = (f32[32768]{0:T(1024)S(1)}, f32[32768]{0:T(1024)S(1)}, u32[]{:S(2)}, u32[]{:S(2)}) collective-permute-start(f32[32768]{0:T(1024)S(1)} %select_add_fusion), channel_id=1, source_target_pairs={{0,64},{32,96},{64,0},{96,32},{128,192},{160,224},{192,128},{224,1... | collective-permute-start | bytes 393224 | tf_op jit(solution)/shard_map/ppermute | solution.py:38
  34.2 60.2 %collective-permute-start.1 = (bf16[8192,256]{1,0:T(8,128)(2,1)}, bf16[8192,256]{1,0:T(8,128)(2,1)}, u32[]{:S(2)}, u32[]{:S(2)}) collective-permute-start(bf16[8192,256]{1,0:T(8,128)(2,1)} %bitcast.74), channel_id=1, source_target_pairs={{0,30},{2,0},{4,2},{6,4},{8,6},{10,8},{12,10},{14,12},{16,14},{18,... | collective-permute-start | bytes 12582920 | tf_op jit(solution)/shard_map/ppermute | solution.py:15
  42.6 8.0 %collective-permute-start.5 = (f32[65536]{0:T(1024)S(1)}, f32[65536]{0:T(1024)S(1)}, u32[]{:S(2)}, u32[]{:S(2)}) collective-permute-start(f32[65536]{0:T(1024)S(1)} %maximum_select_fusion.2), channel_id=1, source_target_pairs={{0,128},{32,160},{64,192},{96,224},{128,0},{160,32},{192,64},{224,... | collective-permute-start | bytes 786440 | tf_op jit(solution)/shard_map/ppermute | solution.py:38
  50.8 28.1 %collective-permute-start.8 = (f32[512,256]{1,0:T(8,128)S(1)}, f32[512,256]{1,0:T(8,128)S(1)}, u32[]{:S(2)}, u32[]{:S(2)}) collective-permute-start(f32[512,256]{1,0:T(8,128)S(1)} %fusion.47), channel_id=1, source_target_pairs={{0,1},{1,2},{2,3},{3,4},{4,5},{5,6},{6,7},{7,8},{8,9},{9,10},{10,1... | collective-permute-start | bytes 1572872 | tf_op jit(solution)/shard_map/ppermute | solution.py:15
  53.9 51.0 %copy-start = (bf16[2,8,512,256]{3,2,0,1:T(8,128)(2,1)}, bf16[2,8,512,256]{3,2,0,1:T(8,128)(2,1)S(1)}, u32[]{:S(2)}) copy-start(bf16[2,8,512,256]{3,2,0,1:T(8,128)(2,1)S(1)} %multiply_convert_fusion) | copy-start | bytes 12582916
  53.9 40.4 %collective-permute-start.6 = (f32[512,256]{1,0:T(8,128)S(1)}, f32[512,256]{1,0:T(8,128)S(1)}, u32[]{:S(2)}, u32[]{:S(2)}) collective-permute-start(f32[512,256]{1,0:T(8,128)S(1)} %fusion.47), channel_id=1, source_target_pairs={{0,30},{2,0},{4,2},{6,4},{8,6},{10,8},{12,10},{14,12},{16,14},{18,... | collective-permute-start | bytes 1572872 | tf_op jit(solution)/shard_map/ppermute | solution.py:15
  82.0 50.4 %collective-permute-start.9 = (bf16[2,8,512,256]{3,2,0,1:T(8,128)(2,1)S(1)}, bf16[2,8,512,256]{3,2,0,1:T(8,128)(2,1)}, u32[]{:S(2)}, u32[]{:S(2)}) collective-permute-start(bf16[2,8,512,256]{3,2,0,1:T(8,128)(2,1)S(1)} %fusion.1), channel_id=1, source_target_pairs={{0,1},{1,2},{2,3},{3,4},{4,5},{5,6},{6,7},{7,8},{8,9},{9,10},{10,1... | collective-permute-start | bytes 12582920 | tf_op jit(solution)/shard_map/ppermute | solution.py:15
  132.4 14.0 %collective-permute-start.10 = (bf16[2,8,512,256]{3,2,0,1:T(8,128)(2,1)}, bf16[2,8,512,256]{3,2,0,1:T(8,128)(2,1)}, u32[]{:S(2)}, u32[]{:S(2)}) collective-permute-start(bf16[2,8,512,256]{3,2,0,1:T(8,128)(2,1)} %collective-permute-done.9), channel_id=1, source_target_pairs={{0,1},{2,3},{4,5},{6,7},{8,9},{10,11},{12,13},{14,15},{16,17},{18,... | collective-permute-start | bytes 12582920 | tf_op jit(solution)/shard_map/ppermute | solution.py:15
  135.6 4.9 %copy-start.1 = (bf16[2,8,512,256]{3,2,0,1:T(8,128)(2,1)S(1)}, bf16[2,8,512,256]{3,2,0,1:T(8,128)(2,1)}, u32[]{:S(2)}) copy-start(bf16[2,8,512,256]{3,2,0,1:T(8,128)(2,1)} %copy-done) | copy-start | bytes 12582916
  135.6 30.5 %collective-permute-start.11 = (bf16[2,8,256,256]{3,2,1,0:T(8,128)(2,1)}, bf16[2,8,256,256]{3,2,1,0:T(8,128)(2,1)S(1)}, u32[]{:S(2)}, u32[]{:S(2)}) collective-permute-start(bf16[2,8,256,256]{3,2,1,0:T(8,128)(2,1)} %fusion.2), channel_id=1, source_target_pairs={{0,2},{2,4},{4,6},{6,8},{8,10},{10,12},{12,14},{14,16},{16,18},{18... | collective-permute-start | bytes 6291464 | tf_op jit(solution)/shard_map/ppermute | solution.py:15
  154.2 1.6 copy-start.3
  156.9 9.2 %copy-start.2 = (bf16[4,2,8,256,256]{4,3,2,1,0:T(8,128)(2,1)}, bf16[4,2,8,256,256]{4,3,2,1,0:T(8,128)(2,1)S(1)}, u32[]{:S(2)}) copy-start(bf16[4,2,8,256,256]{4,3,2,1,0:T(8,128)(2,1)S(1)} %pad_maximum_fusion) | copy-start | bytes 25165828

commit v9 on v8

--- a/solution.py
+++ b/solution.py
@@ -9,9 +9,10 @@
 eps_energy = 1e-06
 
 
-def moved(value, axis, offset, only_even=False):
+def moved(value, axis, offset, only_even=False, only_odd=False):
     count = lax.axis_size(axis)
-    pairs = [(source, (source + offset) % count) for source in range(count) if not only_even or source % 2 == 0]
+    pairs = [(source, (source + offset) % count) for source in range(count)
+             if not (only_even and source % 2) and not (only_odd and source % 2 == 0)]
     return lax.ppermute(value, axis, pairs)
 
 
@@ -62,10 +63,12 @@
     flat_spectra = spectra.reshape(-1, spectra.shape[-1])
     raw_near = moved(flat_spectra, "chan", 1).reshape(spectra.shape)
     raw_ahead = moved(flat_spectra, "chan", -2, only_even=True).reshape(spectra.shape)
+    raw_mate = moved(flat_spectra, "chan", -1, only_odd=True).reshape(spectra.shape)
     energy = band_sum(partial_energy, "band")
     window_gain = valid_mask.astype(jnp.float32) / jnp.sqrt(energy / total_bins + eps_energy)
     gain_near = moved(window_gain, "chan", 1)
     gain_ahead = moved(window_gain, "chan", -2, only_even=True)
+    gain_mate = moved(window_gain, "chan", -1, only_odd=True)
     whitened = whiten(spectra, window_gain)
     near = whiten(raw_near, gain_near)
     ahead = whiten(raw_ahead, gain_ahead)
@@ -74,13 +77,14 @@
     own_lag = cross_block(whitened, whitened, scale)
     near_lag = cross_block(whitened, near, scale)
     for_above, second, own_lag, near_lag = lax.optimization_barrier((for_above, second, own_lag, near_lag))
-    third = moved(second, "chan", 1, only_even=True)
     from_below = moved(for_above, "chan", 2, only_even=True)
+    mate = whiten(raw_mate, gain_mate)
+    for_mate = cross_block(mate, second, scale)
+    from_mate = moved(for_mate, "chan", 1, only_even=True)
     lag_two = cross_block(whitened, second, scale)
-    lag_three = cross_block(whitened, third, scale)
-    early = jnp.stack([own_lag, near_lag, lag_two, lag_three])
+    early = jnp.stack([own_lag, near_lag, lag_two, jnp.zeros_like(own_lag)])
     early, second = lax.optimization_barrier((early, second))
-    last = jnp.where(even, from_below, early[3])
+    last = jnp.where(even, from_below, from_mate)
     return lax.dynamic_update_slice_in_dim(early, last[None], 3, axis=0)
 
 

time: 169 us -> 167 us (0.988)
  other arithmetic: 23.8 us -> 19 us
  waiting for transfers between devices: 89.2 us -> 91.7 us
  starting transfers between devices: 29.8 us -> 32.2 us
    slice x4 -> x3, other arithmetic: 5.55 us -> 0.82 us  [cross_block(): flipped = jnp.stack([partner[1], -partner[0]])]
    ppermute x7 -> x9, waiting for transfers between devices: 62.8 us -> 66.6 us  [moved(): return lax.ppermute(value, axis, pairs)]
    convert_element_type x5, other arithmetic: 5.62 us -> 2.79 us  [cross_block(): return (jnp.stack([real_part, imag_part]) * scale).astype(jnp.bfloat16)]
    another operation x1, other arithmetic: 1.1 us -> 3.88 us  [shards(): early = jnp.stack([own_lag, near_lag, lag_two, jnp.zeros_like(own_lag)])]
    ppermute x7 -> x9, starting transfers between devices: 17.9 us -> 20.3 us  [moved(): return lax.ppermute(value, axis, pairs)]
    dot_general x5, matrix products: 13.8 us -> 11.7 us  [cross_block(): jnp.einsum('pfwa,pfwb->fab', own_block, partner, preferred_element_type=j...]
    dot_general x5, matrix products: 9.53 us -> 11.3 us  [cross_block(): jnp.einsum('pfwa,pfwb->fab', own_block, flipped, preferred_element_type=j...]
  transfers between devices with their start and end apart: 12 -> 14, of which waited for: 8 -> 8; matrix products, arithmetic and copies ran while one was open for 25% -> 22% of each run, Pallas kernels for 0% -> 0%
where the time goes in v9:
time: 167 us
  waiting for transfers between devices  91.7 us (55%)
  starting transfers between devices  32.2 us (19%)
  matrix products  23 us (14%)
  other arithmetic  19 us (11%)
    ppermute x9, waiting for transfers between devices, moved(): return lax.ppermute(value, axis, pairs)  66.6 us
    ppermute x9, starting transfers between devices, moved(): return lax.ppermute(value, axis, pairs)  20.3 us
    ppermute x1, waiting for transfers between devices, shards(): lax.ppermute(partial_energy, 'band', [(s, s ^ 1) for s in range(lax.axis_...  12.9 us
    dot_general x5, matrix products, cross_block(): jnp.einsum('pfwa,pfwb->fab', own_block, partner, preferred_element_type=j...  11.7 us
    dot_general x5, matrix products, cross_block(): jnp.einsum('pfwa,pfwb->fab', own_block, flipped, preferred_element_type=j...  11.3 us
    ppermute x2, waiting for transfers between devices, band_sum(): got = lax.ppermute(jnp.where(bit == 0, high, low), axis, pairs)  8.64 us
    convert_element_type x2, other arithmetic, whiten(): return (raw.astype(jnp.float32) * gain).astype(jnp.bfloat16)  6.1 us
    ppermute x2, starting transfers between devices, band_sum(): got = lax.ppermute(jnp.where(bit == 0, high, low), axis, pairs)  4.94 us
  transfers between devices with their start and end apart: 14, of which 8 were waited for; matrix products, arithmetic and copies ran while one was open for 22% of the time, Pallas kernels for 0%

profile of v9, /device:TPU:4, one launch (start us, length us, event | category | flops | bytes accessed | tf_op | source)
XLA Modules:
  0.0 166.7 jit_solution(11430046429042264260)
XLA Ops:
  0.0 3.1 %multiply_reduce_fusion = f32[512,256]{1,0:T(8,128)S(1)} fusion(bf16[2,8,512,256]{3,2,1,0:T(8,128)(2,1)} %param.2), kind=kLoop, calls=%fused_computation.8 | loop fusion | flops 6160384 | bytes 4718592 | tf_op jit(solution)/shard_map/reduce_sum | solution.py:57
  3.1 2.3 %collective-permute-start = (f32[512,256]{1,0:T(8,128)S(1)}, f32[512,256]{1,0:T(8,128)S(1)}, u32[]{:S(2)}, u32[]{:S(2)}) collective-permute-start(f32[512,256]{1,0:T(8,128)S(1)} %multiply_reduce_fusion), channel_id=1, source_target_pairs={{0,32},{32,0},{64,96},{96,64},{128,160},{160,128},{192,224},{224,1... | collective-permute-start | bytes 1572872 | tf_op jit(solution)/shard_map/ppermute | solution.py:61
  5.4 12.9 %collective-permute-done = f32[512,256]{1,0:T(8,128)S(1)} collective-permute-done((f32[512,256]{1,0:T(8,128)S(1)}, f32[512,256]{1,0:T(8,128)S(1)}, u32[]{:S(2)}, u32[]{:S(2)}) %collective-permute-start) | collective-permute-done | bytes 524320 | tf_op jit(solution)/shard_map/ppermute | solution.py:61
  18.6 3.3 %collective-permute-start.2 = (f32[65536]{0:T(1024)S(1)}, f32[65536]{0:T(1024)S(1)}, u32[]{:S(2)}, u32[]{:S(2)}) collective-permute-start(f32[65536]{0:T(1024)S(1)} %bitcast.71), channel_id=1, source_target_pairs={{0,128},{32,160},{64,192},{96,224},{128,0},{160,32},{192,64},{224,... | collective-permute-start | bytes 786440 | tf_op jit(solution)/shard_map/ppermute | solution.py:34
  22.1 5.3 %collective-permute-done.2 = f32[65536]{0:T(1024)S(1)} collective-permute-done((f32[65536]{0:T(1024)S(1)}, f32[65536]{0:T(1024)S(1)}, u32[]{:S(2)}, u32[]{:S(2)}) %collective-permute-start.2) | collective-permute-done | bytes 262176 | tf_op jit(solution)/shard_map/ppermute | solution.py:34
  27.4 1.7 collective-permute-start.3
  29.1 3.4 %collective-permute-done.3 = f32[32768]{0:T(1024)S(1)} collective-permute-done((f32[32768]{0:T(1024)S(1)}, f32[32768]{0:T(1024)S(1)}, u32[]{:S(2)}, u32[]{:S(2)}) %collective-permute-start.3) | collective-permute-done | bytes 131104 | tf_op jit(solution)/shard_map/ppermute | solution.py:34
  32.5 1.7 collective-permute-start.4
  34.2 8.4 %collective-permute-start.1 = (bf16[8192,256]{1,0:T(8,128)(2,1)}, bf16[8192,256]{1,0:T(8,128)(2,1)}, u32[]{:S(2)}, u32[]{:S(2)}) collective-permute-start(bf16[8192,256]{1,0:T(8,128)(2,1)} %bitcast.66), channel_id=1, source_target_pairs={{0,30},{2,0},{4,2},{6,4},{8,6},{10,8},{12,10},{14,12},{16,14},{18,... | collective-permute-start | bytes 12582920 | tf_op jit(solution)/shard_map/ppermute | solution.py:16
  42.6 3.0 %collective-permute-start.5 = (f32[65536]{0:T(1024)S(1)}, f32[65536]{0:T(1024)S(1)}, u32[]{:S(2)}, u32[]{:S(2)}) collective-permute-start(f32[65536]{0:T(1024)S(1)} %maximum_select_fusion.2), channel_id=1, source_target_pairs={{0,128},{32,160},{64,192},{96,224},{128,0},{160,32},{192,64},{224,... | collective-permute-start | bytes 786440 | tf_op jit(solution)/shard_map/ppermute | solution.py:39
  47.1 3.5 %collective-permute-done.5 = f32[65536]{0:T(1024)S(1)} collective-permute-done((f32[65536]{0:T(1024)S(1)}, f32[65536]{0:T(1024)S(1)}, u32[]{:S(2)}, u32[]{:S(2)}) %collective-permute-start.5) | collective-permute-done | bytes 262176 | tf_op jit(solution)/shard_map/ppermute | solution.py:39
  50.8 3.4 %collective-permute-start.6 = (f32[512,256]{1,0:T(8,128)S(1)}, f32[512,256]{1,0:T(8,128)S(1)}, u32[]{:S(2)}, u32[]{:S(2)}) collective-permute-start(f32[512,256]{1,0:T(8,128)S(1)} %fusion.50), channel_id=1, source_target_pairs={{0,30},{2,0},{4,2},{6,4},{8,6},{10,8},{12,10},{14,12},{16,14},{18,... | collective-permute-start | bytes 1572872 | tf_op jit(solution)/shard_map/ppermute | solution.py:16
  54.2 3.0 %multiply_convert_fusion = bf16[2,8,512,256]{3,2,0,1:T(8,128)(2,1)S(1)} fusion(bf16[2,8,512,256]{3,2,1,0:T(8,128)(2,1)} %param.2, f32[512,256]{1,0:T(8,128)S(1)} %fusion.50), kind=kLoop, calls=%fused_computation.7 | loop fusion | flops 6291456 | bytes 8912896 | tf_op jit(solution)/shard_map/convert_element_type | solution.py:52
  57.3 1.4 convolution_bitcast_fusion.4
  58.7 20.2 %collective-permute-done.8 = f32[512,256]{1,0:T(8,128)S(1)} collective-permute-done((f32[512,256]{1,0:T(8,128)S(1)}, f32[512,256]{1,0:T(8,128)S(1)}, u32[]{:S(2)}, u32[]{:S(2)}) %collective-permute-start.8) | collective-permute-done | bytes 524320 | tf_op jit(solution)/shard_map/ppermute | solution.py:16
  80.2 3.1 %fusion.2 = bf16[2,8,512,256]{3,2,0,1:T(8,128)(2,1)S(1)} fusion(f32[512,256]{1,0:T(8,128)S(1)} %collective-permute-done.8, bf16[2,8,512,256]{3,2,1,0:T(8,128)(2,1)} %bitcast.34), kind=kLoop, calls=%fused_computation.6 | loop fusion | flops 6291456 | bytes 8912896 | tf_op jit(solution)/shard_map/convert_element_type | solution.py:52
  83.3 2.2 %collective-permute-start.9 = (bf16[2,8,512,256]{3,2,0,1:T(8,128)(2,1)S(1)}, bf16[2,8,512,256]{3,2,0,1:T(8,128)(2,1)S(1)}, u32[]{:S(2)}, u32[]{:S(2)}) collective-permute-start(bf16[2,8,512,256]{3,2,0,1:T(8,128)(2,1)S(1)} %fusion.2), channel_id=1, source_target_pairs={{0,1},{1,2},{2,3},{3,4},{4,5},{5,6},{6,7},{7,8},{8,9},{9,10},{10,1... | collective-permute-start | bytes 12582920 | tf_op jit(solution)/shard_map/ppermute | solution.py:16
  85.7 1.5 fusion.24
  88.0 6.3 %collective-permute-done.6 = f32[512,256]{1,0:T(8,128)S(1)} collective-permute-done((f32[512,256]{1,0:T(8,128)S(1)}, f32[512,256]{1,0:T(8,128)S(1)}, u32[]{:S(2)}, u32[]{:S(2)}) %collective-permute-start.6) | collective-permute-done | bytes 524320 | tf_op jit(solution)/shard_map/ppermute | solution.py:16
  94.4 3.4 %fusion.32 = f32[1,8,256,256]{3,2,1,0:T(8,128)S(1)} fusion(bf16[2,8,512,256]{3,2,1,0:T(8,128)(2,1)} %bitcast.33, f32[512,256]{1,0:T(8,128)S(1)} %collective-permute-done.6, bf16[1,8,512,256]{3,2,0,1:T(8,128)(2,1)S(1)} %get-tuple-element.24, bf16[1,8,512,256]{3,2,0,1:T(8,128)(2,1)S(1)} %get-tuple-element.23), kind=kOutput, calls=%fused_computation.44 | convolution fusion | flops 1082130432 | bytes 11010048 | tf_op jit(solution)/shard_map/pfwa,pfwb->fab/dot_general | solution.py:47
  97.8 3.7 %fusion.27 = f32[1,8,256,256]{3,2,1,0:T(8,128)S(1)} fusion(bf16[2,8,512,256]{3,2,0,1:T(8,128)(2,1)S(1)} %fusion.2, bf16[2,8,512,256]{3,2,1,0:T(8,128)(2,1)} %bitcast.33, f32[512,256]{1,0:T(8,128)S(1)} %collective-permute-done.6), kind=kOutput, calls=%fused_computation.43 | convolution fusion | flops 1080033280 | bytes 11010048 | tf_op jit(solution)/shard_map/pfwa,pfwb->fab/dot_general | solution.py:46
  102.1 1.5 convolution_bitcast_fusion.2
  103.5 1.4 convolution_bitcast_fusion.3
  105.5 29.2 %collective-permute-done.9 = bf16[2,8,512,256]{3,2,0,1:T(8,128)(2,1)S(1)} collective-permute-done((bf16[2,8,512,256]{3,2,0,1:T(8,128)(2,1)S(1)}, bf16[2,8,512,256]{3,2,0,1:T(8,128)(2,1)S(1)}, u32[]{:S(2)}, u32[]{:S(2)}) %collective-permute-start.9) | collective-permute-done | bytes 4194336 | tf_op jit(solution)/shard_map/ppermute | solution.py:16
  134.7 2.1 %collective-permute-start.10 = (bf16[2,8,256,256]{3,2,1,0:T(8,128)(2,1)S(1)}, bf16[2,8,256,256]{3,2,1,0:T(8,128)(2,1)S(1)}, u32[]{:S(2)}, u32[]{:S(2)}) collective-permute-start(bf16[2,8,256,256]{3,2,1,0:T(8,128)(2,1)S(1)} %fusion.3), channel_id=1, source_target_pairs={{0,2},{2,4},{4,6},{6,8},{8,10},{10,12},{12,14},{14,16},{16,18},{18... | collective-permute-start | bytes 6291464 | tf_op jit(solution)/shard_map/ppermute | solution.py:16
  137.2 3.8 %fusion.37 = f32[1,8,256,256]{3,2,1,0:T(8,128)S(1)} fusion(bf16[2,8,512,256]{3,2,0,1:T(8,128)(2,1)S(1)} %collective-permute-done.9, bf16[2,8,512,256]{3,2,1,0:T(8,128)(2,1)} %bitcast.37, f32[512,256]{1,0:T(8,128)} %collective-permute-done.12), kind=kOutput, calls=%fused_computation.45 | convolution fusion | flops 1080033280 | bytes 11010048 | tf_op jit(solution)/shard_map/pfwa,pfwb->fab/dot_general | solution.py:46
  141.0 3.5 %fusion.42 = f32[1,8,256,256]{3,2,1,0:T(8,128)S(1)} fusion(bf16[2,8,512,256]{3,2,1,0:T(8,128)(2,1)} %bitcast.37, f32[512,256]{1,0:T(8,128)} %collective-permute-done.12, bf16[1,8,512,256]{3,2,0,1:T(8,128)(2,1)S(1)} %get-tuple-element.20, bf16[1,8,512,256]{3,2,0,1:T(8,128)(2,1)S(1)} %get-tuple-element.19), kind=kOutput, calls=%fused_computation.46 | convolution fusion | flops 1082130432 | bytes 11010048 | tf_op jit(solution)/shard_map/pfwa,pfwb->fab/dot_general | solution.py:47
  145.0 1.4 collective-permute-start.13
  146.4 1.5 convolution_bitcast_fusion
  149.9 3.9 %maximum_maximum_fusion = bf16[4,2,8,256,256]{4,3,2,1,0:T(8,128)(2,1)} fusion(bf16[1,2,8,256,256]{4,3,2,1,0:T(8,128)(2,1)S(1)} %fusion.10, bf16[1,2,8,256,256]{4,3,2,1,0:T(8,128)(2,1)S(1)} %bitcast.69, bf16[1,2,8,256,256]{4,3,2,1,0:T(8,128)(2,1)S(1)} %bitcast.68, bf16[4]{0:T(256)(128)(2,1)S(1)} %pad.5.clone), kind=kLoop, calls=%fused_computation | loop fusion | flops 12582912 | bytes 14680072 | tf_op jit(solution)/shard_map/stack | solution.py:85
  153.8 10.9 %collective-permute-done.10 = bf16[2,8,256,256]{3,2,1,0:T(8,128)(2,1)S(1)} collective-permute-done((bf16[2,8,256,256]{3,2,1,0:T(8,128)(2,1)S(1)}, bf16[2,8,256,256]{3,2,1,0:T(8,128)(2,1)S(1)}, u32[]{:S(2)}, u32[]{:S(2)}) %collective-permute-start.10) | collective-permute-done | bytes 2097184 | tf_op jit(solution)/shard_map/ppermute | solution.py:16
  164.7 2.0 %bitcast_dynamic-update-slice_fusion = bf16[4,2,8,256,256]{4,3,2,1,0:T(8,128)(2,1)} fusion(bf16[4,2,8,256,256]{4,3,2,1,0:T(8,128)(2,1)} %maximum_maximum_fusion, bf16[2,8,256,256]{3,2,1,0:T(8,128)(2,1)S(1)} %collective-permute-done.10, bf16[2,8,256,256]{3,2,1,0:T(8,128)(2,1)S(1)} %collective-permute-done.13, pred[]{:T(512)S(6)} %eq.19), kind=kLoop, calls=%fused_computation.35 | loop fusion | flops 1048576 | bytes 6291457 | tf_op jit(solution)/shard_map/dynamic_update_slice | solution.py:88
  (35 shorter events, 8.6 us)
Async XLA Ops:
  3.1 47.6 %copy-start = (s32[512,256]{1,0:T(8,128)S(1)}, s32[512,256]{1,0:T(8,128)}, u32[]{:S(2)}) copy-start(s32[512,256]{1,0:T(8,128)} %param.3) | copy-start | bytes 1572868
  3.1 15.3 %collective-permute-start = (f32[512,256]{1,0:T(8,128)S(1)}, f32[512,256]{1,0:T(8,128)S(1)}, u32[]{:S(2)}, u32[]{:S(2)}) collective-permute-start(f32[512,256]{1,0:T(8,128)S(1)} %multiply_reduce_fusion), channel_id=1, source_target_pairs={{0,32},{32,0},{64,96},{96,64},{128,160},{160,128},{192,224},{224,1... | collective-permute-start | bytes 1572872 | tf_op jit(solution)/shard_map/ppermute | solution.py:61
  18.6 8.8 %collective-permute-start.2 = (f32[65536]{0:T(1024)S(1)}, f32[65536]{0:T(1024)S(1)}, u32[]{:S(2)}, u32[]{:S(2)}) collective-permute-start(f32[65536]{0:T(1024)S(1)} %bitcast.71), channel_id=1, source_target_pairs={{0,128},{32,160},{64,192},{96,224},{128,0},{160,32},{192,64},{224,... | collective-permute-start | bytes 786440 | tf_op jit(solution)/shard_map/ppermute | solution.py:34
  22.0 58.2 %collective-permute-start.7 = (bf16[8192,256]{1,0:T(8,128)(2,1)}, bf16[8192,256]{1,0:T(8,128)(2,1)}, u32[]{:S(2)}, u32[]{:S(2)}) collective-permute-start(bf16[8192,256]{1,0:T(8,128)(2,1)} %bitcast.65), channel_id=1, source_target_pairs={{0,1},{1,2},{2,3},{3,4},{4,5},{5,6},{6,7},{7,8},{8,9},{9,10},{10,1... | collective-permute-start | bytes 12582920 | tf_op jit(solution)/shard_map/ppermute | solution.py:16
  27.4 5.1 %collective-permute-start.3 = (f32[32768]{0:T(1024)S(1)}, f32[32768]{0:T(1024)S(1)}, u32[]{:S(2)}, u32[]{:S(2)}) collective-permute-start(f32[32768]{0:T(1024)S(1)} %slice_select_fusion), channel_id=1, source_target_pairs={{0,64},{32,96},{64,0},{96,32},{128,192},{160,224},{192,128},{224,1... | collective-permute-start | bytes 393224 | tf_op jit(solution)/shard_map/ppermute | solution.py:34
  32.5 10.1 %collective-permute-start.4 = (f32[32768]{0:T(1024)S(1)}, f32[32768]{0:T(1024)S(1)}, u32[]{:S(2)}, u32[]{:S(2)}) collective-permute-start(f32[32768]{0:T(1024)S(1)} %select_add_fusion), channel_id=1, source_target_pairs={{0,64},{32,96},{64,0},{96,32},{128,192},{160,224},{192,128},{224,1... | collective-permute-start | bytes 393224 | tf_op jit(solution)/shard_map/ppermute | solution.py:39
  34.2 60.2 %collective-permute-start.1 = (bf16[8192,256]{1,0:T(8,128)(2,1)}, bf16[8192,256]{1,0:T(8,128)(2,1)}, u32[]{:S(2)}, u32[]{:S(2)}) collective-permute-start(bf16[8192,256]{1,0:T(8,128)(2,1)} %bitcast.66), channel_id=1, source_target_pairs={{0,30},{2,0},{4,2},{6,4},{8,6},{10,8},{12,10},{14,12},{16,14},{18,... | collective-permute-start | bytes 12582920 | tf_op jit(solution)/shard_map/ppermute | solution.py:16
  42.6 8.0 %collective-permute-start.5 = (f32[65536]{0:T(1024)S(1)}, f32[65536]{0:T(1024)S(1)}, u32[]{:S(2)}, u32[]{:S(2)}) collective-permute-start(f32[65536]{0:T(1024)S(1)} %maximum_select_fusion.2), channel_id=1, source_target_pairs={{0,128},{32,160},{64,192},{96,224},{128,0},{160,32},{192,64},{224,... | collective-permute-start | bytes 786440 | tf_op jit(solution)/shard_map/ppermute | solution.py:39
  45.7 91.5 %collective-permute-start.11 = (bf16[8192,256]{1,0:T(8,128)(2,1)}, bf16[8192,256]{1,0:T(8,128)(2,1)}, u32[]{:S(2)}, u32[]{:S(2)}) collective-permute-start(bf16[8192,256]{1,0:T(8,128)(2,1)} %bitcast.67), channel_id=1, source_target_pairs={{1,0},{3,2},{5,4},{7,6},{9,8},{11,10},{13,12},{15,14},{17,16},{19,... | collective-permute-start | bytes 12582920 | tf_op jit(solution)/shard_map/ppermute | solution.py:16
  50.8 43.6 %collective-permute-start.6 = (f32[512,256]{1,0:T(8,128)S(1)}, f32[512,256]{1,0:T(8,128)S(1)}, u32[]{:S(2)}, u32[]{:S(2)}) collective-permute-start(f32[512,256]{1,0:T(8,128)S(1)} %fusion.50), channel_id=1, source_target_pairs={{0,30},{2,0},{4,2},{6,4},{8,6},{10,8},{12,10},{14,12},{16,14},{18,... | collective-permute-start | bytes 1572872 | tf_op jit(solution)/shard_map/ppermute | solution.py:16
  54.1 24.7 %collective-permute-start.8 = (f32[512,256]{1,0:T(8,128)S(1)}, f32[512,256]{1,0:T(8,128)S(1)}, u32[]{:S(2)}, u32[]{:S(2)}) collective-permute-start(f32[512,256]{1,0:T(8,128)S(1)} %fusion.50), channel_id=1, source_target_pairs={{0,1},{1,2},{2,3},{3,4},{4,5},{5,6},{6,7},{7,8},{8,9},{9,10},{10,1... | collective-permute-start | bytes 1572872 | tf_op jit(solution)/shard_map/ppermute | solution.py:16
  78.9 58.2 %collective-permute-start.12 = (f32[512,256]{1,0:T(8,128)S(1)}, f32[512,256]{1,0:T(8,128)}, u32[]{:S(2)}, u32[]{:S(2)}) collective-permute-start(f32[512,256]{1,0:T(8,128)S(1)} %fusion.50), channel_id=1, source_target_pairs={{1,0},{3,2},{5,4},{7,6},{9,8},{11,10},{13,12},{15,14},{17,16},{19,... | collective-permute-start | bytes 1572872 | tf_op jit(solution)/shard_map/ppermute | solution.py:16
  83.3 51.5 %collective-permute-start.9 = (bf16[2,8,512,256]{3,2,0,1:T(8,128)(2,1)S(1)}, bf16[2,8,512,256]{3,2,0,1:T(8,128)(2,1)S(1)}, u32[]{:S(2)}, u32[]{:S(2)}) collective-permute-start(bf16[2,8,512,256]{3,2,0,1:T(8,128)(2,1)S(1)} %fusion.2), channel_id=1, source_target_pairs={{0,1},{1,2},{2,3},{3,4},{4,5},{5,6},{6,7},{7,8},{8,9},{9,10},{10,1... | collective-permute-start | bytes 12582920 | tf_op jit(solution)/shard_map/ppermute | solution.py:16
  134.7 30.0 %collective-permute-start.10 = (bf16[2,8,256,256]{3,2,1,0:T(8,128)(2,1)S(1)}, bf16[2,8,256,256]{3,2,1,0:T(8,128)(2,1)S(1)}, u32[]{:S(2)}, u32[]{:S(2)}) collective-permute-start(bf16[2,8,256,256]{3,2,1,0:T(8,128)(2,1)S(1)} %fusion.3), channel_id=1, source_target_pairs={{0,2},{2,4},{4,6},{6,8},{8,10},{10,12},{12,14},{14,16},{16,18},{18... | collective-permute-start | bytes 6291464 | tf_op jit(solution)/shard_map/ppermute | solution.py:16
  145.0 19.7 %collective-permute-start.13 = (bf16[2,8,256,256]{3,2,1,0:T(8,128)(2,1)S(1)}, bf16[2,8,256,256]{3,2,1,0:T(8,128)(2,1)S(1)}, u32[]{:S(2)}, u32[]{:S(2)}) collective-permute-start(bf16[2,8,256,256]{3,2,1,0:T(8,128)(2,1)S(1)} %fusion.11), channel_id=1, source_target_pairs={{0,1},{2,3},{4,5},{6,7},{8,9},{10,11},{12,13},{14,15},{16,17},{18,... | collective-permute-start | bytes 6291464 | tf_op jit(solution)/shard_map/ppermute | solution.py:16

commit v10 on v9

--- a/solution.py
+++ b/solution.py
@@ -34,6 +34,7 @@
         got = lax.ppermute(jnp.where(bit == 0, high, low), axis, pairs)
         flat = jnp.where(bit == 0, low, high) + got
         bits.append(bit)
+    flat = flat + lax.ppermute(flat, axis, [(s, s ^ 1) for s in range(count)])
     for d, bit in zip(reversed(dists), reversed(bits)):
         pairs = [(s, s ^ d) for s in range(count)]
         got = lax.ppermute(flat, axis, pairs)
@@ -58,8 +59,6 @@
     total_bins = spectra.shape[1] * lax.axis_size("band")
     scale = 1.0 / math.sqrt(spectra.shape[2])
     even = lax.axis_index("chan") % 2 == 0
-    partial_energy = partial_energy + lax.ppermute(partial_energy, "band", [(s, s ^ 1) for s in range(lax.axis_size("band"))])
-    spectra, partial_energy = lax.optimization_barrier((spectra, partial_energy))
     flat_spectra = spectra.reshape(-1, spectra.shape[-1])
     raw_near = moved(flat_spectra, "chan", 1).reshape(spectra.shape)
     raw_ahead = moved(flat_spectra, "chan", -2, only_even=True).reshape(spectra.shape)

time: 167 us -> 177 us (1.060); the launches traced: 167 us -> 175 us
  waiting for transfers between devices: 91.7 us -> 113 us
  starting transfers between devices: 32.2 us -> 19.5 us
    ppermute x1, waiting for transfers between devices: 12.9 us -> 42 us  [band_sum(): flat = flat + lax.ppermute(flat, axis, [(s, s ^ 1) for s in range(count)])]
    ppermute x9, waiting for transfers between devices: 66.6 us -> 51.5 us  [moved(): return lax.ppermute(value, axis, pairs)]
    ppermute x9, starting transfers between devices: 20.3 us -> 12.2 us  [moved(): return lax.ppermute(value, axis, pairs)]
    ppermute x2, waiting for transfers between devices: 3.49 us -> 9.44 us  [band_sum(): got = lax.ppermute(flat, axis, pairs)]
    ppermute x2, starting transfers between devices: 4.65 us -> 1.63 us  [band_sum(): got = lax.ppermute(flat, axis, pairs)]
  transfers between devices with their start and end apart: 14 -> 14, of which waited for: 8 -> 9; matrix products, arithmetic and copies ran while one was open for 22% -> 21% of each run, Pallas kernels for 0% -> 0%
where the time goes in v10:
time: 177 us; the launch traced here: 175 us
  waiting for transfers between devices  113 us (64%)
  matrix products  23 us (13%)
  starting transfers between devices  19.5 us (11%)
  other arithmetic  18.9 us (11%)
    ppermute x9, waiting for transfers between devices, moved(): return lax.ppermute(value, axis, pairs)  51.5 us
    ppermute x1, waiting for transfers between devices, band_sum(): flat = flat + lax.ppermute(flat, axis, [(s, s ^ 1) for s in range(count)])  42 us
    ppermute x9, starting transfers between devices, moved(): return lax.ppermute(value, axis, pairs)  12.2 us
    dot_general x5, matrix products, cross_block(): jnp.einsum('pfwa,pfwb->fab', own_block, partner, preferred_element_type=j...  11.7 us
    dot_general x5, matrix products, cross_block(): jnp.einsum('pfwa,pfwb->fab', own_block, flipped, preferred_element_type=j...  11.3 us
    ppermute x2, waiting for transfers between devices, band_sum(): got = lax.ppermute(jnp.where(bit == 0, high, low), axis, pairs)  9.59 us
    ppermute x2, waiting for transfers between devices, band_sum(): got = lax.ppermute(flat, axis, pairs)  9.44 us
    convert_element_type x2, other arithmetic, whiten(): return (raw.astype(jnp.float32) * gain).astype(jnp.bfloat16)  6.1 us
  transfers between devices with their start and end apart: 14, of which 9 were waited for; matrix products, arithmetic and copies ran while one was open for 21% of the time, Pallas kernels for 0%

profile of v10, /device:TPU:4, one launch (start us, length us, event | category | flops | bytes accessed | tf_op | source)
XLA Modules:
  0.0 174.8 jit_solution(14600760948100027139)
XLA Ops:
  0.0 3.1 %fusion = f32[512,256]{1,0:T(8,128)S(1)} fusion(bf16[2,8,512,256]{3,2,1,0:T(8,128)(2,1)} %param.2), kind=kLoop, calls=%fused_computation.2 | loop fusion | flops 6160384 | bytes 4718592 | tf_op jit(solution)/shard_map/reduce_sum | solution.py:58
  3.3 3.3 %collective-permute-start.1 = (f32[65536]{0:T(1024)S(1)}, f32[65536]{0:T(1024)S(1)}, u32[]{:S(2)}, u32[]{:S(2)}) collective-permute-start(f32[65536]{0:T(1024)S(1)} %bitcast.71), channel_id=1, source_target_pairs={{0,128},{32,160},{64,192},{96,224},{128,0},{160,32},{192,64},{224,... | collective-permute-start | bytes 786440 | tf_op jit(solution)/shard_map/ppermute | solution.py:34
  6.7 6.2 %collective-permute-done.1 = f32[65536]{0:T(1024)S(1)} collective-permute-done((f32[65536]{0:T(1024)S(1)}, f32[65536]{0:T(1024)S(1)}, u32[]{:S(2)}, u32[]{:S(2)}) %collective-permute-start.1) | collective-permute-done | bytes 262176 | tf_op jit(solution)/shard_map/ppermute | solution.py:34
  13.0 1.7 collective-permute-start.2
  14.6 3.4 %collective-permute-done.2 = f32[32768]{0:T(1024)S(1)} collective-permute-done((f32[32768]{0:T(1024)S(1)}, f32[32768]{0:T(1024)S(1)}, u32[]{:S(2)}, u32[]{:S(2)}) %collective-permute-start.2) | collective-permute-done | bytes 131104 | tf_op jit(solution)/shard_map/ppermute | solution.py:34
  18.7 42.0 %collective-permute-done.3 = f32[32768]{0:T(1024)S(1)} collective-permute-done((f32[32768]{0:T(1024)S(1)}, f32[32768]{0:T(1024)S(1)}, u32[]{:S(2)}, u32[]{:S(2)}) %collective-permute-start.3) | collective-permute-done | bytes 131104 | tf_op jit(solution)/shard_map/ppermute | solution.py:37
  61.5 1.9 %collective-permute-start = (bf16[8192,256]{1,0:T(8,128)(2,1)}, bf16[8192,256]{1,0:T(8,128)(2,1)}, u32[]{:S(2)}, u32[]{:S(2)}) collective-permute-start(bf16[8192,256]{1,0:T(8,128)(2,1)} %bitcast.66), channel_id=1, source_target_pairs={{0,30},{2,0},{4,2},{6,4},{8,6},{10,8},{12,10},{14,12},{16,14},{18,... | collective-permute-start | bytes 12582920 | tf_op jit(solution)/shard_map/ppermute | solution.py:16
  63.4 2.8 %collective-permute-done.4 = f32[32768]{0:T(1024)S(1)} collective-permute-done((f32[32768]{0:T(1024)S(1)}, f32[32768]{0:T(1024)S(1)}, u32[]{:S(2)}, u32[]{:S(2)}) %collective-permute-start.4) | collective-permute-done | bytes 131104 | tf_op jit(solution)/shard_map/ppermute | solution.py:40
  68.6 6.6 %collective-permute-done.5 = f32[65536]{0:T(1024)S(1)} collective-permute-done((f32[65536]{0:T(1024)S(1)}, f32[65536]{0:T(1024)S(1)}, u32[]{:S(2)}, u32[]{:S(2)}) %collective-permute-start.5) | collective-permute-done | bytes 262176 | tf_op jit(solution)/shard_map/ppermute | solution.py:40
  75.5 1.9 %collective-permute-start.6 = (f32[512,256]{1,0:T(8,128)S(1)}, f32[512,256]{1,0:T(8,128)S(1)}, u32[]{:S(2)}, u32[]{:S(2)}) collective-permute-start(f32[512,256]{1,0:T(8,128)S(1)} %fusion.52), channel_id=1, source_target_pairs={{0,30},{2,0},{4,2},{6,4},{8,6},{10,8},{12,10},{14,12},{16,14},{18,... | collective-permute-start | bytes 1572872 | tf_op jit(solution)/shard_map/ppermute | solution.py:16
  77.5 3.0 %fusion.1 = bf16[2,8,512,256]{3,2,0,1:T(8,128)(2,1)S(1)} fusion(f32[512,256]{1,0:T(8,128)S(1)} %fusion.52, bf16[2,8,512,256]{3,2,1,0:T(8,128)(2,1)} %param.2), kind=kLoop, calls=%fused_computation.3 | loop fusion | flops 6291456 | bytes 8912896 | tf_op jit(solution)/shard_map/convert_element_type | solution.py:53
  80.5 1.4 convolution_bitcast_fusion.4
  81.9 6.2 %collective-permute-done.8 = f32[512,256]{1,0:T(8,128)S(1)} collective-permute-done((f32[512,256]{1,0:T(8,128)S(1)}, f32[512,256]{1,0:T(8,128)S(1)}, u32[]{:S(2)}, u32[]{:S(2)}) %collective-permute-start.8) | collective-permute-done | bytes 524320 | tf_op jit(solution)/shard_map/ppermute | solution.py:16
  88.2 1.3 collective-permute-start.12
  89.5 3.1 %fusion.4 = bf16[2,8,512,256]{3,2,0,1:T(8,128)(2,1)S(1)} fusion(f32[512,256]{1,0:T(8,128)S(1)} %collective-permute-done.8, bf16[2,8,512,256]{3,2,1,0:T(8,128)(2,1)} %bitcast.34), kind=kLoop, calls=%fused_computation.10 | loop fusion | flops 6291456 | bytes 8912896 | tf_op jit(solution)/shard_map/convert_element_type | solution.py:53
  92.5 2.2 %collective-permute-start.9 = (bf16[2,8,512,256]{3,2,0,1:T(8,128)(2,1)S(1)}, bf16[2,8,512,256]{3,2,0,1:T(8,128)(2,1)S(1)}, u32[]{:S(2)}, u32[]{:S(2)}) collective-permute-start(bf16[2,8,512,256]{3,2,0,1:T(8,128)(2,1)S(1)} %fusion.4), channel_id=1, source_target_pairs={{0,1},{1,2},{2,3},{3,4},{4,5},{5,6},{6,7},{7,8},{8,9},{9,10},{10,1... | collective-permute-start | bytes 12582920 | tf_op jit(solution)/shard_map/ppermute | solution.py:16
  95.0 1.5 fusion.26
  97.3 20.4 %collective-permute-done.6 = f32[512,256]{1,0:T(8,128)S(1)} collective-permute-done((f32[512,256]{1,0:T(8,128)S(1)}, f32[512,256]{1,0:T(8,128)S(1)}, u32[]{:S(2)}, u32[]{:S(2)}) %collective-permute-start.6) | collective-permute-done | bytes 524320 | tf_op jit(solution)/shard_map/ppermute | solution.py:16
  117.7 3.4 %fusion.34 = f32[1,8,256,256]{3,2,1,0:T(8,128)S(1)} fusion(bf16[2,8,512,256]{3,2,1,0:T(8,128)(2,1)} %bitcast.33, f32[512,256]{1,0:T(8,128)S(1)} %collective-permute-done.6, bf16[1,8,512,256]{3,2,0,1:T(8,128)(2,1)S(1)} %get-tuple-element.20, bf16[1,8,512,256]{3,2,0,1:T(8,128)(2,1)S(1)} %get-tuple-element.19), kind=kOutput, calls=%fused_computation.46 | convolution fusion | flops 1082130432 | bytes 11010048 | tf_op jit(solution)/shard_map/pfwa,pfwb->fab/dot_general | solution.py:48
  121.1 3.7 %fusion.29 = f32[1,8,256,256]{3,2,1,0:T(8,128)S(1)} fusion(bf16[2,8,512,256]{3,2,0,1:T(8,128)(2,1)S(1)} %fusion.4, bf16[2,8,512,256]{3,2,1,0:T(8,128)(2,1)} %bitcast.33, f32[512,256]{1,0:T(8,128)S(1)} %collective-permute-done.6), kind=kOutput, calls=%fused_computation.45 | convolution fusion | flops 1080033280 | bytes 11010048 | tf_op jit(solution)/shard_map/pfwa,pfwb->fab/dot_general | solution.py:47
  125.4 1.5 convolution_bitcast_fusion.2
  126.9 1.4 convolution_bitcast_fusion.3
  128.9 13.9 %collective-permute-done.9 = bf16[2,8,512,256]{3,2,0,1:T(8,128)(2,1)S(1)} collective-permute-done((bf16[2,8,512,256]{3,2,0,1:T(8,128)(2,1)S(1)}, bf16[2,8,512,256]{3,2,0,1:T(8,128)(2,1)S(1)}, u32[]{:S(2)}, u32[]{:S(2)}) %collective-permute-start.9) | collective-permute-done | bytes 4194336 | tf_op jit(solution)/shard_map/ppermute | solution.py:16
  142.8 2.1 %collective-permute-start.10 = (bf16[2,8,256,256]{3,2,1,0:T(8,128)(2,1)S(1)}, bf16[2,8,256,256]{3,2,1,0:T(8,128)(2,1)S(1)}, u32[]{:S(2)}, u32[]{:S(2)}) collective-permute-start(bf16[2,8,256,256]{3,2,1,0:T(8,128)(2,1)S(1)} %fusion.5), channel_id=1, source_target_pairs={{0,2},{2,4},{4,6},{6,8},{8,10},{10,12},{12,14},{14,16},{16,18},{18... | collective-permute-start | bytes 6291464 | tf_op jit(solution)/shard_map/ppermute | solution.py:16
  145.3 3.8 %fusion.39 = f32[1,8,256,256]{3,2,1,0:T(8,128)S(1)} fusion(bf16[2,8,512,256]{3,2,0,1:T(8,128)(2,1)S(1)} %collective-permute-done.9, bf16[2,8,512,256]{3,2,1,0:T(8,128)(2,1)} %bitcast.37, f32[512,256]{1,0:T(8,128)} %collective-permute-done.12), kind=kOutput, calls=%fused_computation.47 | convolution fusion | flops 1080033280 | bytes 11010048 | tf_op jit(solution)/shard_map/pfwa,pfwb->fab/dot_general | solution.py:47
  149.1 3.5 %fusion.44 = f32[1,8,256,256]{3,2,1,0:T(8,128)S(1)} fusion(bf16[2,8,512,256]{3,2,1,0:T(8,128)(2,1)} %bitcast.37, f32[512,256]{1,0:T(8,128)} %collective-permute-done.12, bf16[1,8,512,256]{3,2,0,1:T(8,128)(2,1)S(1)} %get-tuple-element.16, bf16[1,8,512,256]{3,2,0,1:T(8,128)(2,1)S(1)} %get-tuple-element.15), kind=kOutput, calls=%fused_computation.48 | convolution fusion | flops 1082130432 | bytes 11010048 | tf_op jit(solution)/shard_map/pfwa,pfwb->fab/dot_general | solution.py:48
  153.1 1.4 collective-permute-start.13
  154.6 1.5 convolution_bitcast_fusion
  156.0 1.4 convolution_bitcast_fusion.1
  158.1 3.9 %maximum_maximum_fusion = bf16[4,2,8,256,256]{4,3,2,1,0:T(8,128)(2,1)} fusion(bf16[1,2,8,256,256]{4,3,2,1,0:T(8,128)(2,1)S(1)} %fusion.12, bf16[1,2,8,256,256]{4,3,2,1,0:T(8,128)(2,1)S(1)} %bitcast.69, bf16[1,2,8,256,256]{4,3,2,1,0:T(8,128)(2,1)S(1)} %bitcast.68, bf16[4]{0:T(256)(128)(2,1)S(1)} %pad.5.clone), kind=kLoop, calls=%fused_computation.4 | loop fusion | flops 12582912 | bytes 14680072 | tf_op jit(solution)/shard_map/stack | solution.py:84
  161.9 10.9 %collective-permute-done.10 = bf16[2,8,256,256]{3,2,1,0:T(8,128)(2,1)S(1)} collective-permute-done((bf16[2,8,256,256]{3,2,1,0:T(8,128)(2,1)S(1)}, bf16[2,8,256,256]{3,2,1,0:T(8,128)(2,1)S(1)}, u32[]{:S(2)}, u32[]{:S(2)}) %collective-permute-start.10) | collective-permute-done | bytes 2097184 | tf_op jit(solution)/shard_map/ppermute | solution.py:16
  172.9 2.0 %bitcast_dynamic-update-slice_fusion = bf16[4,2,8,256,256]{4,3,2,1,0:T(8,128)(2,1)} fusion(bf16[4,2,8,256,256]{4,3,2,1,0:T(8,128)(2,1)} %maximum_maximum_fusion, bf16[2,8,256,256]{3,2,1,0:T(8,128)(2,1)S(1)} %collective-permute-done.10, bf16[2,8,256,256]{3,2,1,0:T(8,128)(2,1)S(1)} %collective-permute-done.13, pred[]{:T(512)S(6)} %eq.19), kind=kLoop, calls=%fused_computation.37 | loop fusion | flops 1048576 | bytes 6291457 | tf_op jit(solution)/shard_map/dynamic_update_slice | solution.py:87
  (35 shorter events, 8.0 us)
Async XLA Ops:
  3.1 72.3 %copy-start = (s32[512,256]{1,0:T(8,128)S(1)}, s32[512,256]{1,0:T(8,128)}, u32[]{:S(2)}) copy-start(s32[512,256]{1,0:T(8,128)} %param.3) | copy-start | bytes 1572868
  3.3 9.6 %collective-permute-start.1 = (f32[65536]{0:T(1024)S(1)}, f32[65536]{0:T(1024)S(1)}, u32[]{:S(2)}, u32[]{:S(2)}) collective-permute-start(f32[65536]{0:T(1024)S(1)} %bitcast.71), channel_id=1, source_target_pairs={{0,128},{32,160},{64,192},{96,224},{128,0},{160,32},{192,64},{224,... | collective-permute-start | bytes 786440 | tf_op jit(solution)/shard_map/ppermute | solution.py:34
  6.6 82.9 %collective-permute-start.7 = (bf16[8192,256]{1,0:T(8,128)(2,1)}, bf16[8192,256]{1,0:T(8,128)(2,1)}, u32[]{:S(2)}, u32[]{:S(2)}) collective-permute-start(bf16[8192,256]{1,0:T(8,128)(2,1)} %bitcast.65), channel_id=1, source_target_pairs={{0,1},{1,2},{2,3},{3,4},{4,5},{5,6},{6,7},{7,8},{8,9},{9,10},{10,1... | collective-permute-start | bytes 12582920 | tf_op jit(solution)/shard_map/ppermute | solution.py:16
  13.0 5.1 %collective-permute-start.2 = (f32[32768]{0:T(1024)S(1)}, f32[32768]{0:T(1024)S(1)}, u32[]{:S(2)}, u32[]{:S(2)}) collective-permute-start(f32[32768]{0:T(1024)S(1)} %slice_select_fusion), channel_id=1, source_target_pairs={{0,64},{32,96},{64,0},{96,32},{128,192},{160,224},{192,128},{224,1... | collective-permute-start | bytes 393224 | tf_op jit(solution)/shard_map/ppermute | solution.py:34
  18.0 42.7 %collective-permute-start.3 = (f32[32768]{0:T(1024)S(1)}, f32[32768]{0:T(1024)S(1)}, u32[]{:S(2)}, u32[]{:S(2)}) collective-permute-start(f32[32768]{0:T(1024)S(1)} %select_add_fusion), channel_id=1, source_target_pairs={{0,32},{32,0},{64,96},{96,64},{128,160},{160,128},{192,224},{224,1... | collective-permute-start | bytes 393224 | tf_op jit(solution)/shard_map/ppermute | solution.py:37
  60.7 5.5 %collective-permute-start.4 = (f32[32768]{0:T(1024)S(1)}, f32[32768]{0:T(1024)S(1)}, u32[]{:S(2)}, u32[]{:S(2)}) collective-permute-start(f32[32768]{0:T(1024)S(1)} %add.31), channel_id=1, source_target_pairs={{0,64},{32,96},{64,0},{96,32},{128,192},{160,224},{192,128},{224,1... | collective-permute-start | bytes 393224 | tf_op jit(solution)/shard_map/ppermute | solution.py:40
  61.5 56.2 %collective-permute-start = (bf16[8192,256]{1,0:T(8,128)(2,1)}, bf16[8192,256]{1,0:T(8,128)(2,1)}, u32[]{:S(2)}, u32[]{:S(2)}) collective-permute-start(bf16[8192,256]{1,0:T(8,128)(2,1)} %bitcast.66), channel_id=1, source_target_pairs={{0,30},{2,0},{4,2},{6,4},{8,6},{10,8},{12,10},{14,12},{16,14},{18,... | collective-permute-start | bytes 12582920 | tf_op jit(solution)/shard_map/ppermute | solution.py:16
  66.3 9.0 %collective-permute-start.5 = (f32[65536]{0:T(1024)S(1)}, f32[65536]{0:T(1024)S(1)}, u32[]{:S(2)}, u32[]{:S(2)}) collective-permute-start(f32[65536]{0:T(1024)S(1)} %maximum_select_fusion.2), channel_id=1, source_target_pairs={{0,128},{32,160},{64,192},{96,224},{128,0},{160,32},{192,64},{224,... | collective-permute-start | bytes 786440 | tf_op jit(solution)/shard_map/ppermute | solution.py:40
  67.1 78.1 %collective-permute-start.11 = (bf16[8192,256]{1,0:T(8,128)(2,1)}, bf16[8192,256]{1,0:T(8,128)(2,1)}, u32[]{:S(2)}, u32[]{:S(2)}) collective-permute-start(bf16[8192,256]{1,0:T(8,128)(2,1)} %bitcast.67), channel_id=1, source_target_pairs={{1,0},{3,2},{5,4},{7,6},{9,8},{11,10},{13,12},{15,14},{17,16},{19,... | collective-permute-start | bytes 12582920 | tf_op jit(solution)/shard_map/ppermute | solution.py:16
  75.5 42.3 %collective-permute-start.6 = (f32[512,256]{1,0:T(8,128)S(1)}, f32[512,256]{1,0:T(8,128)S(1)}, u32[]{:S(2)}, u32[]{:S(2)}) collective-permute-start(f32[512,256]{1,0:T(8,128)S(1)} %fusion.52), channel_id=1, source_target_pairs={{0,30},{2,0},{4,2},{6,4},{8,6},{10,8},{12,10},{14,12},{16,14},{18,... | collective-permute-start | bytes 1572872 | tf_op jit(solution)/shard_map/ppermute | solution.py:16
  77.4 10.8 %collective-permute-start.8 = (f32[512,256]{1,0:T(8,128)S(1)}, f32[512,256]{1,0:T(8,128)S(1)}, u32[]{:S(2)}, u32[]{:S(2)}) collective-permute-start(f32[512,256]{1,0:T(8,128)S(1)} %fusion.52), channel_id=1, source_target_pairs={{0,1},{1,2},{2,3},{3,4},{4,5},{5,6},{6,7},{7,8},{8,9},{9,10},{10,1... | collective-permute-start | bytes 1572872 | tf_op jit(solution)/shard_map/ppermute | solution.py:16
  88.2 57.1 %collective-permute-start.12 = (f32[512,256]{1,0:T(8,128)S(1)}, f32[512,256]{1,0:T(8,128)}, u32[]{:S(2)}, u32[]{:S(2)}) collective-permute-start(f32[512,256]{1,0:T(8,128)S(1)} %fusion.52), channel_id=1, source_target_pairs={{1,0},{3,2},{5,4},{7,6},{9,8},{11,10},{13,12},{15,14},{17,16},{19,... | collective-permute-start | bytes 1572872 | tf_op jit(solution)/shard_map/ppermute | solution.py:16
  92.5 50.3 %collective-permute-start.9 = (bf16[2,8,512,256]{3,2,0,1:T(8,128)(2,1)S(1)}, bf16[2,8,512,256]{3,2,0,1:T(8,128)(2,1)S(1)}, u32[]{:S(2)}, u32[]{:S(2)}) collective-permute-start(bf16[2,8,512,256]{3,2,0,1:T(8,128)(2,1)S(1)} %fusion.4), channel_id=1, source_target_pairs={{0,1},{1,2},{2,3},{3,4},{4,5},{5,6},{6,7},{7,8},{8,9},{9,10},{10,1... | collective-permute-start | bytes 12582920 | tf_op jit(solution)/shard_map/ppermute | solution.py:16
  142.8 30.0 %collective-permute-start.10 = (bf16[2,8,256,256]{3,2,1,0:T(8,128)(2,1)S(1)}, bf16[2,8,256,256]{3,2,1,0:T(8,128)(2,1)S(1)}, u32[]{:S(2)}, u32[]{:S(2)}) collective-permute-start(bf16[2,8,256,256]{3,2,1,0:T(8,128)(2,1)S(1)} %fusion.5), channel_id=1, source_target_pairs={{0,2},{2,4},{4,6},{6,8},{8,10},{10,12},{12,14},{14,16},{16,18},{18... | collective-permute-start | bytes 6291464 | tf_op jit(solution)/shard_map/ppermute | solution.py:16
  153.1 19.7 %collective-permute-start.13 = (bf16[2,8,256,256]{3,2,1,0:T(8,128)(2,1)S(1)}, bf16[2,8,256,256]{3,2,1,0:T(8,128)(2,1)S(1)}, u32[]{:S(2)}, u32[]{:S(2)}) collective-permute-start(bf16[2,8,256,256]{3,2,1,0:T(8,128)(2,1)S(1)} %fusion.13), channel_id=1, source_target_pairs={{0,1},{2,3},{4,5},{6,7},{8,9},{10,11},{12,13},{14,15},{16,17},{18,... | collective-permute-start | bytes 6291464 | tf_op jit(solution)/shard_map/ppermute | solution.py:16

commit v11 on v5

--- a/solution.py
+++ b/solution.py
@@ -9,9 +9,10 @@
 eps_energy = 1e-06
 
 
-def moved(value, axis, offset, only_even=False):
+def moved(value, axis, offset, only_even=False, only_odd=False):
     count = lax.axis_size(axis)
-    pairs = [(source, (source + offset) % count) for source in range(count) if not only_even or source % 2 == 0]
+    pairs = [(source, (source + offset) % count) for source in range(count)
+             if not (only_even and source % 2) and not (only_odd and source % 2 == 0)]
     return lax.ppermute(value, axis, pairs)
 
 
@@ -59,25 +60,28 @@
     even = lax.axis_index("chan") % 2 == 0
     partial_energy = partial_energy + lax.ppermute(partial_energy, "band", [(s, s ^ 1) for s in range(lax.axis_size("band"))])
     spectra, partial_energy = lax.optimization_barrier((spectra, partial_energy))
-    raw_near = moved(spectra, "chan", 1)
-    raw_ahead = moved(spectra, "chan", -2, only_even=True)
+    flat_spectra = spectra.reshape(-1, spectra.shape[-1])
+    raw_near = moved(flat_spectra, "chan", 1).reshape(spectra.shape)
+    raw_ahead = moved(flat_spectra, "chan", -2, only_even=True).reshape(spectra.shape)
+    raw_odd_ahead = moved(flat_spectra, "chan", -3, only_odd=True).reshape(spectra.shape)
     energy = band_sum(partial_energy, "band")
     window_gain = valid_mask.astype(jnp.float32) / jnp.sqrt(energy / total_bins + eps_energy)
     gain_near = moved(window_gain, "chan", 1)
     gain_ahead = moved(window_gain, "chan", -2, only_even=True)
+    gain_odd_ahead = moved(window_gain, "chan", -3, only_odd=True)
     whitened = whiten(spectra, window_gain)
     near = whiten(raw_near, gain_near)
     ahead = whiten(raw_ahead, gain_ahead)
-    second = moved(near, "chan", 1)
-    for_above = cross_block(ahead, near, scale)
-    for_above, second = lax.optimization_barrier((for_above, second))
-    third = moved(second, "chan", 1, only_even=True)
-    from_below = moved(for_above, "chan", 2, only_even=True)
+    odd_ahead = whiten(raw_odd_ahead, gain_odd_ahead)
+    lag2_above = moved(cross_block(ahead, whitened, scale), "chan", 2, only_even=True)
+    lag3_above = moved(cross_block(ahead, near, scale), "chan", 2, only_even=True)
+    lag3_mate = moved(cross_block(odd_ahead, whitened, scale), "chan", 3, only_even=True)
+    second = moved(near, "chan", 1, only_even=True)
     outputs = [
         cross_block(whitened, whitened, scale),
         cross_block(whitened, near, scale),
-        cross_block(whitened, second, scale),
-        jnp.where(even, from_below, cross_block(whitened, third, scale)),
+        jnp.where(even, lag2_above, cross_block(whitened, second, scale)),
+        jnp.where(even, lag3_above, lag3_mate),
     ]
     return jnp.stack(outputs)
 

time: 184 us -> 218 us (1.18); the launches traced: 184 us -> 214 us
  starting transfers between devices: 28.5 us -> 52.5 us
  matrix products: 24.3 us -> 34.2 us
  local copies, waits for them, and re-layouts: 5 us -> 1.78 us
    ppermute x7 -> x10, starting transfers between devices: 16.9 us -> 40.3 us  [moved(): return lax.ppermute(value, axis, pairs)]
    dot_general x5 -> x6, matrix products: 9.32 us -> 18.9 us  [cross_block(): jnp.einsum('pfwa,pfwb->fab', own_block, flipped, preferred_element_type=j...]
    ppermute x2, waiting for transfers between devices: 4.86 us -> 0.01 us  [band_sum(): got = lax.ppermute(flat, axis, pairs)]
    slice x4 -> x3, other arithmetic: 5.55 us -> 0.82 us  [cross_block(): flipped = jnp.stack([partner[1], -partner[0]])]
    optimization_barrier x1 -> x0, local copies, waits for them, and re-layouts: 4.57 us -> none  [shards(): lax.optimization_barrier((spectra, partial_energy))]
    ppermute x7 -> x10, waiting for transfers between devices: 79 us -> 82.7 us  [moved(): return lax.ppermute(value, axis, pairs)]
    another operation x2 -> x3, other arithmetic: 4.6 us -> 7.9 us  [shards(): return jnp.stack(outputs)]
    ppermute x2, waiting for transfers between devices: 5.24 us -> 7.45 us  [band_sum(): got = lax.ppermute(jnp.where(bit == 0, high, low), axis, pairs)]
  transfers between devices with their start and end apart: 12 -> 15, of which waited for: 8 -> 6; matrix products, arithmetic and copies ran while one was open for 25% -> 22% of each run, Pallas kernels for 0% -> 0%
where the time goes in v11:
time: 218 us; the launch traced here: 214 us
  waiting for transfers between devices  103 us (47%)
  starting transfers between devices  52.5 us (24%)
  matrix products  34.2 us (16%)
  other arithmetic  22.4 us (10%)
    ppermute x10, waiting for transfers between devices, moved(): return lax.ppermute(value, axis, pairs)  82.7 us
    ppermute x10, starting transfers between devices, moved(): return lax.ppermute(value, axis, pairs)  40.3 us
    dot_general x6, matrix products, cross_block(): jnp.einsum('pfwa,pfwb->fab', own_block, flipped, preferred_element_type=j...  18.9 us
    dot_general x6, matrix products, cross_block(): jnp.einsum('pfwa,pfwb->fab', own_block, partner, preferred_element_type=j...  15.3 us
    ppermute x1, waiting for transfers between devices, shards(): lax.ppermute(partial_energy, 'band', [(s, s ^ 1) for s in range(lax.axis_...  12.9 us
    another operation x3, other arithmetic, shards(): return jnp.stack(outputs)  7.9 us
    ppermute x2, waiting for transfers between devices, band_sum(): got = lax.ppermute(jnp.where(bit == 0, high, low), axis, pairs)  7.45 us
    convert_element_type x2, other arithmetic, whiten(): return (raw.astype(jnp.float32) * gain).astype(jnp.bfloat16)  6.08 us
  transfers between devices with their start and end apart: 15, of which 6 were waited for; matrix products, arithmetic and copies ran while one was open for 22% of the time, Pallas kernels for 0%

profile of v11, /device:TPU:4, one launch (start us, length us, event | category | flops | bytes accessed | tf_op | source)
XLA Modules:
  0.0 214.5 jit_solution(16215908648042695113)
XLA Ops:
  0.0 3.1 %multiply_reduce_fusion = f32[512,256]{1,0:T(8,128)S(1)} fusion(bf16[2,8,512,256]{3,2,1,0:T(8,128)(2,1)} %param.2), kind=kLoop, calls=%fused_computation.8 | loop fusion | flops 6160384 | bytes 4718592 | tf_op jit(solution)/shard_map/reduce_sum | solution.py:57
  3.1 2.3 %collective-permute-start = (f32[512,256]{1,0:T(8,128)S(1)}, f32[512,256]{1,0:T(8,128)S(1)}, u32[]{:S(2)}, u32[]{:S(2)}) collective-permute-start(f32[512,256]{1,0:T(8,128)S(1)} %multiply_reduce_fusion), channel_id=1, source_target_pairs={{0,32},{32,0},{64,96},{96,64},{128,160},{160,128},{192,224},{224,1... | collective-permute-start | bytes 1572872 | tf_op jit(solution)/shard_map/ppermute | solution.py:61
  5.4 12.9 %collective-permute-done = f32[512,256]{1,0:T(8,128)S(1)} collective-permute-done((f32[512,256]{1,0:T(8,128)S(1)}, f32[512,256]{1,0:T(8,128)S(1)}, u32[]{:S(2)}, u32[]{:S(2)}) %collective-permute-start) | collective-permute-done | bytes 524320 | tf_op jit(solution)/shard_map/ppermute | solution.py:61
  18.6 3.3 %collective-permute-start.1 = (f32[65536]{0:T(1024)S(1)}, f32[65536]{0:T(1024)S(1)}, u32[]{:S(2)}, u32[]{:S(2)}) collective-permute-start(f32[65536]{0:T(1024)S(1)} %bitcast.76), channel_id=1, source_target_pairs={{0,128},{32,160},{64,192},{96,224},{128,0},{160,32},{192,64},{224,... | collective-permute-start | bytes 786440 | tf_op jit(solution)/shard_map/ppermute | solution.py:34
  22.0 5.3 %collective-permute-done.1 = f32[65536]{0:T(1024)S(1)} collective-permute-done((f32[65536]{0:T(1024)S(1)}, f32[65536]{0:T(1024)S(1)}, u32[]{:S(2)}, u32[]{:S(2)}) %collective-permute-start.1) | collective-permute-done | bytes 262176 | tf_op jit(solution)/shard_map/ppermute | solution.py:34
  27.4 1.7 collective-permute-start.2
  30.4 2.1 collective-permute-done.2
  34.2 5.7 %collective-permute-start.5 = (bf16[8192,256]{1,0:T(8,128)(2,1)}, bf16[8192,256]{1,0:T(8,128)(2,1)}, u32[]{:S(2)}, u32[]{:S(2)}) collective-permute-start(bf16[8192,256]{1,0:T(8,128)(2,1)} %bitcast.73), channel_id=1, source_target_pairs={{0,1},{1,2},{2,3},{3,4},{4,5},{5,6},{6,7},{7,8},{8,9},{9,10},{10,1... | collective-permute-start | bytes 12582920 | tf_op jit(solution)/shard_map/ppermute | solution.py:16
  39.9 3.3 %collective-permute-start.4 = (f32[65536]{0:T(1024)S(1)}, f32[65536]{0:T(1024)S(1)}, u32[]{:S(2)}, u32[]{:S(2)}) collective-permute-start(f32[65536]{0:T(1024)S(1)} %maximum_select_fusion.2), channel_id=1, source_target_pairs={{0,128},{32,160},{64,192},{96,224},{128,0},{160,32},{192,64},{224,... | collective-permute-start | bytes 786440 | tf_op jit(solution)/shard_map/ppermute | solution.py:39
  43.2 7.2 %collective-permute-start.7 = (bf16[8192,256]{1,0:T(8,128)(2,1)}, bf16[8192,256]{1,0:T(8,128)(2,1)}, u32[]{:S(2)}, u32[]{:S(2)}) collective-permute-start(bf16[8192,256]{1,0:T(8,128)(2,1)} %bitcast.74), channel_id=1, source_target_pairs={{0,30},{2,0},{4,2},{6,4},{8,6},{10,8},{12,10},{14,12},{16,14},{18,... | collective-permute-start | bytes 12582920 | tf_op jit(solution)/shard_map/ppermute | solution.py:16
  52.0 6.9 %collective-permute-start.8 = (f32[512,256]{1,0:T(8,128)S(1)}, f32[512,256]{1,0:T(8,128)S(1)}, u32[]{:S(2)}, u32[]{:S(2)}) collective-permute-start(f32[512,256]{1,0:T(8,128)S(1)} %fusion.69), channel_id=1, source_target_pairs={{0,30},{2,0},{4,2},{6,4},{8,6},{10,8},{12,10},{14,12},{16,14},{18,... | collective-permute-start | bytes 1572872 | tf_op jit(solution)/shard_map/ppermute | solution.py:16
  58.9 3.0 %multiply_convert_fusion = bf16[2,8,512,256]{3,2,0,1:T(8,128)(2,1)S(1)} fusion(bf16[2,8,512,256]{3,2,1,0:T(8,128)(2,1)} %param.2, f32[512,256]{1,0:T(8,128)S(1)} %fusion.69), kind=kLoop, calls=%fused_computation.7 | loop fusion | flops 6291456 | bytes 8912896 | tf_op jit(solution)/shard_map/convert_element_type | solution.py:52
  65.7 54.9 %collective-permute-done.13 = f32[512,256]{1,0:T(8,128)S(1)} collective-permute-done((f32[512,256]{1,0:T(8,128)S(1)}, f32[512,256]{1,0:T(8,128)S(1)}, u32[]{:S(2)}, u32[]{:S(2)}) %collective-permute-start.13) | collective-permute-done | bytes 524320 | tf_op jit(solution)/shard_map/ppermute | solution.py:16
  120.5 5.3 %collective-permute-start.6 = (f32[512,256]{1,0:T(8,128)S(1)}, f32[512,256]{1,0:T(8,128)S(1)}, u32[]{:S(2)}, u32[]{:S(2)}) collective-permute-start(f32[512,256]{1,0:T(8,128)S(1)} %fusion.69), channel_id=1, source_target_pairs={{0,1},{1,2},{2,3},{3,4},{4,5},{5,6},{6,7},{7,8},{8,9},{9,10},{10,1... | collective-permute-start | bytes 1572872 | tf_op jit(solution)/shard_map/ppermute | solution.py:16
  125.9 3.7 %fusion.41 = f32[1,8,256,256]{3,2,1,0:T(8,128)S(1)} fusion(bf16[2,8,512,256]{3,2,0,1:T(8,128)(2,1)S(1)} %multiply_convert_fusion, bf16[2,8,512,256]{3,2,1,0:T(8,128)(2,1)} %bitcast.42, f32[512,256]{1,0:T(8,128)S(1)} %collective-permute-done.13), kind=kOutput, calls=%fused_computation.52 | convolution fusion | flops 1080033280 | bytes 11010048 | tf_op jit(solution)/shard_map/pfwa,pfwb->fab/dot_general | solution.py:46
  129.6 3.4 %fusion.51 = f32[1,8,256,256]{3,2,1,0:T(8,128)S(1)} fusion(bf16[2,8,512,256]{3,2,1,0:T(8,128)(2,1)} %bitcast.42, f32[512,256]{1,0:T(8,128)S(1)} %collective-permute-done.13, bf16[1,8,512,256]{3,2,0,1:T(8,128)(2,1)S(1)} %get-tuple-element.12, bf16[1,8,512,256]{3,2,0,1:T(8,128)(2,1)S(1)} %get-tuple-element.11), kind=kOutput, calls=%fused_computation.54 | convolution fusion | flops 1082130432 | bytes 11010048 | tf_op jit(solution)/shard_map/pfwa,pfwb->fab/dot_general | solution.py:47
  133.6 1.7 collective-permute-start.14
  135.3 3.0 %fusion.2 = bf16[2,8,512,256]{3,2,0,1:T(8,128)(2,1)S(1)} fusion(f32[512,256]{1,0:T(8,128)S(1)} %collective-permute-done.6, bf16[2,8,512,256]{3,2,1,0:T(8,128)(2,1)} %bitcast.38), kind=kLoop, calls=%fused_computation.6 | loop fusion | flops 6291456 | bytes 8912896 | tf_op jit(solution)/shard_map/convert_element_type | solution.py:52
  138.4 1.7 collective-permute-start.10
  141.8 3.6 %fusion.61 = f32[1,8,256,256]{3,2,1,0:T(8,128)S(1)} fusion(bf16[2,8,512,256]{3,2,1,0:T(8,128)(2,1)} %bitcast.41, f32[512,256]{1,0:T(8,128)S(1)} %collective-permute-done.8, bf16[1,8,512,256]{3,2,0,1:T(8,128)(2,1)S(1)} %get-tuple-element.14, bf16[1,8,512,256]{3,2,0,1:T(8,128)(2,1)S(1)} %get-tuple-element.13), kind=kOutput, calls=%fused_computation.56 | convolution fusion | flops 1082130432 | bytes 11010048 | tf_op jit(solution)/shard_map/pfwa,pfwb->fab/dot_general | solution.py:47
  145.4 3.7 %fusion.56 = f32[1,8,256,256]{3,2,1,0:T(8,128)S(1)} fusion(bf16[2,8,512,256]{3,2,0,1:T(8,128)(2,1)S(1)} %fusion.2, bf16[2,8,512,256]{3,2,1,0:T(8,128)(2,1)} %bitcast.41, f32[512,256]{1,0:T(8,128)S(1)} %collective-permute-done.8), kind=kOutput, calls=%fused_computation.55 | convolution fusion | flops 1080033280 | bytes 11010048 | tf_op jit(solution)/shard_map/pfwa,pfwb->fab/dot_general | solution.py:46
  149.7 5.0 %collective-permute-start.11 = (bf16[2,8,256,256]{3,2,1,0:T(8,128)(2,1)S(1)}, bf16[2,8,256,256]{3,2,1,0:T(8,128)(2,1)}, u32[]{:S(2)}, u32[]{:S(2)}) collective-permute-start(bf16[2,8,256,256]{3,2,1,0:T(8,128)(2,1)S(1)} %fusion.11), channel_id=1, source_target_pairs={{0,2},{2,4},{4,6},{6,8},{8,10},{10,12},{12,14},{14,16},{16,18},{18... | collective-permute-start | bytes 6291464 | tf_op jit(solution)/shard_map/ppermute | solution.py:16
  154.7 3.7 %fusion.36 = f32[1,8,256,256]{3,2,1,0:T(8,128)S(1)} fusion(bf16[2,8,512,256]{3,2,0,1:T(8,128)(2,1)S(1)} %multiply_convert_fusion, bf16[2,8,512,256]{3,2,1,0:T(8,128)(2,1)} %bitcast.41, f32[512,256]{1,0:T(8,128)S(1)} %collective-permute-done.8), kind=kOutput, calls=%fused_computation.51 | convolution fusion | flops 1080033280 | bytes 11010048 | tf_op jit(solution)/shard_map/pfwa,pfwb->fab/dot_general | solution.py:46
  158.4 4.5 %fusion.46 = f32[1,8,256,256]{3,2,1,0:T(8,128)S(1)} fusion(bf16[2,8,512,256]{3,2,1,0:T(8,128)(2,1)} %bitcast.41, f32[512,256]{1,0:T(8,128)} %copy-done.7, bf16[1,8,512,256]{3,2,0,1:T(8,128)(2,1)} %copy-done.2, bf16[1,8,512,256]{3,2,0,1:T(8,128)(2,1)S(1)} %copy-done.1), kind=kOutput, calls=%fused_computation.53 | convolution fusion | flops 1082130432 | bytes 11010048 | tf_op jit(solution)/shard_map/pfwa,pfwb->fab/dot_general | solution.py:47
  163.5 4.2 %collective-permute-start.9 = (bf16[2,8,256,256]{3,2,1,0:T(8,128)(2,1)S(1)}, bf16[2,8,256,256]{3,2,1,0:T(8,128)(2,1)}, u32[]{:S(2)}, u32[]{:S(2)}) collective-permute-start(bf16[2,8,256,256]{3,2,1,0:T(8,128)(2,1)S(1)} %fusion.5), channel_id=1, source_target_pairs={{0,2},{2,4},{4,6},{6,8},{8,10},{10,12},{12,14},{14,16},{16,18},{18... | collective-permute-start | bytes 6291464 | tf_op jit(solution)/shard_map/ppermute | solution.py:16
  169.1 4.4 %convolution_bitcast_fusion.1 = f32[1,1,8,256,256]{4,3,2,1,0:T(8,128)} fusion(bf16[2,8,512,256]{3,2,0,1:T(8,128)(2,1)S(1)} %multiply_convert_fusion, bf16[1,8,512,256]{3,2,0,1:T(8,128)(2,1)} %copy-done.5, bf16[1,8,512,256]{3,2,0,1:T(8,128)(2,1)S(1)} %copy-done.4), kind=kOutput, calls=%fused_computation.47 | convolution fusion | flops 1075838976 | bytes 10485760 | tf_op jit(solution)/shard_map/pfwa,pfwb->fab/dot_general | solution.py:47
  173.4 2.1 fusion.4
  175.6 10.3 %collective-permute-done.11 = bf16[2,8,256,256]{3,2,1,0:T(8,128)(2,1)} collective-permute-done((bf16[2,8,256,256]{3,2,1,0:T(8,128)(2,1)S(1)}, bf16[2,8,256,256]{3,2,1,0:T(8,128)(2,1)}, u32[]{:S(2)}, u32[]{:S(2)}) %collective-permute-start.11) | collective-permute-done | bytes 2097184 | tf_op jit(solution)/shard_map/ppermute | solution.py:16
  185.9 1.8 select_bitcast_fusion
  190.9 17.5 %collective-permute-done.9 = bf16[2,8,256,256]{3,2,1,0:T(8,128)(2,1)} collective-permute-done((bf16[2,8,256,256]{3,2,1,0:T(8,128)(2,1)S(1)}, bf16[2,8,256,256]{3,2,1,0:T(8,128)(2,1)}, u32[]{:S(2)}, u32[]{:S(2)}) %collective-permute-start.9) | collective-permute-done | bytes 2097184 | tf_op jit(solution)/shard_map/ppermute | solution.py:16
  208.4 2.2 %fusion.28 = bf16[1,2,8,256,256]{4,3,2,1,0:T(8,128)(2,1)S(1)} fusion(bf16[2,8,256,256]{3,2,1,0:T(8,128)(2,1)} %collective-permute-done.9, f32[1,8,256,256]{3,2,1,0:T(8,128)S(1)} %fusion.33, f32[1,8,256,256]{3,2,1,0:T(8,128)S(1)} %convolution_bitcast_fusion, pred[]{:T(512)S(6)} %eq.19), kind=kLoop, calls=%fused_computation.40 | loop fusion | flops 4194304 | bytes 8388609 | tf_op jit(solution)/shard_map/stack | solution.py:86
  210.6 3.9 %pad_maximum_fusion = bf16[4,2,8,256,256]{4,3,2,1,0:T(8,128)(2,1)} fusion(bf16[1,2,8,256,256]{4,3,2,1,0:T(8,128)(2,1)S(1)} %select_bitcast_fusion, bf16[1,2,8,256,256]{4,3,2,1,0:T(8,128)(2,1)S(1)} %fusion.28, bf16[1,2,8,256,256]{4,3,2,1,0:T(8,128)(2,1)S(1)} %fusion.4, bf16[1,2,8,256,256]{4,3,2,1,0:T(8,128)(2,1)S(1)} %fusion.3), kind=kLoop, calls=%fused_computation | loop fusion | flops 12582912 | bytes 16777216 | tf_op jit(solution)/shard_map/stack | solution.py:86
  (53 shorter events, 16.5 us)
Async XLA Ops:
  3.1 47.5 %copy-start.6 = (s32[512,256]{1,0:T(8,128)S(1)}, s32[512,256]{1,0:T(8,128)}, u32[]{:S(2)}) copy-start(s32[512,256]{1,0:T(8,128)} %param.3) | copy-start | bytes 1572868
  3.1 15.3 %collective-permute-start = (f32[512,256]{1,0:T(8,128)S(1)}, f32[512,256]{1,0:T(8,128)S(1)}, u32[]{:S(2)}, u32[]{:S(2)}) collective-permute-start(f32[512,256]{1,0:T(8,128)S(1)} %multiply_reduce_fusion), channel_id=1, source_target_pairs={{0,32},{32,0},{64,96},{96,64},{128,160},{160,128},{192,224},{224,1... | collective-permute-start | bytes 1572872 | tf_op jit(solution)/shard_map/ppermute | solution.py:61
  18.6 8.8 %collective-permute-start.1 = (f32[65536]{0:T(1024)S(1)}, f32[65536]{0:T(1024)S(1)}, u32[]{:S(2)}, u32[]{:S(2)}) collective-permute-start(f32[65536]{0:T(1024)S(1)} %bitcast.76), channel_id=1, source_target_pairs={{0,128},{32,160},{64,192},{96,224},{128,0},{160,32},{192,64},{224,... | collective-permute-start | bytes 786440 | tf_op jit(solution)/shard_map/ppermute | solution.py:34
  27.4 5.1 %collective-permute-start.2 = (f32[32768]{0:T(1024)S(1)}, f32[32768]{0:T(1024)S(1)}, u32[]{:S(2)}, u32[]{:S(2)}) collective-permute-start(f32[32768]{0:T(1024)S(1)} %slice_select_fusion), channel_id=1, source_target_pairs={{0,64},{32,96},{64,0},{96,32},{128,192},{160,224},{192,128},{224,1... | collective-permute-start | bytes 393224 | tf_op jit(solution)/shard_map/ppermute | solution.py:34
  29.1 96.8 %collective-permute-start.12 = (bf16[8192,256]{1,0:T(8,128)(2,1)}, bf16[8192,256]{1,0:T(8,128)(2,1)}, u32[]{:S(2)}, u32[]{:S(2)}) collective-permute-start(bf16[8192,256]{1,0:T(8,128)(2,1)} %bitcast.72), channel_id=1, source_target_pairs={{1,30},{3,0},{5,2},{7,4},{9,6},{11,8},{13,10},{15,12},{17,14},{19,... | collective-permute-start | bytes 12582920 | tf_op jit(solution)/shard_map/ppermute | solution.py:16
  32.5 7.4 %collective-permute-start.3 = (f32[32768]{0:T(1024)S(1)}, f32[32768]{0:T(1024)S(1)}, u32[]{:S(2)}, u32[]{:S(2)}) collective-permute-start(f32[32768]{0:T(1024)S(1)} %select_add_fusion), channel_id=1, source_target_pairs={{0,64},{32,96},{64,0},{96,32},{128,192},{160,224},{192,128},{224,1... | collective-permute-start | bytes 393224 | tf_op jit(solution)/shard_map/ppermute | solution.py:39
  34.2 101.2 %collective-permute-start.5 = (bf16[8192,256]{1,0:T(8,128)(2,1)}, bf16[8192,256]{1,0:T(8,128)(2,1)}, u32[]{:S(2)}, u32[]{:S(2)}) collective-permute-start(bf16[8192,256]{1,0:T(8,128)(2,1)} %bitcast.73), channel_id=1, source_target_pairs={{0,1},{1,2},{2,3},{3,4},{4,5},{5,6},{6,7},{7,8},{8,9},{9,10},{10,1... | collective-permute-start | bytes 12582920 | tf_op jit(solution)/shard_map/ppermute | solution.py:16
  39.9 10.6 %collective-permute-start.4 = (f32[65536]{0:T(1024)S(1)}, f32[65536]{0:T(1024)S(1)}, u32[]{:S(2)}, u32[]{:S(2)}) collective-permute-start(f32[65536]{0:T(1024)S(1)} %maximum_select_fusion.2), channel_id=1, source_target_pairs={{0,128},{32,160},{64,192},{96,224},{128,0},{160,32},{192,64},{224,... | collective-permute-start | bytes 786440 | tf_op jit(solution)/shard_map/ppermute | solution.py:39
  43.2 97.3 %collective-permute-start.7 = (bf16[8192,256]{1,0:T(8,128)(2,1)}, bf16[8192,256]{1,0:T(8,128)(2,1)}, u32[]{:S(2)}, u32[]{:S(2)}) collective-permute-start(bf16[8192,256]{1,0:T(8,128)(2,1)} %bitcast.74), channel_id=1, source_target_pairs={{0,30},{2,0},{4,2},{6,4},{8,6},{10,8},{12,10},{14,12},{16,14},{18,... | collective-permute-start | bytes 12582920 | tf_op jit(solution)/shard_map/ppermute | solution.py:16
  50.7 69.8 %collective-permute-start.13 = (f32[512,256]{1,0:T(8,128)S(1)}, f32[512,256]{1,0:T(8,128)S(1)}, u32[]{:S(2)}, u32[]{:S(2)}) collective-permute-start(f32[512,256]{1,0:T(8,128)S(1)} %fusion.69), channel_id=1, source_target_pairs={{1,30},{3,0},{5,2},{7,4},{9,6},{11,8},{13,10},{15,12},{17,14},{19,... | collective-permute-start | bytes 1572872 | tf_op jit(solution)/shard_map/ppermute | solution.py:16
  52.0 88.4 %collective-permute-start.8 = (f32[512,256]{1,0:T(8,128)S(1)}, f32[512,256]{1,0:T(8,128)S(1)}, u32[]{:S(2)}, u32[]{:S(2)}) collective-permute-start(f32[512,256]{1,0:T(8,128)S(1)} %fusion.69), channel_id=1, source_target_pairs={{0,30},{2,0},{4,2},{6,4},{8,6},{10,8},{12,10},{14,12},{16,14},{18,... | collective-permute-start | bytes 1572872 | tf_op jit(solution)/shard_map/ppermute | solution.py:16
  62.2 67.3 %copy-start = (bf16[1,8,512,256]{3,2,0,1:T(8,128)(2,1)}, bf16[1,8,512,256]{3,2,0,1:T(8,128)(2,1)S(1)}, u32[]{:S(2)}) copy-start(bf16[1,8,512,256]{3,2,0,1:T(8,128)(2,1)S(1)} %get-tuple-element.11) | copy-start | bytes 6291460
  62.2 67.3 %copy-start.2 = (bf16[1,8,512,256]{3,2,0,1:T(8,128)(2,1)}, bf16[1,8,512,256]{3,2,0,1:T(8,128)(2,1)S(1)}, u32[]{:S(2)}) copy-start(bf16[1,8,512,256]{3,2,0,1:T(8,128)(2,1)S(1)} %get-tuple-element.12) | copy-start | bytes 6291460
  120.5 14.8 %collective-permute-start.6 = (f32[512,256]{1,0:T(8,128)S(1)}, f32[512,256]{1,0:T(8,128)S(1)}, u32[]{:S(2)}, u32[]{:S(2)}) collective-permute-start(f32[512,256]{1,0:T(8,128)S(1)} %fusion.69), channel_id=1, source_target_pairs={{0,1},{1,2},{2,3},{3,4},{4,5},{5,6},{6,7},{7,8},{8,9},{9,10},{10,1... | collective-permute-start | bytes 1572872 | tf_op jit(solution)/shard_map/ppermute | solution.py:16
  133.6 42.0 %collective-permute-start.14 = (bf16[2,8,256,256]{3,2,1,0:T(8,128)(2,1)S(1)}, bf16[2,8,256,256]{3,2,1,0:T(8,128)(2,1)S(1)}, u32[]{:S(2)}, u32[]{:S(2)}) collective-permute-start(bf16[2,8,256,256]{3,2,1,0:T(8,128)(2,1)S(1)} %fusion.12), channel_id=1, source_target_pairs={{0,3},{2,5},{4,7},{6,9},{8,11},{10,13},{12,15},{14,17},{16,19},{18... | collective-permute-start | bytes 6291464 | tf_op jit(solution)/shard_map/ppermute | solution.py:16
  138.4 49.4 %collective-permute-start.10 = (bf16[2,8,512,256]{3,2,0,1:T(8,128)(2,1)S(1)}, bf16[2,8,512,256]{3,2,0,1:T(8,128)(2,1)S(1)}, u32[]{:S(2)}, u32[]{:S(2)}) collective-permute-start(bf16[2,8,512,256]{3,2,0,1:T(8,128)(2,1)S(1)} %fusion.2), channel_id=1, source_target_pairs={{0,1},{2,3},{4,5},{6,7},{8,9},{10,11},{12,13},{14,15},{16,17},{18,... | collective-permute-start | bytes 12582920 | tf_op jit(solution)/shard_map/ppermute | solution.py:16
  140.4 1.4 copy-start.3
  140.4 5.0 %copy-start.5 = (bf16[1,8,512,256]{3,2,0,1:T(8,128)(2,1)}, bf16[1,8,512,256]{3,2,0,1:T(8,128)(2,1)S(1)}, u32[]{:S(2)}) copy-start(bf16[1,8,512,256]{3,2,0,1:T(8,128)(2,1)S(1)} %get-tuple-element.14) | copy-start | bytes 6291460
  140.4 14.2 %copy-start.7 = (f32[512,256]{1,0:T(8,128)}, f32[512,256]{1,0:T(8,128)S(1)}, u32[]{:S(2)}) copy-start(f32[512,256]{1,0:T(8,128)S(1)} %collective-permute-done.8) | copy-start | bytes 1572868
  149.6 8.7 %copy-start.1 = (bf16[1,8,512,256]{3,2,0,1:T(8,128)(2,1)S(1)}, bf16[1,8,512,256]{3,2,0,1:T(8,128)(2,1)}, u32[]{:S(2)}) copy-start(bf16[1,8,512,256]{3,2,0,1:T(8,128)(2,1)} %copy-done) | copy-start | bytes 6291460
  149.7 36.2 %collective-permute-start.11 = (bf16[2,8,256,256]{3,2,1,0:T(8,128)(2,1)S(1)}, bf16[2,8,256,256]{3,2,1,0:T(8,128)(2,1)}, u32[]{:S(2)}, u32[]{:S(2)}) collective-permute-start(bf16[2,8,256,256]{3,2,1,0:T(8,128)(2,1)S(1)} %fusion.11), channel_id=1, source_target_pairs={{0,2},{2,4},{4,6},{6,8},{8,10},{10,12},{12,14},{14,16},{16,18},{18... | collective-permute-start | bytes 6291464 | tf_op jit(solution)/shard_map/ppermute | solution.py:16
  163.5 5.6 %copy-start.4 = (bf16[1,8,512,256]{3,2,0,1:T(8,128)(2,1)S(1)}, bf16[1,8,512,256]{3,2,0,1:T(8,128)(2,1)}, u32[]{:S(2)}) copy-start(bf16[1,8,512,256]{3,2,0,1:T(8,128)(2,1)} %copy-done.3) | copy-start | bytes 6291460
  163.5 44.9 %collective-permute-start.9 = (bf16[2,8,256,256]{3,2,1,0:T(8,128)(2,1)S(1)}, bf16[2,8,256,256]{3,2,1,0:T(8,128)(2,1)}, u32[]{:S(2)}, u32[]{:S(2)}) collective-permute-start(bf16[2,8,256,256]{3,2,1,0:T(8,128)(2,1)S(1)} %fusion.5), channel_id=1, source_target_pairs={{0,2},{2,4},{4,6},{6,8},{8,10},{10,12},{12,14},{14,16},{16,18},{18... | collective-permute-start | bytes 6291464 | tf_op jit(solution)/shard_map/ppermute | solution.py:16

commit v12 on v11

--- a/solution.py
+++ b/solution.py
@@ -72,6 +72,7 @@
     whitened = whiten(spectra, window_gain)
     near = whiten(raw_near, gain_near)
     ahead = whiten(raw_ahead, gain_ahead)
+    raw_odd_ahead, gain_near = lax.optimization_barrier((raw_odd_ahead, gain_near))
     odd_ahead = whiten(raw_odd_ahead, gain_odd_ahead)
     lag2_above = moved(cross_block(ahead, whitened, scale), "chan", 2, only_even=True)
     lag3_above = moved(cross_block(ahead, near, scale), "chan", 2, only_even=True)

time: 218 us -> 218 us (level)
  transfers between devices with their start and end apart: 15 -> 15, of which waited for: 6 -> 8; matrix products, arithmetic and copies ran while one was open for 22% -> 22% of each run, Pallas kernels for 0% -> 0%
where the time goes in v12:
time: 218 us; the launch traced here: 214 us
  waiting for transfers between devices  105 us (48%)
  starting transfers between devices  50.6 us (23%)
  matrix products  34.2 us (16%)
  other arithmetic  22.4 us (10%)
    ppermute x10, waiting for transfers between devices, moved(): return lax.ppermute(value, axis, pairs)  84.6 us
    ppermute x10, starting transfers between devices, moved(): return lax.ppermute(value, axis, pairs)  38.4 us
    dot_general x6, matrix products, cross_block(): jnp.einsum('pfwa,pfwb->fab', own_block, flipped, preferred_element_type=j...  18.9 us
    dot_general x6, matrix products, cross_block(): jnp.einsum('pfwa,pfwb->fab', own_block, partner, preferred_element_type=j...  15.3 us
    ppermute x1, waiting for transfers between devices, shards(): lax.ppermute(partial_energy, 'band', [(s, s ^ 1) for s in range(lax.axis_...  12.9 us
    another operation x3, other arithmetic, shards(): return jnp.stack(outputs)  7.9 us
    ppermute x2, waiting for transfers between devices, band_sum(): got = lax.ppermute(jnp.where(bit == 0, high, low), axis, pairs)  7.45 us
    convert_element_type x2, other arithmetic, whiten(): return (raw.astype(jnp.float32) * gain).astype(jnp.bfloat16)  6.07 us
  transfers between devices with their start and end apart: 15, of which 8 were waited for; matrix products, arithmetic and copies ran while one was open for 22% of the time, Pallas kernels for 0%

profile of v12, /device:TPU:4, one launch (start us, length us, event | category | flops | bytes accessed | tf_op | source)
XLA Modules:
  0.0 214.4 jit_solution(8889727775743013539)
XLA Ops:
  0.0 3.1 %multiply_reduce_fusion = f32[512,256]{1,0:T(8,128)S(1)} fusion(bf16[2,8,512,256]{3,2,1,0:T(8,128)(2,1)} %param.2), kind=kLoop, calls=%fused_computation.7 | loop fusion | flops 6160384 | bytes 4718592 | tf_op jit(solution)/shard_map/reduce_sum | solution.py:57
  3.1 2.3 %collective-permute-start = (f32[512,256]{1,0:T(8,128)S(1)}, f32[512,256]{1,0:T(8,128)S(1)}, u32[]{:S(2)}, u32[]{:S(2)}) collective-permute-start(f32[512,256]{1,0:T(8,128)S(1)} %multiply_reduce_fusion), channel_id=1, source_target_pairs={{0,32},{32,0},{64,96},{96,64},{128,160},{160,128},{192,224},{224,1... | collective-permute-start | bytes 1572872 | tf_op jit(solution)/shard_map/ppermute | solution.py:61
  5.4 12.9 %collective-permute-done = f32[512,256]{1,0:T(8,128)S(1)} collective-permute-done((f32[512,256]{1,0:T(8,128)S(1)}, f32[512,256]{1,0:T(8,128)S(1)}, u32[]{:S(2)}, u32[]{:S(2)}) %collective-permute-start) | collective-permute-done | bytes 524320 | tf_op jit(solution)/shard_map/ppermute | solution.py:61
  18.6 3.3 %collective-permute-start.1 = (f32[65536]{0:T(1024)S(1)}, f32[65536]{0:T(1024)S(1)}, u32[]{:S(2)}, u32[]{:S(2)}) collective-permute-start(f32[65536]{0:T(1024)S(1)} %bitcast.75), channel_id=1, source_target_pairs={{0,128},{32,160},{64,192},{96,224},{128,0},{160,32},{192,64},{224,... | collective-permute-start | bytes 786440 | tf_op jit(solution)/shard_map/ppermute | solution.py:34
  22.0 5.3 %collective-permute-done.1 = f32[65536]{0:T(1024)S(1)} collective-permute-done((f32[65536]{0:T(1024)S(1)}, f32[65536]{0:T(1024)S(1)}, u32[]{:S(2)}, u32[]{:S(2)}) %collective-permute-start.1) | collective-permute-done | bytes 262176 | tf_op jit(solution)/shard_map/ppermute | solution.py:34
  30.4 2.1 collective-permute-done.2
  34.2 5.7 %collective-permute-start.5 = (bf16[8192,256]{1,0:T(8,128)(2,1)}, bf16[8192,256]{1,0:T(8,128)(2,1)}, u32[]{:S(2)}, u32[]{:S(2)}) collective-permute-start(bf16[8192,256]{1,0:T(8,128)(2,1)} %bitcast.72), channel_id=1, source_target_pairs={{0,1},{1,2},{2,3},{3,4},{4,5},{5,6},{6,7},{7,8},{8,9},{9,10},{10,1... | collective-permute-start | bytes 12582920 | tf_op jit(solution)/shard_map/ppermute | solution.py:16
  39.9 3.3 %collective-permute-start.4 = (f32[65536]{0:T(1024)S(1)}, f32[65536]{0:T(1024)S(1)}, u32[]{:S(2)}, u32[]{:S(2)}) collective-permute-start(f32[65536]{0:T(1024)S(1)} %maximum_select_fusion.2), channel_id=1, source_target_pairs={{0,128},{32,160},{64,192},{96,224},{128,0},{160,32},{192,64},{224,... | collective-permute-start | bytes 786440 | tf_op jit(solution)/shard_map/ppermute | solution.py:39
  43.2 7.2 %collective-permute-start.7 = (bf16[8192,256]{1,0:T(8,128)(2,1)}, bf16[8192,256]{1,0:T(8,128)(2,1)}, u32[]{:S(2)}, u32[]{:S(2)}) collective-permute-start(bf16[8192,256]{1,0:T(8,128)(2,1)} %bitcast.73), channel_id=1, source_target_pairs={{0,30},{2,0},{4,2},{6,4},{8,6},{10,8},{12,10},{14,12},{16,14},{18,... | collective-permute-start | bytes 12582920 | tf_op jit(solution)/shard_map/ppermute | solution.py:16
  52.0 5.8 %collective-permute-start.6 = (f32[512,256]{1,0:T(8,128)S(1)}, f32[512,256]{1,0:T(8,128)S(1)}, u32[]{:S(2)}, u32[]{:S(2)}) collective-permute-start(f32[512,256]{1,0:T(8,128)S(1)} %fusion.62), channel_id=1, source_target_pairs={{0,1},{1,2},{2,3},{3,4},{4,5},{5,6},{6,7},{7,8},{8,9},{9,10},{10,1... | collective-permute-start | bytes 1572872 | tf_op jit(solution)/shard_map/ppermute | solution.py:16
  57.8 3.0 %multiply_convert_fusion.1 = bf16[2,8,512,256]{3,2,0,1:T(8,128)(2,1)S(1)} fusion(bf16[2,8,512,256]{3,2,1,0:T(8,128)(2,1)} %param.2, f32[512,256]{1,0:T(8,128)S(1)} %fusion.62), kind=kLoop, calls=%fused_computation.6 | loop fusion | flops 6291456 | bytes 8912896 | tf_op jit(solution)/shard_map/convert_element_type | solution.py:52
  64.6 27.9 %collective-permute-done.6 = f32[512,256]{1,0:T(8,128)S(1)} collective-permute-done((f32[512,256]{1,0:T(8,128)S(1)}, f32[512,256]{1,0:T(8,128)S(1)}, u32[]{:S(2)}, u32[]{:S(2)}) %collective-permute-start.6) | collective-permute-done | bytes 524320 | tf_op jit(solution)/shard_map/ppermute | solution.py:16
  92.5 4.0 %collective-permute-start.8 = (f32[512,256]{1,0:T(8,128)S(1)}, f32[512,256]{1,0:T(8,128)S(1)}, u32[]{:S(2)}, u32[]{:S(2)}) collective-permute-start(f32[512,256]{1,0:T(8,128)S(1)} %fusion.62), channel_id=1, source_target_pairs={{0,30},{2,0},{4,2},{6,4},{8,6},{10,8},{12,10},{14,12},{16,14},{18,... | collective-permute-start | bytes 1572872 | tf_op jit(solution)/shard_map/ppermute | solution.py:16
  96.5 12.9 %collective-permute-done.12 = bf16[8192,256]{1,0:T(8,128)(2,1)} collective-permute-done((bf16[8192,256]{1,0:T(8,128)(2,1)}, bf16[8192,256]{1,0:T(8,128)(2,1)}, u32[]{:S(2)}, u32[]{:S(2)}) %collective-permute-start.12) | collective-permute-done | bytes 4194336 | tf_op jit(solution)/shard_map/ppermute | solution.py:16
  109.4 11.1 %collective-permute-done.13 = f32[512,256]{1,0:T(8,128)S(1)} collective-permute-done((f32[512,256]{1,0:T(8,128)S(1)}, f32[512,256]{1,0:T(8,128)S(1)}, u32[]{:S(2)}, u32[]{:S(2)}) %collective-permute-start.13) | collective-permute-done | bytes 524320 | tf_op jit(solution)/shard_map/ppermute | solution.py:16
  120.5 3.4 %fusion.46 = f32[1,8,256,256]{3,2,1,0:T(8,128)S(1)} fusion(bf16[2,8,512,256]{3,2,1,0:T(8,128)(2,1)} %bitcast.30, f32[512,256]{1,0:T(8,128)S(1)} %collective-permute-done.13, bf16[1,8,512,256]{3,2,0,1:T(8,128)(2,1)S(1)} %get-tuple-element.14, bf16[1,8,512,256]{3,2,0,1:T(8,128)(2,1)S(1)} %get-tuple-element.13), kind=kOutput, calls=%fused_computation.53 | convolution fusion | flops 1082130432 | bytes 11010048 | tf_op jit(solution)/shard_map/pfwa,pfwb->fab/dot_general | solution.py:47
  124.0 3.7 %fusion.38 = f32[1,8,256,256]{3,2,1,0:T(8,128)S(1)} fusion(bf16[2,8,512,256]{3,2,0,1:T(8,128)(2,1)S(1)} %multiply_convert_fusion.1, bf16[2,8,512,256]{3,2,1,0:T(8,128)(2,1)} %bitcast.30, f32[512,256]{1,0:T(8,128)S(1)} %collective-permute-done.13), kind=kOutput, calls=%fused_computation.51 | convolution fusion | flops 1080033280 | bytes 11010048 | tf_op jit(solution)/shard_map/pfwa,pfwb->fab/dot_general | solution.py:46
  129.7 3.0 %fusion.1 = bf16[2,8,512,256]{3,2,0,1:T(8,128)(2,1)S(1)} fusion(f32[512,256]{1,0:T(8,128)S(1)} %collective-permute-done.6, bf16[2,8,512,256]{3,2,1,0:T(8,128)(2,1)} %bitcast.38), kind=kLoop, calls=%fused_computation.4 | loop fusion | flops 6291456 | bytes 8912896 | tf_op jit(solution)/shard_map/convert_element_type | solution.py:52
  132.7 7.4 %collective-permute-start.10 = (bf16[2,8,512,256]{3,2,0,1:T(8,128)(2,1)S(1)}, bf16[2,8,512,256]{3,2,0,1:T(8,128)(2,1)S(1)}, u32[]{:S(2)}, u32[]{:S(2)}) collective-permute-start(bf16[2,8,512,256]{3,2,0,1:T(8,128)(2,1)S(1)} %fusion.1), channel_id=1, source_target_pairs={{0,1},{2,3},{4,5},{6,7},{8,9},{10,11},{12,13},{14,15},{16,17},{18,... | collective-permute-start | bytes 12582920 | tf_op jit(solution)/shard_map/ppermute | solution.py:16
  141.7 3.6 %fusion.54 = f32[1,8,256,256]{3,2,1,0:T(8,128)S(1)} fusion(bf16[2,8,512,256]{3,2,1,0:T(8,128)(2,1)} %bitcast.41, f32[512,256]{1,0:T(8,128)S(1)} %collective-permute-done.8, bf16[1,8,512,256]{3,2,0,1:T(8,128)(2,1)S(1)} %get-tuple-element.16, bf16[1,8,512,256]{3,2,0,1:T(8,128)(2,1)S(1)} %get-tuple-element.15), kind=kOutput, calls=%fused_computation.55 | convolution fusion | flops 1082130432 | bytes 11010048 | tf_op jit(solution)/shard_map/pfwa,pfwb->fab/dot_general | solution.py:47
  145.4 3.7 %fusion.49 = f32[1,8,256,256]{3,2,1,0:T(8,128)S(1)} fusion(bf16[2,8,512,256]{3,2,0,1:T(8,128)(2,1)S(1)} %fusion.1, bf16[2,8,512,256]{3,2,1,0:T(8,128)(2,1)} %bitcast.41, f32[512,256]{1,0:T(8,128)S(1)} %collective-permute-done.8), kind=kOutput, calls=%fused_computation.54 | convolution fusion | flops 1080033280 | bytes 11010048 | tf_op jit(solution)/shard_map/pfwa,pfwb->fab/dot_general | solution.py:46
  149.6 2.1 collective-permute-start.11
  151.7 3.7 %fusion.33 = f32[1,8,256,256]{3,2,1,0:T(8,128)S(1)} fusion(bf16[2,8,512,256]{3,2,0,1:T(8,128)(2,1)S(1)} %multiply_convert_fusion.1, bf16[2,8,512,256]{3,2,1,0:T(8,128)(2,1)} %bitcast.41, f32[512,256]{1,0:T(8,128)S(1)} %collective-permute-done.8), kind=kOutput, calls=%fused_computation.50 | convolution fusion | flops 1080033280 | bytes 11010048 | tf_op jit(solution)/shard_map/pfwa,pfwb->fab/dot_general | solution.py:46
  155.4 4.5 %fusion.41 = f32[1,8,256,256]{3,2,1,0:T(8,128)S(1)} fusion(bf16[2,8,512,256]{3,2,1,0:T(8,128)(2,1)} %bitcast.41, f32[512,256]{1,0:T(8,128)} %copy-done.7, bf16[1,8,512,256]{3,2,0,1:T(8,128)(2,1)} %copy-done.2, bf16[1,8,512,256]{3,2,0,1:T(8,128)(2,1)S(1)} %copy-done.1), kind=kOutput, calls=%fused_computation.52 | convolution fusion | flops 1082130432 | bytes 11010048 | tf_op jit(solution)/shard_map/pfwa,pfwb->fab/dot_general | solution.py:47
  160.5 2.3 %collective-permute-start.9 = (bf16[2,8,256,256]{3,2,1,0:T(8,128)(2,1)S(1)}, bf16[2,8,256,256]{3,2,1,0:T(8,128)(2,1)}, u32[]{:S(2)}, u32[]{:S(2)}) collective-permute-start(bf16[2,8,256,256]{3,2,1,0:T(8,128)(2,1)S(1)} %fusion.4), channel_id=1, source_target_pairs={{0,2},{2,4},{4,6},{6,8},{8,10},{10,12},{12,14},{14,16},{16,18},{18... | collective-permute-start | bytes 6291464 | tf_op jit(solution)/shard_map/ppermute | solution.py:16
  164.2 4.4 %convolution_bitcast_fusion.1 = f32[1,1,8,256,256]{4,3,2,1,0:T(8,128)} fusion(bf16[2,8,512,256]{3,2,0,1:T(8,128)(2,1)S(1)} %multiply_convert_fusion.1, bf16[1,8,512,256]{3,2,0,1:T(8,128)(2,1)} %copy-done.5, bf16[1,8,512,256]{3,2,0,1:T(8,128)(2,1)S(1)} %copy-done.4), kind=kOutput, calls=%fused_computation.46 | convolution fusion | flops 1075838976 | bytes 10485760 | tf_op jit(solution)/shard_map/pfwa,pfwb->fab/dot_general | solution.py:47
  168.6 2.1 fusion.3
  170.7 15.2 %collective-permute-done.11 = bf16[2,8,256,256]{3,2,1,0:T(8,128)(2,1)} collective-permute-done((bf16[2,8,256,256]{3,2,1,0:T(8,128)(2,1)S(1)}, bf16[2,8,256,256]{3,2,1,0:T(8,128)(2,1)}, u32[]{:S(2)}, u32[]{:S(2)}) %collective-permute-start.11) | collective-permute-done | bytes 2097184 | tf_op jit(solution)/shard_map/ppermute | solution.py:16
  185.9 1.8 select_bitcast_fusion
  190.9 17.5 %collective-permute-done.9 = bf16[2,8,256,256]{3,2,1,0:T(8,128)(2,1)} collective-permute-done((bf16[2,8,256,256]{3,2,1,0:T(8,128)(2,1)S(1)}, bf16[2,8,256,256]{3,2,1,0:T(8,128)(2,1)}, u32[]{:S(2)}, u32[]{:S(2)}) %collective-permute-start.9) | collective-permute-done | bytes 2097184 | tf_op jit(solution)/shard_map/ppermute | solution.py:16
  208.3 2.2 %fusion.25 = bf16[1,2,8,256,256]{4,3,2,1,0:T(8,128)(2,1)S(1)} fusion(bf16[2,8,256,256]{3,2,1,0:T(8,128)(2,1)} %collective-permute-done.9, f32[1,8,256,256]{3,2,1,0:T(8,128)S(1)} %fusion.30, f32[1,8,256,256]{3,2,1,0:T(8,128)S(1)} %convolution_bitcast_fusion, pred[]{:T(512)S(6)} %eq.19), kind=kLoop, calls=%fused_computation.39 | loop fusion | flops 4194304 | bytes 8388609 | tf_op jit(solution)/shard_map/stack | solution.py:87
  210.6 3.9 %pad_maximum_fusion = bf16[4,2,8,256,256]{4,3,2,1,0:T(8,128)(2,1)} fusion(bf16[1,2,8,256,256]{4,3,2,1,0:T(8,128)(2,1)S(1)} %select_bitcast_fusion, bf16[1,2,8,256,256]{4,3,2,1,0:T(8,128)(2,1)S(1)} %fusion.25, bf16[1,2,8,256,256]{4,3,2,1,0:T(8,128)(2,1)S(1)} %fusion.3, bf16[1,2,8,256,256]{4,3,2,1,0:T(8,128)(2,1)S(1)} %fusion.2), kind=kLoop, calls=%fused_computation | loop fusion | flops 12582912 | bytes 16777216 | tf_op jit(solution)/shard_map/stack | solution.py:87
  (53 shorter events, 19.5 us)
Async XLA Ops:
  3.1 47.5 %copy-start.6 = (s32[512,256]{1,0:T(8,128)S(1)}, s32[512,256]{1,0:T(8,128)}, u32[]{:S(2)}) copy-start(s32[512,256]{1,0:T(8,128)} %param.3) | copy-start | bytes 1572868
  3.1 15.3 %collective-permute-start = (f32[512,256]{1,0:T(8,128)S(1)}, f32[512,256]{1,0:T(8,128)S(1)}, u32[]{:S(2)}, u32[]{:S(2)}) collective-permute-start(f32[512,256]{1,0:T(8,128)S(1)} %multiply_reduce_fusion), channel_id=1, source_target_pairs={{0,32},{32,0},{64,96},{96,64},{128,160},{160,128},{192,224},{224,1... | collective-permute-start | bytes 1572872 | tf_op jit(solution)/shard_map/ppermute | solution.py:61
  18.6 8.8 %collective-permute-start.1 = (f32[65536]{0:T(1024)S(1)}, f32[65536]{0:T(1024)S(1)}, u32[]{:S(2)}, u32[]{:S(2)}) collective-permute-start(f32[65536]{0:T(1024)S(1)} %bitcast.75), channel_id=1, source_target_pairs={{0,128},{32,160},{64,192},{96,224},{128,0},{160,32},{192,64},{224,... | collective-permute-start | bytes 786440 | tf_op jit(solution)/shard_map/ppermute | solution.py:34
  27.4 5.1 %collective-permute-start.2 = (f32[32768]{0:T(1024)S(1)}, f32[32768]{0:T(1024)S(1)}, u32[]{:S(2)}, u32[]{:S(2)}) collective-permute-start(f32[32768]{0:T(1024)S(1)} %slice_select_fusion), channel_id=1, source_target_pairs={{0,64},{32,96},{64,0},{96,32},{128,192},{160,224},{192,128},{224,1... | collective-permute-start | bytes 393224 | tf_op jit(solution)/shard_map/ppermute | solution.py:34
  29.1 80.3 %collective-permute-start.12 = (bf16[8192,256]{1,0:T(8,128)(2,1)}, bf16[8192,256]{1,0:T(8,128)(2,1)}, u32[]{:S(2)}, u32[]{:S(2)}) collective-permute-start(bf16[8192,256]{1,0:T(8,128)(2,1)} %bitcast.71), channel_id=1, source_target_pairs={{1,30},{3,0},{5,2},{7,4},{9,6},{11,8},{13,10},{15,12},{17,14},{19,... | collective-permute-start | bytes 12582920 | tf_op jit(solution)/shard_map/ppermute | solution.py:16
  32.5 7.4 %collective-permute-start.3 = (f32[32768]{0:T(1024)S(1)}, f32[32768]{0:T(1024)S(1)}, u32[]{:S(2)}, u32[]{:S(2)}) collective-permute-start(f32[32768]{0:T(1024)S(1)} %select_add_fusion), channel_id=1, source_target_pairs={{0,64},{32,96},{64,0},{96,32},{128,192},{160,224},{192,128},{224,1... | collective-permute-start | bytes 393224 | tf_op jit(solution)/shard_map/ppermute | solution.py:39
  34.2 95.5 %collective-permute-start.5 = (bf16[8192,256]{1,0:T(8,128)(2,1)}, bf16[8192,256]{1,0:T(8,128)(2,1)}, u32[]{:S(2)}, u32[]{:S(2)}) collective-permute-start(bf16[8192,256]{1,0:T(8,128)(2,1)} %bitcast.72), channel_id=1, source_target_pairs={{0,1},{1,2},{2,3},{3,4},{4,5},{5,6},{6,7},{7,8},{8,9},{9,10},{10,1... | collective-permute-start | bytes 12582920 | tf_op jit(solution)/shard_map/ppermute | solution.py:16
  39.9 10.6 %collective-permute-start.4 = (f32[65536]{0:T(1024)S(1)}, f32[65536]{0:T(1024)S(1)}, u32[]{:S(2)}, u32[]{:S(2)}) collective-permute-start(f32[65536]{0:T(1024)S(1)} %maximum_select_fusion.2), channel_id=1, source_target_pairs={{0,128},{32,160},{64,192},{96,224},{128,0},{160,32},{192,64},{224,... | collective-permute-start | bytes 786440 | tf_op jit(solution)/shard_map/ppermute | solution.py:39
  43.2 97.2 %collective-permute-start.7 = (bf16[8192,256]{1,0:T(8,128)(2,1)}, bf16[8192,256]{1,0:T(8,128)(2,1)}, u32[]{:S(2)}, u32[]{:S(2)}) collective-permute-start(bf16[8192,256]{1,0:T(8,128)(2,1)} %bitcast.73), channel_id=1, source_target_pairs={{0,30},{2,0},{4,2},{6,4},{8,6},{10,8},{12,10},{14,12},{16,14},{18,... | collective-permute-start | bytes 12582920 | tf_op jit(solution)/shard_map/ppermute | solution.py:16
  50.7 69.8 %collective-permute-start.13 = (f32[512,256]{1,0:T(8,128)S(1)}, f32[512,256]{1,0:T(8,128)S(1)}, u32[]{:S(2)}, u32[]{:S(2)}) collective-permute-start(f32[512,256]{1,0:T(8,128)S(1)} %fusion.62), channel_id=1, source_target_pairs={{1,30},{3,0},{5,2},{7,4},{9,6},{11,8},{13,10},{15,12},{17,14},{19,... | collective-permute-start | bytes 1572872 | tf_op jit(solution)/shard_map/ppermute | solution.py:16
  52.0 40.5 %collective-permute-start.6 = (f32[512,256]{1,0:T(8,128)S(1)}, f32[512,256]{1,0:T(8,128)S(1)}, u32[]{:S(2)}, u32[]{:S(2)}) collective-permute-start(f32[512,256]{1,0:T(8,128)S(1)} %fusion.62), channel_id=1, source_target_pairs={{0,1},{1,2},{2,3},{3,4},{4,5},{5,6},{6,7},{7,8},{8,9},{9,10},{10,1... | collective-permute-start | bytes 1572872 | tf_op jit(solution)/shard_map/ppermute | solution.py:16
  61.2 59.4 %copy-start = (bf16[1,8,512,256]{3,2,0,1:T(8,128)(2,1)}, bf16[1,8,512,256]{3,2,0,1:T(8,128)(2,1)S(1)}, u32[]{:S(2)}) copy-start(bf16[1,8,512,256]{3,2,0,1:T(8,128)(2,1)S(1)} %get-tuple-element.13) | copy-start | bytes 6291460
  61.2 59.4 %copy-start.2 = (bf16[1,8,512,256]{3,2,0,1:T(8,128)(2,1)}, bf16[1,8,512,256]{3,2,0,1:T(8,128)(2,1)S(1)}, u32[]{:S(2)}) copy-start(bf16[1,8,512,256]{3,2,0,1:T(8,128)(2,1)S(1)} %get-tuple-element.14) | copy-start | bytes 6291460
  92.5 47.9 %collective-permute-start.8 = (f32[512,256]{1,0:T(8,128)S(1)}, f32[512,256]{1,0:T(8,128)S(1)}, u32[]{:S(2)}, u32[]{:S(2)}) collective-permute-start(f32[512,256]{1,0:T(8,128)S(1)} %fusion.62), channel_id=1, source_target_pairs={{0,30},{2,0},{4,2},{6,4},{8,6},{10,8},{12,10},{14,12},{16,14},{18,... | collective-permute-start | bytes 1572872 | tf_op jit(solution)/shard_map/ppermute | solution.py:16
  128.2 42.5 %collective-permute-start.14 = (bf16[2,8,256,256]{3,2,1,0:T(8,128)(2,1)S(1)}, bf16[2,8,256,256]{3,2,1,0:T(8,128)(2,1)S(1)}, u32[]{:S(2)}, u32[]{:S(2)}) collective-permute-start(bf16[2,8,256,256]{3,2,1,0:T(8,128)(2,1)S(1)} %fusion.11), channel_id=1, source_target_pairs={{0,3},{2,5},{4,7},{6,9},{8,11},{10,13},{12,15},{14,17},{16,19},{18... | collective-permute-start | bytes 6291464 | tf_op jit(solution)/shard_map/ppermute | solution.py:16
  132.7 55.0 %collective-permute-start.10 = (bf16[2,8,512,256]{3,2,0,1:T(8,128)(2,1)S(1)}, bf16[2,8,512,256]{3,2,0,1:T(8,128)(2,1)S(1)}, u32[]{:S(2)}, u32[]{:S(2)}) collective-permute-start(bf16[2,8,512,256]{3,2,0,1:T(8,128)(2,1)S(1)} %fusion.1), channel_id=1, source_target_pairs={{0,1},{2,3},{4,5},{6,7},{8,9},{10,11},{12,13},{14,15},{16,17},{18,... | collective-permute-start | bytes 12582920 | tf_op jit(solution)/shard_map/ppermute | solution.py:16
  140.3 1.4 copy-start.3
  140.4 5.0 %copy-start.5 = (bf16[1,8,512,256]{3,2,0,1:T(8,128)(2,1)}, bf16[1,8,512,256]{3,2,0,1:T(8,128)(2,1)S(1)}, u32[]{:S(2)}) copy-start(bf16[1,8,512,256]{3,2,0,1:T(8,128)(2,1)S(1)} %get-tuple-element.16) | copy-start | bytes 6291460
  140.4 11.3 %copy-start.7 = (f32[512,256]{1,0:T(8,128)}, f32[512,256]{1,0:T(8,128)S(1)}, u32[]{:S(2)}) copy-start(f32[512,256]{1,0:T(8,128)S(1)} %collective-permute-done.8) | copy-start | bytes 1572868
  149.6 5.8 %copy-start.1 = (bf16[1,8,512,256]{3,2,0,1:T(8,128)(2,1)S(1)}, bf16[1,8,512,256]{3,2,0,1:T(8,128)(2,1)}, u32[]{:S(2)}) copy-start(bf16[1,8,512,256]{3,2,0,1:T(8,128)(2,1)} %copy-done) | copy-start | bytes 6291460
  149.6 36.3 %collective-permute-start.11 = (bf16[2,8,256,256]{3,2,1,0:T(8,128)(2,1)S(1)}, bf16[2,8,256,256]{3,2,1,0:T(8,128)(2,1)}, u32[]{:S(2)}, u32[]{:S(2)}) collective-permute-start(bf16[2,8,256,256]{3,2,1,0:T(8,128)(2,1)S(1)} %fusion.10), channel_id=1, source_target_pairs={{0,2},{2,4},{4,6},{6,8},{8,10},{10,12},{12,14},{14,16},{16,18},{18... | collective-permute-start | bytes 6291464 | tf_op jit(solution)/shard_map/ppermute | solution.py:16
  160.5 3.7 %copy-start.4 = (bf16[1,8,512,256]{3,2,0,1:T(8,128)(2,1)S(1)}, bf16[1,8,512,256]{3,2,0,1:T(8,128)(2,1)}, u32[]{:S(2)}) copy-start(bf16[1,8,512,256]{3,2,0,1:T(8,128)(2,1)} %copy-done.3) | copy-start | bytes 6291460
  160.5 47.9 %collective-permute-start.9 = (bf16[2,8,256,256]{3,2,1,0:T(8,128)(2,1)S(1)}, bf16[2,8,256,256]{3,2,1,0:T(8,128)(2,1)}, u32[]{:S(2)}, u32[]{:S(2)}) collective-permute-start(bf16[2,8,256,256]{3,2,1,0:T(8,128)(2,1)S(1)} %fusion.4), channel_id=1, source_target_pairs={{0,2},{2,4},{4,6},{6,8},{8,10},{10,12},{12,14},{14,16},{16,18},{18... | collective-permute-start | bytes 6291464 | tf_op jit(solution)/shard_map/ppermute | solution.py:16

commit v13 on v9

--- a/solution.py
+++ b/solution.py
@@ -66,7 +66,7 @@
     raw_mate = moved(flat_spectra, "chan", -1, only_odd=True).reshape(spectra.shape)
     energy = band_sum(partial_energy, "band")
     window_gain = valid_mask.astype(jnp.float32) / jnp.sqrt(energy / total_bins + eps_energy)
-    gain_near = moved(window_gain, "chan", 1)
+    gain_near = moved(window_gain.astype(jnp.bfloat16), "chan", 1).astype(jnp.float32)
     gain_ahead = moved(window_gain, "chan", -2, only_even=True)
     gain_mate = moved(window_gain, "chan", -1, only_odd=True)
     whitened = whiten(spectra, window_gain)

time: 167 us -> 164 us (0.982)
  waiting for transfers between devices: 91.7 us -> 80.3 us
  matrix products: 23 us -> 29.1 us
    ppermute x9, waiting for transfers between devices: 66.6 us -> 55.3 us  [moved(): return lax.ppermute(value, axis, pairs)]
    dot_general x5, matrix products: 11.3 us -> 16.1 us  [cross_block(): jnp.einsum('pfwa,pfwb->fab', own_block, flipped, preferred_element_type=j...]
    convert_element_type x5 -> x4, other arithmetic: 2.79 us -> 4.39 us  [cross_block(): return (jnp.stack([real_part, imag_part]) * scale).astype(jnp.bfloat16)]
  transfers between devices with their start and end apart: 14 -> 14, of which waited for: 8 -> 8; matrix products, arithmetic and copies ran while one was open for 22% -> 28% of each run, Pallas kernels for 0% -> 0%
where the time goes in v13:
time: 164 us; the launch traced here: 163 us
  waiting for transfers between devices  80.3 us (49%)
  starting transfers between devices  32.3 us (20%)
  matrix products  29.1 us (18%)
  other arithmetic  20.6 us (13%)
    ppermute x9, waiting for transfers between devices, moved(): return lax.ppermute(value, axis, pairs)  55.3 us
    ppermute x9, starting transfers between devices, moved(): return lax.ppermute(value, axis, pairs)  19.9 us
    dot_general x5, matrix products, cross_block(): jnp.einsum('pfwa,pfwb->fab', own_block, flipped, preferred_element_type=j...  16.1 us
    dot_general x5, matrix products, cross_block(): jnp.einsum('pfwa,pfwb->fab', own_block, partner, preferred_element_type=j...  13 us
    ppermute x1, waiting for transfers between devices, shards(): lax.ppermute(partial_energy, 'band', [(s, s ^ 1) for s in range(lax.axis_...  12.9 us
    ppermute x2, waiting for transfers between devices, band_sum(): got = lax.ppermute(jnp.where(bit == 0, high, low), axis, pairs)  8.64 us
    convert_element_type x2, other arithmetic, whiten(): return (raw.astype(jnp.float32) * gain).astype(jnp.bfloat16)  6.07 us
    ppermute x2, starting transfers between devices, band_sum(): got = lax.ppermute(flat, axis, pairs)  5.19 us
  transfers between devices with their start and end apart: 14, of which 8 were waited for; matrix products, arithmetic and copies ran while one was open for 28% of the time, Pallas kernels for 0%

profile of v13, /device:TPU:4, one launch (start us, length us, event | category | flops | bytes accessed | tf_op | source)
XLA Modules:
  0.0 163.1 jit_solution(7261975913294074933)
XLA Ops:
  0.0 3.1 %multiply_reduce_fusion = f32[512,256]{1,0:T(8,128)S(1)} fusion(bf16[2,8,512,256]{3,2,1,0:T(8,128)(2,1)} %param.2), kind=kLoop, calls=%fused_computation.8 | loop fusion | flops 6160384 | bytes 4718592 | tf_op jit(solution)/shard_map/reduce_sum | solution.py:57
  3.1 2.3 %collective-permute-start = (f32[512,256]{1,0:T(8,128)S(1)}, f32[512,256]{1,0:T(8,128)S(1)}, u32[]{:S(2)}, u32[]{:S(2)}) collective-permute-start(f32[512,256]{1,0:T(8,128)S(1)} %multiply_reduce_fusion), channel_id=1, source_target_pairs={{0,32},{32,0},{64,96},{96,64},{128,160},{160,128},{192,224},{224,1... | collective-permute-start | bytes 1572872 | tf_op jit(solution)/shard_map/ppermute | solution.py:61
  5.4 12.9 %collective-permute-done = f32[512,256]{1,0:T(8,128)S(1)} collective-permute-done((f32[512,256]{1,0:T(8,128)S(1)}, f32[512,256]{1,0:T(8,128)S(1)}, u32[]{:S(2)}, u32[]{:S(2)}) %collective-permute-start) | collective-permute-done | bytes 524320 | tf_op jit(solution)/shard_map/ppermute | solution.py:61
  18.6 3.3 %collective-permute-start.2 = (f32[65536]{0:T(1024)S(1)}, f32[65536]{0:T(1024)S(1)}, u32[]{:S(2)}, u32[]{:S(2)}) collective-permute-start(f32[65536]{0:T(1024)S(1)} %bitcast.71), channel_id=1, source_target_pairs={{0,128},{32,160},{64,192},{96,224},{128,0},{160,32},{192,64},{224,... | collective-permute-start | bytes 786440 | tf_op jit(solution)/shard_map/ppermute | solution.py:34
  22.1 5.3 %collective-permute-done.2 = f32[65536]{0:T(1024)S(1)} collective-permute-done((f32[65536]{0:T(1024)S(1)}, f32[65536]{0:T(1024)S(1)}, u32[]{:S(2)}, u32[]{:S(2)}) %collective-permute-start.2) | collective-permute-done | bytes 262176 | tf_op jit(solution)/shard_map/ppermute | solution.py:34
  27.4 1.7 %collective-permute-start.3 = (f32[32768]{0:T(1024)S(1)}, f32[32768]{0:T(1024)S(1)}, u32[]{:S(2)}, u32[]{:S(2)}) collective-permute-start(f32[32768]{0:T(1024)S(1)} %slice_select_fusion), channel_id=1, source_target_pairs={{0,64},{32,96},{64,0},{96,32},{128,192},{160,224},{192,128},{224,1... | collective-permute-start | bytes 393224 | tf_op jit(solution)/shard_map/ppermute | solution.py:34
  29.1 3.4 %collective-permute-done.3 = f32[32768]{0:T(1024)S(1)} collective-permute-done((f32[32768]{0:T(1024)S(1)}, f32[32768]{0:T(1024)S(1)}, u32[]{:S(2)}, u32[]{:S(2)}) %collective-permute-start.3) | collective-permute-done | bytes 131104 | tf_op jit(solution)/shard_map/ppermute | solution.py:34
  32.5 1.7 %collective-permute-start.4 = (f32[32768]{0:T(1024)S(1)}, f32[32768]{0:T(1024)S(1)}, u32[]{:S(2)}, u32[]{:S(2)}) collective-permute-start(f32[32768]{0:T(1024)S(1)} %select_add_fusion), channel_id=1, source_target_pairs={{0,64},{32,96},{64,0},{96,32},{128,192},{160,224},{192,128},{224,1... | collective-permute-start | bytes 393224 | tf_op jit(solution)/shard_map/ppermute | solution.py:39
  34.2 3.4 %collective-permute-done.4 = f32[32768]{0:T(1024)S(1)} collective-permute-done((f32[32768]{0:T(1024)S(1)}, f32[32768]{0:T(1024)S(1)}, u32[]{:S(2)}, u32[]{:S(2)}) %collective-permute-start.4) | collective-permute-done | bytes 131104 | tf_op jit(solution)/shard_map/ppermute | solution.py:39
  37.6 3.5 %collective-permute-start.5 = (f32[65536]{0:T(1024)S(1)}, f32[65536]{0:T(1024)S(1)}, u32[]{:S(2)}, u32[]{:S(2)}) collective-permute-start(f32[65536]{0:T(1024)S(1)} %maximum_select_fusion.2), channel_id=1, source_target_pairs={{0,128},{32,160},{64,192},{96,224},{128,0},{160,32},{192,64},{224,... | collective-permute-start | bytes 786440 | tf_op jit(solution)/shard_map/ppermute | solution.py:39
  41.2 8.4 %collective-permute-start.1 = (bf16[8192,256]{1,0:T(8,128)(2,1)}, bf16[8192,256]{1,0:T(8,128)(2,1)}, u32[]{:S(2)}, u32[]{:S(2)}) collective-permute-start(bf16[8192,256]{1,0:T(8,128)(2,1)} %bitcast.66), channel_id=1, source_target_pairs={{0,30},{2,0},{4,2},{6,4},{8,6},{10,8},{12,10},{14,12},{16,14},{18,... | collective-permute-start | bytes 12582920 | tf_op jit(solution)/shard_map/ppermute | solution.py:16
  51.2 2.9 %collective-permute-start.6 = (f32[512,256]{1,0:T(8,128)S(1)}, f32[512,256]{1,0:T(8,128)S(1)}, u32[]{:S(2)}, u32[]{:S(2)}) collective-permute-start(f32[512,256]{1,0:T(8,128)S(1)} %get-tuple-element.20), channel_id=1, source_target_pairs={{0,30},{2,0},{4,2},{6,4},{8,6},{10,8},{12,10},{14,12},{16,14},{18,... | collective-permute-start | bytes 1572872 | tf_op jit(solution)/shard_map/ppermute | solution.py:16
  55.1 3.0 %multiply_convert_fusion = bf16[2,8,512,256]{3,2,0,1:T(8,128)(2,1)S(1)} fusion(bf16[2,8,512,256]{3,2,1,0:T(8,128)(2,1)} %param.2, f32[512,256]{1,0:T(8,128)S(1)} %get-tuple-element.20), kind=kLoop, calls=%fused_computation.7 | loop fusion | flops 6291456 | bytes 8912896 | tf_op jit(solution)/shard_map/convert_element_type | solution.py:52
  58.4 17.7 %collective-permute-done.8 = bf16[512,256]{1,0:T(8,128)(2,1)S(1)} collective-permute-done((bf16[512,256]{1,0:T(8,128)(2,1)S(1)}, bf16[512,256]{1,0:T(8,128)(2,1)S(1)}, u32[]{:S(2)}, u32[]{:S(2)}) %collective-permute-start.8) | collective-permute-done | bytes 262176 | tf_op jit(solution)/shard_map/ppermute | solution.py:16
  77.4 3.0 %fusion.2 = bf16[2,8,512,256]{3,2,0,1:T(8,128)(2,1)S(1)} fusion(f32[512,256]{1,0:T(8,128)S(1)} %convert_element_type.75, bf16[2,8,512,256]{3,2,1,0:T(8,128)(2,1)} %bitcast.34), kind=kLoop, calls=%fused_computation.6 | loop fusion | flops 6291456 | bytes 8912896 | tf_op jit(solution)/shard_map/convert_element_type | solution.py:52
  80.5 1.4 collective-permute-start.9
  81.9 2.8 %fusion.24 = f32[1,8,256,256]{3,2,1,0:T(8,128)} fusion(bf16[2,8,512,256]{3,2,0,1:T(8,128)(2,1)S(1)} %multiply_convert_fusion, bf16[1,8,512,256]{3,2,0,1:T(8,128)(2,1)S(1)} %get-tuple-element.24, bf16[1,8,512,256]{3,2,0,1:T(8,128)(2,1)S(1)} %get-tuple-element.23), kind=kOutput, calls=%fused_computation.37 | convolution fusion | flops 1075838976 | bytes 10485760 | tf_op jit(solution)/shard_map/pfwa,pfwb->fab/dot_general | solution.py:47
  86.4 1.4 convolution_bitcast_fusion.3
  87.8 2.9 %convolution_bitcast_fusion.2 = f32[1,8,256,256]{3,2,1,0:T(8,128)} fusion(bf16[2,8,512,256]{3,2,0,1:T(8,128)(2,1)S(1)} %multiply_convert_fusion, bf16[1,8,512,256]{3,2,0,1:T(8,128)(2,1)S(1)} %get-tuple-element.26, bf16[1,8,512,256]{3,2,0,1:T(8,128)(2,1)S(1)} %get-tuple-element.25), kind=kOutput, calls=%fused_computation.40 | convolution fusion | flops 1075838976 | bytes 10485760 | tf_op jit(solution)/shard_map/pfwa,pfwb->fab/dot_general | solution.py:47
  90.6 2.7 %fusion.8 = (bf16[2,8,256,256]{3,2,1,0:T(8,128)(2,1)S(1)}, bf16[2,8,256,256]{3,2,1,0:T(8,128)(2,1)S(1)}) fusion(f32[1,8,256,256]{3,2,1,0:T(8,128)} %fusion.24, f32[1,8,256,256]{3,2,1,0:T(8,128)S(1)} %convolution_bitcast_fusion.4, f32[1,8,256,256]{3,2,1,0:T(8,128)} %convolution_bitcast_fusion.2, f32[1,8,256,256]{3,2,1,0:T(8,128)S(1)} %convolution_bitcast_fusion.3), kind=kLoop, calls=%fused_computation.17 | loop fusion | flops 6291456 | bytes 12582912 | tf_op jit(solution)/shard_map/convert_element_type | solution.py:48
  93.4 8.0 %collective-permute-done.6 = f32[512,256]{1,0:T(8,128)S(1)} collective-permute-done((f32[512,256]{1,0:T(8,128)S(1)}, f32[512,256]{1,0:T(8,128)S(1)}, u32[]{:S(2)}, u32[]{:S(2)}) %collective-permute-start.6) | collective-permute-done | bytes 524320 | tf_op jit(solution)/shard_map/ppermute | solution.py:16
  101.4 3.7 %fusion.32 = f32[1,8,256,256]{3,2,1,0:T(8,128)S(1)} fusion(bf16[2,8,512,256]{3,2,1,0:T(8,128)(2,1)} %bitcast.33, f32[512,256]{1,0:T(8,128)S(1)} %collective-permute-done.6, bf16[1,8,512,256]{3,2,0,1:T(8,128)(2,1)S(1)} %get-tuple-element.26, bf16[1,8,512,256]{3,2,0,1:T(8,128)(2,1)S(1)} %get-tuple-element.25), kind=kOutput, calls=%fused_computation.44 | convolution fusion | flops 1082130432 | bytes 11010048 | tf_op jit(solution)/shard_map/pfwa,pfwb->fab/dot_general | solution.py:47
  105.1 4.0 %fusion.27 = f32[1,8,256,256]{3,2,1,0:T(8,128)S(1)} fusion(bf16[2,8,512,256]{3,2,0,1:T(8,128)(2,1)S(1)} %fusion.2, bf16[2,8,512,256]{3,2,1,0:T(8,128)(2,1)} %bitcast.33, f32[512,256]{1,0:T(8,128)S(1)} %collective-permute-done.6), kind=kOutput, calls=%fused_computation.43 | convolution fusion | flops 1080033280 | bytes 11010048 | tf_op jit(solution)/shard_map/pfwa,pfwb->fab/dot_general | solution.py:46
  109.6 21.5 %collective-permute-done.9 = bf16[2,8,512,256]{3,2,0,1:T(8,128)(2,1)S(1)} collective-permute-done((bf16[2,8,512,256]{3,2,0,1:T(8,128)(2,1)S(1)}, bf16[2,8,512,256]{3,2,0,1:T(8,128)(2,1)S(1)}, u32[]{:S(2)}, u32[]{:S(2)}) %collective-permute-start.9) | collective-permute-done | bytes 4194336 | tf_op jit(solution)/shard_map/ppermute | solution.py:16
  131.1 2.1 %collective-permute-start.10 = (bf16[2,8,256,256]{3,2,1,0:T(8,128)(2,1)S(1)}, bf16[2,8,256,256]{3,2,1,0:T(8,128)(2,1)S(1)}, u32[]{:S(2)}, u32[]{:S(2)}) collective-permute-start(bf16[2,8,256,256]{3,2,1,0:T(8,128)(2,1)S(1)} %fusion.3), channel_id=1, source_target_pairs={{0,2},{2,4},{4,6},{6,8},{8,10},{10,12},{12,14},{14,16},{16,18},{18... | collective-permute-start | bytes 6291464 | tf_op jit(solution)/shard_map/ppermute | solution.py:16
  133.6 4.8 %fusion.37 = f32[1,8,256,256]{3,2,1,0:T(8,128)S(1)} fusion(bf16[2,8,512,256]{3,2,0,1:T(8,128)(2,1)S(1)} %collective-permute-done.9, bf16[2,8,512,256]{3,2,1,0:T(8,128)(2,1)} %bitcast.37, f32[512,256]{1,0:T(8,128)S(1)} %collective-permute-done.12), kind=kOutput, calls=%fused_computation.45 | convolution fusion | flops 1080033280 | bytes 11010048 | tf_op jit(solution)/shard_map/pfwa,pfwb->fab/dot_general | solution.py:46
  138.4 3.7 %fusion.42 = f32[1,8,256,256]{3,2,1,0:T(8,128)S(1)} fusion(bf16[2,8,512,256]{3,2,1,0:T(8,128)(2,1)} %bitcast.37, f32[512,256]{1,0:T(8,128)S(1)} %collective-permute-done.12, bf16[1,8,512,256]{3,2,0,1:T(8,128)(2,1)S(1)} %get-tuple-element.22, bf16[1,8,512,256]{3,2,0,1:T(8,128)(2,1)S(1)} %get-tuple-element.21), kind=kOutput, calls=%fused_computation.46 | convolution fusion | flops 1082130432 | bytes 11010048 | tf_op jit(solution)/shard_map/pfwa,pfwb->fab/dot_general | solution.py:47
  142.6 1.4 collective-permute-start.13
  144.0 3.1 %convolution_bitcast_fusion = f32[1,1,8,256,256]{4,3,2,1,0:T(8,128)S(1)} fusion(bf16[2,8,512,256]{3,2,0,1:T(8,128)(2,1)S(1)} %multiply_convert_fusion, bf16[1,8,512,256]{3,2,0,1:T(8,128)(2,1)} %copy-done, bf16[1,8,512,256]{3,2,0,1:T(8,128)(2,1)S(1)} %get-tuple-element.21), kind=kOutput, calls=%fused_computation.38 | convolution fusion | flops 1075838976 | bytes 10485760 | tf_op jit(solution)/shard_map/pfwa,pfwb->fab/dot_general | solution.py:47
  149.1 3.9 %maximum_maximum_fusion = bf16[4,2,8,256,256]{4,3,2,1,0:T(8,128)(2,1)} fusion(bf16[1,2,8,256,256]{4,3,2,1,0:T(8,128)(2,1)S(1)} %fusion.10, bf16[1,2,8,256,256]{4,3,2,1,0:T(8,128)(2,1)S(1)} %bitcast.69, bf16[1,2,8,256,256]{4,3,2,1,0:T(8,128)(2,1)S(1)} %bitcast.68, bf16[4]{0:T(256)(128)(2,1)S(1)} %pad.5.clone), kind=kLoop, calls=%fused_computation | loop fusion | flops 12582912 | bytes 14680072 | tf_op jit(solution)/shard_map/stack | solution.py:85
  153.0 8.2 %collective-permute-done.10 = bf16[2,8,256,256]{3,2,1,0:T(8,128)(2,1)S(1)} collective-permute-done((bf16[2,8,256,256]{3,2,1,0:T(8,128)(2,1)S(1)}, bf16[2,8,256,256]{3,2,1,0:T(8,128)(2,1)S(1)}, u32[]{:S(2)}, u32[]{:S(2)}) %collective-permute-start.10) | collective-permute-done | bytes 2097184 | tf_op jit(solution)/shard_map/ppermute | solution.py:16
  161.2 2.0 %bitcast_dynamic-update-slice_fusion = bf16[4,2,8,256,256]{4,3,2,1,0:T(8,128)(2,1)} fusion(bf16[4,2,8,256,256]{4,3,2,1,0:T(8,128)(2,1)} %maximum_maximum_fusion, bf16[2,8,256,256]{3,2,1,0:T(8,128)(2,1)S(1)} %collective-permute-done.10, bf16[2,8,256,256]{3,2,1,0:T(8,128)(2,1)S(1)} %collective-permute-done.13, pred[]{:T(512)S(6)} %eq.19), kind=kLoop, calls=%fused_computation.35 | loop fusion | flops 1048576 | bytes 6291457 | tf_op jit(solution)/shard_map/dynamic_update_slice | solution.py:88
  (37 shorter events, 9.8 us)
Async XLA Ops:
  3.1 48.0 %copy-start.1 = (s32[512,256]{1,0:T(8,128)S(1)}, s32[512,256]{1,0:T(8,128)}, u32[]{:S(2)}) copy-start(s32[512,256]{1,0:T(8,128)} %param.3) | copy-start | bytes 1572868
  3.1 15.3 %collective-permute-start = (f32[512,256]{1,0:T(8,128)S(1)}, f32[512,256]{1,0:T(8,128)S(1)}, u32[]{:S(2)}, u32[]{:S(2)}) collective-permute-start(f32[512,256]{1,0:T(8,128)S(1)} %multiply_reduce_fusion), channel_id=1, source_target_pairs={{0,32},{32,0},{64,96},{96,64},{128,160},{160,128},{192,224},{224,1... | collective-permute-start | bytes 1572872 | tf_op jit(solution)/shard_map/ppermute | solution.py:61
  18.6 8.8 %collective-permute-start.2 = (f32[65536]{0:T(1024)S(1)}, f32[65536]{0:T(1024)S(1)}, u32[]{:S(2)}, u32[]{:S(2)}) collective-permute-start(f32[65536]{0:T(1024)S(1)} %bitcast.71), channel_id=1, source_target_pairs={{0,128},{32,160},{64,192},{96,224},{128,0},{160,32},{192,64},{224,... | collective-permute-start | bytes 786440 | tf_op jit(solution)/shard_map/ppermute | solution.py:34
  22.0 55.4 %collective-permute-start.7 = (bf16[8192,256]{1,0:T(8,128)(2,1)}, bf16[8192,256]{1,0:T(8,128)(2,1)}, u32[]{:S(2)}, u32[]{:S(2)}) collective-permute-start(bf16[8192,256]{1,0:T(8,128)(2,1)} %bitcast.65), channel_id=1, source_target_pairs={{0,1},{1,2},{2,3},{3,4},{4,5},{5,6},{6,7},{7,8},{8,9},{9,10},{10,1... | collective-permute-start | bytes 12582920 | tf_op jit(solution)/shard_map/ppermute | solution.py:16
  27.4 5.1 %collective-permute-start.3 = (f32[32768]{0:T(1024)S(1)}, f32[32768]{0:T(1024)S(1)}, u32[]{:S(2)}, u32[]{:S(2)}) collective-permute-start(f32[32768]{0:T(1024)S(1)} %slice_select_fusion), channel_id=1, source_target_pairs={{0,64},{32,96},{64,0},{96,32},{128,192},{160,224},{192,128},{224,1... | collective-permute-start | bytes 393224 | tf_op jit(solution)/shard_map/ppermute | solution.py:34
  32.5 5.1 %collective-permute-start.4 = (f32[32768]{0:T(1024)S(1)}, f32[32768]{0:T(1024)S(1)}, u32[]{:S(2)}, u32[]{:S(2)}) collective-permute-start(f32[32768]{0:T(1024)S(1)} %select_add_fusion), channel_id=1, source_target_pairs={{0,64},{32,96},{64,0},{96,32},{128,192},{160,224},{192,128},{224,1... | collective-permute-start | bytes 393224 | tf_op jit(solution)/shard_map/ppermute | solution.py:39
  37.6 13.4 %collective-permute-start.5 = (f32[65536]{0:T(1024)S(1)}, f32[65536]{0:T(1024)S(1)}, u32[]{:S(2)}, u32[]{:S(2)}) collective-permute-start(f32[65536]{0:T(1024)S(1)} %maximum_select_fusion.2), channel_id=1, source_target_pairs={{0,128},{32,160},{64,192},{96,224},{128,0},{160,32},{192,64},{224,... | collective-permute-start | bytes 786440 | tf_op jit(solution)/shard_map/ppermute | solution.py:39
  41.2 60.2 %collective-permute-start.1 = (bf16[8192,256]{1,0:T(8,128)(2,1)}, bf16[8192,256]{1,0:T(8,128)(2,1)}, u32[]{:S(2)}, u32[]{:S(2)}) collective-permute-start(bf16[8192,256]{1,0:T(8,128)(2,1)} %bitcast.66), channel_id=1, source_target_pairs={{0,30},{2,0},{4,2},{6,4},{8,6},{10,8},{12,10},{14,12},{16,14},{18,... | collective-permute-start | bytes 12582920 | tf_op jit(solution)/shard_map/ppermute | solution.py:16
  49.6 84.0 %collective-permute-start.11 = (bf16[8192,256]{1,0:T(8,128)(2,1)}, bf16[8192,256]{1,0:T(8,128)(2,1)}, u32[]{:S(2)}, u32[]{:S(2)}) collective-permute-start(bf16[8192,256]{1,0:T(8,128)(2,1)} %bitcast.67), channel_id=1, source_target_pairs={{1,0},{3,2},{5,4},{7,6},{9,8},{11,10},{13,12},{15,14},{17,16},{19,... | collective-permute-start | bytes 12582920 | tf_op jit(solution)/shard_map/ppermute | solution.py:16
  51.2 50.2 %collective-permute-start.6 = (f32[512,256]{1,0:T(8,128)S(1)}, f32[512,256]{1,0:T(8,128)S(1)}, u32[]{:S(2)}, u32[]{:S(2)}) collective-permute-start(f32[512,256]{1,0:T(8,128)S(1)} %get-tuple-element.20), channel_id=1, source_target_pairs={{0,30},{2,0},{4,2},{6,4},{8,6},{10,8},{12,10},{14,12},{16,14},{18,... | collective-permute-start | bytes 1572872 | tf_op jit(solution)/shard_map/ppermute | solution.py:16
  54.2 21.9 %collective-permute-start.8 = (bf16[512,256]{1,0:T(8,128)(2,1)S(1)}, bf16[512,256]{1,0:T(8,128)(2,1)S(1)}, u32[]{:S(2)}, u32[]{:S(2)}) collective-permute-start(bf16[512,256]{1,0:T(8,128)(2,1)S(1)} %get-tuple-element.19), channel_id=1, source_target_pairs={{0,1},{1,2},{2,3},{3,4},{4,5},{5,6},{6,7},{7,8},{8,9},{9,10},{10,1... | collective-permute-start | bytes 786440 | tf_op jit(solution)/shard_map/ppermute | solution.py:16
  76.1 57.5 %collective-permute-start.12 = (f32[512,256]{1,0:T(8,128)S(1)}, f32[512,256]{1,0:T(8,128)S(1)}, u32[]{:S(2)}, u32[]{:S(2)}) collective-permute-start(f32[512,256]{1,0:T(8,128)S(1)} %get-tuple-element.20), channel_id=1, source_target_pairs={{1,0},{3,2},{5,4},{7,6},{9,8},{11,10},{13,12},{15,14},{17,16},{19,... | collective-permute-start | bytes 1572872 | tf_op jit(solution)/shard_map/ppermute | solution.py:16
  80.5 50.7 %collective-permute-start.9 = (bf16[2,8,512,256]{3,2,0,1:T(8,128)(2,1)S(1)}, bf16[2,8,512,256]{3,2,0,1:T(8,128)(2,1)S(1)}, u32[]{:S(2)}, u32[]{:S(2)}) collective-permute-start(bf16[2,8,512,256]{3,2,0,1:T(8,128)(2,1)S(1)} %fusion.2), channel_id=1, source_target_pairs={{0,1},{1,2},{2,3},{3,4},{4,5},{5,6},{6,7},{7,8},{8,9},{9,10},{10,1... | collective-permute-start | bytes 12582920 | tf_op jit(solution)/shard_map/ppermute | solution.py:16
  131.1 30.0 %collective-permute-start.10 = (bf16[2,8,256,256]{3,2,1,0:T(8,128)(2,1)S(1)}, bf16[2,8,256,256]{3,2,1,0:T(8,128)(2,1)S(1)}, u32[]{:S(2)}, u32[]{:S(2)}) collective-permute-start(bf16[2,8,256,256]{3,2,1,0:T(8,128)(2,1)S(1)} %fusion.3), channel_id=1, source_target_pairs={{0,2},{2,4},{4,6},{6,8},{8,10},{10,12},{12,14},{14,16},{16,18},{18... | collective-permute-start | bytes 6291464 | tf_op jit(solution)/shard_map/ppermute | solution.py:16
  133.5 4.8 %copy-start = (bf16[1,8,512,256]{3,2,0,1:T(8,128)(2,1)}, bf16[1,8,512,256]{3,2,0,1:T(8,128)(2,1)S(1)}, u32[]{:S(2)}) copy-start(bf16[1,8,512,256]{3,2,0,1:T(8,128)(2,1)S(1)} %get-tuple-element.22) | copy-start | bytes 6291460
  142.6 18.6 %collective-permute-start.13 = (bf16[2,8,256,256]{3,2,1,0:T(8,128)(2,1)S(1)}, bf16[2,8,256,256]{3,2,1,0:T(8,128)(2,1)S(1)}, u32[]{:S(2)}, u32[]{:S(2)}) collective-permute-start(bf16[2,8,256,256]{3,2,1,0:T(8,128)(2,1)S(1)} %fusion.11), channel_id=1, source_target_pairs={{0,1},{2,3},{4,5},{6,7},{8,9},{10,11},{12,13},{14,15},{16,17},{18,... | collective-permute-start | bytes 6291464 | tf_op jit(solution)/shard_map/ppermute | solution.py:16

commit v14 on v13

--- a/solution.py
+++ b/solution.py
@@ -54,11 +54,16 @@
 
 def shards(spectra, valid_mask):
     values = spectra.astype(jnp.float32)
-    partial_energy = jnp.sum(values * values, axis=(0, 1))
+    band_pairs = [(s, s ^ 1) for s in range(lax.axis_size("band"))]
+    window_half = spectra.shape[2] // 2
+    halves = []
+    for part in (values[:, :, :window_half], values[:, :, window_half:]):
+        partial = jnp.sum(part * part, axis=(0, 1))
+        halves.append(partial + lax.ppermute(partial, "band", band_pairs))
+    partial_energy = jnp.concatenate(halves, axis=0)
     total_bins = spectra.shape[1] * lax.axis_size("band")
     scale = 1.0 / math.sqrt(spectra.shape[2])
     even = lax.axis_index("chan") % 2 == 0
-    partial_energy = partial_energy + lax.ppermute(partial_energy, "band", [(s, s ^ 1) for s in range(lax.axis_size("band"))])
     spectra, partial_energy = lax.optimization_barrier((spectra, partial_energy))
     flat_spectra = spectra.reshape(-1, spectra.shape[-1])
     raw_near = moved(flat_spectra, "chan", 1).reshape(spectra.shape)

time: 164 us -> 164 us (level)
    convert_element_type x0 -> x1, other arithmetic: none -> 3.08 us  [shards(): values = spectra.astype(jnp.float32)]
    reduce_sum x1, other arithmetic: 3.06 us -> 0.64 us  [shards(): partial = jnp.sum(part * part, axis=(0, 1))]
    ppermute x1 -> x2, waiting for transfers between devices: 12.9 us -> 11.6 us  [shards(): halves.append(partial + lax.ppermute(partial, 'band', band_pairs))]
    ppermute x1 -> x2, starting transfers between devices: 2.33 us -> 3.62 us  [shards(): halves.append(partial + lax.ppermute(partial, 'band', band_pairs))]
  transfers between devices with their start and end apart: 14 -> 15, of which waited for: 8 -> 9; matrix products, arithmetic and copies ran while one was open for 28% -> 27% of each run, Pallas kernels for 0% -> 0%
where the time goes in v14:
time: 164 us
  waiting for transfers between devices  79 us (48%)
  starting transfers between devices  33.6 us (20%)
  matrix products  29.1 us (18%)
  other arithmetic  21.3 us (13%)
    ppermute x9, waiting for transfers between devices, moved(): return lax.ppermute(value, axis, pairs)  55.3 us
    ppermute x9, starting transfers between devices, moved(): return lax.ppermute(value, axis, pairs)  19.9 us
    dot_general x5, matrix products, cross_block(): jnp.einsum('pfwa,pfwb->fab', own_block, flipped, preferred_element_type=j...  16.1 us
    dot_general x5, matrix products, cross_block(): jnp.einsum('pfwa,pfwb->fab', own_block, partner, preferred_element_type=j...  13 us
    ppermute x2, waiting for transfers between devices, shards(): halves.append(partial + lax.ppermute(partial, 'band', band_pairs))  11.6 us
    ppermute x2, waiting for transfers between devices, band_sum(): got = lax.ppermute(jnp.where(bit == 0, high, low), axis, pairs)  8.64 us
    convert_element_type x2, other arithmetic, whiten(): return (raw.astype(jnp.float32) * gain).astype(jnp.bfloat16)  6.07 us
    ppermute x2, starting transfers between devices, band_sum(): got = lax.ppermute(flat, axis, pairs)  5.19 us
  transfers between devices with their start and end apart: 15, of which 9 were waited for; matrix products, arithmetic and copies ran while one was open for 27% of the time, Pallas kernels for 0%

profile of v14, /device:TPU:4, one launch (start us, length us, event | category | flops | bytes accessed | tf_op | source)
XLA Modules:
  0.0 163.8 jit_solution(17816396164598094760)
XLA Ops:
  0.0 3.1 %convert_element_type.67 = f32[2,8,512,256]{3,2,1,0:T(8,128)S(1)} convert(bf16[2,8,512,256]{3,2,1,0:T(8,128)(2,1)} %param.2) | non-fusion elementwise | flops 2097152 | bytes 12582912 | tf_op jit(solution)/shard_map/convert_element_type | solution.py:56
  3.7 2.3 %collective-permute-start.1 = (f32[256,256]{1,0:T(8,128)S(1)}, f32[256,256]{1,0:T(8,128)S(1)}, u32[]{:S(2)}, u32[]{:S(2)}) collective-permute-start(f32[256,256]{1,0:T(8,128)S(1)} %get-tuple-element.20), channel_id=1, source_target_pairs={{0,32},{32,0},{64,96},{96,64},{128,160},{160,128},{192,224},{224,1... | collective-permute-start | bytes 786440 | tf_op jit(solution)/shard_map/ppermute | solution.py:62
  7.4 7.2 %collective-permute-done.1 = f32[256,256]{1,0:T(8,128)S(1)} collective-permute-done((f32[256,256]{1,0:T(8,128)S(1)}, f32[256,256]{1,0:T(8,128)S(1)}, u32[]{:S(2)}, u32[]{:S(2)}) %collective-permute-start.1) | collective-permute-done | bytes 262176 | tf_op jit(solution)/shard_map/ppermute | solution.py:62
  14.6 4.4 %collective-permute-done = f32[256,256]{1,0:T(8,128)S(1)} collective-permute-done((f32[256,256]{1,0:T(8,128)S(1)}, f32[256,256]{1,0:T(8,128)S(1)}, u32[]{:S(2)}, u32[]{:S(2)}) %collective-permute-start) | collective-permute-done | bytes 262176 | tf_op jit(solution)/shard_map/ppermute | solution.py:62
  19.3 3.3 %collective-permute-start.3 = (f32[65536]{0:T(1024)S(1)}, f32[65536]{0:T(1024)S(1)}, u32[]{:S(2)}, u32[]{:S(2)}) collective-permute-start(f32[65536]{0:T(1024)S(1)} %bitcast.71), channel_id=1, source_target_pairs={{0,128},{32,160},{64,192},{96,224},{128,0},{160,32},{192,64},{224,... | collective-permute-start | bytes 786440 | tf_op jit(solution)/shard_map/ppermute | solution.py:34
  22.8 5.3 %collective-permute-done.3 = f32[65536]{0:T(1024)S(1)} collective-permute-done((f32[65536]{0:T(1024)S(1)}, f32[65536]{0:T(1024)S(1)}, u32[]{:S(2)}, u32[]{:S(2)}) %collective-permute-start.3) | collective-permute-done | bytes 262176 | tf_op jit(solution)/shard_map/ppermute | solution.py:34
  28.1 1.7 %collective-permute-start.4 = (f32[32768]{0:T(1024)S(1)}, f32[32768]{0:T(1024)S(1)}, u32[]{:S(2)}, u32[]{:S(2)}) collective-permute-start(f32[32768]{0:T(1024)S(1)} %slice_select_fusion), channel_id=1, source_target_pairs={{0,64},{32,96},{64,0},{96,32},{128,192},{160,224},{192,128},{224,1... | collective-permute-start | bytes 393224 | tf_op jit(solution)/shard_map/ppermute | solution.py:34
  29.7 3.4 %collective-permute-done.4 = f32[32768]{0:T(1024)S(1)} collective-permute-done((f32[32768]{0:T(1024)S(1)}, f32[32768]{0:T(1024)S(1)}, u32[]{:S(2)}, u32[]{:S(2)}) %collective-permute-start.4) | collective-permute-done | bytes 131104 | tf_op jit(solution)/shard_map/ppermute | solution.py:34
  33.2 1.7 %collective-permute-start.5 = (f32[32768]{0:T(1024)S(1)}, f32[32768]{0:T(1024)S(1)}, u32[]{:S(2)}, u32[]{:S(2)}) collective-permute-start(f32[32768]{0:T(1024)S(1)} %select_add_fusion), channel_id=1, source_target_pairs={{0,64},{32,96},{64,0},{96,32},{128,192},{160,224},{192,128},{224,1... | collective-permute-start | bytes 393224 | tf_op jit(solution)/shard_map/ppermute | solution.py:39
  34.8 3.4 %collective-permute-done.5 = f32[32768]{0:T(1024)S(1)} collective-permute-done((f32[32768]{0:T(1024)S(1)}, f32[32768]{0:T(1024)S(1)}, u32[]{:S(2)}, u32[]{:S(2)}) %collective-permute-start.5) | collective-permute-done | bytes 131104 | tf_op jit(solution)/shard_map/ppermute | solution.py:39
  38.2 3.5 %collective-permute-start.6 = (f32[65536]{0:T(1024)S(1)}, f32[65536]{0:T(1024)S(1)}, u32[]{:S(2)}, u32[]{:S(2)}) collective-permute-start(f32[65536]{0:T(1024)S(1)} %maximum_select_fusion.2), channel_id=1, source_target_pairs={{0,128},{32,160},{64,192},{96,224},{128,0},{160,32},{192,64},{224,... | collective-permute-start | bytes 786440 | tf_op jit(solution)/shard_map/ppermute | solution.py:39
  41.8 8.4 %collective-permute-start.2 = (bf16[8192,256]{1,0:T(8,128)(2,1)}, bf16[8192,256]{1,0:T(8,128)(2,1)}, u32[]{:S(2)}, u32[]{:S(2)}) collective-permute-start(bf16[8192,256]{1,0:T(8,128)(2,1)} %bitcast.66), channel_id=1, source_target_pairs={{0,30},{2,0},{4,2},{6,4},{8,6},{10,8},{12,10},{14,12},{16,14},{18,... | collective-permute-start | bytes 12582920 | tf_op jit(solution)/shard_map/ppermute | solution.py:16
  51.9 2.9 %collective-permute-start.7 = (f32[512,256]{1,0:T(8,128)S(1)}, f32[512,256]{1,0:T(8,128)S(1)}, u32[]{:S(2)}, u32[]{:S(2)}) collective-permute-start(f32[512,256]{1,0:T(8,128)S(1)} %get-tuple-element.22), channel_id=1, source_target_pairs={{0,30},{2,0},{4,2},{6,4},{8,6},{10,8},{12,10},{14,12},{16,14},{18,... | collective-permute-start | bytes 1572872 | tf_op jit(solution)/shard_map/ppermute | solution.py:16
  55.8 3.0 %multiply_convert_fusion = bf16[2,8,512,256]{3,2,0,1:T(8,128)(2,1)S(1)} fusion(bf16[2,8,512,256]{3,2,1,0:T(8,128)(2,1)} %param.2, f32[512,256]{1,0:T(8,128)S(1)} %get-tuple-element.22), kind=kLoop, calls=%fused_computation.7 | loop fusion | flops 6291456 | bytes 8912896 | tf_op jit(solution)/shard_map/convert_element_type | solution.py:52
  59.1 17.6 %collective-permute-done.9 = bf16[512,256]{1,0:T(8,128)(2,1)S(1)} collective-permute-done((bf16[512,256]{1,0:T(8,128)(2,1)S(1)}, bf16[512,256]{1,0:T(8,128)(2,1)S(1)}, u32[]{:S(2)}, u32[]{:S(2)}) %collective-permute-start.9) | collective-permute-done | bytes 262176 | tf_op jit(solution)/shard_map/ppermute | solution.py:16
  78.1 3.0 %fusion.2 = bf16[2,8,512,256]{3,2,0,1:T(8,128)(2,1)S(1)} fusion(f32[512,256]{1,0:T(8,128)S(1)} %convert_element_type.75, bf16[2,8,512,256]{3,2,1,0:T(8,128)(2,1)} %bitcast.34), kind=kLoop, calls=%fused_computation.6 | loop fusion | flops 6291456 | bytes 8912896 | tf_op jit(solution)/shard_map/convert_element_type | solution.py:52
  81.1 1.4 collective-permute-start.10
  82.5 2.8 %fusion.26 = f32[1,8,256,256]{3,2,1,0:T(8,128)} fusion(bf16[2,8,512,256]{3,2,0,1:T(8,128)(2,1)S(1)} %multiply_convert_fusion, bf16[1,8,512,256]{3,2,0,1:T(8,128)(2,1)S(1)} %get-tuple-element.26, bf16[1,8,512,256]{3,2,0,1:T(8,128)(2,1)S(1)} %get-tuple-element.25), kind=kOutput, calls=%fused_computation.40 | convolution fusion | flops 1075838976 | bytes 10485760 | tf_op jit(solution)/shard_map/pfwa,pfwb->fab/dot_general | solution.py:47
  88.4 2.9 %convolution_bitcast_fusion.2 = f32[1,8,256,256]{3,2,1,0:T(8,128)} fusion(bf16[2,8,512,256]{3,2,0,1:T(8,128)(2,1)S(1)} %multiply_convert_fusion, bf16[1,8,512,256]{3,2,0,1:T(8,128)(2,1)S(1)} %get-tuple-element.28, bf16[1,8,512,256]{3,2,0,1:T(8,128)(2,1)S(1)} %get-tuple-element.27), kind=kOutput, calls=%fused_computation.43 | convolution fusion | flops 1075838976 | bytes 10485760 | tf_op jit(solution)/shard_map/pfwa,pfwb->fab/dot_general | solution.py:47
  91.3 2.7 %fusion.10 = (bf16[2,8,256,256]{3,2,1,0:T(8,128)(2,1)S(1)}, bf16[2,8,256,256]{3,2,1,0:T(8,128)(2,1)S(1)}) fusion(f32[1,8,256,256]{3,2,1,0:T(8,128)} %fusion.26, f32[1,8,256,256]{3,2,1,0:T(8,128)S(1)} %convolution_bitcast_fusion.4, f32[1,8,256,256]{3,2,1,0:T(8,128)} %convolution_bitcast_fusion.2, f32[1,8,256,256]{3,2,1,0:T(8,128)S(1)} %convolution_bitcast_fusion.3), kind=kLoop, calls=%fused_computation.20 | loop fusion | flops 6291456 | bytes 12582912 | tf_op jit(solution)/shard_map/convert_element_type | solution.py:48
  94.0 8.0 %collective-permute-done.7 = f32[512,256]{1,0:T(8,128)S(1)} collective-permute-done((f32[512,256]{1,0:T(8,128)S(1)}, f32[512,256]{1,0:T(8,128)S(1)}, u32[]{:S(2)}, u32[]{:S(2)}) %collective-permute-start.7) | collective-permute-done | bytes 524320 | tf_op jit(solution)/shard_map/ppermute | solution.py:16
  102.1 3.7 %fusion.34 = f32[1,8,256,256]{3,2,1,0:T(8,128)S(1)} fusion(bf16[2,8,512,256]{3,2,1,0:T(8,128)(2,1)} %bitcast.33, f32[512,256]{1,0:T(8,128)S(1)} %collective-permute-done.7, bf16[1,8,512,256]{3,2,0,1:T(8,128)(2,1)S(1)} %get-tuple-element.28, bf16[1,8,512,256]{3,2,0,1:T(8,128)(2,1)S(1)} %get-tuple-element.27), kind=kOutput, calls=%fused_computation.47 | convolution fusion | flops 1082130432 | bytes 11010048 | tf_op jit(solution)/shard_map/pfwa,pfwb->fab/dot_general | solution.py:47
  105.7 4.0 %fusion.29 = f32[1,8,256,256]{3,2,1,0:T(8,128)S(1)} fusion(bf16[2,8,512,256]{3,2,0,1:T(8,128)(2,1)S(1)} %fusion.2, bf16[2,8,512,256]{3,2,1,0:T(8,128)(2,1)} %bitcast.33, f32[512,256]{1,0:T(8,128)S(1)} %collective-permute-done.7), kind=kOutput, calls=%fused_computation.46 | convolution fusion | flops 1080033280 | bytes 11010048 | tf_op jit(solution)/shard_map/pfwa,pfwb->fab/dot_general | solution.py:46
  110.3 21.5 %collective-permute-done.10 = bf16[2,8,512,256]{3,2,0,1:T(8,128)(2,1)S(1)} collective-permute-done((bf16[2,8,512,256]{3,2,0,1:T(8,128)(2,1)S(1)}, bf16[2,8,512,256]{3,2,0,1:T(8,128)(2,1)S(1)}, u32[]{:S(2)}, u32[]{:S(2)}) %collective-permute-start.10) | collective-permute-done | bytes 4194336 | tf_op jit(solution)/shard_map/ppermute | solution.py:16
  131.8 2.1 %collective-permute-start.11 = (bf16[2,8,256,256]{3,2,1,0:T(8,128)(2,1)S(1)}, bf16[2,8,256,256]{3,2,1,0:T(8,128)(2,1)S(1)}, u32[]{:S(2)}, u32[]{:S(2)}) collective-permute-start(bf16[2,8,256,256]{3,2,1,0:T(8,128)(2,1)S(1)} %fusion.5), channel_id=1, source_target_pairs={{0,2},{2,4},{4,6},{6,8},{8,10},{10,12},{12,14},{14,16},{16,18},{18... | collective-permute-start | bytes 6291464 | tf_op jit(solution)/shard_map/ppermute | solution.py:16
  134.2 4.8 %fusion.39 = f32[1,8,256,256]{3,2,1,0:T(8,128)S(1)} fusion(bf16[2,8,512,256]{3,2,0,1:T(8,128)(2,1)S(1)} %collective-permute-done.10, bf16[2,8,512,256]{3,2,1,0:T(8,128)(2,1)} %bitcast.37, f32[512,256]{1,0:T(8,128)S(1)} %collective-permute-done.13), kind=kOutput, calls=%fused_computation.48 | convolution fusion | flops 1080033280 | bytes 11010048 | tf_op jit(solution)/shard_map/pfwa,pfwb->fab/dot_general | solution.py:46
  139.0 3.7 %fusion.44 = f32[1,8,256,256]{3,2,1,0:T(8,128)S(1)} fusion(bf16[2,8,512,256]{3,2,1,0:T(8,128)(2,1)} %bitcast.37, f32[512,256]{1,0:T(8,128)S(1)} %collective-permute-done.13, bf16[1,8,512,256]{3,2,0,1:T(8,128)(2,1)S(1)} %get-tuple-element.24, bf16[1,8,512,256]{3,2,0,1:T(8,128)(2,1)S(1)} %get-tuple-element.23), kind=kOutput, calls=%fused_computation.49 | convolution fusion | flops 1082130432 | bytes 11010048 | tf_op jit(solution)/shard_map/pfwa,pfwb->fab/dot_general | solution.py:47
  143.3 1.4 collective-permute-start.14
  144.7 3.1 %convolution_bitcast_fusion = f32[1,1,8,256,256]{4,3,2,1,0:T(8,128)S(1)} fusion(bf16[2,8,512,256]{3,2,0,1:T(8,128)(2,1)S(1)} %multiply_convert_fusion, bf16[1,8,512,256]{3,2,0,1:T(8,128)(2,1)} %copy-done, bf16[1,8,512,256]{3,2,0,1:T(8,128)(2,1)S(1)} %get-tuple-element.23), kind=kOutput, calls=%fused_computation.41 | convolution fusion | flops 1075838976 | bytes 10485760 | tf_op jit(solution)/shard_map/pfwa,pfwb->fab/dot_general | solution.py:47
  149.8 3.9 %maximum_maximum_fusion = bf16[4,2,8,256,256]{4,3,2,1,0:T(8,128)(2,1)} fusion(bf16[1,2,8,256,256]{4,3,2,1,0:T(8,128)(2,1)S(1)} %fusion.12, bf16[1,2,8,256,256]{4,3,2,1,0:T(8,128)(2,1)S(1)} %bitcast.69, bf16[1,2,8,256,256]{4,3,2,1,0:T(8,128)(2,1)S(1)} %bitcast.68, bf16[4]{0:T(256)(128)(2,1)S(1)} %pad.5.clone), kind=kLoop, calls=%fused_computation | loop fusion | flops 12582912 | bytes 14680072 | tf_op jit(solution)/shard_map/stack | solution.py:90
  153.7 8.2 %collective-permute-done.11 = bf16[2,8,256,256]{3,2,1,0:T(8,128)(2,1)S(1)} collective-permute-done((bf16[2,8,256,256]{3,2,1,0:T(8,128)(2,1)S(1)}, bf16[2,8,256,256]{3,2,1,0:T(8,128)(2,1)S(1)}, u32[]{:S(2)}, u32[]{:S(2)}) %collective-permute-start.11) | collective-permute-done | bytes 2097184 | tf_op jit(solution)/shard_map/ppermute | solution.py:16
  161.8 2.0 %bitcast_dynamic-update-slice_fusion = bf16[4,2,8,256,256]{4,3,2,1,0:T(8,128)(2,1)} fusion(bf16[4,2,8,256,256]{4,3,2,1,0:T(8,128)(2,1)} %maximum_maximum_fusion, bf16[2,8,256,256]{3,2,1,0:T(8,128)(2,1)S(1)} %collective-permute-done.11, bf16[2,8,256,256]{3,2,1,0:T(8,128)(2,1)S(1)} %collective-permute-done.14, pred[]{:T(512)S(6)} %eq.19), kind=kLoop, calls=%fused_computation.38 | loop fusion | flops 1048576 | bytes 6291457 | tf_op jit(solution)/shard_map/dynamic_update_slice | solution.py:93
  (42 shorter events, 13.1 us)
Async XLA Ops:
  3.7 10.8 %collective-permute-start.1 = (f32[256,256]{1,0:T(8,128)S(1)}, f32[256,256]{1,0:T(8,128)S(1)}, u32[]{:S(2)}, u32[]{:S(2)}) collective-permute-start(f32[256,256]{1,0:T(8,128)S(1)} %get-tuple-element.20), channel_id=1, source_target_pairs={{0,32},{32,0},{64,96},{96,64},{128,160},{160,128},{192,224},{224,1... | collective-permute-start | bytes 786440 | tf_op jit(solution)/shard_map/ppermute | solution.py:62
  6.1 12.9 %collective-permute-start = (f32[256,256]{1,0:T(8,128)S(1)}, f32[256,256]{1,0:T(8,128)S(1)}, u32[]{:S(2)}, u32[]{:S(2)}) collective-permute-start(f32[256,256]{1,0:T(8,128)S(1)} %get-tuple-element.19), channel_id=1, source_target_pairs={{0,32},{32,0},{64,96},{96,64},{128,160},{160,128},{192,224},{224,1... | collective-permute-start | bytes 786440 | tf_op jit(solution)/shard_map/ppermute | solution.py:62
  7.3 44.4 %copy-start.1 = (s32[512,256]{1,0:T(8,128)S(1)}, s32[512,256]{1,0:T(8,128)}, u32[]{:S(2)}) copy-start(s32[512,256]{1,0:T(8,128)} %param.3) | copy-start | bytes 1572868
  19.3 8.8 %collective-permute-start.3 = (f32[65536]{0:T(1024)S(1)}, f32[65536]{0:T(1024)S(1)}, u32[]{:S(2)}, u32[]{:S(2)}) collective-permute-start(f32[65536]{0:T(1024)S(1)} %bitcast.71), channel_id=1, source_target_pairs={{0,128},{32,160},{64,192},{96,224},{128,0},{160,32},{192,64},{224,... | collective-permute-start | bytes 786440 | tf_op jit(solution)/shard_map/ppermute | solution.py:34
  22.7 55.4 %collective-permute-start.8 = (bf16[8192,256]{1,0:T(8,128)(2,1)}, bf16[8192,256]{1,0:T(8,128)(2,1)}, u32[]{:S(2)}, u32[]{:S(2)}) collective-permute-start(bf16[8192,256]{1,0:T(8,128)(2,1)} %bitcast.65), channel_id=1, source_target_pairs={{0,1},{1,2},{2,3},{3,4},{4,5},{5,6},{6,7},{7,8},{8,9},{9,10},{10,1... | collective-permute-start | bytes 12582920 | tf_op jit(solution)/shard_map/ppermute | solution.py:16
  28.1 5.1 %collective-permute-start.4 = (f32[32768]{0:T(1024)S(1)}, f32[32768]{0:T(1024)S(1)}, u32[]{:S(2)}, u32[]{:S(2)}) collective-permute-start(f32[32768]{0:T(1024)S(1)} %slice_select_fusion), channel_id=1, source_target_pairs={{0,64},{32,96},{64,0},{96,32},{128,192},{160,224},{192,128},{224,1... | collective-permute-start | bytes 393224 | tf_op jit(solution)/shard_map/ppermute | solution.py:34
  33.2 5.1 %collective-permute-start.5 = (f32[32768]{0:T(1024)S(1)}, f32[32768]{0:T(1024)S(1)}, u32[]{:S(2)}, u32[]{:S(2)}) collective-permute-start(f32[32768]{0:T(1024)S(1)} %select_add_fusion), channel_id=1, source_target_pairs={{0,64},{32,96},{64,0},{96,32},{128,192},{160,224},{192,128},{224,1... | collective-permute-start | bytes 393224 | tf_op jit(solution)/shard_map/ppermute | solution.py:39
  38.2 13.4 %collective-permute-start.6 = (f32[65536]{0:T(1024)S(1)}, f32[65536]{0:T(1024)S(1)}, u32[]{:S(2)}, u32[]{:S(2)}) collective-permute-start(f32[65536]{0:T(1024)S(1)} %maximum_select_fusion.2), channel_id=1, source_target_pairs={{0,128},{32,160},{64,192},{96,224},{128,0},{160,32},{192,64},{224,... | collective-permute-start | bytes 786440 | tf_op jit(solution)/shard_map/ppermute | solution.py:39
  41.8 60.2 %collective-permute-start.2 = (bf16[8192,256]{1,0:T(8,128)(2,1)}, bf16[8192,256]{1,0:T(8,128)(2,1)}, u32[]{:S(2)}, u32[]{:S(2)}) collective-permute-start(bf16[8192,256]{1,0:T(8,128)(2,1)} %bitcast.66), channel_id=1, source_target_pairs={{0,30},{2,0},{4,2},{6,4},{8,6},{10,8},{12,10},{14,12},{16,14},{18,... | collective-permute-start | bytes 12582920 | tf_op jit(solution)/shard_map/ppermute | solution.py:16
  50.2 84.0 %collective-permute-start.12 = (bf16[8192,256]{1,0:T(8,128)(2,1)}, bf16[8192,256]{1,0:T(8,128)(2,1)}, u32[]{:S(2)}, u32[]{:S(2)}) collective-permute-start(bf16[8192,256]{1,0:T(8,128)(2,1)} %bitcast.67), channel_id=1, source_target_pairs={{1,0},{3,2},{5,4},{7,6},{9,8},{11,10},{13,12},{15,14},{17,16},{19,... | collective-permute-start | bytes 12582920 | tf_op jit(solution)/shard_map/ppermute | solution.py:16
  51.9 50.2 %collective-permute-start.7 = (f32[512,256]{1,0:T(8,128)S(1)}, f32[512,256]{1,0:T(8,128)S(1)}, u32[]{:S(2)}, u32[]{:S(2)}) collective-permute-start(f32[512,256]{1,0:T(8,128)S(1)} %get-tuple-element.22), channel_id=1, source_target_pairs={{0,30},{2,0},{4,2},{6,4},{8,6},{10,8},{12,10},{14,12},{16,14},{18,... | collective-permute-start | bytes 1572872 | tf_op jit(solution)/shard_map/ppermute | solution.py:16
  54.8 21.9 %collective-permute-start.9 = (bf16[512,256]{1,0:T(8,128)(2,1)S(1)}, bf16[512,256]{1,0:T(8,128)(2,1)S(1)}, u32[]{:S(2)}, u32[]{:S(2)}) collective-permute-start(bf16[512,256]{1,0:T(8,128)(2,1)S(1)} %get-tuple-element.21), channel_id=1, source_target_pairs={{0,1},{1,2},{2,3},{3,4},{4,5},{5,6},{6,7},{7,8},{8,9},{9,10},{10,1... | collective-permute-start | bytes 786440 | tf_op jit(solution)/shard_map/ppermute | solution.py:16
  76.7 57.5 %collective-permute-start.13 = (f32[512,256]{1,0:T(8,128)S(1)}, f32[512,256]{1,0:T(8,128)S(1)}, u32[]{:S(2)}, u32[]{:S(2)}) collective-permute-start(f32[512,256]{1,0:T(8,128)S(1)} %get-tuple-element.22), channel_id=1, source_target_pairs={{1,0},{3,2},{5,4},{7,6},{9,8},{11,10},{13,12},{15,14},{17,16},{19,... | collective-permute-start | bytes 1572872 | tf_op jit(solution)/shard_map/ppermute | solution.py:16
  81.1 50.7 %collective-permute-start.10 = (bf16[2,8,512,256]{3,2,0,1:T(8,128)(2,1)S(1)}, bf16[2,8,512,256]{3,2,0,1:T(8,128)(2,1)S(1)}, u32[]{:S(2)}, u32[]{:S(2)}) collective-permute-start(bf16[2,8,512,256]{3,2,0,1:T(8,128)(2,1)S(1)} %fusion.2), channel_id=1, source_target_pairs={{0,1},{1,2},{2,3},{3,4},{4,5},{5,6},{6,7},{7,8},{8,9},{9,10},{10,1... | collective-permute-start | bytes 12582920 | tf_op jit(solution)/shard_map/ppermute | solution.py:16
  131.8 30.0 %collective-permute-start.11 = (bf16[2,8,256,256]{3,2,1,0:T(8,128)(2,1)S(1)}, bf16[2,8,256,256]{3,2,1,0:T(8,128)(2,1)S(1)}, u32[]{:S(2)}, u32[]{:S(2)}) collective-permute-start(bf16[2,8,256,256]{3,2,1,0:T(8,128)(2,1)S(1)} %fusion.5), channel_id=1, source_target_pairs={{0,2},{2,4},{4,6},{6,8},{8,10},{10,12},{12,14},{14,16},{16,18},{18... | collective-permute-start | bytes 6291464 | tf_op jit(solution)/shard_map/ppermute | solution.py:16
  134.2 4.8 %copy-start = (bf16[1,8,512,256]{3,2,0,1:T(8,128)(2,1)}, bf16[1,8,512,256]{3,2,0,1:T(8,128)(2,1)S(1)}, u32[]{:S(2)}) copy-start(bf16[1,8,512,256]{3,2,0,1:T(8,128)(2,1)S(1)} %get-tuple-element.24) | copy-start | bytes 6291460
  143.3 18.6 %collective-permute-start.14 = (bf16[2,8,256,256]{3,2,1,0:T(8,128)(2,1)S(1)}, bf16[2,8,256,256]{3,2,1,0:T(8,128)(2,1)S(1)}, u32[]{:S(2)}, u32[]{:S(2)}) collective-permute-start(bf16[2,8,256,256]{3,2,1,0:T(8,128)(2,1)S(1)} %fusion.13), channel_id=1, source_target_pairs={{0,1},{2,3},{4,5},{6,7},{8,9},{10,11},{12,13},{14,15},{16,17},{18,... | collective-permute-start | bytes 6291464 | tf_op jit(solution)/shard_map/ppermute | solution.py:16

commit v15 on v13

--- a/solution.py
+++ b/solution.py
@@ -70,20 +70,22 @@
     gain_ahead = moved(window_gain, "chan", -2, only_even=True)
     gain_mate = moved(window_gain, "chan", -1, only_odd=True)
     whitened = whiten(spectra, window_gain)
-    near = whiten(raw_near, gain_near)
+    near_parts = [whiten(raw_near[k], gain_near) for k in range(raw_near.shape[0])]
+    near = jnp.stack(near_parts)
     ahead = whiten(raw_ahead, gain_ahead)
-    second = moved(near, "chan", 1)
+    second_parts = tuple(moved(x, "chan", 1) for x in near_parts)
     for_above = cross_block(ahead, near, scale)
     own_lag = cross_block(whitened, whitened, scale)
     near_lag = cross_block(whitened, near, scale)
-    for_above, second, own_lag, near_lag = lax.optimization_barrier((for_above, second, own_lag, near_lag))
+    for_above, second_parts, own_lag, near_lag = lax.optimization_barrier((for_above, second_parts, own_lag, near_lag))
+    second = jnp.stack(second_parts)
     from_below = moved(for_above, "chan", 2, only_even=True)
     mate = whiten(raw_mate, gain_mate)
     for_mate = cross_block(mate, second, scale)
     from_mate = moved(for_mate, "chan", 1, only_even=True)
     lag_two = cross_block(whitened, second, scale)
     early = jnp.stack([own_lag, near_lag, lag_two, jnp.zeros_like(own_lag)])
-    early, second = lax.optimization_barrier((early, second))
+    early, _ = lax.optimization_barrier((early, second_parts[0]))
     last = jnp.where(even, from_below, from_mate)
     return lax.dynamic_update_slice_in_dim(early, last[None], 3, axis=0)
 

time: 164 us -> 180 us (1.098)
  waiting for transfers between devices: 80.3 us -> 87.5 us
  other arithmetic: 20.6 us -> 27.1 us
  starting transfers between devices: 32.3 us -> 34.5 us
    ppermute x9 -> x10, waiting for transfers between devices: 55.3 us -> 62.4 us  [moved(): return lax.ppermute(value, axis, pairs)]
    convert_element_type x2 -> x4, other arithmetic: 6.07 us -> 9.4 us  [whiten(): return (raw.astype(jnp.float32) * gain).astype(jnp.bfloat16)]
    ppermute x9 -> x10, starting transfers between devices: 19.9 us -> 22.2 us  [moved(): return lax.ppermute(value, axis, pairs)]
  transfers between devices with their start and end apart: 14 -> 15, of which waited for: 8 -> 9; matrix products, arithmetic and copies ran while one was open for 28% -> 28% of each run, Pallas kernels for 0% -> 0%
where the time goes in v15:
time: 180 us
  waiting for transfers between devices  87.5 us (49%)
  starting transfers between devices  34.5 us (19%)
  matrix products  29.7 us (16%)
  other arithmetic  27.1 us (15%)
    ppermute x10, waiting for transfers between devices, moved(): return lax.ppermute(value, axis, pairs)  62.4 us
    ppermute x10, starting transfers between devices, moved(): return lax.ppermute(value, axis, pairs)  22.2 us
    dot_general x5, matrix products, cross_block(): jnp.einsum('pfwa,pfwb->fab', own_block, flipped, preferred_element_type=j...  14.9 us
    dot_general x5, matrix products, cross_block(): jnp.einsum('pfwa,pfwb->fab', own_block, partner, preferred_element_type=j...  14.8 us
    ppermute x1, waiting for transfers between devices, shards(): lax.ppermute(partial_energy, 'band', [(s, s ^ 1) for s in range(lax.axis_...  12.9 us
    convert_element_type x4, other arithmetic, whiten(): return (raw.astype(jnp.float32) * gain).astype(jnp.bfloat16)  9.4 us
    ppermute x2, waiting for transfers between devices, band_sum(): got = lax.ppermute(jnp.where(bit == 0, high, low), axis, pairs)  8.73 us
    ppermute x2, starting transfers between devices, band_sum(): got = lax.ppermute(flat, axis, pairs)  4.94 us
  transfers between devices with their start and end apart: 15, of which 9 were waited for; matrix products, arithmetic and copies ran while one was open for 28% of the time, Pallas kernels for 0%

profile of v15, /device:TPU:4, one launch (start us, length us, event | category | flops | bytes accessed | tf_op | source)
XLA Modules:
  0.0 179.7 jit_solution(6201410871338492504)
XLA Ops:
  0.0 3.1 %multiply_reduce_fusion = f32[512,256]{1,0:T(8,128)S(1)} fusion(bf16[2,8,512,256]{3,2,1,0:T(8,128)(2,1)} %param.2), kind=kLoop, calls=%fused_computation.6 | loop fusion | flops 6160384 | bytes 4718592 | tf_op jit(solution)/shard_map/reduce_sum | solution.py:57
  3.1 2.3 %collective-permute-start = (f32[512,256]{1,0:T(8,128)S(1)}, f32[512,256]{1,0:T(8,128)S(1)}, u32[]{:S(2)}, u32[]{:S(2)}) collective-permute-start(f32[512,256]{1,0:T(8,128)S(1)} %multiply_reduce_fusion), channel_id=1, source_target_pairs={{0,32},{32,0},{64,96},{96,64},{128,160},{160,128},{192,224},{224,1... | collective-permute-start | bytes 1572872 | tf_op jit(solution)/shard_map/ppermute | solution.py:61
  5.4 12.9 %collective-permute-done = f32[512,256]{1,0:T(8,128)S(1)} collective-permute-done((f32[512,256]{1,0:T(8,128)S(1)}, f32[512,256]{1,0:T(8,128)S(1)}, u32[]{:S(2)}, u32[]{:S(2)}) %collective-permute-start) | collective-permute-done | bytes 524320 | tf_op jit(solution)/shard_map/ppermute | solution.py:61
  18.6 3.3 %collective-permute-start.2 = (f32[65536]{0:T(1024)S(1)}, f32[65536]{0:T(1024)S(1)}, u32[]{:S(2)}, u32[]{:S(2)}) collective-permute-start(f32[65536]{0:T(1024)S(1)} %bitcast.86), channel_id=1, source_target_pairs={{0,128},{32,160},{64,192},{96,224},{128,0},{160,32},{192,64},{224,... | collective-permute-start | bytes 786440 | tf_op jit(solution)/shard_map/ppermute | solution.py:34
  22.0 5.3 %collective-permute-done.2 = f32[65536]{0:T(1024)S(1)} collective-permute-done((f32[65536]{0:T(1024)S(1)}, f32[65536]{0:T(1024)S(1)}, u32[]{:S(2)}, u32[]{:S(2)}) %collective-permute-start.2) | collective-permute-done | bytes 262176 | tf_op jit(solution)/shard_map/ppermute | solution.py:34
  27.4 1.7 collective-permute-start.3
  29.1 3.4 %collective-permute-done.3 = f32[32768]{0:T(1024)S(1)} collective-permute-done((f32[32768]{0:T(1024)S(1)}, f32[32768]{0:T(1024)S(1)}, u32[]{:S(2)}, u32[]{:S(2)}) %collective-permute-start.3) | collective-permute-done | bytes 131104 | tf_op jit(solution)/shard_map/ppermute | solution.py:34
  32.5 1.7 collective-permute-start.4
  34.2 3.4 %collective-permute-done.4 = f32[32768]{0:T(1024)S(1)} collective-permute-done((f32[32768]{0:T(1024)S(1)}, f32[32768]{0:T(1024)S(1)}, u32[]{:S(2)}, u32[]{:S(2)}) %collective-permute-start.4) | collective-permute-done | bytes 131104 | tf_op jit(solution)/shard_map/ppermute | solution.py:39
  37.6 3.3 %collective-permute-start.5 = (f32[65536]{0:T(1024)S(1)}, f32[65536]{0:T(1024)S(1)}, u32[]{:S(2)}, u32[]{:S(2)}) collective-permute-start(f32[65536]{0:T(1024)S(1)} %maximum_select_fusion.2), channel_id=1, source_target_pairs={{0,128},{32,160},{64,192},{96,224},{128,0},{160,32},{192,64},{224,... | collective-permute-start | bytes 786440 | tf_op jit(solution)/shard_map/ppermute | solution.py:39
  42.2 9.5 %collective-permute-start.1 = (bf16[8192,256]{1,0:T(8,128)(2,1)}, bf16[8192,256]{1,0:T(8,128)(2,1)}, u32[]{:S(2)}, u32[]{:S(2)}) collective-permute-start(bf16[8192,256]{1,0:T(8,128)(2,1)} %bitcast.77), channel_id=1, source_target_pairs={{0,30},{2,0},{4,2},{6,4},{8,6},{10,8},{12,10},{14,12},{16,14},{18,... | collective-permute-start | bytes 12582920 | tf_op jit(solution)/shard_map/ppermute | solution.py:16
  53.5 3.0 %multiply_convert_fusion = bf16[2,8,512,256]{3,2,0,1:T(8,128)(2,1)S(1)} fusion(bf16[2,8,512,256]{3,2,1,0:T(8,128)(2,1)} %param.2, f32[512,256]{1,0:T(8,128)S(1)} %get-tuple-element.24), kind=kLoop, calls=%fused_computation.5 | loop fusion | flops 6291456 | bytes 8912896 | tf_op jit(solution)/shard_map/convert_element_type | solution.py:52
  58.2 2.9 %fusion.23 = f32[1,8,256,256]{3,2,1,0:T(8,128)} fusion(bf16[2,8,512,256]{3,2,0,1:T(8,128)(2,1)S(1)} %multiply_convert_fusion, bf16[1,8,512,256]{3,2,0,1:T(8,128)(2,1)S(1)} %get-tuple-element.26, bf16[1,8,512,256]{3,2,0,1:T(8,128)(2,1)S(1)} %get-tuple-element.25), kind=kOutput, calls=%fused_computation.42 | convolution fusion | flops 1075838976 | bytes 10485760 | tf_op jit(solution)/shard_map/pfwa,pfwb->fab/dot_general | solution.py:47
  61.1 21.1 %collective-permute-done.8 = bf16[512,256]{1,0:T(8,128)(2,1)S(1)} collective-permute-done((bf16[512,256]{1,0:T(8,128)(2,1)S(1)}, bf16[512,256]{1,0:T(8,128)(2,1)S(1)}, u32[]{:S(2)}, u32[]{:S(2)}) %collective-permute-start.8) | collective-permute-done | bytes 262176 | tf_op jit(solution)/shard_map/ppermute | solution.py:16
  82.1 6.5 %collective-permute-start.6 = (f32[512,256]{1,0:T(8,128)S(1)}, f32[512,256]{1,0:T(8,128)}, u32[]{:S(2)}, u32[]{:S(2)}) collective-permute-start(f32[512,256]{1,0:T(8,128)S(1)} %get-tuple-element.24), channel_id=1, source_target_pairs={{0,30},{2,0},{4,2},{6,4},{8,6},{10,8},{12,10},{14,12},{16,14},{18,... | collective-permute-start | bytes 1572872 | tf_op jit(solution)/shard_map/ppermute | solution.py:16
  88.7 2.9 %slice_convert_fusion = (f32[4096,256]{1,0:T(8,128)S(1)}, f32[4096,256]{1,0:T(8,128)S(1)}) fusion(bf16[8192,256]{1,0:T(8,128)(2,1)} %collective-permute-done.7), kind=kLoop, calls=%fused_computation.38 | loop fusion | flops 2097152 | bytes 12582912 | tf_op jit(solution)/shard_map/convert_element_type | solution.py:52
  92.2 3.0 %multiply_convert_fusion.1 = (bf16[8,512,256]{2,1,0:T(8,128)(2,1)}, bf16[8,512,256]{2,1,0:T(8,128)(2,1)}) fusion(f32[8,512,256]{2,1,0:T(8,128)S(1)} %bitcast.73, f32[512,256]{1,0:T(8,128)S(1)} %convert_element_type.134, f32[8,512,256]{2,1,0:T(8,128)S(1)} %bitcast.72), kind=kLoop, calls=%fused_computation.33 | loop fusion | flops 4194304 | bytes 13107200 | tf_op jit(solution)/shard_map/convert_element_type | solution.py:52
  96.5 7.0 %collective-permute-done.6 = f32[512,256]{1,0:T(8,128)} collective-permute-done((f32[512,256]{1,0:T(8,128)S(1)}, f32[512,256]{1,0:T(8,128)}, u32[]{:S(2)}, u32[]{:S(2)}) %collective-permute-start.6) | collective-permute-done | bytes 524320 | tf_op jit(solution)/shard_map/ppermute | solution.py:16
  103.6 5.2 %fusion.31 = f32[1,8,256,256]{3,2,1,0:T(8,128)} fusion(bf16[2,8,512,256]{3,2,0,1:T(8,128)(2,1)S(1)} %get-tuple-element.32, bf16[2,8,512,256]{3,2,1,0:T(8,128)(2,1)} %bitcast.40, f32[512,256]{1,0:T(8,128)} %collective-permute-done.6), kind=kOutput, calls=%fused_computation.49 | convolution fusion | flops 1080033280 | bytes 11010048 | tf_op jit(solution)/shard_map/pfwa,pfwb->fab/dot_general | solution.py:47
  108.7 5.3 %fusion.26 = f32[1,8,256,256]{3,2,1,0:T(8,128)} fusion(bf16[2,8,512,256]{3,2,0,1:T(8,128)(2,1)S(1)} %get-tuple-element.31, bf16[2,8,512,256]{3,2,1,0:T(8,128)(2,1)} %bitcast.40, f32[512,256]{1,0:T(8,128)} %collective-permute-done.6), kind=kOutput, calls=%fused_computation.48 | convolution fusion | flops 1080033280 | bytes 11010048 | tf_op jit(solution)/shard_map/pfwa,pfwb->fab/dot_general | solution.py:46
  114.0 2.1 %fusion.2 = bf16[2,8,256,256]{3,2,1,0:T(8,128)(2,1)S(1)} fusion(f32[1,8,256,256]{3,2,1,0:T(8,128)S(1)} %copy-done, f32[1,8,256,256]{3,2,1,0:T(8,128)} %fusion.26), kind=kLoop, calls=%fused_computation.10 | loop fusion | flops 3145728 | bytes 6291456 | tf_op jit(solution)/shard_map/convert_element_type | solution.py:48
  116.1 1.5 convolution_bitcast_fusion.2
  117.6 1.5 convolution_bitcast_fusion.3
  120.3 3.3 %collective-permute-done.10 = bf16[8,512,256]{2,1,0:T(8,128)(2,1)S(1)} collective-permute-done((bf16[8,512,256]{2,1,0:T(8,128)(2,1)}, bf16[8,512,256]{2,1,0:T(8,128)(2,1)S(1)}, u32[]{:S(2)}, u32[]{:S(2)}) %collective-permute-start.10) | collective-permute-done | bytes 2097184 | tf_op jit(solution)/shard_map/ppermute | solution.py:16
  123.5 22.5 %collective-permute-done.9 = bf16[8,512,256]{2,1,0:T(8,128)(2,1)S(1)} collective-permute-done((bf16[8,512,256]{2,1,0:T(8,128)(2,1)}, bf16[8,512,256]{2,1,0:T(8,128)(2,1)S(1)}, u32[]{:S(2)}, u32[]{:S(2)}) %collective-permute-start.9) | collective-permute-done | bytes 2097184 | tf_op jit(solution)/shard_map/ppermute | solution.py:16
  146.0 2.1 %collective-permute-start.11 = (bf16[2,8,256,256]{3,2,1,0:T(8,128)(2,1)S(1)}, bf16[2,8,256,256]{3,2,1,0:T(8,128)(2,1)}, u32[]{:S(2)}, u32[]{:S(2)}) collective-permute-start(bf16[2,8,256,256]{3,2,1,0:T(8,128)(2,1)S(1)} %fusion.2), channel_id=1, source_target_pairs={{0,2},{2,4},{4,6},{6,8},{8,10},{10,12},{12,14},{14,16},{16,18},{18... | collective-permute-start | bytes 6291464 | tf_op jit(solution)/shard_map/ppermute | solution.py:16
  149.1 5.1 %fusion.36 = f32[1,8,256,256]{3,2,1,0:T(8,128)} fusion(bf16[2,8,512,256]{3,2,0,1:T(8,128)(2,1)S(1)} %get-tuple-element.29, bf16[2,8,512,256]{3,2,1,0:T(8,128)(2,1)} %bitcast.44, f32[512,256]{1,0:T(8,128)} %collective-permute-done.13), kind=kOutput, calls=%fused_computation.50 | convolution fusion | flops 1080033280 | bytes 11010048 | tf_op jit(solution)/shard_map/pfwa,pfwb->fab/dot_general | solution.py:46
  154.2 4.0 %fusion.41 = f32[1,8,256,256]{3,2,1,0:T(8,128)S(1)} fusion(bf16[2,8,512,256]{3,2,0,1:T(8,128)(2,1)S(1)} %get-tuple-element.30, bf16[2,8,512,256]{3,2,1,0:T(8,128)(2,1)} %bitcast.44, f32[512,256]{1,0:T(8,128)} %collective-permute-done.13), kind=kOutput, calls=%fused_computation.51 | convolution fusion | flops 1080033280 | bytes 11010048 | tf_op jit(solution)/shard_map/pfwa,pfwb->fab/dot_general | solution.py:47
  161.6 1.5 convolution_bitcast_fusion.1
  163.7 3.9 %maximum_maximum_fusion = bf16[4,2,8,256,256]{4,3,2,1,0:T(8,128)(2,1)} fusion(bf16[1,2,8,256,256]{4,3,2,1,0:T(8,128)(2,1)S(1)} %fusion.9, bf16[1,2,8,256,256]{4,3,2,1,0:T(8,128)(2,1)S(1)} %bitcast.81, bf16[1,2,8,256,256]{4,3,2,1,0:T(8,128)(2,1)S(1)} %bitcast.80, bf16[4]{0:T(256)(128)(2,1)S(1)} %pad.5.clone), kind=kLoop, calls=%fused_computation | loop fusion | flops 12582912 | bytes 14680072 | tf_op jit(solution)/shard_map/stack | solution.py:87
  167.5 8.6 %collective-permute-done.11 = bf16[2,8,256,256]{3,2,1,0:T(8,128)(2,1)} collective-permute-done((bf16[2,8,256,256]{3,2,1,0:T(8,128)(2,1)S(1)}, bf16[2,8,256,256]{3,2,1,0:T(8,128)(2,1)}, u32[]{:S(2)}, u32[]{:S(2)}) %collective-permute-start.11) | collective-permute-done | bytes 2097184 | tf_op jit(solution)/shard_map/ppermute | solution.py:16
  176.2 3.6 %bitcast_dynamic-update-slice_fusion = bf16[4,2,8,256,256]{4,3,2,1,0:T(8,128)(2,1)} fusion(bf16[4,2,8,256,256]{4,3,2,1,0:T(8,128)(2,1)} %maximum_maximum_fusion, bf16[2,8,256,256]{3,2,1,0:T(8,128)(2,1)} %collective-permute-done.11, bf16[2,8,256,256]{3,2,1,0:T(8,128)(2,1)S(1)} %collective-permute-done.14, pred[]{:T(512)S(6)} %eq.19), kind=kLoop, calls=%fused_computation.40 | loop fusion | flops 1048576 | bytes 6291457 | tf_op jit(solution)/shard_map/dynamic_update_slice | solution.py:90
  (47 shorter events, 13.2 us)
Async XLA Ops:
  3.1 48.9 %copy-start.3 = (s32[512,256]{1,0:T(8,128)S(1)}, s32[512,256]{1,0:T(8,128)}, u32[]{:S(2)}) copy-start(s32[512,256]{1,0:T(8,128)} %param.3) | copy-start | bytes 1572868
  3.1 15.3 %collective-permute-start = (f32[512,256]{1,0:T(8,128)S(1)}, f32[512,256]{1,0:T(8,128)S(1)}, u32[]{:S(2)}, u32[]{:S(2)}) collective-permute-start(f32[512,256]{1,0:T(8,128)S(1)} %multiply_reduce_fusion), channel_id=1, source_target_pairs={{0,32},{32,0},{64,96},{96,64},{128,160},{160,128},{192,224},{224,1... | collective-permute-start | bytes 1572872 | tf_op jit(solution)/shard_map/ppermute | solution.py:61
  18.6 8.8 %collective-permute-start.2 = (f32[65536]{0:T(1024)S(1)}, f32[65536]{0:T(1024)S(1)}, u32[]{:S(2)}, u32[]{:S(2)}) collective-permute-start(f32[65536]{0:T(1024)S(1)} %bitcast.86), channel_id=1, source_target_pairs={{0,128},{32,160},{64,192},{96,224},{128,0},{160,32},{192,64},{224,... | collective-permute-start | bytes 786440 | tf_op jit(solution)/shard_map/ppermute | solution.py:34
  27.4 5.1 %collective-permute-start.3 = (f32[32768]{0:T(1024)S(1)}, f32[32768]{0:T(1024)S(1)}, u32[]{:S(2)}, u32[]{:S(2)}) collective-permute-start(f32[32768]{0:T(1024)S(1)} %slice_select_fusion), channel_id=1, source_target_pairs={{0,64},{32,96},{64,0},{96,32},{128,192},{160,224},{192,128},{224,1... | collective-permute-start | bytes 393224 | tf_op jit(solution)/shard_map/ppermute | solution.py:34
  29.1 59.6 %collective-permute-start.7 = (bf16[8192,256]{1,0:T(8,128)(2,1)}, bf16[8192,256]{1,0:T(8,128)(2,1)}, u32[]{:S(2)}, u32[]{:S(2)}) collective-permute-start(bf16[8192,256]{1,0:T(8,128)(2,1)} %bitcast.75), channel_id=1, source_target_pairs={{0,1},{1,2},{2,3},{3,4},{4,5},{5,6},{6,7},{7,8},{8,9},{9,10},{10,1... | collective-permute-start | bytes 12582920 | tf_op jit(solution)/shard_map/ppermute | solution.py:16
  32.5 5.1 %collective-permute-start.4 = (f32[32768]{0:T(1024)S(1)}, f32[32768]{0:T(1024)S(1)}, u32[]{:S(2)}, u32[]{:S(2)}) collective-permute-start(f32[32768]{0:T(1024)S(1)} %select_add_fusion), channel_id=1, source_target_pairs={{0,64},{32,96},{64,0},{96,32},{128,192},{160,224},{192,128},{224,1... | collective-permute-start | bytes 393224 | tf_op jit(solution)/shard_map/ppermute | solution.py:39
  37.6 14.3 %collective-permute-start.5 = (f32[65536]{0:T(1024)S(1)}, f32[65536]{0:T(1024)S(1)}, u32[]{:S(2)}, u32[]{:S(2)}) collective-permute-start(f32[65536]{0:T(1024)S(1)} %maximum_select_fusion.2), channel_id=1, source_target_pairs={{0,128},{32,160},{64,192},{96,224},{128,0},{160,32},{192,64},{224,... | collective-permute-start | bytes 786440 | tf_op jit(solution)/shard_map/ppermute | solution.py:39
  40.9 108.1 %collective-permute-start.12 = (bf16[8192,256]{1,0:T(8,128)(2,1)}, bf16[8192,256]{1,0:T(8,128)(2,1)}, u32[]{:S(2)}, u32[]{:S(2)}) collective-permute-start(bf16[8192,256]{1,0:T(8,128)(2,1)} %bitcast.76), channel_id=1, source_target_pairs={{1,0},{3,2},{5,4},{7,6},{9,8},{11,10},{13,12},{15,14},{17,16},{19,... | collective-permute-start | bytes 12582920 | tf_op jit(solution)/shard_map/ppermute | solution.py:16
  42.2 61.3 %collective-permute-start.1 = (bf16[8192,256]{1,0:T(8,128)(2,1)}, bf16[8192,256]{1,0:T(8,128)(2,1)}, u32[]{:S(2)}, u32[]{:S(2)}) collective-permute-start(bf16[8192,256]{1,0:T(8,128)(2,1)} %bitcast.77), channel_id=1, source_target_pairs={{0,30},{2,0},{4,2},{6,4},{8,6},{10,8},{12,10},{14,12},{16,14},{18,... | collective-permute-start | bytes 12582920 | tf_op jit(solution)/shard_map/ppermute | solution.py:16
  52.1 30.1 %collective-permute-start.8 = (bf16[512,256]{1,0:T(8,128)(2,1)S(1)}, bf16[512,256]{1,0:T(8,128)(2,1)S(1)}, u32[]{:S(2)}, u32[]{:S(2)}) collective-permute-start(bf16[512,256]{1,0:T(8,128)(2,1)S(1)} %get-tuple-element.23), channel_id=1, source_target_pairs={{0,1},{1,2},{2,3},{3,4},{4,5},{5,6},{6,7},{7,8},{8,9},{9,10},{10,1... | collective-permute-start | bytes 786440 | tf_op jit(solution)/shard_map/ppermute | solution.py:16
  52.2 96.9 %collective-permute-start.13 = (f32[512,256]{1,0:T(8,128)S(1)}, f32[512,256]{1,0:T(8,128)}, u32[]{:S(2)}, u32[]{:S(2)}) collective-permute-start(f32[512,256]{1,0:T(8,128)S(1)} %get-tuple-element.24), channel_id=1, source_target_pairs={{1,0},{3,2},{5,4},{7,6},{9,8},{11,10},{13,12},{15,14},{17,16},{19,... | collective-permute-start | bytes 1572872 | tf_op jit(solution)/shard_map/ppermute | solution.py:16
  82.1 21.4 %collective-permute-start.6 = (f32[512,256]{1,0:T(8,128)S(1)}, f32[512,256]{1,0:T(8,128)}, u32[]{:S(2)}, u32[]{:S(2)}) collective-permute-start(f32[512,256]{1,0:T(8,128)S(1)} %get-tuple-element.24), channel_id=1, source_target_pairs={{0,30},{2,0},{4,2},{6,4},{8,6},{10,8},{12,10},{14,12},{16,14},{18,... | collective-permute-start | bytes 1572872 | tf_op jit(solution)/shard_map/ppermute | solution.py:16
  95.7 27.9 %collective-permute-start.10 = (bf16[8,512,256]{2,1,0:T(8,128)(2,1)}, bf16[8,512,256]{2,1,0:T(8,128)(2,1)S(1)}, u32[]{:S(2)}, u32[]{:S(2)}) collective-permute-start(bf16[8,512,256]{2,1,0:T(8,128)(2,1)} %get-tuple-element.33), channel_id=1, source_target_pairs={{0,1},{1,2},{2,3},{3,4},{4,5},{5,6},{6,7},{7,8},{8,9},{9,10},{10,1... | collective-permute-start | bytes 6291464 | tf_op jit(solution)/shard_map/ppermute | solution.py:16
  103.6 42.5 %collective-permute-start.9 = (bf16[8,512,256]{2,1,0:T(8,128)(2,1)}, bf16[8,512,256]{2,1,0:T(8,128)(2,1)S(1)}, u32[]{:S(2)}, u32[]{:S(2)}) collective-permute-start(bf16[8,512,256]{2,1,0:T(8,128)(2,1)} %get-tuple-element.34), channel_id=1, source_target_pairs={{0,1},{1,2},{2,3},{3,4},{4,5},{5,6},{6,7},{7,8},{8,9},{9,10},{10,1... | collective-permute-start | bytes 6291464 | tf_op jit(solution)/shard_map/ppermute | solution.py:16
  108.7 5.3 %copy-start = (f32[1,8,256,256]{3,2,1,0:T(8,128)S(1)}, f32[1,8,256,256]{3,2,1,0:T(8,128)}, u32[]{:S(2)}) copy-start(f32[1,8,256,256]{3,2,1,0:T(8,128)} %fusion.31) | copy-start | bytes 6291460
  117.6 1.6 copy-start.2
  146.0 30.1 %collective-permute-start.11 = (bf16[2,8,256,256]{3,2,1,0:T(8,128)(2,1)S(1)}, bf16[2,8,256,256]{3,2,1,0:T(8,128)(2,1)}, u32[]{:S(2)}, u32[]{:S(2)}) collective-permute-start(bf16[2,8,256,256]{3,2,1,0:T(8,128)(2,1)S(1)} %fusion.2), channel_id=1, source_target_pairs={{0,2},{2,4},{4,6},{6,8},{8,10},{10,12},{12,14},{14,16},{16,18},{18... | collective-permute-start | bytes 6291464 | tf_op jit(solution)/shard_map/ppermute | solution.py:16
  154.2 4.0 %copy-start.1 = (f32[1,8,256,256]{3,2,1,0:T(8,128)S(1)}, f32[1,8,256,256]{3,2,1,0:T(8,128)}, u32[]{:S(2)}) copy-start(f32[1,8,256,256]{3,2,1,0:T(8,128)} %fusion.36) | copy-start | bytes 6291460
  158.7 17.4 %collective-permute-start.14 = (bf16[2,8,256,256]{3,2,1,0:T(8,128)(2,1)S(1)}, bf16[2,8,256,256]{3,2,1,0:T(8,128)(2,1)S(1)}, u32[]{:S(2)}, u32[]{:S(2)}) collective-permute-start(bf16[2,8,256,256]{3,2,1,0:T(8,128)(2,1)S(1)} %fusion.10), channel_id=1, source_target_pairs={{0,1},{2,3},{4,5},{6,7},{8,9},{10,11},{12,13},{14,15},{16,17},{18,... | collective-permute-start | bytes 6291464 | tf_op jit(solution)/shard_map/ppermute | solution.py:16

commit v16 on v13

--- a/solution.py
+++ b/solution.py
@@ -58,7 +58,7 @@
     total_bins = spectra.shape[1] * lax.axis_size("band")
     scale = 1.0 / math.sqrt(spectra.shape[2])
     even = lax.axis_index("chan") % 2 == 0
-    partial_energy = partial_energy + lax.ppermute(partial_energy, "band", [(s, s ^ 1) for s in range(lax.axis_size("band"))])
+    partial_energy = partial_energy + lax.ppermute(partial_energy.astype(jnp.bfloat16), "band", [(s, s ^ 1) for s in range(lax.axis_size("band"))]).astype(jnp.float32)
     spectra, partial_energy = lax.optimization_barrier((spectra, partial_energy))
     flat_spectra = spectra.reshape(-1, spectra.shape[-1])
     raw_near = moved(flat_spectra, "chan", 1).reshape(spectra.shape)

time: 164 us -> 158 us (0.963)
  waiting for transfers between devices: 80.3 us -> 74.7 us
    ppermute x1, waiting for transfers between devices: 12.9 us -> 7.31 us  [shards(): lax.ppermute(partial_energy.astype(jnp.bfloat16), 'band', [(s, s ^ 1) for...]
where the time goes in v16:
time: 158 us
  waiting for transfers between devices  74.7 us (47%)
  starting transfers between devices  32.3 us (20%)
  matrix products  29.1 us (18%)
  other arithmetic  20.6 us (13%)
    ppermute x9, waiting for transfers between devices, moved(): return lax.ppermute(value, axis, pairs)  55.3 us
    ppermute x9, starting transfers between devices, moved(): return lax.ppermute(value, axis, pairs)  19.9 us
    dot_general x5, matrix products, cross_block(): jnp.einsum('pfwa,pfwb->fab', own_block, flipped, preferred_element_type=j...  16.1 us
    dot_general x5, matrix products, cross_block(): jnp.einsum('pfwa,pfwb->fab', own_block, partner, preferred_element_type=j...  13 us
    ppermute x2, waiting for transfers between devices, band_sum(): got = lax.ppermute(jnp.where(bit == 0, high, low), axis, pairs)  8.64 us
    ppermute x1, waiting for transfers between devices, shards(): lax.ppermute(partial_energy.astype(jnp.bfloat16), 'band', [(s, s ^ 1) for...  7.31 us
    convert_element_type x2, other arithmetic, whiten(): return (raw.astype(jnp.float32) * gain).astype(jnp.bfloat16)  6.07 us
    ppermute x2, starting transfers between devices, band_sum(): got = lax.ppermute(flat, axis, pairs)  5.19 us
  transfers between devices with their start and end apart: 14, of which 8 were waited for; matrix products, arithmetic and copies ran while one was open for 28% of the time, Pallas kernels for 0%

profile of v16, /device:TPU:4, one launch (start us, length us, event | category | flops | bytes accessed | tf_op | source)
XLA Modules:
  0.0 157.5 jit_solution(9605118329741003666)
XLA Ops:
  0.0 3.1 %multiply_reduce_fusion = f32[512,256]{1,0:T(8,128)S(1)} fusion(bf16[2,8,512,256]{3,2,1,0:T(8,128)(2,1)} %param.2), kind=kLoop, calls=%fused_computation.8 | loop fusion | flops 6160384 | bytes 4718592 | tf_op jit(solution)/shard_map/reduce_sum | solution.py:57
  3.1 2.3 %collective-permute-start = (bf16[512,256]{1,0:T(8,128)(2,1)S(1)}, bf16[512,256]{1,0:T(8,128)(2,1)S(1)}, u32[]{:S(2)}, u32[]{:S(2)}) collective-permute-start(bf16[512,256]{1,0:T(8,128)(2,1)S(1)} %convert_element_type.74), channel_id=1, source_target_pairs={{0,32},{32,0},{64,96},{96,64},{128,160},{160,128},{192,224},{224,1... | collective-permute-start | bytes 786440 | tf_op jit(solution)/shard_map/ppermute | solution.py:61
  5.4 7.3 %collective-permute-done = bf16[512,256]{1,0:T(8,128)(2,1)S(1)} collective-permute-done((bf16[512,256]{1,0:T(8,128)(2,1)S(1)}, bf16[512,256]{1,0:T(8,128)(2,1)S(1)}, u32[]{:S(2)}, u32[]{:S(2)}) %collective-permute-start) | collective-permute-done | bytes 262176 | tf_op jit(solution)/shard_map/ppermute | solution.py:61
  13.0 3.3 %collective-permute-start.2 = (f32[65536]{0:T(1024)S(1)}, f32[65536]{0:T(1024)S(1)}, u32[]{:S(2)}, u32[]{:S(2)}) collective-permute-start(f32[65536]{0:T(1024)S(1)} %bitcast.71), channel_id=1, source_target_pairs={{0,128},{32,160},{64,192},{96,224},{128,0},{160,32},{192,64},{224,... | collective-permute-start | bytes 786440 | tf_op jit(solution)/shard_map/ppermute | solution.py:34
  16.5 5.3 %collective-permute-done.2 = f32[65536]{0:T(1024)S(1)} collective-permute-done((f32[65536]{0:T(1024)S(1)}, f32[65536]{0:T(1024)S(1)}, u32[]{:S(2)}, u32[]{:S(2)}) %collective-permute-start.2) | collective-permute-done | bytes 262176 | tf_op jit(solution)/shard_map/ppermute | solution.py:34
  21.8 1.7 %collective-permute-start.3 = (f32[32768]{0:T(1024)S(1)}, f32[32768]{0:T(1024)S(1)}, u32[]{:S(2)}, u32[]{:S(2)}) collective-permute-start(f32[32768]{0:T(1024)S(1)} %slice_select_fusion), channel_id=1, source_target_pairs={{0,64},{32,96},{64,0},{96,32},{128,192},{160,224},{192,128},{224,1... | collective-permute-start | bytes 393224 | tf_op jit(solution)/shard_map/ppermute | solution.py:34
  23.5 3.4 %collective-permute-done.3 = f32[32768]{0:T(1024)S(1)} collective-permute-done((f32[32768]{0:T(1024)S(1)}, f32[32768]{0:T(1024)S(1)}, u32[]{:S(2)}, u32[]{:S(2)}) %collective-permute-start.3) | collective-permute-done | bytes 131104 | tf_op jit(solution)/shard_map/ppermute | solution.py:34
  26.9 1.7 %collective-permute-start.4 = (f32[32768]{0:T(1024)S(1)}, f32[32768]{0:T(1024)S(1)}, u32[]{:S(2)}, u32[]{:S(2)}) collective-permute-start(f32[32768]{0:T(1024)S(1)} %select_add_fusion), channel_id=1, source_target_pairs={{0,64},{32,96},{64,0},{96,32},{128,192},{160,224},{192,128},{224,1... | collective-permute-start | bytes 393224 | tf_op jit(solution)/shard_map/ppermute | solution.py:39
  28.6 3.4 %collective-permute-done.4 = f32[32768]{0:T(1024)S(1)} collective-permute-done((f32[32768]{0:T(1024)S(1)}, f32[32768]{0:T(1024)S(1)}, u32[]{:S(2)}, u32[]{:S(2)}) %collective-permute-start.4) | collective-permute-done | bytes 131104 | tf_op jit(solution)/shard_map/ppermute | solution.py:39
  32.0 3.5 %collective-permute-start.5 = (f32[65536]{0:T(1024)S(1)}, f32[65536]{0:T(1024)S(1)}, u32[]{:S(2)}, u32[]{:S(2)}) collective-permute-start(f32[65536]{0:T(1024)S(1)} %maximum_select_fusion.2), channel_id=1, source_target_pairs={{0,128},{32,160},{64,192},{96,224},{128,0},{160,32},{192,64},{224,... | collective-permute-start | bytes 786440 | tf_op jit(solution)/shard_map/ppermute | solution.py:39
  35.6 8.4 %collective-permute-start.1 = (bf16[8192,256]{1,0:T(8,128)(2,1)}, bf16[8192,256]{1,0:T(8,128)(2,1)}, u32[]{:S(2)}, u32[]{:S(2)}) collective-permute-start(bf16[8192,256]{1,0:T(8,128)(2,1)} %bitcast.66), channel_id=1, source_target_pairs={{0,30},{2,0},{4,2},{6,4},{8,6},{10,8},{12,10},{14,12},{16,14},{18,... | collective-permute-start | bytes 12582920 | tf_op jit(solution)/shard_map/ppermute | solution.py:16
  45.6 2.9 %collective-permute-start.6 = (f32[512,256]{1,0:T(8,128)S(1)}, f32[512,256]{1,0:T(8,128)S(1)}, u32[]{:S(2)}, u32[]{:S(2)}) collective-permute-start(f32[512,256]{1,0:T(8,128)S(1)} %get-tuple-element.20), channel_id=1, source_target_pairs={{0,30},{2,0},{4,2},{6,4},{8,6},{10,8},{12,10},{14,12},{16,14},{18,... | collective-permute-start | bytes 1572872 | tf_op jit(solution)/shard_map/ppermute | solution.py:16
  49.5 3.0 %multiply_convert_fusion = bf16[2,8,512,256]{3,2,0,1:T(8,128)(2,1)S(1)} fusion(bf16[2,8,512,256]{3,2,1,0:T(8,128)(2,1)} %param.2, f32[512,256]{1,0:T(8,128)S(1)} %get-tuple-element.20), kind=kLoop, calls=%fused_computation.7 | loop fusion | flops 6291456 | bytes 8912896 | tf_op jit(solution)/shard_map/convert_element_type | solution.py:52
  52.8 17.7 %collective-permute-done.8 = bf16[512,256]{1,0:T(8,128)(2,1)S(1)} collective-permute-done((bf16[512,256]{1,0:T(8,128)(2,1)S(1)}, bf16[512,256]{1,0:T(8,128)(2,1)S(1)}, u32[]{:S(2)}, u32[]{:S(2)}) %collective-permute-start.8) | collective-permute-done | bytes 262176 | tf_op jit(solution)/shard_map/ppermute | solution.py:16
  71.8 3.0 %fusion.2 = bf16[2,8,512,256]{3,2,0,1:T(8,128)(2,1)S(1)} fusion(f32[512,256]{1,0:T(8,128)S(1)} %convert_element_type.83, bf16[2,8,512,256]{3,2,1,0:T(8,128)(2,1)} %bitcast.34), kind=kLoop, calls=%fused_computation.6 | loop fusion | flops 6291456 | bytes 8912896 | tf_op jit(solution)/shard_map/convert_element_type | solution.py:52
  74.9 1.4 collective-permute-start.9
  76.3 2.8 %fusion.24 = f32[1,8,256,256]{3,2,1,0:T(8,128)} fusion(bf16[2,8,512,256]{3,2,0,1:T(8,128)(2,1)S(1)} %multiply_convert_fusion, bf16[1,8,512,256]{3,2,0,1:T(8,128)(2,1)S(1)} %get-tuple-element.24, bf16[1,8,512,256]{3,2,0,1:T(8,128)(2,1)S(1)} %get-tuple-element.23), kind=kOutput, calls=%fused_computation.37 | convolution fusion | flops 1075838976 | bytes 10485760 | tf_op jit(solution)/shard_map/pfwa,pfwb->fab/dot_general | solution.py:47
  82.2 2.9 %convolution_bitcast_fusion.2 = f32[1,8,256,256]{3,2,1,0:T(8,128)} fusion(bf16[2,8,512,256]{3,2,0,1:T(8,128)(2,1)S(1)} %multiply_convert_fusion, bf16[1,8,512,256]{3,2,0,1:T(8,128)(2,1)S(1)} %get-tuple-element.26, bf16[1,8,512,256]{3,2,0,1:T(8,128)(2,1)S(1)} %get-tuple-element.25), kind=kOutput, calls=%fused_computation.40 | convolution fusion | flops 1075838976 | bytes 10485760 | tf_op jit(solution)/shard_map/pfwa,pfwb->fab/dot_general | solution.py:47
  85.0 2.7 %fusion.8 = (bf16[2,8,256,256]{3,2,1,0:T(8,128)(2,1)S(1)}, bf16[2,8,256,256]{3,2,1,0:T(8,128)(2,1)S(1)}) fusion(f32[1,8,256,256]{3,2,1,0:T(8,128)} %fusion.24, f32[1,8,256,256]{3,2,1,0:T(8,128)S(1)} %convolution_bitcast_fusion.4, f32[1,8,256,256]{3,2,1,0:T(8,128)} %convolution_bitcast_fusion.2, f32[1,8,256,256]{3,2,1,0:T(8,128)S(1)} %convolution_bitcast_fusion.3), kind=kLoop, calls=%fused_computation.17 | loop fusion | flops 6291456 | bytes 12582912 | tf_op jit(solution)/shard_map/convert_element_type | solution.py:48
  87.8 8.0 %collective-permute-done.6 = f32[512,256]{1,0:T(8,128)S(1)} collective-permute-done((f32[512,256]{1,0:T(8,128)S(1)}, f32[512,256]{1,0:T(8,128)S(1)}, u32[]{:S(2)}, u32[]{:S(2)}) %collective-permute-start.6) | collective-permute-done | bytes 524320 | tf_op jit(solution)/shard_map/ppermute | solution.py:16
  95.8 3.7 %fusion.32 = f32[1,8,256,256]{3,2,1,0:T(8,128)S(1)} fusion(bf16[2,8,512,256]{3,2,1,0:T(8,128)(2,1)} %bitcast.33, f32[512,256]{1,0:T(8,128)S(1)} %collective-permute-done.6, bf16[1,8,512,256]{3,2,0,1:T(8,128)(2,1)S(1)} %get-tuple-element.26, bf16[1,8,512,256]{3,2,0,1:T(8,128)(2,1)S(1)} %get-tuple-element.25), kind=kOutput, calls=%fused_computation.44 | convolution fusion | flops 1082130432 | bytes 11010048 | tf_op jit(solution)/shard_map/pfwa,pfwb->fab/dot_general | solution.py:47
  99.5 4.0 %fusion.27 = f32[1,8,256,256]{3,2,1,0:T(8,128)S(1)} fusion(bf16[2,8,512,256]{3,2,0,1:T(8,128)(2,1)S(1)} %fusion.2, bf16[2,8,512,256]{3,2,1,0:T(8,128)(2,1)} %bitcast.33, f32[512,256]{1,0:T(8,128)S(1)} %collective-permute-done.6), kind=kOutput, calls=%fused_computation.43 | convolution fusion | flops 1080033280 | bytes 11010048 | tf_op jit(solution)/shard_map/pfwa,pfwb->fab/dot_general | solution.py:46
  104.1 21.5 %collective-permute-done.9 = bf16[2,8,512,256]{3,2,0,1:T(8,128)(2,1)S(1)} collective-permute-done((bf16[2,8,512,256]{3,2,0,1:T(8,128)(2,1)S(1)}, bf16[2,8,512,256]{3,2,0,1:T(8,128)(2,1)S(1)}, u32[]{:S(2)}, u32[]{:S(2)}) %collective-permute-start.9) | collective-permute-done | bytes 4194336 | tf_op jit(solution)/shard_map/ppermute | solution.py:16
  125.5 2.1 %collective-permute-start.10 = (bf16[2,8,256,256]{3,2,1,0:T(8,128)(2,1)S(1)}, bf16[2,8,256,256]{3,2,1,0:T(8,128)(2,1)S(1)}, u32[]{:S(2)}, u32[]{:S(2)}) collective-permute-start(bf16[2,8,256,256]{3,2,1,0:T(8,128)(2,1)S(1)} %fusion.3), channel_id=1, source_target_pairs={{0,2},{2,4},{4,6},{6,8},{8,10},{10,12},{12,14},{14,16},{16,18},{18... | collective-permute-start | bytes 6291464 | tf_op jit(solution)/shard_map/ppermute | solution.py:16
  128.0 4.8 %fusion.37 = f32[1,8,256,256]{3,2,1,0:T(8,128)S(1)} fusion(bf16[2,8,512,256]{3,2,0,1:T(8,128)(2,1)S(1)} %collective-permute-done.9, bf16[2,8,512,256]{3,2,1,0:T(8,128)(2,1)} %bitcast.37, f32[512,256]{1,0:T(8,128)S(1)} %collective-permute-done.12), kind=kOutput, calls=%fused_computation.45 | convolution fusion | flops 1080033280 | bytes 11010048 | tf_op jit(solution)/shard_map/pfwa,pfwb->fab/dot_general | solution.py:46
  132.8 3.7 %fusion.42 = f32[1,8,256,256]{3,2,1,0:T(8,128)S(1)} fusion(bf16[2,8,512,256]{3,2,1,0:T(8,128)(2,1)} %bitcast.37, f32[512,256]{1,0:T(8,128)S(1)} %collective-permute-done.12, bf16[1,8,512,256]{3,2,0,1:T(8,128)(2,1)S(1)} %get-tuple-element.22, bf16[1,8,512,256]{3,2,0,1:T(8,128)(2,1)S(1)} %get-tuple-element.21), kind=kOutput, calls=%fused_computation.46 | convolution fusion | flops 1082130432 | bytes 11010048 | tf_op jit(solution)/shard_map/pfwa,pfwb->fab/dot_general | solution.py:47
  137.0 1.4 collective-permute-start.13
  138.4 3.1 %convolution_bitcast_fusion = f32[1,1,8,256,256]{4,3,2,1,0:T(8,128)S(1)} fusion(bf16[2,8,512,256]{3,2,0,1:T(8,128)(2,1)S(1)} %multiply_convert_fusion, bf16[1,8,512,256]{3,2,0,1:T(8,128)(2,1)} %copy-done, bf16[1,8,512,256]{3,2,0,1:T(8,128)(2,1)S(1)} %get-tuple-element.21), kind=kOutput, calls=%fused_computation.38 | convolution fusion | flops 1075838976 | bytes 10485760 | tf_op jit(solution)/shard_map/pfwa,pfwb->fab/dot_general | solution.py:47
  141.5 1.4 convolution_bitcast_fusion.1
  143.5 3.9 %maximum_maximum_fusion = bf16[4,2,8,256,256]{4,3,2,1,0:T(8,128)(2,1)} fusion(bf16[1,2,8,256,256]{4,3,2,1,0:T(8,128)(2,1)S(1)} %fusion.10, bf16[1,2,8,256,256]{4,3,2,1,0:T(8,128)(2,1)S(1)} %bitcast.69, bf16[1,2,8,256,256]{4,3,2,1,0:T(8,128)(2,1)S(1)} %bitcast.68, bf16[4]{0:T(256)(128)(2,1)S(1)} %pad.5.clone), kind=kLoop, calls=%fused_computation | loop fusion | flops 12582912 | bytes 14680072 | tf_op jit(solution)/shard_map/stack | solution.py:85
  147.4 8.2 %collective-permute-done.10 = bf16[2,8,256,256]{3,2,1,0:T(8,128)(2,1)S(1)} collective-permute-done((bf16[2,8,256,256]{3,2,1,0:T(8,128)(2,1)S(1)}, bf16[2,8,256,256]{3,2,1,0:T(8,128)(2,1)S(1)}, u32[]{:S(2)}, u32[]{:S(2)}) %collective-permute-start.10) | collective-permute-done | bytes 2097184 | tf_op jit(solution)/shard_map/ppermute | solution.py:16
  155.6 2.0 %bitcast_dynamic-update-slice_fusion = bf16[4,2,8,256,256]{4,3,2,1,0:T(8,128)(2,1)} fusion(bf16[4,2,8,256,256]{4,3,2,1,0:T(8,128)(2,1)} %maximum_maximum_fusion, bf16[2,8,256,256]{3,2,1,0:T(8,128)(2,1)S(1)} %collective-permute-done.10, bf16[2,8,256,256]{3,2,1,0:T(8,128)(2,1)S(1)} %collective-permute-done.13, pred[]{:T(512)S(6)} %eq.19), kind=kLoop, calls=%fused_computation.35 | loop fusion | flops 1048576 | bytes 6291457 | tf_op jit(solution)/shard_map/dynamic_update_slice | solution.py:88
  (38 shorter events, 9.8 us)
Async XLA Ops:
  3.1 42.4 %copy-start.1 = (s32[512,256]{1,0:T(8,128)S(1)}, s32[512,256]{1,0:T(8,128)}, u32[]{:S(2)}) copy-start(s32[512,256]{1,0:T(8,128)} %param.3) | copy-start | bytes 1572868
  3.1 9.6 %collective-permute-start = (bf16[512,256]{1,0:T(8,128)(2,1)S(1)}, bf16[512,256]{1,0:T(8,128)(2,1)S(1)}, u32[]{:S(2)}, u32[]{:S(2)}) collective-permute-start(bf16[512,256]{1,0:T(8,128)(2,1)S(1)} %convert_element_type.74), channel_id=1, source_target_pairs={{0,32},{32,0},{64,96},{96,64},{128,160},{160,128},{192,224},{224,1... | collective-permute-start | bytes 786440 | tf_op jit(solution)/shard_map/ppermute | solution.py:61
  13.0 8.8 %collective-permute-start.2 = (f32[65536]{0:T(1024)S(1)}, f32[65536]{0:T(1024)S(1)}, u32[]{:S(2)}, u32[]{:S(2)}) collective-permute-start(f32[65536]{0:T(1024)S(1)} %bitcast.71), channel_id=1, source_target_pairs={{0,128},{32,160},{64,192},{96,224},{128,0},{160,32},{192,64},{224,... | collective-permute-start | bytes 786440 | tf_op jit(solution)/shard_map/ppermute | solution.py:34
  16.4 55.4 %collective-permute-start.7 = (bf16[8192,256]{1,0:T(8,128)(2,1)}, bf16[8192,256]{1,0:T(8,128)(2,1)}, u32[]{:S(2)}, u32[]{:S(2)}) collective-permute-start(bf16[8192,256]{1,0:T(8,128)(2,1)} %bitcast.65), channel_id=1, source_target_pairs={{0,1},{1,2},{2,3},{3,4},{4,5},{5,6},{6,7},{7,8},{8,9},{9,10},{10,1... | collective-permute-start | bytes 12582920 | tf_op jit(solution)/shard_map/ppermute | solution.py:16
  21.8 5.1 %collective-permute-start.3 = (f32[32768]{0:T(1024)S(1)}, f32[32768]{0:T(1024)S(1)}, u32[]{:S(2)}, u32[]{:S(2)}) collective-permute-start(f32[32768]{0:T(1024)S(1)} %slice_select_fusion), channel_id=1, source_target_pairs={{0,64},{32,96},{64,0},{96,32},{128,192},{160,224},{192,128},{224,1... | collective-permute-start | bytes 393224 | tf_op jit(solution)/shard_map/ppermute | solution.py:34
  26.9 5.1 %collective-permute-start.4 = (f32[32768]{0:T(1024)S(1)}, f32[32768]{0:T(1024)S(1)}, u32[]{:S(2)}, u32[]{:S(2)}) collective-permute-start(f32[32768]{0:T(1024)S(1)} %select_add_fusion), channel_id=1, source_target_pairs={{0,64},{32,96},{64,0},{96,32},{128,192},{160,224},{192,128},{224,1... | collective-permute-start | bytes 393224 | tf_op jit(solution)/shard_map/ppermute | solution.py:39
  32.0 13.4 %collective-permute-start.5 = (f32[65536]{0:T(1024)S(1)}, f32[65536]{0:T(1024)S(1)}, u32[]{:S(2)}, u32[]{:S(2)}) collective-permute-start(f32[65536]{0:T(1024)S(1)} %maximum_select_fusion.2), channel_id=1, source_target_pairs={{0,128},{32,160},{64,192},{96,224},{128,0},{160,32},{192,64},{224,... | collective-permute-start | bytes 786440 | tf_op jit(solution)/shard_map/ppermute | solution.py:39
  35.6 60.2 %collective-permute-start.1 = (bf16[8192,256]{1,0:T(8,128)(2,1)}, bf16[8192,256]{1,0:T(8,128)(2,1)}, u32[]{:S(2)}, u32[]{:S(2)}) collective-permute-start(bf16[8192,256]{1,0:T(8,128)(2,1)} %bitcast.66), channel_id=1, source_target_pairs={{0,30},{2,0},{4,2},{6,4},{8,6},{10,8},{12,10},{14,12},{16,14},{18,... | collective-permute-start | bytes 12582920 | tf_op jit(solution)/shard_map/ppermute | solution.py:16
  44.0 84.0 %collective-permute-start.11 = (bf16[8192,256]{1,0:T(8,128)(2,1)}, bf16[8192,256]{1,0:T(8,128)(2,1)}, u32[]{:S(2)}, u32[]{:S(2)}) collective-permute-start(bf16[8192,256]{1,0:T(8,128)(2,1)} %bitcast.67), channel_id=1, source_target_pairs={{1,0},{3,2},{5,4},{7,6},{9,8},{11,10},{13,12},{15,14},{17,16},{19,... | collective-permute-start | bytes 12582920 | tf_op jit(solution)/shard_map/ppermute | solution.py:16
  45.6 50.2 %collective-permute-start.6 = (f32[512,256]{1,0:T(8,128)S(1)}, f32[512,256]{1,0:T(8,128)S(1)}, u32[]{:S(2)}, u32[]{:S(2)}) collective-permute-start(f32[512,256]{1,0:T(8,128)S(1)} %get-tuple-element.20), channel_id=1, source_target_pairs={{0,30},{2,0},{4,2},{6,4},{8,6},{10,8},{12,10},{14,12},{16,14},{18,... | collective-permute-start | bytes 1572872 | tf_op jit(solution)/shard_map/ppermute | solution.py:16
  48.6 21.9 %collective-permute-start.8 = (bf16[512,256]{1,0:T(8,128)(2,1)S(1)}, bf16[512,256]{1,0:T(8,128)(2,1)S(1)}, u32[]{:S(2)}, u32[]{:S(2)}) collective-permute-start(bf16[512,256]{1,0:T(8,128)(2,1)S(1)} %get-tuple-element.19), channel_id=1, source_target_pairs={{0,1},{1,2},{2,3},{3,4},{4,5},{5,6},{6,7},{7,8},{8,9},{9,10},{10,1... | collective-permute-start | bytes 786440 | tf_op jit(solution)/shard_map/ppermute | solution.py:16
  70.5 57.5 %collective-permute-start.12 = (f32[512,256]{1,0:T(8,128)S(1)}, f32[512,256]{1,0:T(8,128)S(1)}, u32[]{:S(2)}, u32[]{:S(2)}) collective-permute-start(f32[512,256]{1,0:T(8,128)S(1)} %get-tuple-element.20), channel_id=1, source_target_pairs={{1,0},{3,2},{5,4},{7,6},{9,8},{11,10},{13,12},{15,14},{17,16},{19,... | collective-permute-start | bytes 1572872 | tf_op jit(solution)/shard_map/ppermute | solution.py:16
  74.9 50.7 %collective-permute-start.9 = (bf16[2,8,512,256]{3,2,0,1:T(8,128)(2,1)S(1)}, bf16[2,8,512,256]{3,2,0,1:T(8,128)(2,1)S(1)}, u32[]{:S(2)}, u32[]{:S(2)}) collective-permute-start(bf16[2,8,512,256]{3,2,0,1:T(8,128)(2,1)S(1)} %fusion.2), channel_id=1, source_target_pairs={{0,1},{1,2},{2,3},{3,4},{4,5},{5,6},{6,7},{7,8},{8,9},{9,10},{10,1... | collective-permute-start | bytes 12582920 | tf_op jit(solution)/shard_map/ppermute | solution.py:16
  125.5 30.0 %collective-permute-start.10 = (bf16[2,8,256,256]{3,2,1,0:T(8,128)(2,1)S(1)}, bf16[2,8,256,256]{3,2,1,0:T(8,128)(2,1)S(1)}, u32[]{:S(2)}, u32[]{:S(2)}) collective-permute-start(bf16[2,8,256,256]{3,2,1,0:T(8,128)(2,1)S(1)} %fusion.3), channel_id=1, source_target_pairs={{0,2},{2,4},{4,6},{6,8},{8,10},{10,12},{12,14},{14,16},{16,18},{18... | collective-permute-start | bytes 6291464 | tf_op jit(solution)/shard_map/ppermute | solution.py:16
  127.9 4.8 %copy-start = (bf16[1,8,512,256]{3,2,0,1:T(8,128)(2,1)}, bf16[1,8,512,256]{3,2,0,1:T(8,128)(2,1)S(1)}, u32[]{:S(2)}) copy-start(bf16[1,8,512,256]{3,2,0,1:T(8,128)(2,1)S(1)} %get-tuple-element.22) | copy-start | bytes 6291460
  137.0 18.6 %collective-permute-start.13 = (bf16[2,8,256,256]{3,2,1,0:T(8,128)(2,1)S(1)}, bf16[2,8,256,256]{3,2,1,0:T(8,128)(2,1)S(1)}, u32[]{:S(2)}, u32[]{:S(2)}) collective-permute-start(bf16[2,8,256,256]{3,2,1,0:T(8,128)(2,1)S(1)} %fusion.11), channel_id=1, source_target_pairs={{0,1},{2,3},{4,5},{6,7},{8,9},{10,11},{12,13},{14,15},{16,17},{18,... | collective-permute-start | bytes 6291464 | tf_op jit(solution)/shard_map/ppermute | solution.py:16
